TPU v7x, 128 devices: a whole 4x4x4 slice. The times are simulated.
128 devices in a mesh: pipe: 4 (over x_hi, core), dp: 16 (over y, z), tensor: 2 (over x_lo).
Axes of the slice: x: 4 (x_hi: 2, x_lo: 2; x = x_hi * 2 + x_lo), y: 4, z: 4, core: 2. Of those that a mesh axis runs over, the one named last changes fastest.
Arguments:
- hidden_states: bfloat16 [4, 4096, 8192], P('pipe', 'dp'), may hold values from -60 to 60
- norm_gain: bfloat16 [4, 8192], P('pipe'), may hold values from 0.5 to 2
- key_weight: bfloat16 [4, 8192, 512], P('pipe', 'dp', 'tensor'), may hold values from -0.0625 to 0.0625
- value_weight: bfloat16 [4, 8192, 512], P('pipe', 'dp', 'tensor'), may hold values from -0.0625 to 0.0625
- queries: bfloat16 [4, 4096, 4096], P('pipe', 'dp', 'tensor'), may hold values from -128 to 128
- context_cotangent: bfloat16 [4, 4096, 4096], P('pipe', 'dp', 'tensor'), may hold values from -96 to 96
- lengths: int32 [4, 16], P('pipe', 'dp'), may hold values from 64 to 256, as said below
- policy_logp: float32 [4, 16], P('pipe', 'dp'), may hold values from -90 to -30
- reference_logp: float32 [4, 16], P('pipe', 'dp'), may hold values from -90 to -30
Outputs:
- key_weight_grad: bfloat16 [4, 8192, 512], P('pipe', 'dp', 'tensor')
- value_weight_grad: bfloat16 [4, 8192, 512], P('pipe', 'dp', 'tensor')
- lower_cotangent: bfloat16 [4, 4096, 8192], P('pipe', 'dp')
Inputs may be any that keep to these rules, and one draw needn't show every extreme that they name: `lengths`: each sequence's live tokens; positions at or beyond it are padding.
All inputs are finite; a program needn't handle non-finite values.
Results may differ from a plain program's by a relative error of at most 0.015.
The roundings to bfloat16 on the way count: a program that leaves them out, or rounds other values in their place, can miss the bound.
Values may be sent and summed in bfloat16 or wider, within the bound.
No kernel may reach another device: no remote copies, remote signals or barrier semaphores. Data moves between devices by JAX's collectives and lax.ppermute only.
A program may use at most 128 MiB of HBM per device.

v0:
```python
import math

import jax
import jax.numpy as jnp
from jax import lax
from jax.sharding import PartitionSpec as P

HD = 128


npo_beta = 0.1
norm_eps = 1e-05
rope_base = 500000.0


def shifted(value, axis, steps):
    count = lax.axis_size(axis)
    leading, last = (max(0, -steps), min(count, count - steps))
    return lax.ppermute(value, axis, [(source, source + steps) for source in range(leading, last)])


def rope_tables(length, head_dim):
    positions = jnp.arange(length).astype(jnp.float32)
    freq_index = jnp.arange(head_dim // 2).astype(jnp.float32)
    inverse = 1.0 / rope_base ** (2.0 * freq_index / head_dim)
    angles = positions[:, None] * inverse[None, :]
    cosine = jnp.concatenate([jnp.cos(angles), jnp.cos(angles)], axis=1)
    sine = jnp.concatenate([jnp.sin(angles), jnp.sin(angles)], axis=1)
    return (cosine, sine)


def rotate_half(values):
    half = values.shape[-1] // 2
    return jnp.concatenate([-values[..., half:], values[..., :half]], axis=-1)


def rotate_back(values):
    half = values.shape[-1] // 2
    return jnp.concatenate([values[..., half:], -values[..., :half]], axis=-1)


def sequence_grads(query_seq, key_seq, value_seq, cotan_seq, length_seq, cosine, sine):
    seq_len, kv_heads, head_dim = key_seq.shape
    group = query_seq.shape[1] // kv_heads
    scale = 1.0 / math.sqrt(head_dim)
    query_g = query_seq.reshape(seq_len, kv_heads, group, head_dim)
    cotan_g = cotan_seq.reshape(seq_len, kv_heads, group, head_dim)
    scores = (
        jnp.einsum("ikgd,jkd->kgij", query_g, key_seq, preferred_element_type=jnp.float32) * scale
    )
    row_pos = jnp.arange(seq_len)[:, None]
    col_pos = jnp.arange(seq_len)[None, :]
    allowed = (col_pos <= row_pos) & (col_pos < length_seq)
    scores = jnp.where(allowed, scores, -1e30)
    highest = jnp.max(scores, axis=-1, keepdims=True)
    expd = jnp.where(allowed, jnp.exp(scores - highest), 0.0)
    probs = expd / jnp.sum(expd, axis=-1, keepdims=True)
    probs_low = probs.astype(jnp.bfloat16)
    value_grad = jnp.einsum(
        "kgij,ikgd->jkd", probs_low, cotan_g, preferred_element_type=jnp.float32
    ).astype(jnp.bfloat16)
    prob_grad = jnp.einsum("ikgd,jkd->kgij", cotan_g, value_seq, preferred_element_type=jnp.float32)
    centre = jnp.sum(probs * prob_grad, axis=-1, keepdims=True)
    score_grad = (probs * (prob_grad - centre) * scale).astype(jnp.bfloat16)
    rotated_grad = jnp.einsum(
        "kgij,ikgd->jkd", score_grad, query_g, preferred_element_type=jnp.float32
    )
    key_grad = rotated_grad * cosine[:, None, :] + rotate_back(rotated_grad * sine[:, None, :])
    return (key_grad.astype(jnp.bfloat16), value_grad)


def norm_backward(normed_grad, gain_f, nhat, inv_rms):
    gain_grad_in = normed_grad * gain_f
    centre = jnp.mean(gain_grad_in * nhat, axis=-1, keepdims=True)
    return ((gain_grad_in - nhat * centre) * inv_rms).astype(jnp.bfloat16)


def on_device(
    hidden_states,
    norm_gain,
    key_weight,
    value_weight,
    queries,
    context_cotangent,
    lengths,
    policy_logp,
    reference_logp,
):
    key_full, value_full = (
        lax.all_gather(key_weight[0], "dp", axis=0, tiled=True),
        lax.all_gather(value_weight[0], "dp", axis=0, tiled=True),
    )
    hidden = hidden_states[0]
    gain_f = norm_gain[0].astype(jnp.float32)
    tok_rows = hidden.shape[0]
    seq_count = lengths.shape[1]
    seq_len = tok_rows // seq_count
    kv_cols = key_full.shape[1]
    kv_local = kv_cols // HD
    q_local = queries.shape[2] // HD
    hidden_f = hidden.astype(jnp.float32)
    inv_rms = lax.rsqrt(jnp.mean(hidden_f * hidden_f, axis=-1, keepdims=True) + norm_eps)
    nhat = hidden_f * inv_rms
    normed = (nhat * gain_f).astype(jnp.bfloat16)
    key_raw = jnp.dot(normed, key_full, preferred_element_type=jnp.float32)
    values = jnp.dot(normed, value_full, preferred_element_type=jnp.float32).astype(jnp.bfloat16)
    cosine, sine = rope_tables(seq_len, HD)
    key_four = key_raw.reshape(seq_count, seq_len, kv_local, HD)
    keys = (
        key_four * cosine[None, :, None, :] + rotate_half(key_four) * sine[None, :, None, :]
    ).astype(jnp.bfloat16)
    total_seqs = seq_count * lax.axis_size("dp")
    seq_weight = 2.0 * jax.nn.sigmoid(npo_beta * (policy_logp[0] - reference_logp[0])) / total_seqs
    live = jnp.arange(seq_len)[None, :] < lengths[0][:, None]
    factor = jnp.where(live, seq_weight[:, None], 0.0)
    scaled = (
        context_cotangent[0].reshape(seq_count, seq_len, q_local, HD).astype(jnp.float32)
        * factor[:, :, None, None]
    ).astype(jnp.bfloat16)

    def one_sequence(items):
        return sequence_grads(items[0], items[1], items[2], items[3], items[4], cosine, sine)

    key_grad, value_grad = lax.map(
        one_sequence,
        (
            queries[0].reshape(seq_count, seq_len, q_local, HD),
            keys,
            values.reshape(seq_count, seq_len, kv_local, HD),
            scaled,
            lengths[0],
        ),
    )
    key_grad = key_grad.reshape(tok_rows, kv_cols)
    value_grad = value_grad.reshape(tok_rows, kv_cols)
    combined = jnp.concatenate([key_grad, value_grad], axis=1)
    grad_total = lax.psum_scatter(
        lax.dot_general(
            normed, combined, (((0,), (0,)), ((), ())), preferred_element_type=jnp.float32
        ).astype(jnp.bfloat16),
        "dp",
        scatter_dimension=0,
        tiled=True,
    )
    part = lax.dot_general(
        key_grad, key_full, (((1,), (1,)), ((), ())), preferred_element_type=jnp.float32
    )
    part = part + lax.dot_general(
        value_grad, value_full, (((1,), (1,)), ((), ())), preferred_element_type=jnp.float32
    )
    normed_grad = lax.psum(part.astype(jnp.bfloat16), "tensor").astype(jnp.float32)
    section_cot = norm_backward(normed_grad, gain_f, nhat, inv_rms)
    lower = shifted(section_cot, "pipe", -1)
    return (grad_total[:, :kv_cols][None], grad_total[:, kv_cols:][None], lower[None])


def solution(mesh):
    in_specs = (
        P("pipe", "dp", None),
        P("pipe", None),
        P("pipe", "dp", "tensor"),
        P("pipe", "dp", "tensor"),
        P("pipe", "dp", "tensor"),
        P("pipe", "dp", "tensor"),
        P("pipe", "dp"),
        P("pipe", "dp"),
        P("pipe", "dp"),
    )
    out_specs = (P("pipe", "dp", "tensor"), P("pipe", "dp", "tensor"), P("pipe", "dp", None))
    return jax.shard_map(
        on_device, mesh=mesh, in_specs=in_specs, out_specs=out_specs, check_vma=False
    )
```

profile of v0, /device:TPU:1, one launch (start us, length us, event | category | flops | bytes accessed | tf_op | source)
XLA Modules:
  0.0 366.0 jit_solution(2905376184291214419)
XLA Ops:
  10.7 0.8 mul.201
  13.4 2.3 copy.36
  16.2 3.1 fusion.11
  19.4 45.6 %all-gather.5.cloned.1.call-done = bf16[1,8192,256]{2,1,0:T(8,128)(2,1)} async-done(((bf16[1,512,256]{2,1,0:T(8,128)(2,1)}), bf16[1,8192,256]{2,1,0:T(8,128)(2,1)}) %all-gather.5.cloned.1.call-update) | async-done | bytes 4194320 | tf_op jit(solution)/shard_map/all_gather | solution.py:90
  65.1 5.5 %fusion.20 = f32[256,256]{0,1:T(8,128)S(1)} fusion(bf16[1,8192,256]{2,1,0:T(8,128)(2,1)} %all-gather.5.cloned.1.call-done, bf16[1,256,8192]{2,1,0:T(8,128)(2,1)} %param.9, f32[8192]{0:T(1024)S(1)} %bitcast.110, f32[256]{0:T(256)S(1)} %add_rsqrt_fusion), kind=kOutput, calls=%fused_computation.28 | convolution fusion | flops 1082130432 | bytes 8684544 | tf_op jit(solution)/shard_map/dot_general | solution.py:105
  70.6 0.8 copy.13
  71.6 0.8 copy.35
  73.2 45.3 %all-gather.7.cloned.1.call-done = bf16[1,8192,256]{2,1,0:T(8,128)(2,1)} async-done(((bf16[1,512,256]{2,1,0:T(8,128)(2,1)}), bf16[1,8192,256]{2,1,0:T(8,128)(2,1)}) %all-gather.7.cloned.1.call-update) | async-done | bytes 4194320 | tf_op jit(solution)/shard_map/all_gather | solution.py:91
  118.5 5.6 %fusion.37 = bf16[256,256]{0,1:T(8,128)(2,1)S(1)} fusion(bf16[1,8192,256]{2,1,0:T(8,128)(2,1)} %all-gather.7.cloned.1.call-done, bf16[1,256,8192]{2,1,0:T(8,128)(2,1)} %param.9, f32[8192]{0:T(1024)S(1)} %bitcast.111, f32[256]{0:T(256)S(1)} %add_rsqrt_fusion), kind=kOutput, calls=%fused_computation.44 | convolution fusion | flops 1082195968 | bytes 8553472 | tf_op jit(solution)/shard_map/dot_general | solution.py:106
  124.1 2.7 fusion.40
  126.8 5.0 %fusion.61 = (f32[2,8,256]{2,1,0:T(8,128)S(1)}, f32[2,8,256,256]{2,3,1,0:T(8,128)}) fusion(pred[256,256]{0,1:T(8,128)(4,1)S(1)} %fusion.49, bf16[256,2,8,128]{0,3,2,1:T(8,128)(2,1)S(1)} %bitcast.104, f32[256,2,64]{2,0,1:T(8,128)} %bitcast.115, f32[256,2,64]{2,0,1:T(8,128)} %negate_bitcast_fusion, f32[256,2,128]{2,0,1:T(8,128)} %copy.13, ...), kind=kOutput, calls=%fused_computation.80 | convolution fusion | flops 274006272 | bytes 6111232 | tf_op jit(solution)/shard_map/while/body/eval_jaxpr/sub | solution.py:56
  131.8 3.7 %fusion.34 = bf16[2,128,256]{2,1,0:T(8,128)(2,1)} fusion(f32[256,2,8,128]{0,3,2,1:T(8,128)S(1)} %bitcast.103, f32[256]{0:T(256)S(1)} %broadcast_select_fusion, f32[2,8,256,256]{2,3,1,0:T(8,128)} %get-tuple-element.42, f32[2,8,256]{2,1,0:T(8,128)S(1)} %get-tuple-element.41), kind=kOutput, calls=%fused_computation.43 | convolution fusion | flops 271646720 | bytes 6439936 | tf_op jit(solution)/shard_map/while/body/eval_jaxpr/kgij,ikgd->jkd/dot_general | solution.py:59
  135.5 7.2 %fusion.30 = f32[2,256,128]{1,2,0:T(8,128)S(1)} fusion(bf16[256,2,8,128]{0,3,2,1:T(8,128)(2,1)S(1)} %bitcast.105, f32[2,256,256,8]{2,1,3,0:T(8,128)} %fusion.40, f32[2,8,256,256]{2,3,1,0:T(8,128)} %get-tuple-element.42, f32[2,8,256]{2,1,0:T(8,128)S(1)} %get-tuple-element.41), kind=kOutput, calls=%fused_computation.41 | convolution fusion | flops 275779840 | bytes 9715712 | tf_op jit(solution)/shard_map/while/body/eval_jaxpr/kgij,ikgd->jkd/dot_general | solution.py:65
  142.9 3.6 fusion.18
  146.6 3.6 fusion.5
  150.3 7.9 %convolution_convert_fusion = bf16[8192,512]{1,0:T(8,128)(2,1)} fusion(bf16[256,256]{0,1:T(8,128)(2,1)S(1)} %bitcast.117, bf16[256,256]{0,1:T(8,128)(2,1)S(1)} %bitcast.109, bf16[1,256,8192]{2,1,0:T(8,128)(2,1)} %param.9, f32[8192]{0:T(1024)S(1)} %bitcast.112, f32[256]{0:T(256)S(1)} %add_rsqrt_fusion), kind=kOutput, calls=%fused_computation.2 | convolution fusion | flops 2160590848 | bytes 12878848 | tf_op jit(solution)/shard_map/dot_general | solution.py:138
  158.2 106.2 %all-reduce.2.cloned.1.call-done = bf16[256,8192]{1,0:T(8,128)(2,1)} async-done(((bf16[256,8192]{1,0:T(8,128)(2,1)}), bf16[256,8192]{1,0:T(8,128)(2,1)}) %all-reduce.2.cloned.1.call-update) | async-done | bytes 4194320 | tf_op jit(solution)/shard_map/psum | solution.py:151
  264.4 5.4 %fusion.7 = f32[256]{0:T(256)S(1)} fusion(bf16[256,8192]{1,0:T(8,128)(2,1)} %all-reduce.2.cloned.1.call-done, bf16[1,256,8192]{2,1,0:T(8,128)(2,1)} %param.9, f32[8192]{0:T(1024)S(1)} %bitcast.113, f32[256]{0:T(256)S(1)} %add_rsqrt_fusion), kind=kLoop, calls=%fused_computation.11 | loop fusion | flops 12582656 | bytes 8423424 | tf_op jit(solution)/shard_map/reduce_sum | solution.py:74
  270.3 2.3 fusion.10
  272.6 2.6 collective-permute-start
  275.2 48.8 %collective-permute-done = bf16[256,8192]{1,0:T(8,128)(2,1)} collective-permute-done((bf16[256,8192]{1,0:T(8,128)(2,1)S(1)}, bf16[256,8192]{1,0:T(8,128)(2,1)}, u32[]{:S(2)}, u32[]{:S(2)}) %collective-permute-start) | collective-permute-done | bytes 4194336 | tf_op jit(solution)/shard_map/ppermute | solution.py:19
  324.0 28.9 %reduce-scatter.2.cloned.1.call-done = bf16[512,512]{1,0:T(8,128)(2,1)} async-done(((bf16[8192,512]{1,0:T(8,128)(2,1)}), bf16[512,512]{1,0:T(8,128)(2,1)}) %reduce-scatter.2.cloned.1.call-update) | async-done | bytes 524304 | tf_op jit(solution)/shard_map/reduce_scatter | solution.py:137
  353.0 1.9 slice_bitcast_fusion
  354.8 4.6 %copy.42 = bf16[1,256,8192]{2,1,0:T(8,128)(2,1)} copy(bf16[1,256,8192]{2,1,0:T(8,128)(2,1)} %bitcast.30) | data formatting | bytes 8388608
  (38 shorter events, 5.6 us)
Async XLA Ops:
  7.2 8.5 %copy-start.3 = (bf16[1,256,2048]{2,1,0:T(8,128)(2,1)S(1)}, bf16[1,256,2048]{2,1,0:T(8,128)(2,1)}, u32[]{:S(2)}) copy-start(bf16[1,256,2048]{2,1,0:T(8,128)(2,1)} %param.14) | copy-start | bytes 3145732
  7.2 57.9 %all-gather.5.cloned.1.call-start = ((), (), s32[]{:S(2)}) async-start(), calls=%async_computation.3 | async-start | bytes 4456448 | tf_op jit(solution)/shard_map/all_gather | solution.py:90
  7.9 110.6 %all-gather.7.cloned.1.call-start = ((), (), s32[]{:S(2)}) async-start(), calls=%async_computation.4 | async-start | bytes 4456448 | tf_op jit(solution)/shard_map/all_gather | solution.py:91
  8.7 255.7 %all-reduce.2.cloned.1.call-start = ((), (), s32[]{:S(2)}) async-start(), calls=%async_computation.2 | async-start | bytes 8388608 | tf_op jit(solution)/shard_map/psum | solution.py:151
  124.1 2.7 copy-start.4
  142.9 3.7 %copy-start.2 = (bf16[1,8192,256]{2,1,0:T(8,128)(2,1)S(1)}, bf16[1,8192,256]{2,1,0:T(8,128)(2,1)}, u32[]{:S(2)}) copy-start(bf16[1,8192,256]{2,1,0:T(8,128)(2,1)} %all-gather.7.cloned.1.call-done) | copy-start | bytes 12582916
  142.9 3.7 %copy-start.5 = (bf16[2,128,256]{2,1,0:T(8,128)(2,1)S(1)}, bf16[2,128,256]{2,1,0:T(8,128)(2,1)}, u32[]{:S(2)}) copy-start(bf16[2,128,256]{2,1,0:T(8,128)(2,1)} %fusion.34) | copy-start | bytes 393220
  150.2 202.8 %reduce-scatter.2.cloned.1.call-start = ((), (), s32[]{:S(2)}) async-start(), calls=%async_computation.1 | async-start | bytes 8912896 | tf_op jit(solution)/shard_map/reduce_scatter | solution.py:137
  264.4 5.4 %copy-start = (bf16[1,256,8192]{2,1,0:T(8,128)(2,1)S(1)}, bf16[1,256,8192]{2,1,0:T(8,128)(2,1)}, u32[]{:S(2)}) copy-start(bf16[1,256,8192]{2,1,0:T(8,128)(2,1)} %param.9) | copy-start | bytes 12582916
  264.4 5.9 %copy-start.1 = (bf16[256,8192]{1,0:T(8,128)(2,1)S(1)}, bf16[256,8192]{1,0:T(8,128)(2,1)}, u32[]{:S(2)}) copy-start(bf16[256,8192]{1,0:T(8,128)(2,1)} %all-reduce.2.cloned.1.call-done) | copy-start | bytes 12582916
  272.6 51.4 %collective-permute-start = (bf16[256,8192]{1,0:T(8,128)(2,1)S(1)}, bf16[256,8192]{1,0:T(8,128)(2,1)}, u32[]{:S(2)}, u32[]{:S(2)}) collective-permute-start(bf16[256,8192]{1,0:T(8,128)(2,1)S(1)} %fusion.10), channel_id=1, source_target_pairs={{32,0},{64,32},{96,64},{33,1},{65,33},{97,65},{34,2},{66,34},{98,6... | collective-permute-start | bytes 12582920 | tf_op jit(solution)/shard_map/ppermute | solution.py:19
Sparse Core Ops, SparseCore 0:
  10.2 54.8 all-gather.4
  67.2 51.2 all-gather.6
  150.3 114.0 all-reduce.1
  268.0 84.8 reduce-scatter.1
where the time goes:
time: 367 us; the launch traced here: 366 us
  waiting for transfers between devices  276 us (75%)
  matrix products  45 us (12%)
  between operations  16 us (4%)
  local copies, waits for them, and re-layouts  13.2 us (4%)
  other arithmetic  12.8 us (3%)
    psum x1, waiting for transfers between devices, on_device(): lax.psum(part.astype(jnp.bfloat16), 'tensor').astype(jnp.float32)  106 us
    ppermute x1, waiting for transfers between devices, shifted(): lax.ppermute(value, axis, [(source, source + steps) for source in range(l...  48.8 us
    all_gather x1, waiting for transfers between devices, on_device(): lax.all_gather(key_weight[0], 'dp', axis=0, tiled=True)  45.6 us
    all_gather x1, waiting for transfers between devices, on_device(): lax.all_gather(value_weight[0], 'dp', axis=0, tiled=True)  45.3 us
    reduce_scatter x1, waiting for transfers between devices, on_device(): lax.psum_scatter(lax.dot_general(normed, combined, (((0,), (0,)), ((), ()...  28.9 us
    dot_general x1, matrix products, on_device(): lax.dot_general(normed, combined, (((0,), (0,)), ((), ())), preferred_ele...  7.92 us
  transfers between devices with their start and end apart: 5, of which 5 were waited for; matrix products, arithmetic and copies ran while one was open for 9% of the time, Pallas kernels for 0%

commit v1 on v0

--- a/solution.py
+++ b/solution.py
@@ -86,10 +86,10 @@
     policy_logp,
     reference_logp,
 ):
-    key_full, value_full = (
-        lax.all_gather(key_weight[0], "dp", axis=0, tiled=True),
-        lax.all_gather(value_weight[0], "dp", axis=0, tiled=True),
+    both_full = lax.all_gather(
+        jnp.stack([key_weight[0], value_weight[0]]), "dp", axis=1, tiled=True
     )
+    key_full, value_full = both_full[0], both_full[1]
     hidden = hidden_states[0]
     gain_f = norm_gain[0].astype(jnp.float32)
     tok_rows = hidden.shape[0]
@@ -148,7 +148,12 @@
     part = part + lax.dot_general(
         value_grad, value_full, (((1,), (1,)), ((), ())), preferred_element_type=jnp.float32
     )
-    normed_grad = lax.psum(part.astype(jnp.bfloat16), "tensor").astype(jnp.float32)
+    part_low = part.astype(jnp.bfloat16)
+    count = lax.axis_size("tensor")
+    normed_grad = part_low.astype(jnp.float32)
+    for step in range(1, count):
+        pairs = [(source, (source + step) % count) for source in range(count)]
+        normed_grad = normed_grad + lax.ppermute(part_low, "tensor", pairs).astype(jnp.float32)
     section_cot = norm_backward(normed_grad, gain_f, nhat, inv_rms)
     lower = shifted(section_cot, "pipe", -1)
     return (grad_total[:, :kv_cols][None], grad_total[:, kv_cols:][None], lower[None])

time: 367 us -> 297 us (0.81)
  waiting for transfers between devices: 276 us -> 203 us
    psum x1 -> x0, waiting for transfers between devices: 106 us -> none  [on_device(): lax.psum(part.astype(jnp.bfloat16), 'tensor').astype(jnp.float32)]
    ppermute x0 -> x1, waiting for transfers between devices: none -> 90.3 us  [on_device(): lax.ppermute(part_low, 'tensor', pairs).astype(jnp.float32)]
    reduce_scatter x1, waiting for transfers between devices: 28.9 us -> 0.01 us  [on_device(): lax.psum_scatter(lax.dot_general(normed, combined, (((0,), (0,)), ((), ()...]
    all_gather x2 -> x1, waiting for transfers between devices: 90.9 us -> 64.3 us  [on_device(): lax.all_gather(jnp.stack([key_weight[0], value_weight[0]]), 'dp', axis=1,...]
    unnamed x15 -> x13, local copies, waits for them, and re-layouts: 6.16 us -> 7.55 us
  transfers between devices with their start and end apart: 5 -> 4, of which waited for: 5 -> 3; matrix products, arithmetic and copies ran while one was open for 9% -> 7% of each run, Pallas kernels for 0% -> 0%
where the time goes in v1:
time: 297 us
  waiting for transfers between devices  203 us (68%)
  matrix products  45.2 us (15%)
  between operations  16.3 us (5%)
  local copies, waits for them, and re-layouts  14.5 us (5%)
  other arithmetic  12.8 us (4%)
  starting transfers between devices  4.8 us (2%)
    ppermute x1, waiting for transfers between devices, on_device(): lax.ppermute(part_low, 'tensor', pairs).astype(jnp.float32)  90.3 us
    all_gather x1, waiting for transfers between devices, on_device(): lax.all_gather(jnp.stack([key_weight[0], value_weight[0]]), 'dp', axis=1,...  64.3 us
    ppermute x1, waiting for transfers between devices, shifted(): lax.ppermute(value, axis, [(source, source + steps) for source in range(l...  48.8 us
    dot_general x1, matrix products, on_device(): lax.dot_general(normed, combined, (((0,), (0,)), ((), ())), preferred_ele...  8.12 us
    unnamed x13, local copies, waits for them, and re-layouts  7.55 us
    dot_general x1, matrix products, sequence_grads(): jnp.einsum('kgij,ikgd->jkd', score_grad, query_g, preferred_element_type=...  7.26 us
  transfers between devices with their start and end apart: 4, of which 3 were waited for; matrix products, arithmetic and copies ran while one was open for 7% of the time, Pallas kernels for 0%

profile of v1, /device:TPU:1, one launch (start us, length us, event | category | flops | bytes accessed | tf_op | source)
XLA Modules:
  0.0 297.0 jit_solution(5778648964715060964)
XLA Ops:
  7.2 2.0 pad_maximum_fusion
  14.0 2.3 copy.36
  16.8 3.1 %fusion.13 = f32[256]{0:T(256)S(1)} fusion(bf16[1,256,8192]{2,1,0:T(8,128)(2,1)} %param.9), kind=kLoop, calls=%fused_computation.17 | loop fusion | flops 6291200 | bytes 4195328 | tf_op jit(solution)/shard_map/reduce_sum | solution.py:102
  20.0 64.3 %all-gather.2.cloned.1.call-done = bf16[2,8192,256]{2,1,0:T(8,128)(2,1)} async-done(((bf16[2,512,256]{2,1,0:T(8,128)(2,1)}), bf16[2,8192,256]{2,1,0:T(8,128)(2,1)}) %all-gather.2.cloned.1.call-update) | async-done | bytes 8388624 | tf_op jit(solution)/shard_map/all_gather | solution.py:89
  84.3 5.5 %fusion.24 = f32[256,256]{0,1:T(8,128)S(1)} fusion(bf16[2,8192,256]{2,1,0:T(8,128)(2,1)} %all-gather.2.cloned.1.call-done, bf16[1,256,8192]{2,1,0:T(8,128)(2,1)} %param.9, f32[8192]{0:T(1024)S(1)} %bitcast.131, f32[256]{0:T(256)S(1)} %add_rsqrt_fusion), kind=kOutput, calls=%fused_computation.34 | convolution fusion | flops 1082130432 | bytes 8684544 | tf_op jit(solution)/shard_map/dot_general | solution.py:105
  89.9 0.8 copy.13
  91.6 0.8 copy.35
  92.4 5.6 %fusion.43 = bf16[256,256]{0,1:T(8,128)(2,1)S(1)} fusion(bf16[2,8192,256]{2,1,0:T(8,128)(2,1)} %all-gather.2.cloned.1.call-done, bf16[1,256,8192]{2,1,0:T(8,128)(2,1)} %param.9, f32[8192]{0:T(1024)S(1)} %bitcast.132, f32[256]{0:T(256)S(1)} %add_rsqrt_fusion), kind=kOutput, calls=%fused_computation.49 | convolution fusion | flops 1082195968 | bytes 8553472 | tf_op jit(solution)/shard_map/dot_general | solution.py:106
  98.0 2.7 fusion.46
  100.7 5.0 %fusion.64 = (f32[2,8,256]{2,1,0:T(8,128)S(1)}, f32[2,8,256,256]{2,3,1,0:T(8,128)}) fusion(pred[256,256]{0,1:T(8,128)(4,1)S(1)} %fusion.55, bf16[256,2,8,128]{0,3,2,1:T(8,128)(2,1)S(1)} %bitcast.125, f32[256,2,64]{2,0,1:T(8,128)} %bitcast.136, f32[256,2,64]{2,0,1:T(8,128)} %negate_bitcast_fusion, f32[256,2,128]{2,0,1:T(8,128)} %copy.13, ...), kind=kOutput, calls=%fused_computation.86 | convolution fusion | flops 274006272 | bytes 6111232 | tf_op jit(solution)/shard_map/while/body/eval_jaxpr/sub | solution.py:56
  105.8 3.7 %fusion.40 = bf16[2,128,256]{2,1,0:T(8,128)(2,1)} fusion(f32[256,2,8,128]{0,3,2,1:T(8,128)S(1)} %bitcast.123, f32[256]{0:T(256)S(1)} %broadcast_select_fusion, f32[2,8,256,256]{2,3,1,0:T(8,128)} %get-tuple-element.42, f32[2,8,256]{2,1,0:T(8,128)S(1)} %get-tuple-element.41), kind=kOutput, calls=%fused_computation.48 | convolution fusion | flops 271646720 | bytes 6439936 | tf_op jit(solution)/shard_map/while/body/eval_jaxpr/kgij,ikgd->jkd/dot_general | solution.py:59
  109.5 7.3 %fusion.36 = f32[2,256,128]{1,2,0:T(8,128)S(1)} fusion(bf16[256,2,8,128]{0,3,2,1:T(8,128)(2,1)S(1)} %bitcast.126, f32[2,256,256,8]{2,1,3,0:T(8,128)} %fusion.46, f32[2,8,256,256]{2,3,1,0:T(8,128)} %get-tuple-element.42, f32[2,8,256]{2,1,0:T(8,128)S(1)} %get-tuple-element.41), kind=kOutput, calls=%fused_computation.46 | convolution fusion | flops 275779840 | bytes 9715712 | tf_op jit(solution)/shard_map/while/body/eval_jaxpr/kgij,ikgd->jkd/dot_general | solution.py:65
  116.9 8.1 %convolution_convert_fusion = bf16[8192,512]{1,0:T(8,128)(2,1)} fusion(bf16[1,256,8192]{2,1,0:T(8,128)(2,1)} %param.9, f32[8192]{0:T(1024)S(1)} %bitcast.133, f32[256]{0:T(256)S(1)} %add_rsqrt_fusion, bf16[256,256]{0,1:T(8,128)(2,1)S(1)} %bitcast.137, bf16[256,256]{0,1:T(8,128)(2,1)S(1)} %bitcast.129), kind=kOutput, calls=%fused_computation.2 | convolution fusion | flops 2160590848 | bytes 12878848 | tf_op jit(solution)/shard_map/dot_general | solution.py:138
  125.0 3.5 %fusion.23 = f32[256,8192]{1,0:T(8,128)S(1)} fusion(bf16[256,256]{0,1:T(8,128)(2,1)S(1)} %bitcast.130, bf16[2,8192,256]{2,1,0:T(8,128)(2,1)} %all-gather.2.cloned.1.call-done), kind=kOutput, calls=%fused_computation.33 | convolution fusion | flops 1073741824 | bytes 12713984 | tf_op jit(solution)/shard_map/dot_general | solution.py:145
  128.5 3.8 %fusion.7 = bf16[256,8192]{1,0:T(8,128)(2,1)S(1)} fusion(f32[256,8192]{1,0:T(8,128)S(1)} %fusion.23, bf16[256,256]{0,1:T(8,128)(2,1)S(1)} %bitcast.138, bf16[2,8192,256]{2,1,0:T(8,128)(2,1)} %all-gather.2.cloned.1.call-done), kind=kOutput, calls=%fused_computation.11 | convolution fusion | flops 1077936128 | bytes 16908288 | tf_op jit(solution)/shard_map/dot_general | solution.py:148
  132.3 1.3 collective-permute-start
  133.6 90.3 %collective-permute-done = bf16[256,8192]{1,0:T(8,128)(2,1)S(1)} collective-permute-done((bf16[256,8192]{1,0:T(8,128)(2,1)S(1)}, bf16[256,8192]{1,0:T(8,128)(2,1)S(1)}, u32[]{:S(2)}, u32[]{:S(2)}) %collective-permute-start) | collective-permute-done | bytes 4194336 | tf_op jit(solution)/shard_map/ppermute | solution.py:156
  223.9 2.6 fusion.9
  226.5 3.0 %fusion.12 = bf16[256,8192]{1,0:T(8,128)(2,1)S(1)} fusion(bf16[1,256,8192]{2,1,0:T(8,128)(2,1)S(1)} %copy-done, bf16[256,8192]{1,0:T(8,128)(2,1)S(1)} %collective-permute-done, bf16[256,8192]{1,0:T(8,128)(2,1)S(1)} %fusion.7, f32[256]{0:T(256)S(1)} %broadcast_multiply_fusion, f32[8192]{0:T(1024)S(1)} %bitcast.135, f32[256]{0:T(256)S(1)} %add_rsqrt_fusion), kind=kLoop, calls=%fused_computation.16 | loop fusion | flops 20971520 | bytes 16812032 | tf_op jit(solution)/shard_map/convert_element_type | solution.py:75
  229.5 3.5 %collective-permute-start.1 = (bf16[256,8192]{1,0:T(8,128)(2,1)S(1)}, bf16[256,8192]{1,0:T(8,128)(2,1)S(1)}, u32[]{:S(2)}, u32[]{:S(2)}) collective-permute-start(bf16[256,8192]{1,0:T(8,128)(2,1)S(1)} %fusion.12), channel_id=1, source_target_pairs={{32,0},{64,32},{96,64},{33,1},{65,33},{97,65},{34,2},{66,34},{98,6... | collective-permute-start | bytes 12582920 | tf_op jit(solution)/shard_map/ppermute | solution.py:19
  232.9 48.8 %collective-permute-done.1 = bf16[256,8192]{1,0:T(8,128)(2,1)S(1)} collective-permute-done((bf16[256,8192]{1,0:T(8,128)(2,1)S(1)}, bf16[256,8192]{1,0:T(8,128)(2,1)S(1)}, u32[]{:S(2)}, u32[]{:S(2)}) %collective-permute-start.1) | collective-permute-done | bytes 4194336 | tf_op jit(solution)/shard_map/ppermute | solution.py:19
  281.7 1.9 copy-done.1
  283.6 1.9 slice_bitcast_fusion.8
  285.5 4.6 %copy.41 = bf16[1,256,8192]{2,1,0:T(8,128)(2,1)} copy(bf16[1,256,8192]{2,1,0:T(8,128)(2,1)} %bitcast.124) | data formatting | bytes 8388608
  (33 shorter events, 4.4 us)
Async XLA Ops:
  7.2 9.1 %copy-start.2 = (bf16[1,256,2048]{2,1,0:T(8,128)(2,1)S(1)}, bf16[1,256,2048]{2,1,0:T(8,128)(2,1)}, u32[]{:S(2)}) copy-start(bf16[1,256,2048]{2,1,0:T(8,128)(2,1)} %param.14) | copy-start | bytes 3145732
  7.2 77.2 %all-gather.2.cloned.1.call-start = ((), (), s32[]{:S(2)}) async-start(), calls=%async_computation.1 | async-start | bytes 8912896 | tf_op jit(solution)/shard_map/all_gather | solution.py:89
  9.3 274.4 %reduce-scatter.2.cloned.1.call-start = ((), (), s32[]{:S(2)}) async-start(), calls=%async_computation.2 | async-start | bytes 8912896 | tf_op jit(solution)/shard_map/reduce_scatter | solution.py:137
  98.0 2.7 copy-start.3
  109.5 7.4 %copy-start.4 = (bf16[2,128,256]{2,1,0:T(8,128)(2,1)S(1)}, bf16[2,128,256]{2,1,0:T(8,128)(2,1)}, u32[]{:S(2)}) copy-start(bf16[2,128,256]{2,1,0:T(8,128)(2,1)} %fusion.40) | copy-start | bytes 393220
  128.5 95.3 %copy-start = (bf16[1,256,8192]{2,1,0:T(8,128)(2,1)S(1)}, bf16[1,256,8192]{2,1,0:T(8,128)(2,1)}, u32[]{:S(2)}) copy-start(bf16[1,256,8192]{2,1,0:T(8,128)(2,1)} %param.9) | copy-start | bytes 12582916
  132.3 91.5 %collective-permute-start = (bf16[256,8192]{1,0:T(8,128)(2,1)S(1)}, bf16[256,8192]{1,0:T(8,128)(2,1)S(1)}, u32[]{:S(2)}, u32[]{:S(2)}) collective-permute-start(bf16[256,8192]{1,0:T(8,128)(2,1)S(1)} %fusion.7), channel_id=1, source_target_pairs={{0,1},{1,0},{2,3},{3,2},{4,5},{5,4},{6,7},{7,6},{8,9},{9,8},{10,11... | collective-permute-start | bytes 12582920 | tf_op jit(solution)/shard_map/ppermute | solution.py:156
  229.5 52.2 %collective-permute-start.1 = (bf16[256,8192]{1,0:T(8,128)(2,1)S(1)}, bf16[256,8192]{1,0:T(8,128)(2,1)S(1)}, u32[]{:S(2)}, u32[]{:S(2)}) collective-permute-start(bf16[256,8192]{1,0:T(8,128)(2,1)S(1)} %fusion.12), channel_id=1, source_target_pairs={{32,0},{64,32},{96,64},{33,1},{65,33},{97,65},{34,2},{66,34},{98,6... | collective-permute-start | bytes 12582920 | tf_op jit(solution)/shard_map/ppermute | solution.py:19
  281.7 1.9 copy-start.1
Sparse Core Ops, SparseCore 0:
  10.2 74.0 all-gather.1
  125.1 83.6 reduce-scatter.1

commit v2 on v1

--- a/solution.py
+++ b/solution.py
@@ -142,20 +142,50 @@
         scatter_dimension=0,
         tiled=True,
     )
-    part = lax.dot_general(
-        key_grad, key_full, (((1,), (1,)), ((), ())), preferred_element_type=jnp.float32
-    )
-    part = part + lax.dot_general(
-        value_grad, value_full, (((1,), (1,)), ((), ())), preferred_element_type=jnp.float32
-    )
-    part_low = part.astype(jnp.bfloat16)
-    count = lax.axis_size("tensor")
-    normed_grad = part_low.astype(jnp.float32)
-    for step in range(1, count):
-        pairs = [(source, (source + step) % count) for source in range(count)]
-        normed_grad = normed_grad + lax.ppermute(part_low, "tensor", pairs).astype(jnp.float32)
-    section_cot = norm_backward(normed_grad, gain_f, nhat, inv_rms)
-    lower = shifted(section_cot, "pipe", -1)
+    n_pipe = lax.axis_size("pipe")
+    n_tensor = lax.axis_size("tensor")
+    chunks = 4
+    rows = tok_rows // chunks
+    exchange_steps = [
+        [
+            (p * n_tensor + t, p * n_tensor + (t + step) % n_tensor)
+            for p in range(1, n_pipe)
+            for t in range(n_tensor)
+        ]
+        for step in range(1, n_tensor)
+    ]
+    shift_pairs = [
+        ((p + 1) * n_tensor + (t if (p + 1) // 2 == p // 2 else n_tensor - 1 - t), p * n_tensor + t)
+        for p in range(n_pipe - 1)
+        for t in range(n_tensor)
+    ]
+    lowers = []
+    held = None
+    for c in range(chunks):
+        sl = slice(c * rows, (c + 1) * rows)
+        part = lax.dot_general(
+            key_grad[sl], key_full, (((1,), (1,)), ((), ())), preferred_element_type=jnp.float32
+        )
+        part = part + lax.dot_general(
+            value_grad[sl], value_full, (((1,), (1,)), ((), ())), preferred_element_type=jnp.float32
+        )
+        part_low = part.astype(jnp.bfloat16)
+        if held is not None:
+            if len(lowers) > 0:
+                part_low, held, lowers[-1] = lax.optimization_barrier(
+                    (part_low, held, lowers[-1])
+                )
+            else:
+                part_low, held = lax.optimization_barrier((part_low, held))
+            lowers.append(lax.ppermute(held, ("pipe", "tensor"), shift_pairs))
+        normed_grad = part_low.astype(jnp.float32)
+        for pairs in exchange_steps:
+            normed_grad = normed_grad + lax.ppermute(
+                part_low, ("pipe", "tensor"), pairs
+            ).astype(jnp.float32)
+        held = norm_backward(normed_grad, gain_f, nhat[sl], inv_rms[sl])
+    lowers.append(lax.ppermute(held, ("pipe", "tensor"), shift_pairs))
+    lower = jnp.concatenate(lowers, axis=0)
     return (grad_total[:, :kv_cols][None], grad_total[:, kv_cols:][None], lower[None])
 
 

time: 297 us -> 263 us (0.89)
  waiting for transfers between devices: 203 us -> 146 us
  starting transfers between devices: 4.8 us -> 17.7 us
  other arithmetic: 12.8 us -> 19.9 us
  matrix products: 45.2 us -> 48.5 us
    ppermute x2 -> x8, waiting for transfers between devices: 139 us -> 79.8 us  [the longest x4 50.4 us: on_device(): lowers.append(lax.ppermute(held, ('pipe', 'tensor'), shift_pairs))]
    dot_general x2 -> x9, matrix products: 7.3 us -> 22.3 us  [the longest x4 10.4 us: on_device(): lax.dot_general(value_grad[sl], value_full, (((1,), (1,)), ((), ())), pre...]
    ppermute x2 -> x8, starting transfers between devices: 4.72 us -> 17.6 us  [the longest x4 9.93 us: on_device(): lax.ppermute(part_low, ('pipe', 'tensor'), pairs).astype(jnp.float32)]
    sub x1 -> x0, matrix products: 5.04 us -> none  [sequence_grads(): expd = jnp.where(allowed, jnp.exp(scores - highest), 0.0)]
    dot_general x1, matrix products: 5.58 us -> 2.24 us  [on_device(): jnp.dot(normed, value_full, preferred_element_type=jnp.float32)]
    mul x0 -> x1, other arithmetic: none -> 3.25 us  [on_device(): nhat = hidden_f * inv_rms]
    unnamed x13 -> x20, local copies, waits for them, and re-layouts: 7.55 us -> 7 us
  transfers between devices with their start and end apart: 4 -> 10, of which waited for: 3 -> 8; matrix products, arithmetic and copies ran while one was open for 7% -> 14% of each run, Pallas kernels for 0% -> 0%
where the time goes in v2:
time: 263 us; the launch traced here: 262 us
  waiting for transfers between devices  146 us (56%)
  matrix products  48.5 us (18%)
  other arithmetic  19.9 us (8%)
  starting transfers between devices  17.7 us (7%)
  between operations  16.4 us (6%)
  local copies, waits for them, and re-layouts  14.1 us (5%)
    all_gather x1, waiting for transfers between devices, on_device(): lax.all_gather(jnp.stack([key_weight[0], value_weight[0]]), 'dp', axis=1,...  66 us
    ppermute x4, waiting for transfers between devices, on_device(): lowers.append(lax.ppermute(held, ('pipe', 'tensor'), shift_pairs))  50.4 us
    ppermute x4, waiting for transfers between devices, on_device(): lax.ppermute(part_low, ('pipe', 'tensor'), pairs).astype(jnp.float32)  29.4 us
    dot_general x4, matrix products, on_device(): lax.dot_general(value_grad[sl], value_full, (((1,), (1,)), ((), ())), pre...  10.4 us
    ppermute x4, starting transfers between devices, on_device(): lax.ppermute(part_low, ('pipe', 'tensor'), pairs).astype(jnp.float32)  9.93 us
    dot_general x4, matrix products, on_device(): lax.dot_general(key_grad[sl], key_full, (((1,), (1,)), ((), ())), preferr...  9.88 us
    ppermute x4, starting transfers between devices, on_device(): lowers.append(lax.ppermute(held, ('pipe', 'tensor'), shift_pairs))  7.67 us
    dot_general x1, matrix products, sequence_grads(): jnp.einsum('kgij,ikgd->jkd', score_grad, query_g, preferred_element_type=...  7.62 us
  transfers between devices with their start and end apart: 10, of which 8 were waited for; matrix products, arithmetic and copies ran while one was open for 14% of the time, Pallas kernels for 0%

profile of v2, /device:TPU:1, one launch (start us, length us, event | category | flops | bytes accessed | tf_op | source)
XLA Modules:
  0.0 262.5 jit_solution(6118094384386589423)
XLA Ops:
  15.7 3.1 %fusion.8 = f32[256]{0:T(256)S(1)} fusion(bf16[1,256,8192]{2,1,0:T(8,128)(2,1)} %param.9), kind=kLoop, calls=%fused_computation.15 | loop fusion | flops 6291200 | bytes 4195328 | tf_op jit(solution)/shard_map/reduce_sum | solution.py:102
  18.9 66.0 %all-gather.2.cloned.1.call-done = bf16[2,8192,256]{2,1,0:T(8,128)(2,1)} async-done(((bf16[2,512,256]{2,1,0:T(8,128)(2,1)}), bf16[2,8192,256]{2,1,0:T(8,128)(2,1)}) %all-gather.2.cloned.1.call-update) | async-done | bytes 8388624 | tf_op jit(solution)/shard_map/all_gather | solution.py:89
  84.9 6.2 %fusion.21 = f32[256,256]{0,1:T(8,128)} fusion(bf16[2,8192,256]{2,1,0:T(8,128)(2,1)} %all-gather.2.cloned.1.call-done, bf16[1,256,8192]{2,1,0:T(8,128)(2,1)} %param.9, f32[8192]{0:T(1024)S(1)} %bitcast.147, f32[256]{0:T(256)S(1)} %add_rsqrt_fusion), kind=kOutput, calls=%fused_computation.36 | convolution fusion | flops 1082130432 | bytes 8684544 | tf_op jit(solution)/shard_map/dot_general | solution.py:105
  105.3 2.2 fusion.39
  107.5 2.8 %fusion.45 = f32[2,256,256,8]{2,1,3,0:T(8,128)} fusion(bf16[256,2,128,1]{0,2,3,1:T(8,128)(2,1)S(1)} %bitcast.168, f32[256,2,8,128]{0,3,2,1:T(8,128)S(1)} %bitcast.143, f32[256]{0:T(256)S(1)} %broadcast_select_fusion), kind=kOutput, calls=%fused_computation.67 | convolution fusion | flops 269484032 | bytes 6423552 | tf_op jit(solution)/shard_map/while/body/eval_jaxpr/ikgd,jkd->kgij/dot_general | solution.py:62
  111.8 7.6 %fusion.32 = f32[2,256,128]{2,1,0:T(8,128)S(1)} fusion(f32[2,256,256,8]{2,1,3,0:T(8,128)} %fusion.45, bf16[256,2,8,128]{3,2,1,0:T(8,128)(2,1)S(1)} %bitcast.146, f32[2,8,256,256]{2,3,1,0:T(8,128)} %copy-done.3, f32[2,8,256]{2,1,0:T(8,128)S(1)} %get-tuple-element.69), kind=kOutput, calls=%fused_computation.59 | convolution fusion | flops 275779840 | bytes 9715712 | tf_op jit(solution)/shard_map/while/body/eval_jaxpr/kgij,ikgd->jkd/dot_general | solution.py:65
  120.0 3.6 %fusion.18 = f32[64,8192]{1,0:T(8,128)S(1)} fusion(bf16[2,8192,256]{2,1,0:T(8,128)(2,1)} %all-gather.2.cloned.1.call-done, bf16[2,8,8,128]{3,2,1,0:T(8,128)(2,1)S(1)} %get-tuple-element.59), kind=kOutput, calls=%fused_computation.33 | convolution fusion | flops 268435456 | bytes 6324224 | tf_op jit(solution)/shard_map/dot_general | solution.py:166
  123.6 3.8 %fusion.6 = bf16[64,8192]{1,0:T(8,128)(2,1)S(1)} fusion(f32[64,8192]{1,0:T(8,128)S(1)} %fusion.18, bf16[64,256]{0,1:T(8,128)(2,1)S(1)} %bitcast.167, bf16[2,8192,256]{2,1,0:T(8,128)(2,1)} %all-gather.2.cloned.1.call-done), kind=kOutput, calls=%fused_computation.13 | convolution fusion | flops 269484032 | bytes 7372800 | tf_op jit(solution)/shard_map/dot_general | solution.py:169
  127.4 3.3 %collective-permute-start = (bf16[64,8192]{1,0:T(8,128)(2,1)S(1)}, bf16[64,8192]{1,0:T(8,128)(2,1)S(1)}, u32[]{:S(2)}, u32[]{:S(2)}) collective-permute-start(bf16[64,8192]{1,0:T(8,128)(2,1)S(1)} %fusion.6), channel_id=1, source_target_pairs={{32,33},{33,32},{64,65},{65,64},{96,97},{97,96},{34,35},{35,34},{6... | collective-permute-start | bytes 3145736 | tf_op jit(solution)/shard_map/ppermute | solution.py:183
  130.6 5.8 %convolution_convert_fusion = bf16[8192,512]{1,0:T(8,128)(2,1)} fusion(f32[8192]{0:T(1024)S(1)} %bitcast.149, bf16[256,256]{0,1:T(8,128)(2,1)S(1)} %bitcast.163, bf16[256,256]{0,1:T(8,128)(2,1)S(1)} %bitcast.169, bf16[1,256,8192]{2,1,0:T(8,128)(2,1)S(1)} %copy-done.1, f32[256]{0:T(256)S(1)} %add_rsqrt_fusion), kind=kOutput, calls=%fused_computation.2 | convolution fusion | flops 2160590848 | bytes 12878848 | tf_op jit(solution)/shard_map/dot_general | solution.py:138
  136.5 3.3 %fusion.2 = f32[256,8192]{1,0:T(8,128)S(1)} fusion(bf16[1,256,8192]{2,1,0:T(8,128)(2,1)} %param.9, f32[256]{0:T(256)S(1)} %add_rsqrt_fusion), kind=kLoop, calls=%fused_computation.5 | loop fusion | flops 4194304 | bytes 12583936 | tf_op jit(solution)/shard_map/mul | solution.py:103
  139.8 3.6 %fusion.19 = f32[64,8192]{1,0:T(8,128)S(1)} fusion(bf16[2,8192,256]{2,1,0:T(8,128)(2,1)} %all-gather.2.cloned.1.call-done, bf16[2,8,8,128]{3,2,1,0:T(8,128)(2,1)S(1)} %get-tuple-element.61), kind=kOutput, calls=%fused_computation.34 | convolution fusion | flops 268435456 | bytes 6324224 | tf_op jit(solution)/shard_map/dot_general | solution.py:166
  143.4 3.8 %fusion.5 = bf16[64,8192]{1,0:T(8,128)(2,1)S(1)} fusion(f32[64,8192]{1,0:T(8,128)S(1)} %fusion.19, bf16[64,256]{0,1:T(8,128)(2,1)S(1)} %bitcast.166, bf16[2,8192,256]{2,1,0:T(8,128)(2,1)} %all-gather.2.cloned.1.call-done), kind=kOutput, calls=%fused_computation.12 | convolution fusion | flops 269484032 | bytes 7372800 | tf_op jit(solution)/shard_map/dot_general | solution.py:169
  148.3 2.3 collective-permute-start.1
  155.4 9.0 %collective-permute-done.1 = bf16[64,8192]{1,0:T(8,128)(2,1)S(1)} collective-permute-done((bf16[64,8192]{1,0:T(8,128)(2,1)S(1)}, bf16[64,8192]{1,0:T(8,128)(2,1)S(1)}, u32[]{:S(2)}, u32[]{:S(2)}) %collective-permute-start.1) | collective-permute-done | bytes 1048608 | tf_op jit(solution)/shard_map/ppermute | solution.py:183
  165.5 13.2 %collective-permute-done.2 = bf16[64,8192]{1,0:T(8,128)(2,1)S(1)} collective-permute-done((bf16[64,8192]{1,0:T(8,128)(2,1)S(1)}, bf16[64,8192]{1,0:T(8,128)(2,1)S(1)}, u32[]{:S(2)}, u32[]{:S(2)}) %collective-permute-start.2) | collective-permute-done | bytes 1048608 | tf_op jit(solution)/shard_map/ppermute | solution.py:180
  178.7 2.2 collective-permute-start.3
  185.6 9.0 %collective-permute-done.3 = bf16[64,8192]{1,0:T(8,128)(2,1)S(1)} collective-permute-done((bf16[64,8192]{1,0:T(8,128)(2,1)S(1)}, bf16[64,8192]{1,0:T(8,128)(2,1)S(1)}, u32[]{:S(2)}, u32[]{:S(2)}) %collective-permute-start.3) | collective-permute-done | bytes 1048608 | tf_op jit(solution)/shard_map/ppermute | solution.py:183
  195.8 9.7 %collective-permute-done.4 = bf16[64,8192]{1,0:T(8,128)(2,1)S(1)} collective-permute-done((bf16[64,8192]{1,0:T(8,128)(2,1)S(1)}, bf16[64,8192]{1,0:T(8,128)(2,1)S(1)}, u32[]{:S(2)}, u32[]{:S(2)}) %collective-permute-start.4) | collective-permute-done | bytes 1048608 | tf_op jit(solution)/shard_map/ppermute | solution.py:180
  205.4 2.2 collective-permute-start.6
  209.5 11.4 %collective-permute-done.6 = bf16[64,8192]{1,0:T(8,128)(2,1)S(1)} collective-permute-done((bf16[64,8192]{1,0:T(8,128)(2,1)S(1)}, bf16[64,8192]{1,0:T(8,128)(2,1)S(1)}, u32[]{:S(2)}, u32[]{:S(2)}) %collective-permute-start.6) | collective-permute-done | bytes 1048608 | tf_op jit(solution)/shard_map/ppermute | solution.py:183
  224.0 4.9 %collective-permute-done.5 = bf16[64,8192]{1,0:T(8,128)(2,1)S(1)} collective-permute-done((bf16[64,8192]{1,0:T(8,128)(2,1)S(1)}, bf16[64,8192]{1,0:T(8,128)(2,1)S(1)}, u32[]{:S(2)}, u32[]{:S(2)}) %collective-permute-start.5) | collective-permute-done | bytes 1048608 | tf_op jit(solution)/shard_map/ppermute | solution.py:180
  228.9 22.7 %collective-permute-done.7 = bf16[64,8192]{1,0:T(8,128)(2,1)S(1)} collective-permute-done((bf16[64,8192]{1,0:T(8,128)(2,1)S(1)}, bf16[64,8192]{1,0:T(8,128)(2,1)S(1)}, u32[]{:S(2)}, u32[]{:S(2)}) %collective-permute-start.7) | collective-permute-done | bytes 1048608 | tf_op jit(solution)/shard_map/ppermute | solution.py:187
  251.6 2.2 maximum_bitcast_fusion
  (72 shorter events, 42.5 us)
Async XLA Ops:
  7.2 77.7 %all-gather.2.cloned.1.call-start = ((), (), s32[]{:S(2)}) async-start(), calls=%async_computation.1 | async-start | bytes 8912896 | tf_op jit(solution)/shard_map/all_gather | solution.py:89
  9.1 244.7 %reduce-scatter.2.cloned.1.call-start = ((), (), s32[]{:S(2)}) async-start(), calls=%async_computation.2 | async-start | bytes 8912896 | tf_op jit(solution)/shard_map/reduce_scatter | solution.py:137
  99.8 3.5 %slice-start = ((s8[8388608]{0:T(1024)(128)(4,1)}), s8[4194304]{0:T(1024)(128)(4,1)S(1)}, s32[]{:S(2)}) async-start(s8[8388608]{0:T(1024)(128)(4,1)} %bitcast.139), calls=%async_computation.3 | async-start | bytes 8388608
  101.8 2.3 slice-start.1
  101.8 3.5 %copy-start = (bf16[1,256,8192]{2,1,0:T(8,128)(2,1)S(1)}, bf16[1,256,8192]{2,1,0:T(8,128)(2,1)}, u32[]{:S(2)}) copy-start(bf16[1,256,8192]{2,1,0:T(8,128)(2,1)} %param.9) | copy-start | bytes 12582916
  105.3 5.0 %copy-start.3 = (f32[2,8,256,256]{2,3,1,0:T(8,128)}, f32[2,8,256,256]{2,3,1,0:T(8,128)S(1)}, u32[]{:S(2)}) copy-start(f32[2,8,256,256]{2,3,1,0:T(8,128)S(1)} %get-tuple-element.70) | copy-start | bytes 12582916
  111.8 8.1 %copy-start.2 = (bf16[2,128,256]{2,1,0:T(8,128)(2,1)S(1)}, bf16[2,128,256]{2,1,0:T(8,128)(2,1)}, u32[]{:S(2)}) copy-start(bf16[2,128,256]{2,1,0:T(8,128)(2,1)} %fusion.36) | copy-start | bytes 393220
  123.6 7.1 %copy-start.1 = (bf16[1,256,8192]{2,1,0:T(8,128)(2,1)S(1)}, bf16[1,256,8192]{2,1,0:T(8,128)(2,1)}, u32[]{:S(2)}) copy-start(bf16[1,256,8192]{2,1,0:T(8,128)(2,1)} %param.9) | copy-start | bytes 12582916
  127.4 19.8 %collective-permute-start = (bf16[64,8192]{1,0:T(8,128)(2,1)S(1)}, bf16[64,8192]{1,0:T(8,128)(2,1)S(1)}, u32[]{:S(2)}, u32[]{:S(2)}) collective-permute-start(bf16[64,8192]{1,0:T(8,128)(2,1)S(1)} %fusion.6), channel_id=1, source_target_pairs={{32,33},{33,32},{64,65},{65,64},{96,97},{97,96},{34,35},{35,34},{6... | collective-permute-start | bytes 3145736 | tf_op jit(solution)/shard_map/ppermute | solution.py:183
  143.4 7.2 %slice-start.2 = ((s8[8388608]{0:T(1024)(128)(4,1)}), s8[4194304]{0:T(1024)(128)(4,1)S(1)}, s32[]{:S(2)}) async-start(s8[8388608]{0:T(1024)(128)(4,1)} %bitcast.141), calls=%async_computation.5 | async-start | bytes 8388608
  147.1 3.5 %slice-start.3 = ((s8[8388608]{0:T(1024)(128)(4,1)}), s8[4194304]{0:T(1024)(128)(4,1)S(1)}, s32[]{:S(2)}) async-start(s8[8388608]{0:T(1024)(128)(4,1)} %bitcast.141), calls=%async_computation.6 | async-start | bytes 8388608
  148.3 16.1 %collective-permute-start.1 = (bf16[64,8192]{1,0:T(8,128)(2,1)S(1)}, bf16[64,8192]{1,0:T(8,128)(2,1)S(1)}, u32[]{:S(2)}, u32[]{:S(2)}) collective-permute-start(bf16[64,8192]{1,0:T(8,128)(2,1)S(1)} %fusion.5), channel_id=1, source_target_pairs={{32,33},{33,32},{64,65},{65,64},{96,97},{97,96},{34,35},{35,34},{6... | collective-permute-start | bytes 3145736 | tf_op jit(solution)/shard_map/ppermute | solution.py:183
  153.5 25.2 %collective-permute-start.2 = (bf16[64,8192]{1,0:T(8,128)(2,1)S(1)}, bf16[64,8192]{1,0:T(8,128)(2,1)S(1)}, u32[]{:S(2)}, u32[]{:S(2)}) collective-permute-start(bf16[64,8192]{1,0:T(8,128)(2,1)S(1)} %multiply_convert_fusion.5), channel_id=1, source_target_pairs={{32,0},{33,1},{65,32},{64,33},{96,64},{97,65},{34,2},{35,3},{67,34... | collective-permute-start | bytes 3145736 | tf_op jit(solution)/shard_map/ppermute | solution.py:180
  178.7 15.9 %collective-permute-start.3 = (bf16[64,8192]{1,0:T(8,128)(2,1)S(1)}, bf16[64,8192]{1,0:T(8,128)(2,1)S(1)}, u32[]{:S(2)}, u32[]{:S(2)}) collective-permute-start(bf16[64,8192]{1,0:T(8,128)(2,1)S(1)} %fusion.4), channel_id=1, source_target_pairs={{32,33},{33,32},{64,65},{65,64},{96,97},{97,96},{34,35},{35,34},{6... | collective-permute-start | bytes 3145736 | tf_op jit(solution)/shard_map/ppermute | solution.py:183
  183.7 21.7 %collective-permute-start.4 = (bf16[64,8192]{1,0:T(8,128)(2,1)S(1)}, bf16[64,8192]{1,0:T(8,128)(2,1)S(1)}, u32[]{:S(2)}, u32[]{:S(2)}) collective-permute-start(bf16[64,8192]{1,0:T(8,128)(2,1)S(1)} %multiply_convert_fusion.4), channel_id=1, source_target_pairs={{32,0},{33,1},{65,32},{64,33},{96,64},{97,65},{34,2},{35,3},{67,34... | collective-permute-start | bytes 3145736 | tf_op jit(solution)/shard_map/ppermute | solution.py:180
  205.4 15.5 %collective-permute-start.6 = (bf16[64,8192]{1,0:T(8,128)(2,1)S(1)}, bf16[64,8192]{1,0:T(8,128)(2,1)S(1)}, u32[]{:S(2)}, u32[]{:S(2)}) collective-permute-start(bf16[64,8192]{1,0:T(8,128)(2,1)S(1)} %fusion.7), channel_id=1, source_target_pairs={{32,33},{33,32},{64,65},{65,64},{96,97},{97,96},{34,35},{35,34},{6... | collective-permute-start | bytes 3145736 | tf_op jit(solution)/shard_map/ppermute | solution.py:183
  207.6 21.3 %collective-permute-start.5 = (bf16[64,8192]{1,0:T(8,128)(2,1)S(1)}, bf16[64,8192]{1,0:T(8,128)(2,1)S(1)}, u32[]{:S(2)}, u32[]{:S(2)}) collective-permute-start(bf16[64,8192]{1,0:T(8,128)(2,1)S(1)} %multiply_convert_fusion.3), channel_id=1, source_target_pairs={{32,0},{33,1},{65,32},{64,33},{96,64},{97,65},{34,2},{35,3},{67,34... | collective-permute-start | bytes 3145736 | tf_op jit(solution)/shard_map/ppermute | solution.py:180
  222.1 29.5 %collective-permute-start.7 = (bf16[64,8192]{1,0:T(8,128)(2,1)S(1)}, bf16[64,8192]{1,0:T(8,128)(2,1)S(1)}, u32[]{:S(2)}, u32[]{:S(2)}) collective-permute-start(bf16[64,8192]{1,0:T(8,128)(2,1)S(1)} %multiply_convert_fusion.2), channel_id=1, source_target_pairs={{32,0},{33,1},{65,32},{64,33},{96,64},{97,65},{34,2},{35,3},{67,34... | collective-permute-start | bytes 3145736 | tf_op jit(solution)/shard_map/ppermute | solution.py:187
Sparse Core Ops, SparseCore 0:
  10.8 74.0 all-gather.1
  136.6 83.2 reduce-scatter.1

commit v3 on v2

--- a/solution.py
+++ b/solution.py
@@ -102,8 +102,9 @@
     inv_rms = lax.rsqrt(jnp.mean(hidden_f * hidden_f, axis=-1, keepdims=True) + norm_eps)
     nhat = hidden_f * inv_rms
     normed = (nhat * gain_f).astype(jnp.bfloat16)
-    key_raw = jnp.dot(normed, key_full, preferred_element_type=jnp.float32)
-    values = jnp.dot(normed, value_full, preferred_element_type=jnp.float32).astype(jnp.bfloat16)
+    projected = jnp.einsum("td,wdc->wtc", normed, both_full, preferred_element_type=jnp.float32)
+    key_raw = projected[0]
+    values = projected[1].astype(jnp.bfloat16)
     cosine, sine = rope_tables(seq_len, HD)
     key_four = key_raw.reshape(seq_count, seq_len, kv_local, HD)
     keys = (
@@ -142,6 +143,7 @@
         scatter_dimension=0,
         tiled=True,
     )
+    both_grads = jnp.stack([key_grad, value_grad])
     n_pipe = lax.axis_size("pipe")
     n_tensor = lax.axis_size("tensor")
     chunks = 4
@@ -163,11 +165,8 @@
     held = None
     for c in range(chunks):
         sl = slice(c * rows, (c + 1) * rows)
-        part = lax.dot_general(
-            key_grad[sl], key_full, (((1,), (1,)), ((), ())), preferred_element_type=jnp.float32
-        )
-        part = part + lax.dot_general(
-            value_grad[sl], value_full, (((1,), (1,)), ((), ())), preferred_element_type=jnp.float32
+        part = jnp.einsum(
+            "wtc,wdc->td", both_grads[:, sl], both_full, preferred_element_type=jnp.float32
         )
         part_low = part.astype(jnp.bfloat16)
         if held is not None:

time: 263 us -> 257 us (0.977)
  waiting for transfers between devices: 146 us -> 153 us
  local copies, waits for them, and re-layouts: 14.1 us -> 8.48 us
  other arithmetic: 19.9 us -> 15.9 us
  matrix products: 48.5 us -> 44.7 us
    dot_general x11 -> x5, matrix products: 30.8 us -> 20.4 us  [the longest x4 13.4 us: on_device(): jnp.einsum('wtc,wdc->td', both_grads[:, sl], both_full, preferred_element...]
    sub x0 -> x1, matrix products: none -> 5.24 us  [sequence_grads(): expd = jnp.where(allowed, jnp.exp(scores - highest), 0.0)]
    all_gather x1, waiting for transfers between devices: 66 us -> 71.1 us  [on_device(): lax.all_gather(jnp.stack([key_weight[0], value_weight[0]]), 'dp', axis=1,...]
    unnamed x20 -> x12, local copies, waits for them, and re-layouts: 7 us -> 2.52 us
    ppermute x4, waiting for transfers between devices: 29.4 us -> 32.1 us  [on_device(): lax.ppermute(part_low, ('pipe', 'tensor'), pairs).astype(jnp.float32)]
  transfers between devices with their start and end apart: 10 -> 10, of which waited for: 8 -> 8; matrix products, arithmetic and copies ran while one was open for 14% -> 12% of each run, Pallas kernels for 0% -> 0%
where the time goes in v3:
time: 257 us; the launch traced here: 256 us
  waiting for transfers between devices  153 us (60%)
  matrix products  44.7 us (17%)
  starting transfers between devices  17.7 us (7%)
  between operations  16.5 us (6%)
  other arithmetic  15.9 us (6%)
  local copies, waits for them, and re-layouts  8.48 us (3%)
    all_gather x1, waiting for transfers between devices, on_device(): lax.all_gather(jnp.stack([key_weight[0], value_weight[0]]), 'dp', axis=1,...  71.1 us
    ppermute x4, waiting for transfers between devices, on_device(): lowers.append(lax.ppermute(held, ('pipe', 'tensor'), shift_pairs))  49.6 us
    ppermute x4, waiting for transfers between devices, on_device(): lax.ppermute(part_low, ('pipe', 'tensor'), pairs).astype(jnp.float32)  32.1 us
    dot_general x4, matrix products, on_device(): jnp.einsum('wtc,wdc->td', both_grads[:, sl], both_full, preferred_element...  13.4 us
    ppermute x4, starting transfers between devices, on_device(): lax.ppermute(part_low, ('pipe', 'tensor'), pairs).astype(jnp.float32)  9.98 us
    ppermute x4, starting transfers between devices, on_device(): lowers.append(lax.ppermute(held, ('pipe', 'tensor'), shift_pairs))  7.68 us
    dot_general x1, matrix products, sequence_grads(): jnp.einsum('kgij,ikgd->jkd', score_grad, query_g, preferred_element_type=...  7.51 us
    dot_general x1, matrix products, on_device(): jnp.einsum('td,wdc->wtc', normed, both_full, preferred_element_type=jnp.f...  7.02 us
  transfers between devices with their start and end apart: 10, of which 8 were waited for; matrix products, arithmetic and copies ran while one was open for 12% of the time, Pallas kernels for 0%

profile of v3, /device:TPU:1, one launch (start us, length us, event | category | flops | bytes accessed | tf_op | source)
XLA Modules:
  0.0 256.1 jit_solution(15793995850095596194)
XLA Ops:
  17.3 3.1 %fusion.6 = f32[256]{0:T(256)S(1)} fusion(bf16[1,256,8192]{2,1,0:T(8,128)(2,1)} %param.9), kind=kLoop, calls=%fused_computation.13 | loop fusion | flops 6291200 | bytes 4195328 | tf_op jit(solution)/shard_map/reduce_sum | solution.py:102
  20.5 71.1 %all-gather.2.cloned.1.call-done = bf16[2,8192,256]{1,2,0:T(8,128)(2,1)} async-done(((bf16[2,512,256]{1,2,0:T(8,128)(2,1)}), bf16[2,8192,256]{1,2,0:T(8,128)(2,1)}) %all-gather.2.cloned.1.call-update) | async-done | bytes 8388624 | tf_op jit(solution)/shard_map/all_gather | solution.py:89
  91.7 7.0 %fusion.20 = f32[2,256,256]{1,2,0:T(8,128)S(1)} fusion(bf16[2,8192,256]{1,2,0:T(8,128)(2,1)} %all-gather.2.cloned.1.call-done, f32[8192]{0:T(1024)S(1)} %bitcast.125, bf16[1,256,8192]{2,1,0:T(8,128)(2,1)} %param.9, f32[256]{0:T(256)S(1)} %add_rsqrt_fusion), kind=kOutput, calls=%fused_computation.47 | convolution fusion | flops 2155872256 | bytes 13140992 | tf_op jit(solution)/shard_map/td,wdc->wtc/dot_general | solution.py:105
  99.9 5.2 %fusion.60 = (f32[2,8,256]{2,1,0:T(8,128)S(1)}, f32[2,8,256,256]{2,3,1,0:T(8,128)}) fusion(pred[256,256]{0,1:T(8,128)(4,1)S(1)} %fusion.39, bf16[256,2,8,128]{0,3,2,1:T(8,128)(2,1)} %bitcast.137, f32[256,2,64]{2,0,1:T(8,128)S(1)} %bitcast.142, f32[256,2,64]{2,0,1:T(8,128)} %negate_bitcast_fusion, f32[256,2,128]{2,0,1:T(8,128)S(1)} %copy.15, ...), kind=kOutput, calls=%fused_computation.107 | convolution fusion | flops 274006272 | bytes 6111232 | tf_op jit(solution)/shard_map/while/body/eval_jaxpr/sub | solution.py:56
  105.1 3.0 %fusion.27 = bf16[2,128,256]{2,1,0:T(8,128)(2,1)S(1)} fusion(f32[256,2,8,128]{0,3,2,1:T(8,128)S(1)} %bitcast.123, f32[256]{0:T(256)S(1)} %broadcast_select_fusion, f32[2,8,256,256]{2,3,1,0:T(8,128)} %get-tuple-element.62, f32[2,8,256]{2,1,0:T(8,128)S(1)} %get-tuple-element.61), kind=kOutput, calls=%fused_computation.50 | convolution fusion | flops 271646720 | bytes 6439936 | tf_op jit(solution)/shard_map/while/body/eval_jaxpr/kgij,ikgd->jkd/dot_general | solution.py:59
  108.3 2.7 %fusion.30 = f32[2,256,256,8]{2,1,3,0:T(8,128)} fusion(bf16[256,2,128,1]{0,2,3,1:T(8,128)(2,1)S(1)} %bitcast.139, f32[256,2,8,128]{0,3,2,1:T(8,128)S(1)} %bitcast.124, f32[256]{0:T(256)S(1)} %broadcast_select_fusion), kind=kOutput, calls=%fused_computation.52 | convolution fusion | flops 269484032 | bytes 6423552 | tf_op jit(solution)/shard_map/while/body/eval_jaxpr/ikgd,jkd->kgij/dot_general | solution.py:62
  111.0 7.5 %fusion.23 = f32[2,256,128]{1,2,0:T(8,128)S(1)} fusion(bf16[256,2,8,128]{0,3,2,1:T(8,128)(2,1)} %bitcast.138, f32[2,256,256,8]{2,1,3,0:T(8,128)} %fusion.30, f32[2,8,256,256]{2,3,1,0:T(8,128)} %get-tuple-element.62, f32[2,8,256]{2,1,0:T(8,128)S(1)} %get-tuple-element.61), kind=kOutput, calls=%fused_computation.48 | convolution fusion | flops 275779840 | bytes 9715712 | tf_op jit(solution)/shard_map/while/body/eval_jaxpr/kgij,ikgd->jkd/dot_general | solution.py:65
  118.7 5.1 %fusion.4 = bf16[64,8192]{1,0:T(8,128)(2,1)S(1)} fusion(bf16[2,8192,256]{1,2,0:T(8,128)(2,1)} %all-gather.2.cloned.1.call-done, bf16[1,256,256]{2,1,0:T(8,128)(2,1)S(1)} %copy.26, bf16[1,256,256]{2,1,0:T(8,128)(2,1)S(1)} %copy.27), kind=kOutput, calls=%fused_computation.11 | convolution fusion | flops 537427968 | bytes 9699328 | tf_op jit(solution)/shard_map/wtc,wdc->td/dot_general | solution.py:168
  123.8 3.3 %collective-permute-start = (bf16[64,8192]{1,0:T(8,128)(2,1)S(1)}, bf16[64,8192]{1,0:T(8,128)(2,1)S(1)}, u32[]{:S(2)}, u32[]{:S(2)}) collective-permute-start(bf16[64,8192]{1,0:T(8,128)(2,1)S(1)} %fusion.4), channel_id=1, source_target_pairs={{32,33},{33,32},{64,65},{65,64},{96,97},{97,96},{34,35},{35,34},{6... | collective-permute-start | bytes 3145736 | tf_op jit(solution)/shard_map/ppermute | solution.py:182
  127.2 5.8 %convolution_convert_fusion = bf16[8192,512]{1,0:T(8,128)(2,1)} fusion(f32[8192]{0:T(1024)S(1)} %bitcast.126, bf16[256,256]{0,1:T(8,128)(2,1)S(1)} %bitcast.144, bf16[256,256]{0,1:T(8,128)(2,1)S(1)} %bitcast.141, bf16[1,256,8192]{2,1,0:T(8,128)(2,1)S(1)} %copy-done, f32[256]{0:T(256)S(1)} %add_rsqrt_fusion), kind=kOutput, calls=%fused_computation.2 | convolution fusion | flops 2160590848 | bytes 12878848 | tf_op jit(solution)/shard_map/dot_general | solution.py:139
  133.0 3.3 %convert_multiply_fusion = f32[256,8192]{1,0:T(8,128)S(1)} fusion(bf16[1,256,8192]{2,1,0:T(8,128)(2,1)} %param.9, f32[256]{0:T(256)S(1)} %add_rsqrt_fusion), kind=kLoop, calls=%fused_computation.3 | loop fusion | flops 4194304 | bytes 12583936 | tf_op jit(solution)/shard_map/mul | solution.py:103
  136.3 5.1 %fusion.3 = bf16[64,8192]{1,0:T(8,128)(2,1)S(1)} fusion(bf16[2,8192,256]{1,2,0:T(8,128)(2,1)} %all-gather.2.cloned.1.call-done, bf16[1,256,256]{2,1,0:T(8,128)(2,1)S(1)} %copy.26, bf16[1,256,256]{2,1,0:T(8,128)(2,1)S(1)} %copy.27), kind=kOutput, calls=%fused_computation.10 | convolution fusion | flops 537427968 | bytes 9699328 | tf_op jit(solution)/shard_map/wtc,wdc->td/dot_general | solution.py:168
  142.6 2.2 collective-permute-start.1
  148.3 10.2 %collective-permute-done.1 = bf16[64,8192]{1,0:T(8,128)(2,1)S(1)} collective-permute-done((bf16[64,8192]{1,0:T(8,128)(2,1)S(1)}, bf16[64,8192]{1,0:T(8,128)(2,1)S(1)}, u32[]{:S(2)}, u32[]{:S(2)}) %collective-permute-start.1) | collective-permute-done | bytes 1048608 | tf_op jit(solution)/shard_map/ppermute | solution.py:182
  159.6 14.1 %collective-permute-done.2 = bf16[64,8192]{1,0:T(8,128)(2,1)S(1)} collective-permute-done((bf16[64,8192]{1,0:T(8,128)(2,1)S(1)}, bf16[64,8192]{1,0:T(8,128)(2,1)S(1)}, u32[]{:S(2)}, u32[]{:S(2)}) %collective-permute-start.2) | collective-permute-done | bytes 1048608 | tf_op jit(solution)/shard_map/ppermute | solution.py:179
  173.8 2.3 collective-permute-start.3
  179.6 10.1 %collective-permute-done.3 = bf16[64,8192]{1,0:T(8,128)(2,1)S(1)} collective-permute-done((bf16[64,8192]{1,0:T(8,128)(2,1)S(1)}, bf16[64,8192]{1,0:T(8,128)(2,1)S(1)}, u32[]{:S(2)}, u32[]{:S(2)}) %collective-permute-start.3) | collective-permute-done | bytes 1048608 | tf_op jit(solution)/shard_map/ppermute | solution.py:182
  190.8 8.9 %collective-permute-done.4 = bf16[64,8192]{1,0:T(8,128)(2,1)S(1)} collective-permute-done((bf16[64,8192]{1,0:T(8,128)(2,1)S(1)}, bf16[64,8192]{1,0:T(8,128)(2,1)S(1)}, u32[]{:S(2)}, u32[]{:S(2)}) %collective-permute-start.4) | collective-permute-done | bytes 1048608 | tf_op jit(solution)/shard_map/ppermute | solution.py:179
  199.7 2.2 collective-permute-start.6
  201.9 1.9 collective-permute-start.5
  203.9 11.8 %collective-permute-done.6 = bf16[64,8192]{1,0:T(8,128)(2,1)S(1)} collective-permute-done((bf16[64,8192]{1,0:T(8,128)(2,1)S(1)}, bf16[64,8192]{1,0:T(8,128)(2,1)S(1)}, u32[]{:S(2)}, u32[]{:S(2)}) %collective-permute-start.6) | collective-permute-done | bytes 1048608 | tf_op jit(solution)/shard_map/ppermute | solution.py:182
  218.7 4.8 %collective-permute-done.5 = bf16[64,8192]{1,0:T(8,128)(2,1)S(1)} collective-permute-done((bf16[64,8192]{1,0:T(8,128)(2,1)S(1)}, bf16[64,8192]{1,0:T(8,128)(2,1)S(1)}, u32[]{:S(2)}, u32[]{:S(2)}) %collective-permute-start.5) | collective-permute-done | bytes 1048608 | tf_op jit(solution)/shard_map/ppermute | solution.py:179
  223.6 21.8 %collective-permute-done.7 = bf16[64,8192]{1,0:T(8,128)(2,1)S(1)} collective-permute-done((bf16[64,8192]{1,0:T(8,128)(2,1)S(1)}, bf16[64,8192]{1,0:T(8,128)(2,1)S(1)}, u32[]{:S(2)}, u32[]{:S(2)}) %collective-permute-start.7) | collective-permute-done | bytes 1048608 | tf_op jit(solution)/shard_map/ppermute | solution.py:186
  245.3 2.1 maximum_bitcast_fusion
  (62 shorter events, 24.9 us)
Async XLA Ops:
  7.2 7.3 %copy-start.1 = (bf16[1,256,2048]{2,1,0:T(8,128)(2,1)S(1)}, bf16[1,256,2048]{2,1,0:T(8,128)(2,1)}, u32[]{:S(2)}) copy-start(bf16[1,256,2048]{2,1,0:T(8,128)(2,1)} %param.13) | copy-start | bytes 3145732
  7.2 84.5 %all-gather.2.cloned.1.call-start = ((), (), s32[]{:S(2)}) async-start(), calls=%async_computation.1 | async-start | bytes 8912896 | tf_op jit(solution)/shard_map/all_gather | solution.py:89
  10.4 237.1 %reduce-scatter.2.cloned.1.call-start = ((), (), s32[]{:S(2)}) async-start(), calls=%async_computation.2 | async-start | bytes 8912896 | tf_op jit(solution)/shard_map/reduce_scatter | solution.py:138
  118.7 8.4 %copy-start = (bf16[1,256,8192]{2,1,0:T(8,128)(2,1)S(1)}, bf16[1,256,8192]{2,1,0:T(8,128)(2,1)}, u32[]{:S(2)}) copy-start(bf16[1,256,8192]{2,1,0:T(8,128)(2,1)} %param.9) | copy-start | bytes 12582916
  123.8 17.6 %collective-permute-start = (bf16[64,8192]{1,0:T(8,128)(2,1)S(1)}, bf16[64,8192]{1,0:T(8,128)(2,1)S(1)}, u32[]{:S(2)}, u32[]{:S(2)}) collective-permute-start(bf16[64,8192]{1,0:T(8,128)(2,1)S(1)} %fusion.4), channel_id=1, source_target_pairs={{32,33},{33,32},{64,65},{65,64},{96,97},{97,96},{34,35},{35,34},{6... | collective-permute-start | bytes 3145736 | tf_op jit(solution)/shard_map/ppermute | solution.py:182
  136.2 8.5 %slice-start = ((s8[8388608]{0:T(1024)(128)(4,1)}), s8[4194304]{0:T(1024)(128)(4,1)S(1)}, s32[]{:S(2)}) async-start(s8[8388608]{0:T(1024)(128)(4,1)} %bitcast.121), calls=%async_computation.3 | async-start | bytes 8388608
  136.3 8.5 %slice-start.1 = ((s8[8388608]{0:T(1024)(128)(4,1)}), s8[4194304]{0:T(1024)(128)(4,1)S(1)}, s32[]{:S(2)}) async-start(s8[8388608]{0:T(1024)(128)(4,1)} %bitcast.121), calls=%async_computation.4 | async-start | bytes 8388608
  142.6 15.9 %collective-permute-start.1 = (bf16[64,8192]{1,0:T(8,128)(2,1)S(1)}, bf16[64,8192]{1,0:T(8,128)(2,1)S(1)}, u32[]{:S(2)}, u32[]{:S(2)}) collective-permute-start(bf16[64,8192]{1,0:T(8,128)(2,1)S(1)} %fusion.3), channel_id=1, source_target_pairs={{32,33},{33,32},{64,65},{65,64},{96,97},{97,96},{34,35},{35,34},{6... | collective-permute-start | bytes 3145736 | tf_op jit(solution)/shard_map/ppermute | solution.py:182
  146.4 27.4 %collective-permute-start.2 = (bf16[64,8192]{1,0:T(8,128)(2,1)S(1)}, bf16[64,8192]{1,0:T(8,128)(2,1)S(1)}, u32[]{:S(2)}, u32[]{:S(2)}) collective-permute-start(bf16[64,8192]{1,0:T(8,128)(2,1)S(1)} %multiply_convert_fusion.4), channel_id=1, source_target_pairs={{32,0},{33,1},{65,32},{64,33},{96,64},{97,65},{34,2},{35,3},{67,34... | collective-permute-start | bytes 3145736 | tf_op jit(solution)/shard_map/ppermute | solution.py:179
  173.8 15.9 %collective-permute-start.3 = (bf16[64,8192]{1,0:T(8,128)(2,1)S(1)}, bf16[64,8192]{1,0:T(8,128)(2,1)S(1)}, u32[]{:S(2)}, u32[]{:S(2)}) collective-permute-start(bf16[64,8192]{1,0:T(8,128)(2,1)S(1)} %fusion.2), channel_id=1, source_target_pairs={{32,33},{33,32},{64,65},{65,64},{96,97},{97,96},{34,35},{35,34},{6... | collective-permute-start | bytes 3145736 | tf_op jit(solution)/shard_map/ppermute | solution.py:182
  177.7 22.0 %collective-permute-start.4 = (bf16[64,8192]{1,0:T(8,128)(2,1)S(1)}, bf16[64,8192]{1,0:T(8,128)(2,1)S(1)}, u32[]{:S(2)}, u32[]{:S(2)}) collective-permute-start(bf16[64,8192]{1,0:T(8,128)(2,1)S(1)} %multiply_convert_fusion.3), channel_id=1, source_target_pairs={{32,0},{33,1},{65,32},{64,33},{96,64},{97,65},{34,2},{35,3},{67,34... | collective-permute-start | bytes 3145736 | tf_op jit(solution)/shard_map/ppermute | solution.py:179
  199.7 15.9 %collective-permute-start.6 = (bf16[64,8192]{1,0:T(8,128)(2,1)S(1)}, bf16[64,8192]{1,0:T(8,128)(2,1)S(1)}, u32[]{:S(2)}, u32[]{:S(2)}) collective-permute-start(bf16[64,8192]{1,0:T(8,128)(2,1)S(1)} %fusion.5), channel_id=1, source_target_pairs={{32,33},{33,32},{64,65},{65,64},{96,97},{97,96},{34,35},{35,34},{6... | collective-permute-start | bytes 3145736 | tf_op jit(solution)/shard_map/ppermute | solution.py:182
  201.9 21.6 %collective-permute-start.5 = (bf16[64,8192]{1,0:T(8,128)(2,1)S(1)}, bf16[64,8192]{1,0:T(8,128)(2,1)S(1)}, u32[]{:S(2)}, u32[]{:S(2)}) collective-permute-start(bf16[64,8192]{1,0:T(8,128)(2,1)S(1)} %multiply_convert_fusion.2), channel_id=1, source_target_pairs={{32,0},{33,1},{65,32},{64,33},{96,64},{97,65},{34,2},{35,3},{67,34... | collective-permute-start | bytes 3145736 | tf_op jit(solution)/shard_map/ppermute | solution.py:179
  216.8 28.5 %collective-permute-start.7 = (bf16[64,8192]{1,0:T(8,128)(2,1)S(1)}, bf16[64,8192]{1,0:T(8,128)(2,1)S(1)}, u32[]{:S(2)}, u32[]{:S(2)}) collective-permute-start(bf16[64,8192]{1,0:T(8,128)(2,1)S(1)} %multiply_convert_fusion.1), channel_id=1, source_target_pairs={{32,0},{33,1},{65,32},{64,33},{96,64},{97,65},{34,2},{35,3},{67,34... | collective-permute-start | bytes 3145736 | tf_op jit(solution)/shard_map/ppermute | solution.py:186
Sparse Core Ops, SparseCore 0:
  10.7 80.9 all-gather.1
  133.1 84.1 reduce-scatter.1

commit v4 on v3

--- a/solution.py
+++ b/solution.py
@@ -86,9 +86,18 @@
     policy_logp,
     reference_logp,
 ):
-    both_full = lax.all_gather(
-        jnp.stack([key_weight[0], value_weight[0]]), "dp", axis=1, tiled=True
-    )
+    own_block = jnp.stack([key_weight[0], value_weight[0]])
+    n_dp = lax.axis_size("dp")
+    me_dp = lax.axis_index("dp")
+    block_rows = own_block.shape[1]
+    both_full = jnp.zeros((2, n_dp * block_rows, own_block.shape[2]), own_block.dtype)
+    for k in range(n_dp):
+        if k == 0:
+            piece = own_block
+        else:
+            piece = lax.ppermute(own_block, "dp", [(s, (s + k) % n_dp) for s in range(n_dp)])
+        start = ((me_dp - k) % n_dp) * block_rows
+        both_full = lax.dynamic_update_slice(both_full, piece, (0, start, 0))
     key_full, value_full = both_full[0], both_full[1]
     hidden = hidden_states[0]
     gain_f = norm_gain[0].astype(jnp.float32)

time: 257 us -> 370 us (1.44)
  starting transfers between devices: 17.7 us -> 96.9 us
  local copies, waits for them, and re-layouts: 8.48 us -> 31.7 us
  matrix products: 44.7 us -> 57.2 us
  other arithmetic: 15.9 us -> 12 us
    ppermute x0 -> x15, waiting for transfers between devices: none -> 78.7 us  [on_device(): lax.ppermute(own_block, 'dp', [(s, (s + k) % n_dp) for s in range(n_dp)])]
    ppermute x0 -> x15, starting transfers between devices: none -> 78.4 us  [on_device(): lax.ppermute(own_block, 'dp', [(s, (s + k) % n_dp) for s in range(n_dp)])]
    all_gather x1 -> x0, waiting for transfers between devices: 71.1 us -> none  [on_device(): lax.all_gather(jnp.stack([key_weight[0], value_weight[0]]), 'dp', axis=1,...]
    dynamic_update_slice x0 -> x16, local copies, waits for them, and re-layouts: none -> 17.4 us  [on_device(): both_full = lax.dynamic_update_slice(both_full, piece, (0, start, 0))]
    dot_general x4, matrix products: 13.4 us -> 24.8 us  [on_device(): jnp.einsum('wtc,wdc->td', both_grads[:, sl], both_full, preferred_element...]
    ppermute x4, waiting for transfers between devices: 32.1 us -> 26.9 us  [on_device(): lax.ppermute(part_low, ('pipe', 'tensor'), pairs).astype(jnp.float32)]
    broadcast_in_dim x0 -> x1, local copies, waits for them, and re-layouts: none -> 3.78 us  [on_device(): jnp.zeros((2, n_dp * block_rows, own_block.shape[2]), own_block.dtype)]
  transfers between devices with their start and end apart: 10 -> 24, of which waited for: 8 -> 13; matrix products, arithmetic and copies ran while one was open for 12% -> 17% of each run, Pallas kernels for 0% -> 0%
where the time goes in v4:
time: 370 us; the launch traced here: 369 us
  waiting for transfers between devices  155 us (42%)
  starting transfers between devices  96.9 us (26%)
  matrix products  57.2 us (15%)
  local copies, waits for them, and re-layouts  31.7 us (9%)
  between operations  16.7 us (5%)
  other arithmetic  12 us (3%)
    ppermute x15, waiting for transfers between devices, on_device(): lax.ppermute(own_block, 'dp', [(s, (s + k) % n_dp) for s in range(n_dp)])  78.7 us
    ppermute x15, starting transfers between devices, on_device(): lax.ppermute(own_block, 'dp', [(s, (s + k) % n_dp) for s in range(n_dp)])  78.4 us
    ppermute x4, waiting for transfers between devices, on_device(): lowers.append(lax.ppermute(held, ('pipe', 'tensor'), shift_pairs))  49 us
    ppermute x4, waiting for transfers between devices, on_device(): lax.ppermute(part_low, ('pipe', 'tensor'), pairs).astype(jnp.float32)  26.9 us
    dot_general x4, matrix products, on_device(): jnp.einsum('wtc,wdc->td', both_grads[:, sl], both_full, preferred_element...  24.8 us
    dynamic_update_slice x16, local copies, waits for them, and re-layouts, on_device(): both_full = lax.dynamic_update_slice(both_full, piece, (0, start, 0))  17.4 us
    ppermute x4, starting transfers between devices, on_device(): lax.ppermute(part_low, ('pipe', 'tensor'), pairs).astype(jnp.float32)  10.8 us
    dot_general x1, matrix products, on_device(): lax.dot_general(normed, combined, (((0,), (0,)), ((), ())), preferred_ele...  7.92 us
  transfers between devices with their start and end apart: 24, of which 13 were waited for; matrix products, arithmetic and copies ran while one was open for 17% of the time, Pallas kernels for 0%

profile of v4, /device:TPU:1, one launch (start us, length us, event | category | flops | bytes accessed | tf_op | source)
XLA Modules:
  0.0 369.0 jit_solution(17059203798710339382)
XLA Ops:
  38.4 8.6 %collective-permute-done.1 = bf16[2,512,256]{2,1,0:T(8,128)(2,1)} collective-permute-done((bf16[2,512,256]{2,1,0:T(8,128)(2,1)S(1)}, bf16[2,512,256]{2,1,0:T(8,128)(2,1)}, u32[]{:S(2)}, u32[]{:S(2)}) %collective-permute-start.1) | collective-permute-done | bytes 524320 | tf_op jit(solution)/shard_map/ppermute | solution.py:98
  47.0 5.0 %collective-permute-start.6 = (bf16[2,512,256]{2,1,0:T(8,128)(2,1)S(1)}, bf16[2,512,256]{2,1,0:T(8,128)(2,1)S(1)}, u32[]{:S(2)}, u32[]{:S(2)}) collective-permute-start(bf16[2,512,256]{2,1,0:T(8,128)(2,1)S(1)} %constant_dynamic-update-slice_fusion), channel_id=1, source_target_pairs={{0,14},{2,16},{4,18},{6,20},{8,22},{10,24},{12,26},{14,28},{16,30}... | collective-permute-start | bytes 1572872 | tf_op jit(solution)/shard_map/ppermute | solution.py:98
  53.8 16.6 %collective-permute-start.7 = (bf16[2,512,256]{2,1,0:T(8,128)(2,1)S(1)}, bf16[2,512,256]{2,1,0:T(8,128)(2,1)S(1)}, u32[]{:S(2)}, u32[]{:S(2)}) collective-permute-start(bf16[2,512,256]{2,1,0:T(8,128)(2,1)S(1)} %constant_dynamic-update-slice_fusion), channel_id=1, source_target_pairs={{0,16},{2,18},{4,20},{6,22},{8,24},{10,26},{12,28},{14,30},{16,0},... | collective-permute-start | bytes 1572872 | tf_op jit(solution)/shard_map/ppermute | solution.py:98
  72.3 3.9 %collective-permute-start.8 = (bf16[2,512,256]{2,1,0:T(8,128)(2,1)S(1)}, bf16[2,512,256]{2,1,0:T(8,128)(2,1)S(1)}, u32[]{:S(2)}, u32[]{:S(2)}) collective-permute-start(bf16[2,512,256]{2,1,0:T(8,128)(2,1)S(1)} %constant_dynamic-update-slice_fusion), channel_id=1, source_target_pairs={{0,18},{2,20},{4,22},{6,24},{8,26},{10,28},{12,30},{14,0},{16,2},{... | collective-permute-start | bytes 1572872 | tf_op jit(solution)/shard_map/ppermute | solution.py:98
  78.0 48.2 %collective-permute-done.4 = bf16[2,512,256]{2,1,0:T(8,128)(2,1)S(1)} collective-permute-done((bf16[2,512,256]{2,1,0:T(8,128)(2,1)S(1)}, bf16[2,512,256]{2,1,0:T(8,128)(2,1)S(1)}, u32[]{:S(2)}, u32[]{:S(2)}) %collective-permute-start.4) | collective-permute-done | bytes 524320 | tf_op jit(solution)/shard_map/ppermute | solution.py:98
  127.1 13.4 %collective-permute-start.10 = (bf16[2,512,256]{2,1,0:T(8,128)(2,1)S(1)}, bf16[2,512,256]{2,1,0:T(8,128)(2,1)S(1)}, u32[]{:S(2)}, u32[]{:S(2)}) collective-permute-start(bf16[2,512,256]{2,1,0:T(8,128)(2,1)S(1)} %constant_dynamic-update-slice_fusion), channel_id=1, source_target_pairs={{0,22},{2,24},{4,26},{6,28},{8,30},{10,0},{12,2},{14,4},{16,6},{18... | collective-permute-start | bytes 1572872 | tf_op jit(solution)/shard_map/ppermute | solution.py:98
  143.0 29.2 %collective-permute-start.13 = (bf16[2,512,256]{2,1,0:T(8,128)(2,1)S(1)}, bf16[2,512,256]{2,1,0:T(8,128)(2,1)S(1)}, u32[]{:S(2)}, u32[]{:S(2)}) collective-permute-start(bf16[2,512,256]{2,1,0:T(8,128)(2,1)S(1)} %constant_dynamic-update-slice_fusion), channel_id=1, source_target_pairs={{0,28},{2,30},{4,0},{6,2},{8,4},{10,6},{12,8},{14,10},{16,12},{18,... | collective-permute-start | bytes 1572872 | tf_op jit(solution)/shard_map/ppermute | solution.py:98
  175.5 11.3 %collective-permute-done.12 = bf16[2,512,256]{2,1,0:T(8,128)(2,1)S(1)} collective-permute-done((bf16[2,512,256]{2,1,0:T(8,128)(2,1)S(1)}, bf16[2,512,256]{2,1,0:T(8,128)(2,1)S(1)}, u32[]{:S(2)}, u32[]{:S(2)}) %collective-permute-start.12) | collective-permute-done | bytes 524320 | tf_op jit(solution)/shard_map/ppermute | solution.py:98
  188.5 9.4 %collective-permute-done.14 = bf16[2,512,256]{2,1,0:T(8,128)(2,1)S(1)} collective-permute-done((bf16[2,512,256]{2,1,0:T(8,128)(2,1)S(1)}, bf16[2,512,256]{2,1,0:T(8,128)(2,1)S(1)}, u32[]{:S(2)}, u32[]{:S(2)}) %collective-permute-start.14) | collective-permute-done | bytes 524320 | tf_op jit(solution)/shard_map/ppermute | solution.py:98
  198.7 6.0 %fusion.20 = f32[2,256,256]{1,2,0:T(8,128)S(1)} fusion(bf16[2,8192,256]{2,1,0:T(8,128)(2,1)} %constant_dynamic-update-slice_fusion.2, f32[8192]{0:T(1024)S(1)} %bitcast.123, bf16[1,256,8192]{2,1,0:T(8,128)(2,1)S(1)} %copy-done, f32[256]{0:T(256)S(1)} %add_rsqrt_fusion), kind=kOutput, calls=%fused_computation.47 | convolution fusion | flops 2155872256 | bytes 13140992 | tf_op jit(solution)/shard_map/td,wdc->wtc/dot_general | solution.py:114
  209.3 5.2 %fusion.60 = (f32[2,8,256]{2,1,0:T(8,128)S(1)}, f32[2,8,256,256]{2,3,1,0:T(8,128)}) fusion(pred[256,256]{0,1:T(8,128)(4,1)S(1)} %fusion.39, bf16[256,2,8,128]{0,3,2,1:T(8,128)(2,1)} %bitcast.135, f32[256,2,64]{2,0,1:T(8,128)S(1)} %bitcast.140, f32[256,2,64]{2,0,1:T(8,128)S(1)} %copy-done.2, f32[256,2,128]{2,0,1:T(8,128)S(1)} %copy-done.3, ...), kind=kOutput, calls=%fused_computation.124 | convolution fusion | flops 274006272 | bytes 6111232 | tf_op jit(solution)/shard_map/while/body/eval_jaxpr/sub | solution.py:56
  217.5 7.6 %fusion.23 = f32[2,256,128]{1,2,0:T(8,128)S(1)} fusion(bf16[256,2,8,128]{0,3,2,1:T(8,128)(2,1)} %bitcast.136, f32[2,256,256,8]{2,1,3,0:T(8,128)} %fusion.30, f32[2,8,256,256]{2,3,1,0:T(8,128)} %get-tuple-element.62, f32[2,8,256]{2,1,0:T(8,128)S(1)} %get-tuple-element.61), kind=kOutput, calls=%fused_computation.48 | convolution fusion | flops 275779840 | bytes 9715712 | tf_op jit(solution)/shard_map/while/body/eval_jaxpr/kgij,ikgd->jkd/dot_general | solution.py:65
  225.2 7.9 %convolution_convert_fusion = bf16[8192,512]{1,0:T(8,128)(2,1)} fusion(f32[8192]{0:T(1024)S(1)} %bitcast.124, bf16[256,256]{0,1:T(8,128)(2,1)S(1)} %bitcast.141, bf16[256,256]{0,1:T(8,128)(2,1)S(1)} %bitcast.138, bf16[1,256,8192]{2,1,0:T(8,128)(2,1)} %param.9, f32[256]{0:T(256)S(1)} %add_rsqrt_fusion), kind=kOutput, calls=%fused_computation.2 | convolution fusion | flops 2160590848 | bytes 12878848 | tf_op jit(solution)/shard_map/dot_general | solution.py:148
  233.4 6.2 %fusion.4 = bf16[64,8192]{1,0:T(8,128)(2,1)S(1)} fusion(bf16[2,8192,256]{2,1,0:T(8,128)(2,1)} %constant_dynamic-update-slice_fusion.2, bf16[1,256,256]{2,1,0:T(8,128)(2,1)S(1)} %copy.25, bf16[1,256,256]{2,1,0:T(8,128)(2,1)S(1)} %copy.26), kind=kOutput, calls=%fused_computation.11 | convolution fusion | flops 537427968 | bytes 9699328 | tf_op jit(solution)/shard_map/wtc,wdc->td/dot_general | solution.py:177
  244.0 6.4 %fusion.3 = bf16[64,8192]{1,0:T(8,128)(2,1)S(1)} fusion(bf16[2,8192,256]{2,1,0:T(8,128)(2,1)} %constant_dynamic-update-slice_fusion.2, bf16[1,256,256]{2,1,0:T(8,128)(2,1)S(1)} %copy.25, bf16[1,256,256]{2,1,0:T(8,128)(2,1)S(1)} %copy.26), kind=kOutput, calls=%fused_computation.10 | convolution fusion | flops 537427968 | bytes 9699328 | tf_op jit(solution)/shard_map/wtc,wdc->td/dot_general | solution.py:177
  250.5 5.0 %collective-permute-done.15 = bf16[64,8192]{1,0:T(8,128)(2,1)S(1)} collective-permute-done((bf16[64,8192]{1,0:T(8,128)(2,1)S(1)}, bf16[64,8192]{1,0:T(8,128)(2,1)S(1)}, u32[]{:S(2)}, u32[]{:S(2)}) %collective-permute-start.15) | collective-permute-done | bytes 1048608 | tf_op jit(solution)/shard_map/ppermute | solution.py:191
  259.7 6.2 %fusion.2 = bf16[64,8192]{1,0:T(8,128)(2,1)S(1)} fusion(bf16[2,8192,256]{2,1,0:T(8,128)(2,1)} %constant_dynamic-update-slice_fusion.2, bf16[1,256,256]{2,1,0:T(8,128)(2,1)S(1)} %copy.25, bf16[1,256,256]{2,1,0:T(8,128)(2,1)S(1)} %copy.26), kind=kOutput, calls=%fused_computation.9 | convolution fusion | flops 537427968 | bytes 9699328 | tf_op jit(solution)/shard_map/wtc,wdc->td/dot_general | solution.py:177
  267.9 4.7 %collective-permute-done.16 = bf16[64,8192]{1,0:T(8,128)(2,1)S(1)} collective-permute-done((bf16[64,8192]{1,0:T(8,128)(2,1)S(1)}, bf16[64,8192]{1,0:T(8,128)(2,1)S(1)}, u32[]{:S(2)}, u32[]{:S(2)}) %collective-permute-start.16) | collective-permute-done | bytes 1048608 | tf_op jit(solution)/shard_map/ppermute | solution.py:191
  273.6 20.4 %collective-permute-done.17 = bf16[64,8192]{1,0:T(8,128)(2,1)S(1)} collective-permute-done((bf16[64,8192]{1,0:T(8,128)(2,1)S(1)}, bf16[64,8192]{1,0:T(8,128)(2,1)S(1)}, u32[]{:S(2)}, u32[]{:S(2)}) %collective-permute-start.17) | collective-permute-done | bytes 1048608 | tf_op jit(solution)/shard_map/ppermute | solution.py:188
  296.5 6.0 %fusion.5 = bf16[64,8192]{1,0:T(8,128)(2,1)S(1)} fusion(bf16[2,8192,256]{2,1,0:T(8,128)(2,1)} %constant_dynamic-update-slice_fusion.2, bf16[1,256,256]{2,1,0:T(8,128)(2,1)S(1)} %copy.26, bf16[1,256,256]{2,1,0:T(8,128)(2,1)S(1)} %copy.25), kind=kOutput, calls=%fused_computation.12 | convolution fusion | flops 537526272 | bytes 9699328 | tf_op jit(solution)/shard_map/wtc,wdc->td/dot_general | solution.py:177
  304.4 5.5 %collective-permute-done.18 = bf16[64,8192]{1,0:T(8,128)(2,1)S(1)} collective-permute-done((bf16[64,8192]{1,0:T(8,128)(2,1)S(1)}, bf16[64,8192]{1,0:T(8,128)(2,1)S(1)}, u32[]{:S(2)}, u32[]{:S(2)}) %collective-permute-start.18) | collective-permute-done | bytes 1048608 | tf_op jit(solution)/shard_map/ppermute | solution.py:191
  311.0 9.2 %collective-permute-done.19 = bf16[64,8192]{1,0:T(8,128)(2,1)S(1)} collective-permute-done((bf16[64,8192]{1,0:T(8,128)(2,1)S(1)}, bf16[64,8192]{1,0:T(8,128)(2,1)S(1)}, u32[]{:S(2)}, u32[]{:S(2)}) %collective-permute-start.19) | collective-permute-done | bytes 1048608 | tf_op jit(solution)/shard_map/ppermute | solution.py:188
  324.0 11.7 %collective-permute-done.21 = bf16[64,8192]{1,0:T(8,128)(2,1)S(1)} collective-permute-done((bf16[64,8192]{1,0:T(8,128)(2,1)S(1)}, bf16[64,8192]{1,0:T(8,128)(2,1)S(1)}, u32[]{:S(2)}, u32[]{:S(2)}) %collective-permute-start.21) | collective-permute-done | bytes 1048608 | tf_op jit(solution)/shard_map/ppermute | solution.py:191
  339.4 18.7 %collective-permute-done.22 = bf16[64,8192]{1,0:T(8,128)(2,1)S(1)} collective-permute-done((bf16[64,8192]{1,0:T(8,128)(2,1)S(1)}, bf16[64,8192]{1,0:T(8,128)(2,1)S(1)}, u32[]{:S(2)}, u32[]{:S(2)}) %collective-permute-start.22) | collective-permute-done | bytes 1048608 | tf_op jit(solution)/shard_map/ppermute | solution.py:195
  (108 shorter events, 80.1 us)
Async XLA Ops:
  7.2 353.2 %reduce-scatter.2.cloned.1.call-start = ((), (), s32[]{:S(2)}) async-start(), calls=%async_computation.1 | async-start | bytes 8912896 | tf_op jit(solution)/shard_map/reduce_scatter | solution.py:147
  9.2 27.3 %collective-permute-start = (bf16[2,512,256]{2,1,0:T(8,128)(2,1)S(1)}, bf16[2,512,256]{2,1,0:T(8,128)(2,1)}, u32[]{:S(2)}, u32[]{:S(2)}) collective-permute-start(bf16[2,512,256]{2,1,0:T(8,128)(2,1)S(1)} %constant_dynamic-update-slice_fusion), channel_id=1, source_target_pairs={{0,2},{2,4},{4,6},{6,8},{8,10},{10,12},{12,14},{14,16},{16,18},{18... | collective-permute-start | bytes 1572872 | tf_op jit(solution)/shard_map/ppermute | solution.py:98
  11.7 35.3 %collective-permute-start.1 = (bf16[2,512,256]{2,1,0:T(8,128)(2,1)S(1)}, bf16[2,512,256]{2,1,0:T(8,128)(2,1)}, u32[]{:S(2)}, u32[]{:S(2)}) collective-permute-start(bf16[2,512,256]{2,1,0:T(8,128)(2,1)S(1)} %constant_dynamic-update-slice_fusion), channel_id=1, source_target_pairs={{0,4},{2,6},{4,8},{6,10},{8,12},{10,14},{12,16},{14,18},{16,20},{1... | collective-permute-start | bytes 1572872 | tf_op jit(solution)/shard_map/ppermute | solution.py:98
  15.0 38.8 %collective-permute-start.2 = (bf16[2,512,256]{2,1,0:T(8,128)(2,1)S(1)}, bf16[2,512,256]{2,1,0:T(8,128)(2,1)}, u32[]{:S(2)}, u32[]{:S(2)}) collective-permute-start(bf16[2,512,256]{2,1,0:T(8,128)(2,1)S(1)} %constant_dynamic-update-slice_fusion), channel_id=1, source_target_pairs={{0,6},{2,8},{4,10},{6,12},{8,14},{10,16},{12,18},{14,20},{16,22},{... | collective-permute-start | bytes 1572872 | tf_op jit(solution)/shard_map/ppermute | solution.py:98
  16.7 55.6 %collective-permute-start.3 = (bf16[2,512,256]{2,1,0:T(8,128)(2,1)S(1)}, bf16[2,512,256]{2,1,0:T(8,128)(2,1)}, u32[]{:S(2)}, u32[]{:S(2)}) collective-permute-start(bf16[2,512,256]{2,1,0:T(8,128)(2,1)S(1)} %constant_dynamic-update-slice_fusion), channel_id=1, source_target_pairs={{0,8},{2,10},{4,12},{6,14},{8,16},{10,18},{12,20},{14,22},{16,24},... | collective-permute-start | bytes 1572872 | tf_op jit(solution)/shard_map/ppermute | solution.py:98
  18.0 108.2 %collective-permute-start.4 = (bf16[2,512,256]{2,1,0:T(8,128)(2,1)S(1)}, bf16[2,512,256]{2,1,0:T(8,128)(2,1)S(1)}, u32[]{:S(2)}, u32[]{:S(2)}) collective-permute-start(bf16[2,512,256]{2,1,0:T(8,128)(2,1)S(1)} %constant_dynamic-update-slice_fusion), channel_id=1, source_target_pairs={{0,10},{2,12},{4,14},{6,16},{8,18},{10,20},{12,22},{14,24},{16,26}... | collective-permute-start | bytes 1572872 | tf_op jit(solution)/shard_map/ppermute | solution.py:98
  36.5 90.6 %collective-permute-start.5 = (bf16[2,512,256]{2,1,0:T(8,128)(2,1)S(1)}, bf16[2,512,256]{2,1,0:T(8,128)(2,1)S(1)}, u32[]{:S(2)}, u32[]{:S(2)}) collective-permute-start(bf16[2,512,256]{2,1,0:T(8,128)(2,1)S(1)} %constant_dynamic-update-slice_fusion), channel_id=1, source_target_pairs={{0,12},{2,14},{4,16},{6,18},{8,20},{10,22},{12,24},{14,26},{16,28}... | collective-permute-start | bytes 1572872 | tf_op jit(solution)/shard_map/ppermute | solution.py:98
  47.0 94.3 %collective-permute-start.6 = (bf16[2,512,256]{2,1,0:T(8,128)(2,1)S(1)}, bf16[2,512,256]{2,1,0:T(8,128)(2,1)S(1)}, u32[]{:S(2)}, u32[]{:S(2)}) collective-permute-start(bf16[2,512,256]{2,1,0:T(8,128)(2,1)S(1)} %constant_dynamic-update-slice_fusion), channel_id=1, source_target_pairs={{0,14},{2,16},{4,18},{6,20},{8,22},{10,24},{12,26},{14,28},{16,30}... | collective-permute-start | bytes 1572872 | tf_op jit(solution)/shard_map/ppermute | solution.py:98
  53.8 88.3 %collective-permute-start.7 = (bf16[2,512,256]{2,1,0:T(8,128)(2,1)S(1)}, bf16[2,512,256]{2,1,0:T(8,128)(2,1)S(1)}, u32[]{:S(2)}, u32[]{:S(2)}) collective-permute-start(bf16[2,512,256]{2,1,0:T(8,128)(2,1)S(1)} %constant_dynamic-update-slice_fusion), channel_id=1, source_target_pairs={{0,16},{2,18},{4,20},{6,22},{8,24},{10,26},{12,28},{14,30},{16,0},... | collective-permute-start | bytes 1572872 | tf_op jit(solution)/shard_map/ppermute | solution.py:98
  72.3 70.7 %collective-permute-start.8 = (bf16[2,512,256]{2,1,0:T(8,128)(2,1)S(1)}, bf16[2,512,256]{2,1,0:T(8,128)(2,1)S(1)}, u32[]{:S(2)}, u32[]{:S(2)}) collective-permute-start(bf16[2,512,256]{2,1,0:T(8,128)(2,1)S(1)} %constant_dynamic-update-slice_fusion), channel_id=1, source_target_pairs={{0,18},{2,20},{4,22},{6,24},{8,26},{10,28},{12,30},{14,0},{16,2},{... | collective-permute-start | bytes 1572872 | tf_op jit(solution)/shard_map/ppermute | solution.py:98
  126.2 46.8 %collective-permute-start.9 = (bf16[2,512,256]{2,1,0:T(8,128)(2,1)S(1)}, bf16[2,512,256]{2,1,0:T(8,128)(2,1)S(1)}, u32[]{:S(2)}, u32[]{:S(2)}) collective-permute-start(bf16[2,512,256]{2,1,0:T(8,128)(2,1)S(1)} %constant_dynamic-update-slice_fusion), channel_id=1, source_target_pairs={{0,20},{2,22},{4,24},{6,26},{8,28},{10,30},{12,0},{14,2},{16,4},{1... | collective-permute-start | bytes 1572872 | tf_op jit(solution)/shard_map/ppermute | solution.py:98
  127.1 46.8 %collective-permute-start.10 = (bf16[2,512,256]{2,1,0:T(8,128)(2,1)S(1)}, bf16[2,512,256]{2,1,0:T(8,128)(2,1)S(1)}, u32[]{:S(2)}, u32[]{:S(2)}) collective-permute-start(bf16[2,512,256]{2,1,0:T(8,128)(2,1)S(1)} %constant_dynamic-update-slice_fusion), channel_id=1, source_target_pairs={{0,22},{2,24},{4,26},{6,28},{8,30},{10,0},{12,2},{14,4},{16,6},{18... | collective-permute-start | bytes 1572872 | tf_op jit(solution)/shard_map/ppermute | solution.py:98
  141.3 33.4 %collective-permute-start.11 = (bf16[2,512,256]{2,1,0:T(8,128)(2,1)S(1)}, bf16[2,512,256]{2,1,0:T(8,128)(2,1)S(1)}, u32[]{:S(2)}, u32[]{:S(2)}) collective-permute-start(bf16[2,512,256]{2,1,0:T(8,128)(2,1)S(1)} %constant_dynamic-update-slice_fusion), channel_id=1, source_target_pairs={{0,24},{2,26},{4,28},{6,30},{8,0},{10,2},{12,4},{14,6},{16,8},{18,... | collective-permute-start | bytes 1572872 | tf_op jit(solution)/shard_map/ppermute | solution.py:98
  142.2 44.7 %collective-permute-start.12 = (bf16[2,512,256]{2,1,0:T(8,128)(2,1)S(1)}, bf16[2,512,256]{2,1,0:T(8,128)(2,1)S(1)}, u32[]{:S(2)}, u32[]{:S(2)}) collective-permute-start(bf16[2,512,256]{2,1,0:T(8,128)(2,1)S(1)} %constant_dynamic-update-slice_fusion), channel_id=1, source_target_pairs={{0,26},{2,28},{4,30},{6,0},{8,2},{10,4},{12,6},{14,8},{16,10},{18,... | collective-permute-start | bytes 1572872 | tf_op jit(solution)/shard_map/ppermute | solution.py:98
  143.0 44.7 %collective-permute-start.13 = (bf16[2,512,256]{2,1,0:T(8,128)(2,1)S(1)}, bf16[2,512,256]{2,1,0:T(8,128)(2,1)S(1)}, u32[]{:S(2)}, u32[]{:S(2)}) collective-permute-start(bf16[2,512,256]{2,1,0:T(8,128)(2,1)S(1)} %constant_dynamic-update-slice_fusion), channel_id=1, source_target_pairs={{0,28},{2,30},{4,0},{6,2},{8,4},{10,6},{12,8},{14,10},{16,12},{18,... | collective-permute-start | bytes 1572872 | tf_op jit(solution)/shard_map/ppermute | solution.py:98
  173.1 24.8 %collective-permute-start.14 = (bf16[2,512,256]{2,1,0:T(8,128)(2,1)S(1)}, bf16[2,512,256]{2,1,0:T(8,128)(2,1)S(1)}, u32[]{:S(2)}, u32[]{:S(2)}) collective-permute-start(bf16[2,512,256]{2,1,0:T(8,128)(2,1)S(1)} %constant_dynamic-update-slice_fusion), channel_id=1, source_target_pairs={{0,30},{2,0},{4,2},{6,4},{8,6},{10,8},{12,10},{14,12},{16,14},{18,... | collective-permute-start | bytes 1572872 | tf_op jit(solution)/shard_map/ppermute | solution.py:98
  239.5 15.9 %collective-permute-start.15 = (bf16[64,8192]{1,0:T(8,128)(2,1)S(1)}, bf16[64,8192]{1,0:T(8,128)(2,1)S(1)}, u32[]{:S(2)}, u32[]{:S(2)}) collective-permute-start(bf16[64,8192]{1,0:T(8,128)(2,1)S(1)} %fusion.4), channel_id=1, source_target_pairs={{32,33},{33,32},{64,65},{65,64},{96,97},{97,96},{34,35},{35,34},{6... | collective-permute-start | bytes 3145736 | tf_op jit(solution)/shard_map/ppermute | solution.py:191
  256.6 15.9 %collective-permute-start.16 = (bf16[64,8192]{1,0:T(8,128)(2,1)S(1)}, bf16[64,8192]{1,0:T(8,128)(2,1)S(1)}, u32[]{:S(2)}, u32[]{:S(2)}) collective-permute-start(bf16[64,8192]{1,0:T(8,128)(2,1)S(1)} %fusion.3), channel_id=1, source_target_pairs={{32,33},{33,32},{64,65},{65,64},{96,97},{97,96},{34,35},{35,34},{6... | collective-permute-start | bytes 3145736 | tf_op jit(solution)/shard_map/ppermute | solution.py:191
  265.9 28.1 %collective-permute-start.17 = (bf16[64,8192]{1,0:T(8,128)(2,1)S(1)}, bf16[64,8192]{1,0:T(8,128)(2,1)S(1)}, u32[]{:S(2)}, u32[]{:S(2)}) collective-permute-start(bf16[64,8192]{1,0:T(8,128)(2,1)S(1)} %multiply_convert_fusion.4), channel_id=1, source_target_pairs={{32,0},{33,1},{65,32},{64,33},{96,64},{97,65},{34,2},{35,3},{67,34... | collective-permute-start | bytes 3145736 | tf_op jit(solution)/shard_map/ppermute | solution.py:188
  294.0 15.9 %collective-permute-start.18 = (bf16[64,8192]{1,0:T(8,128)(2,1)S(1)}, bf16[64,8192]{1,0:T(8,128)(2,1)S(1)}, u32[]{:S(2)}, u32[]{:S(2)}) collective-permute-start(bf16[64,8192]{1,0:T(8,128)(2,1)S(1)} %fusion.2), channel_id=1, source_target_pairs={{32,33},{33,32},{64,65},{65,64},{96,97},{97,96},{34,35},{35,34},{6... | collective-permute-start | bytes 3145736 | tf_op jit(solution)/shard_map/ppermute | solution.py:191
  302.5 17.7 %collective-permute-start.19 = (bf16[64,8192]{1,0:T(8,128)(2,1)S(1)}, bf16[64,8192]{1,0:T(8,128)(2,1)S(1)}, u32[]{:S(2)}, u32[]{:S(2)}) collective-permute-start(bf16[64,8192]{1,0:T(8,128)(2,1)S(1)} %multiply_convert_fusion.3), channel_id=1, source_target_pairs={{32,0},{33,1},{65,32},{64,33},{96,64},{97,65},{34,2},{35,3},{67,34... | collective-permute-start | bytes 3145736 | tf_op jit(solution)/shard_map/ppermute | solution.py:188
  320.2 15.5 %collective-permute-start.21 = (bf16[64,8192]{1,0:T(8,128)(2,1)S(1)}, bf16[64,8192]{1,0:T(8,128)(2,1)S(1)}, u32[]{:S(2)}, u32[]{:S(2)}) collective-permute-start(bf16[64,8192]{1,0:T(8,128)(2,1)S(1)} %fusion.5), channel_id=1, source_target_pairs={{32,33},{33,32},{64,65},{65,64},{96,97},{97,96},{34,35},{35,34},{6... | collective-permute-start | bytes 3145736 | tf_op jit(solution)/shard_map/ppermute | solution.py:191
  322.1 17.3 %collective-permute-start.20 = (bf16[64,8192]{1,0:T(8,128)(2,1)S(1)}, bf16[64,8192]{1,0:T(8,128)(2,1)S(1)}, u32[]{:S(2)}, u32[]{:S(2)}) collective-permute-start(bf16[64,8192]{1,0:T(8,128)(2,1)S(1)} %multiply_convert_fusion.2), channel_id=1, source_target_pairs={{32,0},{33,1},{65,32},{64,33},{96,64},{97,65},{34,2},{35,3},{67,34... | collective-permute-start | bytes 3145736 | tf_op jit(solution)/shard_map/ppermute | solution.py:188
  336.8 21.3 %collective-permute-start.22 = (bf16[64,8192]{1,0:T(8,128)(2,1)S(1)}, bf16[64,8192]{1,0:T(8,128)(2,1)S(1)}, u32[]{:S(2)}, u32[]{:S(2)}) collective-permute-start(bf16[64,8192]{1,0:T(8,128)(2,1)S(1)} %multiply_convert_fusion.1), channel_id=1, source_target_pairs={{32,0},{33,1},{65,32},{64,33},{96,64},{97,65},{34,2},{35,3},{67,34... | collective-permute-start | bytes 3145736 | tf_op jit(solution)/shard_map/ppermute | solution.py:195
  (6 other events, 82.9 us)
Sparse Core Ops, SparseCore 0:
  233.3 87.1 reduce-scatter.1

commit v5 on v3

--- a/solution.py
+++ b/solution.py
@@ -1,3 +1,4 @@
+import functools
 import math
 
 import jax
@@ -148,19 +149,42 @@
     n_tensor = lax.axis_size("tensor")
     chunks = 4
     rows = tok_rows // chunks
-    exchange_steps = [
-        [
-            (p * n_tensor + t, p * n_tensor + (t + step) % n_tensor)
-            for p in range(1, n_pipe)
-            for t in range(n_tensor)
-        ]
-        for step in range(1, n_tensor)
+    width = hidden.shape[1] // n_tensor
+    me_pipe = lax.axis_index("pipe")
+    me_tensor = lax.axis_index("tensor")
+    other = n_tensor - 1 - me_tensor
+    feature_count = hidden.shape[1]
+
+    def at(p, t):
+        return p * n_tensor + t
+
+    cross = [q for q in range(1, n_pipe) if q // 2 != (q - 1) // 2]
+    near = [q for q in range(1, n_pipe) if q not in cross]
+    swap = lambda qs: [(at(q, t), at(q, n_tensor - 1 - t)) for q in qs for t in range(n_tensor)]
+    pairs_first = swap(range(1, n_pipe))
+    pairs_second = swap(near)
+    pairs_centre = swap(cross)
+    pairs_down = [(at(q, t), at(q - 1, t)) for q in near for t in range(n_tensor)]
+    pairs_mine = pairs_down + [
+        (at(q, t), at(q - 1, n_tensor - 1 - t)) for q in cross for t in range(n_tensor)
     ]
-    shift_pairs = [
-        ((p + 1) * n_tensor + (t if (p + 1) // 2 == p // 2 else n_tensor - 1 - t), p * n_tensor + t)
-        for p in range(n_pipe - 1)
-        for t in range(n_tensor)
-    ]
+    pairs_relay = swap([q - 1 for q in cross])
+    cross_src = functools.reduce(jnp.logical_or, [me_pipe == q for q in cross], me_pipe < 0)
+    cross_dst = functools.reduce(jnp.logical_or, [me_pipe == q - 1 for q in cross], me_pipe < 0)
+    axes = ("pipe", "tensor")
+    halve = lambda x, which: lax.dynamic_slice_in_dim(x, which * width, width, axis=x.ndim - 1)
+    gain_mine, gain_other = halve(gain_f, me_tensor), halve(gain_f, other)
+
+    def send_down(cot_mine, cot_other):
+        got_mine = lax.ppermute(cot_mine, axes, pairs_mine)
+        got_rest = lax.ppermute(cot_other, axes, pairs_down)
+        relayed = lax.ppermute(got_mine, axes, pairs_relay)
+        half_mine = jnp.where(cross_dst, relayed, got_mine)
+        half_other = jnp.where(cross_dst, got_mine, got_rest)
+        full = jnp.zeros((cot_mine.shape[0], feature_count), cot_mine.dtype)
+        full = lax.dynamic_update_slice_in_dim(full, half_mine, me_tensor * width, axis=1)
+        return lax.dynamic_update_slice_in_dim(full, half_other, other * width, axis=1)
+
     lowers = []
     held = None
     for c in range(chunks):
@@ -176,14 +200,31 @@
                 )
             else:
                 part_low, held = lax.optimization_barrier((part_low, held))
-            lowers.append(lax.ppermute(held, ("pipe", "tensor"), shift_pairs))
-        normed_grad = part_low.astype(jnp.float32)
-        for pairs in exchange_steps:
-            normed_grad = normed_grad + lax.ppermute(
-                part_low, ("pipe", "tensor"), pairs
-            ).astype(jnp.float32)
-        held = norm_backward(normed_grad, gain_f, nhat[sl], inv_rms[sl])
-    lowers.append(lax.ppermute(held, ("pipe", "tensor"), shift_pairs))
+            lowers.append(send_down(*held))
+        mine, theirs = halve(part_low, me_tensor), halve(part_low, other)
+        grad_mine = mine.astype(jnp.float32) + lax.ppermute(theirs, axes, pairs_first).astype(
+            jnp.float32
+        )
+        grad_other = theirs.astype(jnp.float32) + lax.ppermute(
+            mine, axes, pairs_second
+        ).astype(jnp.float32)
+        nhat_c = nhat[sl]
+        nhat_mine, nhat_other = halve(nhat_c, me_tensor), halve(nhat_c, other)
+        gin_mine = grad_mine * gain_mine
+        gin_other = grad_other * gain_other
+        sum_mine = jnp.sum(gin_mine * nhat_mine, axis=-1, keepdims=True)
+        sum_other = jnp.where(
+            cross_src,
+            lax.ppermute(sum_mine, axes, pairs_centre),
+            jnp.sum(gin_other * nhat_other, axis=-1, keepdims=True),
+        )
+        centre = (sum_mine + sum_other) / feature_count
+        scale_c = inv_rms[sl]
+        held = (
+            ((gin_mine - nhat_mine * centre) * scale_c).astype(jnp.bfloat16),
+            ((gin_other - nhat_other * centre) * scale_c).astype(jnp.bfloat16),
+        )
+    lowers.append(send_down(*held))
     lower = jnp.concatenate(lowers, axis=0)
     return (grad_total[:, :kv_cols][None], grad_total[:, kv_cols:][None], lower[None])
 

time: 257 us -> 285 us (1.11)
  starting transfers between devices: 17.7 us -> 48.9 us
  waiting for transfers between devices: 153 us -> 129 us
  local copies, waits for them, and re-layouts: 8.48 us -> 16.1 us
  other arithmetic: 15.9 us -> 22.5 us
  matrix products: 44.7 us -> 50.9 us
    ppermute x8 -> x24, starting transfers between devices: 17.7 us -> 48.8 us  [the longest x4 12.6 us: on_device(): lax.ppermute(mine, axes, pairs_second).astype(jnp.float32)]
    ppermute x8 -> x24, waiting for transfers between devices: 81.7 us -> 62.5 us  [the longest x4 22.3 us: send_down(): relayed = lax.ppermute(got_mine, axes, pairs_relay)]
    all_gather x1, waiting for transfers between devices: 71.1 us -> 66.2 us  [on_device(): lax.all_gather(jnp.stack([key_weight[0], value_weight[0]]), 'dp', axis=1,...]
    dot_general x4, matrix products: 13.4 us -> 17.3 us  [on_device(): jnp.einsum('wtc,wdc->td', both_grads[:, sl], both_full, preferred_element...]
    reduce_sum x4, other arithmetic: 2.18 us -> 5.94 us  [on_device(): jnp.sum(gin_other * nhat_other, axis=-1, keepdims=True)]
    convert_element_type x4, other arithmetic: 2.25 us -> 5.95 us  [on_device(): ((gin_other - nhat_other * centre) * scale_c).astype(jnp.bfloat16)]
    slice x1 -> x2, local copies, waits for them, and re-layouts: 0.07 us -> 3.5 us  [the longest x1 2.86 us: on_device(): nhat_c = nhat[sl]]
  transfers between devices with their start and end apart: 10 -> 26, of which waited for: 8 -> 13; matrix products, arithmetic and copies ran while one was open for 12% -> 17% of each run, Pallas kernels for 0% -> 0%
where the time goes in v5:
time: 285 us; the launch traced here: 284 us
  waiting for transfers between devices  129 us (45%)
  matrix products  50.9 us (18%)
  starting transfers between devices  48.9 us (17%)
  other arithmetic  22.5 us (8%)
  between operations  16.9 us (6%)
  local copies, waits for them, and re-layouts  16.1 us (6%)
    all_gather x1, waiting for transfers between devices, on_device(): lax.all_gather(jnp.stack([key_weight[0], value_weight[0]]), 'dp', axis=1,...  66.2 us
    ppermute x4, waiting for transfers between devices, send_down(): relayed = lax.ppermute(got_mine, axes, pairs_relay)  22.3 us
    ppermute x4, waiting for transfers between devices, on_device(): lax.ppermute(theirs, axes, pairs_first).astype(jnp.float32)  21.4 us
    dot_general x4, matrix products, on_device(): jnp.einsum('wtc,wdc->td', both_grads[:, sl], both_full, preferred_element...  17.3 us
    ppermute x4, starting transfers between devices, on_device(): lax.ppermute(mine, axes, pairs_second).astype(jnp.float32)  12.6 us
    ppermute x4, starting transfers between devices, send_down(): relayed = lax.ppermute(got_mine, axes, pairs_relay)  11.1 us
    ppermute x4, waiting for transfers between devices, send_down(): got_mine = lax.ppermute(cot_mine, axes, pairs_mine)  10.4 us
    ppermute x4, starting transfers between devices, on_device(): lax.ppermute(theirs, axes, pairs_first).astype(jnp.float32)  9.21 us
  transfers between devices with their start and end apart: 26, of which 13 were waited for; matrix products, arithmetic and copies ran while one was open for 17% of the time, Pallas kernels for 0%

profile of v5, /device:TPU:1, one launch (start us, length us, event | category | flops | bytes accessed | tf_op | source)
XLA Modules:
  0.0 284.0 jit_solution(16225646225869524614)
XLA Ops:
  17.4 3.3 %fusion.6 = f32[256]{0:T(256)S(1)} fusion(bf16[1,256,8192]{2,1,0:T(8,128)(2,1)} %param.9), kind=kLoop, calls=%fused_computation.13 | loop fusion | flops 6291200 | bytes 4195328 | tf_op jit(solution)/shard_map/reduce_sum | solution.py:103
  25.4 66.2 %all-gather.2.cloned.1.call-done = bf16[2,8192,256]{1,2,0:T(8,128)(2,1)} async-done(((bf16[2,512,256]{1,2,0:T(8,128)(2,1)}), bf16[2,8192,256]{1,2,0:T(8,128)(2,1)}) %all-gather.2.cloned.1.call-update) | async-done | bytes 8388624 | tf_op jit(solution)/shard_map/all_gather | solution.py:90
  91.6 7.0 %fusion.20 = f32[2,256,256]{1,2,0:T(8,128)S(1)} fusion(bf16[2,8192,256]{1,2,0:T(8,128)(2,1)} %all-gather.2.cloned.1.call-done, f32[8192]{0:T(1024)S(1)} %bitcast.185, bf16[1,256,8192]{2,1,0:T(8,128)(2,1)} %param.9, f32[256]{0:T(256)S(1)} %add_rsqrt_fusion), kind=kOutput, calls=%fused_computation.35 | convolution fusion | flops 2155872256 | bytes 13140992 | tf_op jit(solution)/shard_map/td,wdc->wtc/dot_general | solution.py:106
  99.8 5.3 %fusion.73 = (f32[2,8,256]{2,1,0:T(8,128)S(1)}, f32[2,8,256,256]{2,3,1,0:T(8,128)}) fusion(pred[256,256]{0,1:T(8,128)(4,1)S(1)} %fusion.39, bf16[256,2,8,128]{0,3,2,1:T(8,128)(2,1)} %bitcast.177, f32[256,2,64]{2,0,1:T(8,128)S(1)} %bitcast.182, f32[256,2,64]{2,0,1:T(8,128)} %negate_bitcast_fusion, f32[256,2,128]{2,0,1:T(8,128)S(1)} %copy.15, ...), kind=kOutput, calls=%fused_computation.150 | convolution fusion | flops 274006272 | bytes 6111232 | tf_op jit(solution)/shard_map/while/body/eval_jaxpr/sub | solution.py:57
  105.1 3.7 %fusion.27 = bf16[2,128,256]{2,1,0:T(8,128)(2,1)S(1)} fusion(f32[256,2,8,128]{0,3,2,1:T(8,128)} %bitcast.157, f32[256]{0:T(256)S(1)} %broadcast_select_fusion.4, f32[2,8,256,256]{2,3,1,0:T(8,128)} %get-tuple-element.98, f32[2,8,256]{2,1,0:T(8,128)S(1)} %get-tuple-element.97), kind=kOutput, calls=%fused_computation.38 | convolution fusion | flops 271646720 | bytes 6439936 | tf_op jit(solution)/shard_map/while/body/eval_jaxpr/kgij,ikgd->jkd/dot_general | solution.py:60
  109.4 4.3 %fusion.30 = f32[2,256,256,8]{2,1,3,0:T(8,128)} fusion(bf16[256,2,128,1]{0,2,3,1:T(8,128)(2,1)S(1)} %bitcast.179, f32[256,2,8,128]{0,3,2,1:T(8,128)} %bitcast.158, f32[256]{0:T(256)S(1)} %broadcast_select_fusion.4), kind=kOutput, calls=%fused_computation.72 | convolution fusion | flops 269484032 | bytes 6423552 | tf_op jit(solution)/shard_map/while/body/eval_jaxpr/ikgd,jkd->kgij/dot_general | solution.py:63
  113.7 7.5 %fusion.23 = f32[2,256,128]{1,2,0:T(8,128)S(1)} fusion(bf16[256,2,8,128]{0,3,2,1:T(8,128)(2,1)} %bitcast.178, f32[2,256,256,8]{2,1,3,0:T(8,128)} %fusion.30, f32[2,8,256,256]{2,3,1,0:T(8,128)} %get-tuple-element.98, f32[2,8,256]{2,1,0:T(8,128)S(1)} %get-tuple-element.97), kind=kOutput, calls=%fused_computation.36 | convolution fusion | flops 275779840 | bytes 9715712 | tf_op jit(solution)/shard_map/while/body/eval_jaxpr/kgij,ikgd->jkd/dot_general | solution.py:66
  122.2 5.1 %fusion.4 = bf16[64,8192]{1,0:T(8,128)(2,1)S(1)} fusion(bf16[2,8192,256]{1,2,0:T(8,128)(2,1)} %all-gather.2.cloned.1.call-done, bf16[1,256,256]{2,1,0:T(8,128)(2,1)S(1)} %copy.26, bf16[1,256,256]{2,1,0:T(8,128)(2,1)S(1)} %copy.27), kind=kOutput, calls=%fused_computation.11 | convolution fusion | flops 537427968 | bytes 9699328 | tf_op jit(solution)/shard_map/wtc,wdc->td/dot_general | solution.py:192
  128.6 3.1 %collective-permute-start.2 = (bf16[64,4096]{1,0:T(8,128)(2,1)}, bf16[64,4096]{1,0:T(8,128)(2,1)}, u32[]{:S(2)}, u32[]{:S(2)}) collective-permute-start(bf16[64,4096]{1,0:T(8,128)(2,1)} %get-tuple-element.81), channel_id=1, source_target_pairs={{32,33},{33,32},{96,97},{97,96},{34,35},{35,34},{98,99},{99,98},{3... | collective-permute-start | bytes 1572872 | tf_op jit(solution)/shard_map/ppermute | solution.py:208
  134.1 5.8 %convolution_convert_fusion = bf16[8192,512]{1,0:T(8,128)(2,1)} fusion(f32[8192]{0:T(1024)S(1)} %bitcast.186, bf16[256,256]{0,1:T(8,128)(2,1)S(1)} %bitcast.184, bf16[256,256]{0,1:T(8,128)(2,1)S(1)} %bitcast.181, bf16[1,256,8192]{2,1,0:T(8,128)(2,1)S(1)} %copy-done.4, f32[256]{0:T(256)S(1)} %add_rsqrt_fusion), kind=kOutput, calls=%fused_computation.2 | convolution fusion | flops 2160590848 | bytes 12878848 | tf_op jit(solution)/shard_map/dot_general | solution.py:140
  139.9 4.5 %collective-permute-done = bf16[64,4096]{1,0:T(8,128)(2,1)} collective-permute-done((bf16[64,4096]{1,0:T(8,128)(2,1)}, bf16[64,4096]{1,0:T(8,128)(2,1)}, u32[]{:S(2)}, u32[]{:S(2)}) %collective-permute-start) | collective-permute-done | bytes 524320 | tf_op jit(solution)/shard_map/ppermute | solution.py:205
  147.6 5.5 %fusion.3 = bf16[64,8192]{1,0:T(8,128)(2,1)S(1)} fusion(bf16[2,8192,256]{1,2,0:T(8,128)(2,1)} %all-gather.2.cloned.1.call-done, bf16[1,256,256]{2,1,0:T(8,128)(2,1)S(1)} %copy.26, bf16[1,256,256]{2,1,0:T(8,128)(2,1)S(1)} %copy.27), kind=kOutput, calls=%fused_computation.10 | convolution fusion | flops 537427968 | bytes 9699328 | tf_op jit(solution)/shard_map/wtc,wdc->td/dot_general | solution.py:192
  157.0 3.1 %collective-permute-start.5 = (bf16[64,4096]{1,0:T(8,128)(2,1)}, bf16[64,4096]{1,0:T(8,128)(2,1)}, u32[]{:S(2)}, u32[]{:S(2)}) collective-permute-start(bf16[64,4096]{1,0:T(8,128)(2,1)} %get-tuple-element.79), channel_id=1, source_target_pairs={{32,33},{33,32},{96,97},{97,96},{34,35},{35,34},{98,99},{99,98},{3... | collective-permute-start | bytes 1572872 | tf_op jit(solution)/shard_map/ppermute | solution.py:208
  164.2 3.3 %collective-permute-done.5 = bf16[64,4096]{1,0:T(8,128)(2,1)} collective-permute-done((bf16[64,4096]{1,0:T(8,128)(2,1)}, bf16[64,4096]{1,0:T(8,128)(2,1)}, u32[]{:S(2)}, u32[]{:S(2)}) %collective-permute-start.5) | collective-permute-done | bytes 524320 | tf_op jit(solution)/shard_map/ppermute | solution.py:208
  167.5 5.6 %collective-permute-done.3 = bf16[64,4096]{1,0:T(8,128)(2,1)} collective-permute-done((bf16[64,4096]{1,0:T(8,128)(2,1)}, bf16[64,4096]{1,0:T(8,128)(2,1)}, u32[]{:S(2)}, u32[]{:S(2)}) %collective-permute-start.3) | collective-permute-done | bytes 524320 | tf_op jit(solution)/shard_map/ppermute | solution.py:205
  176.4 5.2 %fusion.2 = bf16[64,8192]{1,0:T(8,128)(2,1)S(1)} fusion(bf16[2,8192,256]{1,2,0:T(8,128)(2,1)} %all-gather.2.cloned.1.call-done, bf16[1,256,256]{2,1,0:T(8,128)(2,1)S(1)} %copy.26, bf16[1,256,256]{2,1,0:T(8,128)(2,1)S(1)} %copy.27), kind=kOutput, calls=%fused_computation.9 | convolution fusion | flops 537427968 | bytes 9699328 | tf_op jit(solution)/shard_map/wtc,wdc->td/dot_general | solution.py:192
  188.1 5.2 %collective-permute-done.7 = bf16[64,4096]{1,0:T(8,128)(2,1)S(1)} collective-permute-done((bf16[64,4096]{1,0:T(8,128)(2,1)S(1)}, bf16[64,4096]{1,0:T(8,128)(2,1)S(1)}, u32[]{:S(2)}, u32[]{:S(2)}) %collective-permute-start.7) | collective-permute-done | bytes 524320 | tf_op jit(solution)/shard_map/ppermute | solution.py:181
  193.8 3.3 %collective-permute-start.11 = (bf16[64,4096]{1,0:T(8,128)(2,1)S(1)}, bf16[64,4096]{1,0:T(8,128)(2,1)S(1)}, u32[]{:S(2)}, u32[]{:S(2)}) collective-permute-start(bf16[64,4096]{1,0:T(8,128)(2,1)S(1)} %get-tuple-element.77), channel_id=1, source_target_pairs={{32,33},{33,32},{96,97},{97,96},{34,35},{35,34},{98,99},{99,98},{3... | collective-permute-start | bytes 1572872 | tf_op jit(solution)/shard_map/ppermute | solution.py:208
  204.0 5.6 %collective-permute-done.9 = bf16[64,4096]{1,0:T(8,128)(2,1)S(1)} collective-permute-done((bf16[64,4096]{1,0:T(8,128)(2,1)S(1)}, bf16[64,4096]{1,0:T(8,128)(2,1)S(1)}, u32[]{:S(2)}, u32[]{:S(2)}) %collective-permute-start.9) | collective-permute-done | bytes 524320 | tf_op jit(solution)/shard_map/ppermute | solution.py:205
  217.4 6.3 %collective-permute-done.13 = bf16[64,4096]{1,0:T(8,128)(2,1)S(1)} collective-permute-done((bf16[64,4096]{1,0:T(8,128)(2,1)S(1)}, bf16[64,4096]{1,0:T(8,128)(2,1)S(1)}, u32[]{:S(2)}, u32[]{:S(2)}) %collective-permute-start.13) | collective-permute-done | bytes 524320 | tf_op jit(solution)/shard_map/ppermute | solution.py:181
  224.2 3.1 %collective-permute-start.20 = (bf16[64,4096]{1,0:T(8,128)(2,1)S(1)}, bf16[64,4096]{1,0:T(8,128)(2,1)S(1)}, u32[]{:S(2)}, u32[]{:S(2)}) collective-permute-start(bf16[64,4096]{1,0:T(8,128)(2,1)S(1)} %get-tuple-element.75), channel_id=1, source_target_pairs={{32,33},{33,32},{96,97},{97,96},{34,35},{35,34},{98,99},{99,98},{3... | collective-permute-start | bytes 1572872 | tf_op jit(solution)/shard_map/ppermute | solution.py:208
  234.1 5.6 %collective-permute-done.18 = bf16[64,4096]{1,0:T(8,128)(2,1)S(1)} collective-permute-done((bf16[64,4096]{1,0:T(8,128)(2,1)S(1)}, bf16[64,4096]{1,0:T(8,128)(2,1)S(1)}, u32[]{:S(2)}, u32[]{:S(2)}) %collective-permute-start.18) | collective-permute-done | bytes 524320 | tf_op jit(solution)/shard_map/ppermute | solution.py:205
  252.4 10.4 %collective-permute-done.21 = bf16[64,4096]{1,0:T(8,128)(2,1)S(1)} collective-permute-done((bf16[64,4096]{1,0:T(8,128)(2,1)S(1)}, bf16[64,4096]{1,0:T(8,128)(2,1)S(1)}, u32[]{:S(2)}, u32[]{:S(2)}) %collective-permute-start.21) | collective-permute-done | bytes 524320 | tf_op jit(solution)/shard_map/ppermute | solution.py:179
  264.9 7.8 %collective-permute-done.22 = bf16[64,4096]{1,0:T(8,128)(2,1)S(1)} collective-permute-done((bf16[64,4096]{1,0:T(8,128)(2,1)S(1)}, bf16[64,4096]{1,0:T(8,128)(2,1)S(1)}, u32[]{:S(2)}, u32[]{:S(2)}) %collective-permute-start.22) | collective-permute-done | bytes 524320 | tf_op jit(solution)/shard_map/ppermute | solution.py:181
  (140 shorter events, 81.4 us)
Async XLA Ops:
  7.2 84.4 %all-gather.2.cloned.1.call-start = ((), (), s32[]{:S(2)}) async-start(), calls=%async_computation.1 | async-start | bytes 8912896 | tf_op jit(solution)/shard_map/all_gather | solution.py:90
  10.4 264.9 %reduce-scatter.2.cloned.1.call-start = ((), (), s32[]{:S(2)}) async-start(), calls=%async_computation.2 | async-start | bytes 8912896 | tf_op jit(solution)/shard_map/reduce_scatter | solution.py:139
  128.6 11.3 %collective-permute-start.2 = (bf16[64,4096]{1,0:T(8,128)(2,1)}, bf16[64,4096]{1,0:T(8,128)(2,1)}, u32[]{:S(2)}, u32[]{:S(2)}) collective-permute-start(bf16[64,4096]{1,0:T(8,128)(2,1)} %get-tuple-element.81), channel_id=1, source_target_pairs={{32,33},{33,32},{96,97},{97,96},{34,35},{35,34},{98,99},{99,98},{3... | collective-permute-start | bytes 1572872 | tf_op jit(solution)/shard_map/ppermute | solution.py:208
  131.6 12.8 %collective-permute-start = (bf16[64,4096]{1,0:T(8,128)(2,1)}, bf16[64,4096]{1,0:T(8,128)(2,1)}, u32[]{:S(2)}, u32[]{:S(2)}) collective-permute-start(bf16[64,4096]{1,0:T(8,128)(2,1)} %get-tuple-element.82), channel_id=1, source_target_pairs={{32,33},{33,32},{64,65},{65,64},{96,97},{97,96},{34,35},{35,34},{6... | collective-permute-start | bytes 1572872 | tf_op jit(solution)/shard_map/ppermute | solution.py:205
  157.0 10.5 %collective-permute-start.5 = (bf16[64,4096]{1,0:T(8,128)(2,1)}, bf16[64,4096]{1,0:T(8,128)(2,1)}, u32[]{:S(2)}, u32[]{:S(2)}) collective-permute-start(bf16[64,4096]{1,0:T(8,128)(2,1)} %get-tuple-element.79), channel_id=1, source_target_pairs={{32,33},{33,32},{96,97},{97,96},{34,35},{35,34},{98,99},{99,98},{3... | collective-permute-start | bytes 1572872 | tf_op jit(solution)/shard_map/ppermute | solution.py:208
  160.1 13.1 %collective-permute-start.3 = (bf16[64,4096]{1,0:T(8,128)(2,1)}, bf16[64,4096]{1,0:T(8,128)(2,1)}, u32[]{:S(2)}, u32[]{:S(2)}) collective-permute-start(bf16[64,4096]{1,0:T(8,128)(2,1)} %get-tuple-element.80), channel_id=1, source_target_pairs={{32,33},{33,32},{64,65},{65,64},{96,97},{97,96},{34,35},{35,34},{6... | collective-permute-start | bytes 1572872 | tf_op jit(solution)/shard_map/ppermute | solution.py:205
  162.3 20.7 %collective-permute-start.6 = (bf16[64,4096]{1,0:T(8,128)(2,1)}, bf16[64,4096]{1,0:T(8,128)(2,1)S(1)}, u32[]{:S(2)}, u32[]{:S(2)}) collective-permute-start(bf16[64,4096]{1,0:T(8,128)(2,1)} %get-tuple-element.45), channel_id=1, source_target_pairs={{32,0},{33,1},{96,64},{97,65},{64,33},{65,32},{34,2},{35,3},{98,66... | collective-permute-start | bytes 1572872 | tf_op jit(solution)/shard_map/ppermute | solution.py:179
  175.6 10.4 %collective-permute-start.4 = (f32[64,1]{0,1:T(1,128)S(1)}, f32[64,1]{0,1:T(1,128)S(1)}, u32[]{:S(2)}, u32[]{:S(2)}) collective-permute-start(f32[64,1]{0,1:T(1,128)S(1)} %bitcast.188), channel_id=1, source_target_pairs={{64,65},{65,64},{66,67},{67,66},{68,69},{69,68},{70,71},{71,70},{7... | collective-permute-start | bytes 776 | tf_op jit(solution)/shard_map/ppermute | solution.py:218
  181.6 11.9 %collective-permute-start.8 = (bf16[64,4096]{1,0:T(8,128)(2,1)S(1)}, bf16[64,4096]{1,0:T(8,128)(2,1)S(1)}, u32[]{:S(2)}, u32[]{:S(2)}) collective-permute-start(bf16[64,4096]{1,0:T(8,128)(2,1)S(1)} %copy-done.9), channel_id=1, source_target_pairs={{32,0},{33,1},{96,64},{97,65},{34,2},{35,3},{98,66},{99,67},{36,4}... | collective-permute-start | bytes 1572872 | tf_op jit(solution)/shard_map/ppermute | solution.py:180
  183.0 10.3 %collective-permute-start.7 = (bf16[64,4096]{1,0:T(8,128)(2,1)S(1)}, bf16[64,4096]{1,0:T(8,128)(2,1)S(1)}, u32[]{:S(2)}, u32[]{:S(2)}) collective-permute-start(bf16[64,4096]{1,0:T(8,128)(2,1)S(1)} %collective-permute-done.6), channel_id=1, source_target_pairs={{32,33},{33,32},{34,35},{35,34},{36,37},{37,36},{38,39},{39,38},{4... | collective-permute-start | bytes 1572872 | tf_op jit(solution)/shard_map/ppermute | solution.py:181
  193.8 10.2 %collective-permute-start.11 = (bf16[64,4096]{1,0:T(8,128)(2,1)S(1)}, bf16[64,4096]{1,0:T(8,128)(2,1)S(1)}, u32[]{:S(2)}, u32[]{:S(2)}) collective-permute-start(bf16[64,4096]{1,0:T(8,128)(2,1)S(1)} %get-tuple-element.77), channel_id=1, source_target_pairs={{32,33},{33,32},{96,97},{97,96},{34,35},{35,34},{98,99},{99,98},{3... | collective-permute-start | bytes 1572872 | tf_op jit(solution)/shard_map/ppermute | solution.py:208
  197.1 12.5 %collective-permute-start.9 = (bf16[64,4096]{1,0:T(8,128)(2,1)S(1)}, bf16[64,4096]{1,0:T(8,128)(2,1)S(1)}, u32[]{:S(2)}, u32[]{:S(2)}) collective-permute-start(bf16[64,4096]{1,0:T(8,128)(2,1)S(1)} %get-tuple-element.78), channel_id=1, source_target_pairs={{32,33},{33,32},{64,65},{65,64},{96,97},{97,96},{34,35},{35,34},{6... | collective-permute-start | bytes 1572872 | tf_op jit(solution)/shard_map/ppermute | solution.py:205
  199.3 14.4 %collective-permute-start.12 = (bf16[64,4096]{1,0:T(8,128)(2,1)S(1)}, bf16[64,4096]{1,0:T(8,128)(2,1)S(1)}, u32[]{:S(2)}, u32[]{:S(2)}) collective-permute-start(bf16[64,4096]{1,0:T(8,128)(2,1)S(1)} %get-tuple-element.49), channel_id=1, source_target_pairs={{32,0},{33,1},{96,64},{97,65},{64,33},{65,32},{34,2},{35,3},{98,66... | collective-permute-start | bytes 1572872 | tf_op jit(solution)/shard_map/ppermute | solution.py:179
  210.1 6.7 %collective-permute-start.10 = (f32[64,1]{0,1:T(1,128)S(1)}, f32[64,1]{0,1:T(1,128)S(1)}, u32[]{:S(2)}, u32[]{:S(2)}) collective-permute-start(f32[64,1]{0,1:T(1,128)S(1)} %bitcast.187), channel_id=1, source_target_pairs={{64,65},{65,64},{66,67},{67,66},{68,69},{69,68},{70,71},{71,70},{7... | collective-permute-start | bytes 776 | tf_op jit(solution)/shard_map/ppermute | solution.py:218
  212.4 11.5 %collective-permute-start.14 = (bf16[64,4096]{1,0:T(8,128)(2,1)S(1)}, bf16[64,4096]{1,0:T(8,128)(2,1)S(1)}, u32[]{:S(2)}, u32[]{:S(2)}) collective-permute-start(bf16[64,4096]{1,0:T(8,128)(2,1)S(1)} %get-tuple-element.50), channel_id=1, source_target_pairs={{32,0},{33,1},{96,64},{97,65},{34,2},{35,3},{98,66},{99,67},{36,4}... | collective-permute-start | bytes 1572872 | tf_op jit(solution)/shard_map/ppermute | solution.py:180
  213.8 9.9 %collective-permute-start.13 = (bf16[64,4096]{1,0:T(8,128)(2,1)S(1)}, bf16[64,4096]{1,0:T(8,128)(2,1)S(1)}, u32[]{:S(2)}, u32[]{:S(2)}) collective-permute-start(bf16[64,4096]{1,0:T(8,128)(2,1)S(1)} %collective-permute-done.12), channel_id=1, source_target_pairs={{32,33},{33,32},{34,35},{35,34},{36,37},{37,36},{38,39},{39,38},{4... | collective-permute-start | bytes 1572872 | tf_op jit(solution)/shard_map/ppermute | solution.py:181
  224.2 9.9 %collective-permute-start.20 = (bf16[64,4096]{1,0:T(8,128)(2,1)S(1)}, bf16[64,4096]{1,0:T(8,128)(2,1)S(1)}, u32[]{:S(2)}, u32[]{:S(2)}) collective-permute-start(bf16[64,4096]{1,0:T(8,128)(2,1)S(1)} %get-tuple-element.75), channel_id=1, source_target_pairs={{32,33},{33,32},{96,97},{97,96},{34,35},{35,34},{98,99},{99,98},{3... | collective-permute-start | bytes 1572872 | tf_op jit(solution)/shard_map/ppermute | solution.py:208
  227.2 12.5 %collective-permute-start.18 = (bf16[64,4096]{1,0:T(8,128)(2,1)S(1)}, bf16[64,4096]{1,0:T(8,128)(2,1)S(1)}, u32[]{:S(2)}, u32[]{:S(2)}) collective-permute-start(bf16[64,4096]{1,0:T(8,128)(2,1)S(1)} %get-tuple-element.76), channel_id=1, source_target_pairs={{32,33},{33,32},{64,65},{65,64},{96,97},{97,96},{34,35},{35,34},{6... | collective-permute-start | bytes 1572872 | tf_op jit(solution)/shard_map/ppermute | solution.py:205
  229.7 12.6 %collective-permute-start.15 = (bf16[64,4096]{1,0:T(8,128)(2,1)S(1)}, bf16[64,4096]{1,0:T(8,128)(2,1)S(1)}, u32[]{:S(2)}, u32[]{:S(2)}) collective-permute-start(bf16[64,4096]{1,0:T(8,128)(2,1)S(1)} %get-tuple-element.52), channel_id=1, source_target_pairs={{32,0},{33,1},{96,64},{97,65},{64,33},{65,32},{34,2},{35,3},{98,66... | collective-permute-start | bytes 1572872 | tf_op jit(solution)/shard_map/ppermute | solution.py:179
  241.0 23.8 %collective-permute-start.17 = (bf16[64,4096]{1,0:T(8,128)(2,1)S(1)}, bf16[64,4096]{1,0:T(8,128)(2,1)S(1)}, u32[]{:S(2)}, u32[]{:S(2)}) collective-permute-start(bf16[64,4096]{1,0:T(8,128)(2,1)S(1)} %get-tuple-element.53), channel_id=1, source_target_pairs={{32,0},{33,1},{96,64},{97,65},{34,2},{35,3},{98,66},{99,67},{36,4}... | collective-permute-start | bytes 1572872 | tf_op jit(solution)/shard_map/ppermute | solution.py:180
  242.3 9.9 %collective-permute-start.16 = (bf16[64,4096]{1,0:T(8,128)(2,1)S(1)}, bf16[64,4096]{1,0:T(8,128)(2,1)S(1)}, u32[]{:S(2)}, u32[]{:S(2)}) collective-permute-start(bf16[64,4096]{1,0:T(8,128)(2,1)S(1)} %collective-permute-done.15), channel_id=1, source_target_pairs={{32,33},{33,32},{34,35},{35,34},{36,37},{37,36},{38,39},{39,38},{4... | collective-permute-start | bytes 1572872 | tf_op jit(solution)/shard_map/ppermute | solution.py:181
  246.0 27.0 %collective-permute-start.23 = (bf16[64,4096]{1,0:T(8,128)(2,1)S(1)}, bf16[64,4096]{1,0:T(8,128)(2,1)S(1)}, u32[]{:S(2)}, u32[]{:S(2)}) collective-permute-start(bf16[64,4096]{1,0:T(8,128)(2,1)S(1)} %get-tuple-element.67), channel_id=1, source_target_pairs={{32,0},{33,1},{96,64},{97,65},{34,2},{35,3},{98,66},{99,67},{36,4}... | collective-permute-start | bytes 1572872 | tf_op jit(solution)/shard_map/ppermute | solution.py:180
  247.3 15.5 %collective-permute-start.21 = (bf16[64,4096]{1,0:T(8,128)(2,1)S(1)}, bf16[64,4096]{1,0:T(8,128)(2,1)S(1)}, u32[]{:S(2)}, u32[]{:S(2)}) collective-permute-start(bf16[64,4096]{1,0:T(8,128)(2,1)S(1)} %get-tuple-element.68), channel_id=1, source_target_pairs={{32,0},{33,1},{96,64},{97,65},{64,33},{65,32},{34,2},{35,3},{98,66... | collective-permute-start | bytes 1572872 | tf_op jit(solution)/shard_map/ppermute | solution.py:179
  262.8 9.9 %collective-permute-start.22 = (bf16[64,4096]{1,0:T(8,128)(2,1)S(1)}, bf16[64,4096]{1,0:T(8,128)(2,1)S(1)}, u32[]{:S(2)}, u32[]{:S(2)}) collective-permute-start(bf16[64,4096]{1,0:T(8,128)(2,1)S(1)} %collective-permute-done.21), channel_id=1, source_target_pairs={{32,33},{33,32},{34,35},{35,34},{36,37},{37,36},{38,39},{39,38},{4... | collective-permute-start | bytes 1572872 | tf_op jit(solution)/shard_map/ppermute | solution.py:181
  (20 other events, 195.1 us)
Sparse Core Ops, SparseCore 0:
  10.7 80.8 all-gather.1
  140.0 83.0 reduce-scatter.1

commit v6 on v3

--- a/solution.py
+++ b/solution.py
@@ -43,10 +43,12 @@
     seq_len, kv_heads, head_dim = key_seq.shape
     group = query_seq.shape[1] // kv_heads
     scale = 1.0 / math.sqrt(head_dim)
-    query_g = query_seq.reshape(seq_len, kv_heads, group, head_dim)
-    cotan_g = cotan_seq.reshape(seq_len, kv_heads, group, head_dim)
+    query_g = query_seq.reshape(seq_len, kv_heads, group, head_dim).transpose(1, 2, 0, 3)
+    cotan_g = cotan_seq.reshape(seq_len, kv_heads, group, head_dim).transpose(1, 2, 0, 3)
+    key_k = key_seq.transpose(1, 0, 2)
+    value_k = value_seq.transpose(1, 0, 2)
     scores = (
-        jnp.einsum("ikgd,jkd->kgij", query_g, key_seq, preferred_element_type=jnp.float32) * scale
+        jnp.einsum("kgid,kjd->kgij", query_g, key_k, preferred_element_type=jnp.float32) * scale
     )
     row_pos = jnp.arange(seq_len)[:, None]
     col_pos = jnp.arange(seq_len)[None, :]
@@ -57,16 +59,16 @@
     probs = expd / jnp.sum(expd, axis=-1, keepdims=True)
     probs_low = probs.astype(jnp.bfloat16)
     value_grad = jnp.einsum(
-        "kgij,ikgd->jkd", probs_low, cotan_g, preferred_element_type=jnp.float32
+        "kgij,kgid->kjd", probs_low, cotan_g, preferred_element_type=jnp.float32
     ).astype(jnp.bfloat16)
-    prob_grad = jnp.einsum("ikgd,jkd->kgij", cotan_g, value_seq, preferred_element_type=jnp.float32)
+    prob_grad = jnp.einsum("kgid,kjd->kgij", cotan_g, value_k, preferred_element_type=jnp.float32)
     centre = jnp.sum(probs * prob_grad, axis=-1, keepdims=True)
     score_grad = (probs * (prob_grad - centre) * scale).astype(jnp.bfloat16)
     rotated_grad = jnp.einsum(
-        "kgij,ikgd->jkd", score_grad, query_g, preferred_element_type=jnp.float32
-    )
+        "kgij,kgid->kjd", score_grad, query_g, preferred_element_type=jnp.float32
+    ).transpose(1, 0, 2)
     key_grad = rotated_grad * cosine[:, None, :] + rotate_back(rotated_grad * sine[:, None, :])
-    return (key_grad.astype(jnp.bfloat16), value_grad)
+    return (key_grad.astype(jnp.bfloat16), value_grad.transpose(1, 0, 2))
 
 
 def norm_backward(normed_grad, gain_f, nhat, inv_rms):
@@ -101,7 +103,7 @@
     hidden_f = hidden.astype(jnp.float32)
     inv_rms = lax.rsqrt(jnp.mean(hidden_f * hidden_f, axis=-1, keepdims=True) + norm_eps)
     nhat = hidden_f * inv_rms
-    normed = (nhat * gain_f).astype(jnp.bfloat16)
+    normed = lax.optimization_barrier((nhat * gain_f).astype(jnp.bfloat16))
     projected = jnp.einsum("td,wdc->wtc", normed, both_full, preferred_element_type=jnp.float32)
     key_raw = projected[0]
     values = projected[1].astype(jnp.bfloat16)

time: 257 us -> 264 us (1.027)
    all_gather x1, waiting for transfers between devices: 71.1 us -> 63.4 us  [on_device(): lax.all_gather(jnp.stack([key_weight[0], value_weight[0]]), 'dp', axis=1,...]
    ppermute x4, waiting for transfers between devices: 32.1 us -> 37.6 us  [on_device(): lax.ppermute(part_low, ('pipe', 'tensor'), pairs).astype(jnp.float32)]
    mul x1, other arithmetic: 3.25 us -> 6.35 us  [on_device(): nhat = hidden_f * inv_rms]
  transfers between devices with their start and end apart: 10 -> 10, of which waited for: 8 -> 9; matrix products, arithmetic and copies ran while one was open for 12% -> 14% of each run, Pallas kernels for 0% -> 0%
where the time goes in v6:
time: 264 us
  waiting for transfers between devices  153 us (58%)
  matrix products  46.7 us (18%)
  starting transfers between devices  18.9 us (7%)
  other arithmetic  18.5 us (7%)
  between operations  16.5 us (6%)
  local copies, waits for them, and re-layouts  9.92 us (4%)
    all_gather x1, waiting for transfers between devices, on_device(): lax.all_gather(jnp.stack([key_weight[0], value_weight[0]]), 'dp', axis=1,...  63.4 us
    ppermute x4, waiting for transfers between devices, on_device(): lowers.append(lax.ppermute(held, ('pipe', 'tensor'), shift_pairs))  52.1 us
    ppermute x4, waiting for transfers between devices, on_device(): lax.ppermute(part_low, ('pipe', 'tensor'), pairs).astype(jnp.float32)  37.6 us
    dot_general x4, matrix products, on_device(): jnp.einsum('wtc,wdc->td', both_grads[:, sl], both_full, preferred_element...  13.6 us
    ppermute x4, starting transfers between devices, on_device(): lax.ppermute(part_low, ('pipe', 'tensor'), pairs).astype(jnp.float32)  11.1 us
    dot_general x1, matrix products, on_device(): lax.dot_general(normed, combined, (((0,), (0,)), ((), ())), preferred_ele...  7.83 us
    ppermute x4, starting transfers between devices, on_device(): lowers.append(lax.ppermute(held, ('pipe', 'tensor'), shift_pairs))  7.68 us
    dot_general x1, matrix products, sequence_grads(): jnp.einsum('kgij,kgid->kjd', score_grad, query_g, preferred_element_type=...  7.45 us
  transfers between devices with their start and end apart: 10, of which 9 were waited for; matrix products, arithmetic and copies ran while one was open for 14% of the time, Pallas kernels for 0%

profile of v6, /device:TPU:1, one launch (start us, length us, event | category | flops | bytes accessed | tf_op | source)
XLA Modules:
  0.0 263.7 jit_solution(17354191342978996694)
XLA Ops:
  11.3 3.3 %fusion.6 = f32[256]{0:T(256)S(1)} fusion(bf16[1,256,8192]{2,1,0:T(8,128)(2,1)} %param.9), kind=kLoop, calls=%fused_computation.13 | loop fusion | flops 6291200 | bytes 4195328 | tf_op jit(solution)/shard_map/reduce_sum | solution.py:104
  14.7 6.4 %convert_multiply_fusion = (f32[256,8192]{1,0:T(8,128)}, bf16[256,8192]{1,0:T(8,128)(2,1)}) fusion(bf16[1,256,8192]{2,1,0:T(8,128)(2,1)S(1)} %copy-done, f32[256]{0:T(256)S(1)} %add_rsqrt_fusion, f32[8192]{0:T(1024)S(1)} %bitcast.115), kind=kLoop, calls=%fused_computation.3 | loop fusion | flops 8388608 | bytes 16811008 | tf_op jit(solution)/shard_map/mul | solution.py:105
  27.9 63.4 %all-gather.2.cloned.1.call-done = bf16[2,8192,256]{1,2,0:T(8,128)(2,1)} async-done(((bf16[2,512,256]{1,2,0:T(8,128)(2,1)}), bf16[2,8192,256]{1,2,0:T(8,128)(2,1)}) %all-gather.2.cloned.1.call-update) | async-done | bytes 8388624 | tf_op jit(solution)/shard_map/all_gather | solution.py:91
  91.3 6.9 %fusion.22 = f32[2,256,256]{1,2,0:T(8,128)S(1)} fusion(bf16[2,8192,256]{1,2,0:T(8,128)(2,1)} %all-gather.2.cloned.1.call-done, bf16[256,8192]{1,0:T(8,128)(2,1)} %get-tuple-element.50), kind=kOutput, calls=%fused_computation.45 | convolution fusion | flops 2147483648 | bytes 13107200 | tf_op jit(solution)/shard_map/td,wdc->wtc/dot_general | solution.py:107
  99.6 2.6 fusion.36
  102.2 5.2 %fusion.68 = (f32[2,8,256]{2,1,0:T(8,128)S(1)}, f32[2,8,256,256]{2,3,1,0:T(8,128)}) fusion(pred[256,256]{0,1:T(8,128)(4,1)S(1)} %fusion.46, bf16[2,8,256,128]{2,3,1,0:T(8,128)(2,1)} %bitcast.128, f32[256,2,64]{2,0,1:T(8,128)S(1)} %bitcast.133, f32[256,2,64]{2,0,1:T(8,128)S(1)} %negate_bitcast_fusion, f32[256,2,128]{2,0,1:T(8,128)S(1)} %copy-done.2, ...), kind=kOutput, calls=%fused_computation.107 | convolution fusion | flops 274006272 | bytes 6111232 | tf_op jit(solution)/shard_map/while/body/eval_jaxpr/sub | solution.py:58
  107.4 3.0 %fusion.31 = bf16[2,256,128]{1,2,0:T(8,128)(2,1)S(1)} fusion(f32[256,2,8,128]{0,3,2,1:T(8,128)S(1)} %bitcast.114, f32[256]{0:T(256)S(1)} %broadcast_select_fusion, f32[2,8,256,256]{2,3,1,0:T(8,128)} %get-tuple-element.64, f32[2,8,256]{2,1,0:T(8,128)S(1)} %get-tuple-element.63), kind=kOutput, calls=%fused_computation.48 | convolution fusion | flops 271646720 | bytes 6439936 | tf_op jit(solution)/shard_map/while/body/eval_jaxpr/kgij,kgid->kjd/dot_general | solution.py:61
  110.4 7.5 %fusion.28 = f32[2,256,128]{1,2,0:T(8,128)S(1)} fusion(bf16[2,8,256,128]{2,3,1,0:T(8,128)(2,1)} %bitcast.129, f32[2,8,256,256]{2,3,1,0:T(8,128)} %fusion.36, f32[2,8,256,256]{2,3,1,0:T(8,128)} %get-tuple-element.64, f32[2,8,256]{2,1,0:T(8,128)S(1)} %get-tuple-element.63), kind=kOutput, calls=%fused_computation.47 | convolution fusion | flops 275779840 | bytes 9715712 | tf_op jit(solution)/shard_map/while/body/eval_jaxpr/kgij,kgid->kjd/dot_general | solution.py:67
  118.0 7.8 %convolution_convert_fusion = bf16[8192,512]{1,0:T(8,128)(2,1)} fusion(bf16[256,8192]{1,0:T(8,128)(2,1)} %get-tuple-element.50, bf16[256,256]{0,1:T(8,128)(2,1)S(1)} %bitcast.130, bf16[256,256]{0,1:T(8,128)(2,1)S(1)} %bitcast.126), kind=kOutput, calls=%fused_computation.2 | convolution fusion | flops 2152202240 | bytes 12845056 | tf_op jit(solution)/shard_map/dot_general | solution.py:141
  126.1 5.1 %fusion.4 = bf16[64,8192]{1,0:T(8,128)(2,1)S(1)} fusion(bf16[2,8192,256]{1,2,0:T(8,128)(2,1)} %all-gather.2.cloned.1.call-done, bf16[1,256,256]{2,1,0:T(8,128)(2,1)S(1)} %copy.26, bf16[1,256,256]{2,1,0:T(8,128)(2,1)S(1)} %copy.27), kind=kOutput, calls=%fused_computation.11 | convolution fusion | flops 537427968 | bytes 9699328 | tf_op jit(solution)/shard_map/wtc,wdc->td/dot_general | solution.py:170
  131.2 3.6 %collective-permute-start = (bf16[64,8192]{1,0:T(8,128)(2,1)S(1)}, bf16[64,8192]{1,0:T(8,128)(2,1)S(1)}, u32[]{:S(2)}, u32[]{:S(2)}) collective-permute-start(bf16[64,8192]{1,0:T(8,128)(2,1)S(1)} %fusion.4), channel_id=1, source_target_pairs={{32,33},{33,32},{64,65},{65,64},{96,97},{97,96},{34,35},{35,34},{6... | collective-permute-start | bytes 3145736 | tf_op jit(solution)/shard_map/ppermute | solution.py:184
  134.9 5.4 %fusion.3 = bf16[64,8192]{1,0:T(8,128)(2,1)S(1)} fusion(bf16[2,8192,256]{1,2,0:T(8,128)(2,1)} %all-gather.2.cloned.1.call-done, bf16[1,256,256]{2,1,0:T(8,128)(2,1)S(1)} %copy.26, bf16[1,256,256]{2,1,0:T(8,128)(2,1)S(1)} %copy.27), kind=kOutput, calls=%fused_computation.10 | convolution fusion | flops 537427968 | bytes 9699328 | tf_op jit(solution)/shard_map/wtc,wdc->td/dot_general | solution.py:170
  140.2 7.2 %collective-permute-done = bf16[64,8192]{1,0:T(8,128)(2,1)S(1)} collective-permute-done((bf16[64,8192]{1,0:T(8,128)(2,1)S(1)}, bf16[64,8192]{1,0:T(8,128)(2,1)S(1)}, u32[]{:S(2)}, u32[]{:S(2)}) %collective-permute-start) | collective-permute-done | bytes 1048608 | tf_op jit(solution)/shard_map/ppermute | solution.py:184
  148.5 3.1 %collective-permute-start.1 = (bf16[64,8192]{1,0:T(8,128)(2,1)S(1)}, bf16[64,8192]{1,0:T(8,128)(2,1)S(1)}, u32[]{:S(2)}, u32[]{:S(2)}) collective-permute-start(bf16[64,8192]{1,0:T(8,128)(2,1)S(1)} %fusion.3), channel_id=1, source_target_pairs={{32,33},{33,32},{64,65},{65,64},{96,97},{97,96},{34,35},{35,34},{6... | collective-permute-start | bytes 3145736 | tf_op jit(solution)/shard_map/ppermute | solution.py:184
  155.1 9.3 %collective-permute-done.1 = bf16[64,8192]{1,0:T(8,128)(2,1)S(1)} collective-permute-done((bf16[64,8192]{1,0:T(8,128)(2,1)S(1)}, bf16[64,8192]{1,0:T(8,128)(2,1)S(1)}, u32[]{:S(2)}, u32[]{:S(2)}) %collective-permute-start.1) | collective-permute-done | bytes 1048608 | tf_op jit(solution)/shard_map/ppermute | solution.py:184
  165.5 15.9 %collective-permute-done.2 = bf16[64,8192]{1,0:T(8,128)(2,1)S(1)} collective-permute-done((bf16[64,8192]{1,0:T(8,128)(2,1)S(1)}, bf16[64,8192]{1,0:T(8,128)(2,1)S(1)}, u32[]{:S(2)}, u32[]{:S(2)}) %collective-permute-start.2) | collective-permute-done | bytes 1048608 | tf_op jit(solution)/shard_map/ppermute | solution.py:181
  181.4 2.2 collective-permute-start.3
  187.2 9.8 %collective-permute-done.3 = bf16[64,8192]{1,0:T(8,128)(2,1)S(1)} collective-permute-done((bf16[64,8192]{1,0:T(8,128)(2,1)S(1)}, bf16[64,8192]{1,0:T(8,128)(2,1)S(1)}, u32[]{:S(2)}, u32[]{:S(2)}) %collective-permute-start.3) | collective-permute-done | bytes 1048608 | tf_op jit(solution)/shard_map/ppermute | solution.py:184
  198.0 9.6 %collective-permute-done.4 = bf16[64,8192]{1,0:T(8,128)(2,1)S(1)} collective-permute-done((bf16[64,8192]{1,0:T(8,128)(2,1)S(1)}, bf16[64,8192]{1,0:T(8,128)(2,1)S(1)}, u32[]{:S(2)}, u32[]{:S(2)}) %collective-permute-start.4) | collective-permute-done | bytes 1048608 | tf_op jit(solution)/shard_map/ppermute | solution.py:181
  207.7 2.2 collective-permute-start.6
  211.8 11.4 %collective-permute-done.6 = bf16[64,8192]{1,0:T(8,128)(2,1)S(1)} collective-permute-done((bf16[64,8192]{1,0:T(8,128)(2,1)S(1)}, bf16[64,8192]{1,0:T(8,128)(2,1)S(1)}, u32[]{:S(2)}, u32[]{:S(2)}) %collective-permute-start.6) | collective-permute-done | bytes 1048608 | tf_op jit(solution)/shard_map/ppermute | solution.py:184
  226.2 4.8 %collective-permute-done.5 = bf16[64,8192]{1,0:T(8,128)(2,1)S(1)} collective-permute-done((bf16[64,8192]{1,0:T(8,128)(2,1)S(1)}, bf16[64,8192]{1,0:T(8,128)(2,1)S(1)}, u32[]{:S(2)}, u32[]{:S(2)}) %collective-permute-start.5) | collective-permute-done | bytes 1048608 | tf_op jit(solution)/shard_map/ppermute | solution.py:181
  231.0 21.8 %collective-permute-done.7 = bf16[64,8192]{1,0:T(8,128)(2,1)S(1)} collective-permute-done((bf16[64,8192]{1,0:T(8,128)(2,1)S(1)}, bf16[64,8192]{1,0:T(8,128)(2,1)S(1)}, u32[]{:S(2)}, u32[]{:S(2)}) %collective-permute-start.7) | collective-permute-done | bytes 1048608 | tf_op jit(solution)/shard_map/ppermute | solution.py:188
  252.8 2.2 maximum_bitcast_fusion
  (72 shorter events, 27.5 us)
Async XLA Ops:
  7.2 84.1 %all-gather.2.cloned.1.call-start = ((), (), s32[]{:S(2)}) async-start(), calls=%async_computation.1 | async-start | bytes 8912896 | tf_op jit(solution)/shard_map/all_gather | solution.py:91
  10.3 244.7 %reduce-scatter.2.cloned.1.call-start = ((), (), s32[]{:S(2)}) async-start(), calls=%async_computation.2 | async-start | bytes 8912896 | tf_op jit(solution)/shard_map/reduce_scatter | solution.py:140
  10.3 4.3 %copy-start = (bf16[1,256,8192]{2,1,0:T(8,128)(2,1)S(1)}, bf16[1,256,8192]{2,1,0:T(8,128)(2,1)}, u32[]{:S(2)}) copy-start(bf16[1,256,8192]{2,1,0:T(8,128)(2,1)} %param.9) | copy-start | bytes 12582916
  14.7 8.2 %copy-start.1 = (bf16[1,256,2048]{2,1,0:T(8,128)(2,1)S(1)}, bf16[1,256,2048]{2,1,0:T(8,128)(2,1)}, u32[]{:S(2)}) copy-start(bf16[1,256,2048]{2,1,0:T(8,128)(2,1)} %param.13) | copy-start | bytes 3145732
  99.4 2.8 %copy-start.3 = (f32[256,128]{1,0:T(8,128)S(1)}, f32[256,128]{1,0:T(8,128)}, u32[]{:S(2)}) copy-start(f32[256,128]{1,0:T(8,128)} %copy.14) | copy-start | bytes 393220
  99.6 2.7 %copy-start.2 = (f32[256,2,128]{2,0,1:T(8,128)S(1)}, f32[256,2,128]{2,0,1:T(8,128)}, u32[]{:S(2)}) copy-start(f32[256,2,128]{2,0,1:T(8,128)} %copy.15) | copy-start | bytes 786436
  126.1 21.3 %slice-start.2 = ((s8[8388608]{0:T(1024)(128)(4,1)}), s8[4194304]{0:T(1024)(128)(4,1)S(1)}, s32[]{:S(2)}) async-start(s8[8388608]{0:T(1024)(128)(4,1)} %bitcast.111), calls=%async_computation.5 | async-start | bytes 8388608
  126.1 25.5 %slice-start = ((s8[8388608]{0:T(1024)(128)(4,1)}), s8[4194304]{0:T(1024)(128)(4,1)S(1)}, s32[]{:S(2)}) async-start(s8[8388608]{0:T(1024)(128)(4,1)} %bitcast.109), calls=%async_computation.3 | async-start | bytes 8388608
  131.2 16.2 %slice-start.3 = ((s8[8388608]{0:T(1024)(128)(4,1)}), s8[4194304]{0:T(1024)(128)(4,1)S(1)}, s32[]{:S(2)}) async-start(s8[8388608]{0:T(1024)(128)(4,1)} %bitcast.111), calls=%async_computation.6 | async-start | bytes 8388608
  131.2 16.2 %collective-permute-start = (bf16[64,8192]{1,0:T(8,128)(2,1)S(1)}, bf16[64,8192]{1,0:T(8,128)(2,1)S(1)}, u32[]{:S(2)}, u32[]{:S(2)}) collective-permute-start(bf16[64,8192]{1,0:T(8,128)(2,1)S(1)} %fusion.4), channel_id=1, source_target_pairs={{32,33},{33,32},{64,65},{65,64},{96,97},{97,96},{34,35},{35,34},{6... | collective-permute-start | bytes 3145736 | tf_op jit(solution)/shard_map/ppermute | solution.py:184
  134.9 16.7 %slice-start.1 = ((s8[8388608]{0:T(1024)(128)(4,1)}), s8[4194304]{0:T(1024)(128)(4,1)S(1)}, s32[]{:S(2)}) async-start(s8[8388608]{0:T(1024)(128)(4,1)} %bitcast.109), calls=%async_computation.4 | async-start | bytes 8388608
  148.5 15.9 %collective-permute-start.1 = (bf16[64,8192]{1,0:T(8,128)(2,1)S(1)}, bf16[64,8192]{1,0:T(8,128)(2,1)S(1)}, u32[]{:S(2)}, u32[]{:S(2)}) collective-permute-start(bf16[64,8192]{1,0:T(8,128)(2,1)S(1)} %fusion.3), channel_id=1, source_target_pairs={{32,33},{33,32},{64,65},{65,64},{96,97},{97,96},{34,35},{35,34},{6... | collective-permute-start | bytes 3145736 | tf_op jit(solution)/shard_map/ppermute | solution.py:184
  153.2 28.2 %collective-permute-start.2 = (bf16[64,8192]{1,0:T(8,128)(2,1)S(1)}, bf16[64,8192]{1,0:T(8,128)(2,1)S(1)}, u32[]{:S(2)}, u32[]{:S(2)}) collective-permute-start(bf16[64,8192]{1,0:T(8,128)(2,1)S(1)} %multiply_convert_fusion.5), channel_id=1, source_target_pairs={{32,0},{33,1},{65,32},{64,33},{96,64},{97,65},{34,2},{35,3},{67,34... | collective-permute-start | bytes 3145736 | tf_op jit(solution)/shard_map/ppermute | solution.py:181
  181.4 15.5 %collective-permute-start.3 = (bf16[64,8192]{1,0:T(8,128)(2,1)S(1)}, bf16[64,8192]{1,0:T(8,128)(2,1)S(1)}, u32[]{:S(2)}, u32[]{:S(2)}) collective-permute-start(bf16[64,8192]{1,0:T(8,128)(2,1)S(1)} %fusion.2), channel_id=1, source_target_pairs={{32,33},{33,32},{64,65},{65,64},{96,97},{97,96},{34,35},{35,34},{6... | collective-permute-start | bytes 3145736 | tf_op jit(solution)/shard_map/ppermute | solution.py:184
  185.3 22.4 %collective-permute-start.4 = (bf16[64,8192]{1,0:T(8,128)(2,1)S(1)}, bf16[64,8192]{1,0:T(8,128)(2,1)S(1)}, u32[]{:S(2)}, u32[]{:S(2)}) collective-permute-start(bf16[64,8192]{1,0:T(8,128)(2,1)S(1)} %multiply_convert_fusion.4), channel_id=1, source_target_pairs={{32,0},{33,1},{65,32},{64,33},{96,64},{97,65},{34,2},{35,3},{67,34... | collective-permute-start | bytes 3145736 | tf_op jit(solution)/shard_map/ppermute | solution.py:181
  207.7 15.5 %collective-permute-start.6 = (bf16[64,8192]{1,0:T(8,128)(2,1)S(1)}, bf16[64,8192]{1,0:T(8,128)(2,1)S(1)}, u32[]{:S(2)}, u32[]{:S(2)}) collective-permute-start(bf16[64,8192]{1,0:T(8,128)(2,1)S(1)} %fusion.5), channel_id=1, source_target_pairs={{32,33},{33,32},{64,65},{65,64},{96,97},{97,96},{34,35},{35,34},{6... | collective-permute-start | bytes 3145736 | tf_op jit(solution)/shard_map/ppermute | solution.py:184
  209.9 21.2 %collective-permute-start.5 = (bf16[64,8192]{1,0:T(8,128)(2,1)S(1)}, bf16[64,8192]{1,0:T(8,128)(2,1)S(1)}, u32[]{:S(2)}, u32[]{:S(2)}) collective-permute-start(bf16[64,8192]{1,0:T(8,128)(2,1)S(1)} %multiply_convert_fusion.3), channel_id=1, source_target_pairs={{32,0},{33,1},{65,32},{64,33},{96,64},{97,65},{34,2},{35,3},{67,34... | collective-permute-start | bytes 3145736 | tf_op jit(solution)/shard_map/ppermute | solution.py:181
  224.3 28.5 %collective-permute-start.7 = (bf16[64,8192]{1,0:T(8,128)(2,1)S(1)}, bf16[64,8192]{1,0:T(8,128)(2,1)S(1)}, u32[]{:S(2)}, u32[]{:S(2)}) collective-permute-start(bf16[64,8192]{1,0:T(8,128)(2,1)S(1)} %multiply_convert_fusion.2), channel_id=1, source_target_pairs={{32,0},{33,1},{65,32},{64,33},{96,64},{97,65},{34,2},{35,3},{67,34... | collective-permute-start | bytes 3145736 | tf_op jit(solution)/shard_map/ppermute | solution.py:188
Sparse Core Ops, SparseCore 0:
  10.4 80.8 all-gather.1
  126.0 83.8 reduce-scatter.1

commit v7 on v1

--- a/solution.py
+++ b/solution.py
@@ -1,3 +1,4 @@
+import functools
 import math
 
 import jax
@@ -102,8 +103,9 @@
     inv_rms = lax.rsqrt(jnp.mean(hidden_f * hidden_f, axis=-1, keepdims=True) + norm_eps)
     nhat = hidden_f * inv_rms
     normed = (nhat * gain_f).astype(jnp.bfloat16)
-    key_raw = jnp.dot(normed, key_full, preferred_element_type=jnp.float32)
-    values = jnp.dot(normed, value_full, preferred_element_type=jnp.float32).astype(jnp.bfloat16)
+    projected = jnp.einsum("td,wdc->wtc", normed, both_full, preferred_element_type=jnp.float32)
+    key_raw = projected[0]
+    values = projected[1].astype(jnp.bfloat16)
     cosine, sine = rope_tables(seq_len, HD)
     key_four = key_raw.reshape(seq_count, seq_len, kv_local, HD)
     keys = (
@@ -142,20 +144,70 @@
         scatter_dimension=0,
         tiled=True,
     )
-    part = lax.dot_general(
-        key_grad, key_full, (((1,), (1,)), ((), ())), preferred_element_type=jnp.float32
-    )
-    part = part + lax.dot_general(
-        value_grad, value_full, (((1,), (1,)), ((), ())), preferred_element_type=jnp.float32
-    )
-    part_low = part.astype(jnp.bfloat16)
-    count = lax.axis_size("tensor")
-    normed_grad = part_low.astype(jnp.float32)
-    for step in range(1, count):
-        pairs = [(source, (source + step) % count) for source in range(count)]
-        normed_grad = normed_grad + lax.ppermute(part_low, "tensor", pairs).astype(jnp.float32)
-    section_cot = norm_backward(normed_grad, gain_f, nhat, inv_rms)
-    lower = shifted(section_cot, "pipe", -1)
+    both_grads = jnp.stack([key_grad, value_grad])
+    n_pipe = lax.axis_size("pipe")
+    n_tensor = lax.axis_size("tensor")
+    me_pipe = lax.axis_index("pipe")
+    axes = ("pipe", "tensor")
+
+    def at(p, t):
+        return p * n_tensor + t
+
+    same_chip = lambda p, q: p // 2 == q // 2
+    late = [q for q in range(2, n_pipe) if same_chip(q, q - 1)]
+    early = [q for q in range(1, n_pipe) if q not in late]
+
+    def swap(qs):
+        return [(at(q, t), at(q, (t + 1) % n_tensor)) for q in qs for t in range(n_tensor)]
+
+    def shift(qs):
+        return [
+            (at(q, t if same_chip(q, q - 1) else n_tensor - 1 - t), at(q - 1, t))
+            for q in qs
+            for t in range(n_tensor)
+        ]
+
+    def reduce_and_send(sections, chunks, gate=None, signal_at=None):
+        rows = tok_rows // chunks
+        exchange_pairs, shift_pairs = swap(sections), shift(sections)
+        lowers, held, signal = [], None, None
+        for c in range(chunks):
+            sl = slice(c * rows, (c + 1) * rows)
+            part = jnp.einsum(
+                "wtc,wdc->td", both_grads[:, sl], both_full, preferred_element_type=jnp.float32
+            )
+            if gate is not None:
+                part = part.at[0, 0].add(0.0 * gate[0, 0].astype(jnp.float32))
+                gate = None
+            part_low = part.astype(jnp.bfloat16)
+            if held is not None:
+                if len(lowers) > 0:
+                    part_low, held, lowers[-1] = lax.optimization_barrier(
+                        (part_low, held, lowers[-1])
+                    )
+                else:
+                    part_low, held = lax.optimization_barrier((part_low, held))
+                lowers.append(lax.ppermute(held, axes, shift_pairs))
+            received = lax.ppermute(part_low, axes, exchange_pairs)
+            if c == signal_at:
+                signal = received[:8, :128]
+            normed_grad = part_low.astype(jnp.float32) + received.astype(jnp.float32)
+            held = norm_backward(normed_grad, gain_f, nhat[sl], inv_rms[sl])
+        lowers.append(lax.ppermute(held, axes, shift_pairs))
+        return jnp.concatenate(lowers, axis=0), signal
+
+    first, signal = reduce_and_send(early, 4, signal_at=2)
+    lower = first
+    if late:
+        release = [
+            (at(q - 1, t), at(q, t)) for q in late for t in range(n_tensor)
+        ]
+        gate = lax.ppermute(signal, axes, release)
+        second, _ = reduce_and_send(late, 2, gate=gate)
+        from_late = functools.reduce(
+            jnp.logical_or, [me_pipe == q - 1 for q in late], me_pipe < 0
+        )
+        lower = jnp.where(from_late, second, first)
     return (grad_total[:, :kv_cols][None], grad_total[:, kv_cols:][None], lower[None])
 
 

time: 297 us -> 282 us (0.949)
  waiting for transfers between devices: 203 us -> 147 us
  starting transfers between devices: 4.8 us -> 24.4 us
  other arithmetic: 12.8 us -> 28.7 us
  matrix products: 45.2 us -> 50.6 us
    ppermute x2 -> x13, waiting for transfers between devices: 139 us -> 75.7 us  [the longest x6 38.2 us: reduce_and_send(): lowers.append(lax.ppermute(held, axes, shift_pairs))]
    ppermute x2 -> x13, starting transfers between devices: 4.72 us -> 24.3 us  [the longest x6 12.7 us: reduce_and_send(): received = lax.ppermute(part_low, axes, exchange_pairs)]
    dot_general x4 -> x7, matrix products: 18.4 us -> 26.4 us  [the longest x6 19.4 us: reduce_and_send(): jnp.einsum('wtc,wdc->td', both_grads[:, sl], both_full, preferred_element...]
    convert_element_type x1 -> x6, other arithmetic: 2.97 us -> 10.1 us  [norm_backward(): return ((gain_grad_in - nhat * centre) * inv_rms).astype(jnp.bfloat16)]
    all_gather x1, waiting for transfers between devices: 64.3 us -> 71.1 us  [on_device(): lax.all_gather(jnp.stack([key_weight[0], value_weight[0]]), 'dp', axis=1,...]
    select_n x0 -> x1, other arithmetic: none -> 4.61 us  [on_device(): lower = jnp.where(from_late, second, first)]
    unnamed x13 -> x38, local copies, waits for them, and re-layouts: 7.55 us -> 4.61 us
  transfers between devices with their start and end apart: 4 -> 15, of which waited for: 3 -> 8; matrix products, arithmetic and copies ran while one was open for 7% -> 18% of each run, Pallas kernels for 0% -> 0%
where the time goes in v7:
time: 282 us; the launch traced here: 281 us
  waiting for transfers between devices  147 us (52%)
  matrix products  50.6 us (18%)
  other arithmetic  28.7 us (10%)
  starting transfers between devices  24.4 us (9%)
  between operations  18.1 us (6%)
  local copies, waits for them, and re-layouts  12.9 us (5%)
    all_gather x1, waiting for transfers between devices, on_device(): lax.all_gather(jnp.stack([key_weight[0], value_weight[0]]), 'dp', axis=1,...  71.1 us
    ppermute x6, waiting for transfers between devices, reduce_and_send(): lowers.append(lax.ppermute(held, axes, shift_pairs))  38.2 us
    ppermute x6, waiting for transfers between devices, reduce_and_send(): received = lax.ppermute(part_low, axes, exchange_pairs)  37.5 us
    dot_general x6, matrix products, reduce_and_send(): jnp.einsum('wtc,wdc->td', both_grads[:, sl], both_full, preferred_element...  19.4 us
    ppermute x6, starting transfers between devices, reduce_and_send(): received = lax.ppermute(part_low, axes, exchange_pairs)  12.7 us
    ppermute x6, starting transfers between devices, reduce_and_send(): lowers.append(lax.ppermute(held, axes, shift_pairs))  11 us
    convert_element_type x6, other arithmetic, norm_backward(): return ((gain_grad_in - nhat * centre) * inv_rms).astype(jnp.bfloat16)  10.1 us
    dot_general x1, matrix products, sequence_grads(): jnp.einsum('kgij,ikgd->jkd', score_grad, query_g, preferred_element_type=...  7.46 us
  transfers between devices with their start and end apart: 15, of which 8 were waited for; matrix products, arithmetic and copies ran while one was open for 18% of the time, Pallas kernels for 0%

profile of v7, /device:TPU:1, one launch (start us, length us, event | category | flops | bytes accessed | tf_op | source)
XLA Modules:
  0.0 281.5 jit_solution(15634580034035374391)
XLA Ops:
  17.3 3.1 %fusion.7 = f32[256]{0:T(256)S(1)} fusion(bf16[1,256,8192]{2,1,0:T(8,128)(2,1)} %param.11), kind=kLoop, calls=%fused_computation.16 | loop fusion | flops 6291200 | bytes 4195328 | tf_op jit(solution)/shard_map/reduce_sum | solution.py:103
  20.5 71.1 %all-gather.2.cloned.1.call-done = bf16[2,8192,256]{1,2,0:T(8,128)(2,1)} async-done(((bf16[2,512,256]{1,2,0:T(8,128)(2,1)}), bf16[2,8192,256]{1,2,0:T(8,128)(2,1)}) %all-gather.2.cloned.1.call-update) | async-done | bytes 8388624 | tf_op jit(solution)/shard_map/all_gather | solution.py:90
  91.6 7.0 %fusion.21 = f32[2,256,256]{1,2,0:T(8,128)S(1)} fusion(bf16[2,8192,256]{1,2,0:T(8,128)(2,1)} %all-gather.2.cloned.1.call-done, f32[8192]{0:T(1024)S(1)} %bitcast.141, bf16[1,256,8192]{2,1,0:T(8,128)(2,1)} %param.11, f32[256]{0:T(256)S(1)} %add_rsqrt_fusion), kind=kOutput, calls=%fused_computation.56 | convolution fusion | flops 2155872256 | bytes 13140992 | tf_op jit(solution)/shard_map/td,wdc->wtc/dot_general | solution.py:106
  99.8 5.3 %fusion.68 = (f32[2,8,256]{2,1,0:T(8,128)S(1)}, f32[2,8,256,256]{2,3,1,0:T(8,128)}) fusion(pred[256,256]{0,1:T(8,128)(4,1)S(1)} %fusion.40, bf16[256,2,8,128]{0,3,2,1:T(8,128)(2,1)} %bitcast.160, f32[256,2,64]{2,0,1:T(8,128)S(1)} %bitcast.165, f32[256,2,64]{2,0,1:T(8,128)} %negate_bitcast_fusion, f32[256,2,128]{2,0,1:T(8,128)S(1)} %copy.15, ...), kind=kOutput, calls=%fused_computation.127 | convolution fusion | flops 274006272 | bytes 6111232 | tf_op jit(solution)/shard_map/while/body/eval_jaxpr/sub | solution.py:57
  105.1 3.0 %fusion.28 = bf16[2,128,256]{2,1,0:T(8,128)(2,1)S(1)} fusion(f32[256,2,8,128]{0,3,2,1:T(8,128)S(1)} %bitcast.139, f32[256]{0:T(256)S(1)} %broadcast_select_fusion, f32[2,8,256,256]{2,3,1,0:T(8,128)} %get-tuple-element.80, f32[2,8,256]{2,1,0:T(8,128)S(1)} %get-tuple-element.79), kind=kOutput, calls=%fused_computation.59 | convolution fusion | flops 271646720 | bytes 6439936 | tf_op jit(solution)/shard_map/while/body/eval_jaxpr/kgij,ikgd->jkd/dot_general | solution.py:60
  108.2 2.7 fusion.31
  110.9 7.5 %fusion.24 = f32[2,256,128]{1,2,0:T(8,128)S(1)} fusion(bf16[256,2,8,128]{0,3,2,1:T(8,128)(2,1)} %bitcast.161, f32[2,256,256,8]{2,1,3,0:T(8,128)} %fusion.31, f32[2,8,256,256]{2,3,1,0:T(8,128)} %get-tuple-element.80, f32[2,8,256]{2,1,0:T(8,128)S(1)} %get-tuple-element.79), kind=kOutput, calls=%fused_computation.57 | convolution fusion | flops 275779840 | bytes 9715712 | tf_op jit(solution)/shard_map/while/body/eval_jaxpr/kgij,ikgd->jkd/dot_general | solution.py:66
  118.7 5.1 %fusion.5 = bf16[64,8192]{1,0:T(8,128)(2,1)S(1)} fusion(bf16[2,8192,256]{1,2,0:T(8,128)(2,1)} %all-gather.2.cloned.1.call-done, bf16[1,256,256]{2,1,0:T(8,128)(2,1)S(1)} %copy.26, bf16[1,256,256]{2,1,0:T(8,128)(2,1)S(1)} %copy.27), kind=kOutput, calls=%fused_computation.14 | convolution fusion | flops 537427968 | bytes 9699328 | tf_op jit(solution)/shard_map/wtc,wdc->td/dot_general | solution.py:176
  123.8 3.5 %collective-permute-start = (bf16[64,8192]{1,0:T(8,128)(2,1)S(1)}, bf16[64,8192]{1,0:T(8,128)(2,1)S(1)}, u32[]{:S(2)}, u32[]{:S(2)}) collective-permute-start(bf16[64,8192]{1,0:T(8,128)(2,1)S(1)} %fusion.5), channel_id=1, source_target_pairs={{32,33},{33,32},{64,65},{65,64},{34,35},{35,34},{66,67},{67,66},{3... | collective-permute-start | bytes 3145736 | tf_op jit(solution)/shard_map/ppermute | solution.py:191
  130.1 9.5 %collective-permute-done = bf16[64,8192]{1,0:T(8,128)(2,1)S(1)} collective-permute-done((bf16[64,8192]{1,0:T(8,128)(2,1)S(1)}, bf16[64,8192]{1,0:T(8,128)(2,1)S(1)}, u32[]{:S(2)}, u32[]{:S(2)}) %collective-permute-start) | collective-permute-done | bytes 1048608 | tf_op jit(solution)/shard_map/ppermute | solution.py:191
  140.7 3.1 %collective-permute-start.1 = (bf16[64,8192]{1,0:T(8,128)(2,1)S(1)}, bf16[64,8192]{1,0:T(8,128)(2,1)S(1)}, u32[]{:S(2)}, u32[]{:S(2)}) collective-permute-start(bf16[64,8192]{1,0:T(8,128)(2,1)S(1)} %fusion.4), channel_id=1, source_target_pairs={{32,33},{33,32},{64,65},{65,64},{34,35},{35,34},{66,67},{67,66},{3... | collective-permute-start | bytes 3145736 | tf_op jit(solution)/shard_map/ppermute | solution.py:191
  147.5 8.8 %collective-permute-done.1 = bf16[64,8192]{1,0:T(8,128)(2,1)S(1)} collective-permute-done((bf16[64,8192]{1,0:T(8,128)(2,1)S(1)}, bf16[64,8192]{1,0:T(8,128)(2,1)S(1)}, u32[]{:S(2)}, u32[]{:S(2)}) %collective-permute-start.1) | collective-permute-done | bytes 1048608 | tf_op jit(solution)/shard_map/ppermute | solution.py:191
  158.5 5.5 %collective-permute-done.2 = bf16[64,8192]{1,0:T(8,128)(2,1)S(1)} collective-permute-done((bf16[64,8192]{1,0:T(8,128)(2,1)S(1)}, bf16[64,8192]{1,0:T(8,128)(2,1)S(1)}, u32[]{:S(2)}, u32[]{:S(2)}) %collective-permute-start.2) | collective-permute-done | bytes 1048608 | tf_op jit(solution)/shard_map/ppermute | solution.py:190
  166.2 5.8 %convolution_convert_fusion = bf16[8192,512]{1,0:T(8,128)(2,1)} fusion(f32[8192]{0:T(1024)S(1)} %bitcast.146, bf16[256,256]{0,1:T(8,128)(2,1)S(1)} %bitcast.167, bf16[256,256]{0,1:T(8,128)(2,1)S(1)} %bitcast.164, bf16[1,256,8192]{2,1,0:T(8,128)(2,1)S(1)} %copy-done.3, f32[256]{0:T(256)S(1)} %add_rsqrt_fusion), kind=kOutput, calls=%fused_computation.2 | convolution fusion | flops 2160590848 | bytes 12878848 | tf_op jit(solution)/shard_map/dot_general | solution.py:140
  172.0 7.5 %collective-permute-done.3 = bf16[64,8192]{1,0:T(8,128)(2,1)S(1)} collective-permute-done((bf16[64,8192]{1,0:T(8,128)(2,1)S(1)}, bf16[64,8192]{1,0:T(8,128)(2,1)S(1)}, u32[]{:S(2)}, u32[]{:S(2)}) %collective-permute-start.3) | collective-permute-done | bytes 1048608 | tf_op jit(solution)/shard_map/ppermute | solution.py:191
  180.2 4.6 %convolution_bitcast_fusion = f32[128,8192]{1,0:T(8,128)S(1)} fusion(bf16[2,8192,256]{1,2,0:T(8,128)(2,1)} %all-gather.2.cloned.1.call-done, bf16[1,256,256]{2,1,0:T(8,128)(2,1)S(1)} %copy.26, bf16[1,256,256]{2,1,0:T(8,128)(2,1)S(1)} %copy.27), kind=kOutput, calls=%fused_computation.5 | convolution fusion | flops 1073807360 | bytes 12845056 | tf_op jit(solution)/shard_map/wtc,wdc->td/dot_general | solution.py:176
  190.5 2.9 %convert_element_type.188 = bf16[128,8192]{1,0:T(8,128)(2,1)S(1)} convert(f32[128,8192]{1,0:T(8,128)} %scatter-add.4) | non-fusion elementwise | flops 1048576 | bytes 6291456 | tf_op jit(solution)/shard_map/convert_element_type | solution.py:182
  194.6 5.2 %fusion.6 = bf16[64,8192]{1,0:T(8,128)(2,1)S(1)} fusion(bf16[2,8192,256]{1,2,0:T(8,128)(2,1)} %all-gather.2.cloned.1.call-done, bf16[1,256,256]{2,1,0:T(8,128)(2,1)S(1)} %copy.27, bf16[1,256,256]{2,1,0:T(8,128)(2,1)S(1)} %copy.26), kind=kOutput, calls=%fused_computation.15 | convolution fusion | flops 537526272 | bytes 9699328 | tf_op jit(solution)/shard_map/wtc,wdc->td/dot_general | solution.py:176
  204.9 2.5 multiply_convert_fusion.2
  209.7 9.5 %collective-permute-done.9 = bf16[64,8192]{1,0:T(8,128)(2,1)S(1)} collective-permute-done((bf16[64,8192]{1,0:T(8,128)(2,1)S(1)}, bf16[64,8192]{1,0:T(8,128)(2,1)S(1)}, u32[]{:S(2)}, u32[]{:S(2)}) %collective-permute-start.9) | collective-permute-done | bytes 1048608 | tf_op jit(solution)/shard_map/ppermute | solution.py:190
  223.0 11.7 %collective-permute-done.11 = bf16[64,8192]{1,0:T(8,128)(2,1)S(1)} collective-permute-done((bf16[64,8192]{1,0:T(8,128)(2,1)S(1)}, bf16[64,8192]{1,0:T(8,128)(2,1)S(1)}, u32[]{:S(2)}, u32[]{:S(2)}) %collective-permute-start.11) | collective-permute-done | bytes 1048608 | tf_op jit(solution)/shard_map/ppermute | solution.py:191
  237.0 2.4 multiply_convert_fusion.1
  244.9 23.2 %collective-permute-done.12 = bf16[64,8192]{1,0:T(8,128)(2,1)} collective-permute-done((bf16[64,8192]{1,0:T(8,128)(2,1)}, bf16[64,8192]{1,0:T(8,128)(2,1)}, u32[]{:S(2)}, u32[]{:S(2)}) %collective-permute-start.12) | collective-permute-done | bytes 1048608 | tf_op jit(solution)/shard_map/ppermute | solution.py:196
  268.1 4.6 %maximum_select_fusion = bf16[1,256,8192]{2,1,0:T(8,128)(2,1)} fusion(bf16[1,128,8192]{2,1,0:T(8,128)(2,1)} %bitcast.37, bf16[1,128,8192]{2,1,0:T(8,128)(2,1)S(1)} %bitcast.157, bf16[1,64,8192]{2,1,0:T(8,128)(2,1)} %bitcast.42, bf16[1,64,8192]{2,1,0:T(8,128)(2,1)} %bitcast.41, bf16[1,64,8192]{2,1,0:T(8,128)(2,1)} %bitcast.159, ...), kind=kLoop, calls=%fused_computation.18 | loop fusion | flops 27262976 | bytes 12582913 | tf_op jit(solution)/shard_map/jit(_where)/select_n | solution.py:210
  (114 shorter events, 48.3 us)
Async XLA Ops:
  7.2 84.4 %all-gather.2.cloned.1.call-start = ((), (), s32[]{:S(2)}) async-start(), calls=%async_computation.1 | async-start | bytes 8912896 | tf_op jit(solution)/shard_map/all_gather | solution.py:90
  10.4 262.4 %reduce-scatter.2.cloned.1.call-start = ((), (), s32[]{:S(2)}) async-start(), calls=%async_computation.2 | async-start | bytes 8912896 | tf_op jit(solution)/shard_map/reduce_scatter | solution.py:139
  108.1 10.3 %copy-start.9 = (bf16[2,128,256]{2,1,0:T(8,128)(2,1)}, bf16[2,128,256]{2,1,0:T(8,128)(2,1)S(1)}, u32[]{:S(2)}) copy-start(bf16[2,128,256]{2,1,0:T(8,128)(2,1)S(1)} %fusion.28) | copy-start | bytes 393220
  118.6 8.7 %copy-start.3 = (bf16[1,256,8192]{2,1,0:T(8,128)(2,1)S(1)}, bf16[1,256,8192]{2,1,0:T(8,128)(2,1)}, u32[]{:S(2)}) copy-start(bf16[1,256,8192]{2,1,0:T(8,128)(2,1)} %param.11) | copy-start | bytes 12582916
  118.6 9.9 %slice-start = ((s8[8388608]{0:T(1024)(128)(4,1)}), s8[4194304]{0:T(1024)(128)(4,1)S(1)}, s32[]{:S(2)}) async-start(s8[8388608]{0:T(1024)(128)(4,1)} %bitcast.133), calls=%async_computation.3 | async-start | bytes 8388608
  123.8 15.8 %collective-permute-start = (bf16[64,8192]{1,0:T(8,128)(2,1)S(1)}, bf16[64,8192]{1,0:T(8,128)(2,1)S(1)}, u32[]{:S(2)}, u32[]{:S(2)}) collective-permute-start(bf16[64,8192]{1,0:T(8,128)(2,1)S(1)} %fusion.5), channel_id=1, source_target_pairs={{32,33},{33,32},{64,65},{65,64},{34,35},{35,34},{66,67},{67,66},{3... | collective-permute-start | bytes 3145736 | tf_op jit(solution)/shard_map/ppermute | solution.py:191
  128.4 28.4 %copy-start = (f32[256,8192]{1,0:T(8,128)}, f32[256,8192]{1,0:T(8,128)S(1)}, u32[]{:S(2)}) copy-start(f32[256,8192]{1,0:T(8,128)S(1)} %convert_multiply_fusion) | copy-start | bytes 25165828
  140.7 15.5 %collective-permute-start.1 = (bf16[64,8192]{1,0:T(8,128)(2,1)S(1)}, bf16[64,8192]{1,0:T(8,128)(2,1)S(1)}, u32[]{:S(2)}, u32[]{:S(2)}) collective-permute-start(bf16[64,8192]{1,0:T(8,128)(2,1)S(1)} %fusion.4), channel_id=1, source_target_pairs={{32,33},{33,32},{64,65},{65,64},{34,35},{35,34},{66,67},{67,66},{3... | collective-permute-start | bytes 3145736 | tf_op jit(solution)/shard_map/ppermute | solution.py:191
  145.4 20.8 %copy-start.8 = (bf16[256,2,128]{0,2,1:T(8,128)(2,1)S(1)}, bf16[256,2,128]{0,2,1:T(8,128)(2,1)}, u32[]{:S(2)}) copy-start(bf16[256,2,128]{0,2,1:T(8,128)(2,1)} %copy-done.7) | copy-start | bytes 393220
  145.4 20.8 %copy-start.10 = (bf16[2,128,256]{2,1,0:T(8,128)(2,1)S(1)}, bf16[2,128,256]{2,1,0:T(8,128)(2,1)}, u32[]{:S(2)}) copy-start(bf16[2,128,256]{2,1,0:T(8,128)(2,1)} %copy-done.9) | copy-start | bytes 393220
  145.5 18.6 %collective-permute-start.2 = (bf16[64,8192]{1,0:T(8,128)(2,1)S(1)}, bf16[64,8192]{1,0:T(8,128)(2,1)S(1)}, u32[]{:S(2)}, u32[]{:S(2)}) collective-permute-start(bf16[64,8192]{1,0:T(8,128)(2,1)S(1)} %multiply_convert_fusion.6), channel_id=1, source_target_pairs={{32,0},{33,1},{65,32},{64,33},{34,2},{35,3},{67,34},{66,35},{36,4}... | collective-permute-start | bytes 3145736 | tf_op jit(solution)/shard_map/ppermute | solution.py:190
  164.0 15.5 %collective-permute-start.3 = (bf16[64,8192]{1,0:T(8,128)(2,1)S(1)}, bf16[64,8192]{1,0:T(8,128)(2,1)S(1)}, u32[]{:S(2)}, u32[]{:S(2)}) collective-permute-start(bf16[64,8192]{1,0:T(8,128)(2,1)S(1)} %fusion.3), channel_id=1, source_target_pairs={{32,33},{33,32},{64,65},{65,64},{34,35},{35,34},{66,67},{67,66},{3... | collective-permute-start | bytes 3145736 | tf_op jit(solution)/shard_map/ppermute | solution.py:191
  179.5 7.8 %collective-permute-start.4 = (bf16[8,128]{1,0:T(8,128)(2,1)S(1)}, bf16[8,128]{1,0:T(8,128)(2,1)S(1)}, u32[]{:S(2)}, u32[]{:S(2)}) collective-permute-start(bf16[8,128]{1,0:T(8,128)(2,1)S(1)} %slice.162), channel_id=1, source_target_pairs={{64,96},{65,97},{66,98},{67,99},{68,100},{69,101},{70,102},{71,103... | collective-permute-start | bytes 6152 | tf_op jit(solution)/shard_map/ppermute | solution.py:205
  190.5 9.3 %slice-start.2 = ((s8[8388608]{0:T(1024)(128)(4,1)}), s8[4194304]{0:T(1024)(128)(4,1)S(1)}, s32[]{:S(2)}) async-start(s8[8388608]{0:T(1024)(128)(4,1)} %bitcast.135), calls=%async_computation.5 | async-start | bytes 8388608
  193.4 10.6 %collective-permute-start.5 = (bf16[128,8192]{1,0:T(8,128)(2,1)S(1)}, bf16[128,8192]{1,0:T(8,128)(2,1)S(1)}, u32[]{:S(2)}, u32[]{:S(2)}) collective-permute-start(bf16[128,8192]{1,0:T(8,128)(2,1)S(1)} %convert_element_type.188), channel_id=1, source_target_pairs={{96,97},{97,96},{98,99},{99,98},{100,101},{101,100},{102,103},{103... | collective-permute-start | bytes 6291464 | tf_op jit(solution)/shard_map/ppermute | solution.py:191
  194.6 8.9 %slice-start.4 = ((s8[8388608]{0:T(1024)(128)(4,1)}), s8[4194304]{0:T(1024)(128)(4,1)S(1)}, s32[]{:S(2)}) async-start(s8[8388608]{0:T(1024)(128)(4,1)} %bitcast.137), calls=%async_computation.7 | async-start | bytes 8388608
  201.2 18.0 %collective-permute-start.9 = (bf16[64,8192]{1,0:T(8,128)(2,1)S(1)}, bf16[64,8192]{1,0:T(8,128)(2,1)S(1)}, u32[]{:S(2)}, u32[]{:S(2)}) collective-permute-start(bf16[64,8192]{1,0:T(8,128)(2,1)S(1)} %copy-done.6), channel_id=1, source_target_pairs={{32,0},{33,1},{65,32},{64,33},{34,2},{35,3},{67,34},{66,35},{36,4}... | collective-permute-start | bytes 3145736 | tf_op jit(solution)/shard_map/ppermute | solution.py:190
  207.4 28.7 %collective-permute-start.7 = (bf16[128,8192]{1,0:T(8,128)(2,1)S(1)}, bf16[128,8192]{1,0:T(8,128)(2,1)S(1)}, u32[]{:S(2)}, u32[]{:S(2)}) collective-permute-start(bf16[128,8192]{1,0:T(8,128)(2,1)S(1)} %fusion.2), channel_id=1, source_target_pairs={{96,97},{97,96},{98,99},{99,98},{100,101},{101,100},{102,103},{103... | collective-permute-start | bytes 6291464 | tf_op jit(solution)/shard_map/ppermute | solution.py:191
  219.2 17.9 %copy-start.4 = (bf16[64,8192]{1,0:T(8,128)(2,1)}, bf16[64,8192]{1,0:T(8,128)(2,1)S(1)}, u32[]{:S(2)}) copy-start(bf16[64,8192]{1,0:T(8,128)(2,1)S(1)} %collective-permute-done.9) | copy-start | bytes 3145732
  219.2 15.5 %collective-permute-start.11 = (bf16[64,8192]{1,0:T(8,128)(2,1)S(1)}, bf16[64,8192]{1,0:T(8,128)(2,1)S(1)}, u32[]{:S(2)}, u32[]{:S(2)}) collective-permute-start(bf16[64,8192]{1,0:T(8,128)(2,1)S(1)} %fusion.6), channel_id=1, source_target_pairs={{32,33},{33,32},{64,65},{65,64},{34,35},{35,34},{66,67},{67,66},{3... | collective-permute-start | bytes 3145736 | tf_op jit(solution)/shard_map/ppermute | solution.py:191
  221.1 23.8 %collective-permute-start.10 = (bf16[64,8192]{1,0:T(8,128)(2,1)}, bf16[64,8192]{1,0:T(8,128)(2,1)}, u32[]{:S(2)}, u32[]{:S(2)}) collective-permute-start(bf16[64,8192]{1,0:T(8,128)(2,1)} %multiply_convert_fusion.4), channel_id=1, source_target_pairs={{32,0},{33,1},{65,32},{64,33},{34,2},{35,3},{67,34},{66,35},{36,4}... | collective-permute-start | bytes 3145736 | tf_op jit(solution)/shard_map/ppermute | solution.py:190
  235.2 32.9 %collective-permute-start.6 = (bf16[128,8192]{1,0:T(8,128)(2,1)}, bf16[128,8192]{1,0:T(8,128)(2,1)S(1)}, u32[]{:S(2)}, u32[]{:S(2)}) collective-permute-start(bf16[128,8192]{1,0:T(8,128)(2,1)} %multiply_convert_fusion.2), channel_id=1, source_target_pairs={{96,64},{97,65},{98,66},{99,67},{100,68},{101,69},{102,70},{103,71... | collective-permute-start | bytes 6291464 | tf_op jit(solution)/shard_map/ppermute | solution.py:190
  239.5 28.7 %collective-permute-start.8 = (bf16[128,8192]{1,0:T(8,128)(2,1)}, bf16[128,8192]{1,0:T(8,128)(2,1)}, u32[]{:S(2)}, u32[]{:S(2)}) collective-permute-start(bf16[128,8192]{1,0:T(8,128)(2,1)} %multiply_convert_fusion.1), channel_id=1, source_target_pairs={{96,64},{97,65},{98,66},{99,67},{100,68},{101,69},{102,70},{103,71... | collective-permute-start | bytes 6291464 | tf_op jit(solution)/shard_map/ppermute | solution.py:196
  243.0 25.2 %collective-permute-start.12 = (bf16[64,8192]{1,0:T(8,128)(2,1)}, bf16[64,8192]{1,0:T(8,128)(2,1)}, u32[]{:S(2)}, u32[]{:S(2)}) collective-permute-start(bf16[64,8192]{1,0:T(8,128)(2,1)} %multiply_convert_fusion.3), channel_id=1, source_target_pairs={{32,0},{33,1},{65,32},{64,33},{34,2},{35,3},{67,34},{66,35},{36,4}... | collective-permute-start | bytes 3145736 | tf_op jit(solution)/shard_map/ppermute | solution.py:196
  (8 other events, 32.4 us)
Sparse Core Ops, SparseCore 0:
  10.7 80.8 all-gather.1
  172.2 81.3 reduce-scatter.1

commit v8 on v3

--- a/solution.py
+++ b/solution.py
@@ -146,8 +146,9 @@
     both_grads = jnp.stack([key_grad, value_grad])
     n_pipe = lax.axis_size("pipe")
     n_tensor = lax.axis_size("tensor")
-    chunks = 4
-    rows = tok_rows // chunks
+    sizes = [tok_rows // 4, tok_rows * 5 // 16, tok_rows * 5 // 16, tok_rows // 8]
+    bounds = [sum(sizes[:c]) for c in range(len(sizes) + 1)]
+    chunks = len(sizes)
     exchange_steps = [
         [
             (p * n_tensor + t, p * n_tensor + (t + step) % n_tensor)
@@ -164,7 +165,7 @@
     lowers = []
     held = None
     for c in range(chunks):
-        sl = slice(c * rows, (c + 1) * rows)
+        sl = slice(bounds[c], bounds[c + 1])
         part = jnp.einsum(
             "wtc,wdc->td", both_grads[:, sl], both_full, preferred_element_type=jnp.float32
         )

time: 257 us -> 255 us (level)
  transfers between devices with their start and end apart: 10 -> 10, of which waited for: 8 -> 7; matrix products, arithmetic and copies ran while one was open for 12% -> 13% of each run, Pallas kernels for 0% -> 0%
where the time goes in v8:
time: 255 us
  waiting for transfers between devices  151 us (59%)
  matrix products  44.6 us (17%)
  starting transfers between devices  17.6 us (7%)
  between operations  16.5 us (6%)
  other arithmetic  16 us (6%)
  local copies, waits for them, and re-layouts  8.69 us (3%)
    all_gather x1, waiting for transfers between devices, on_device(): lax.all_gather(jnp.stack([key_weight[0], value_weight[0]]), 'dp', axis=1,...  71.1 us
    ppermute x4, waiting for transfers between devices, on_device(): lowers.append(lax.ppermute(held, ('pipe', 'tensor'), shift_pairs))  48.4 us
    ppermute x4, waiting for transfers between devices, on_device(): lax.ppermute(part_low, ('pipe', 'tensor'), pairs).astype(jnp.float32)  31.7 us
    dot_general x4, matrix products, on_device(): jnp.einsum('wtc,wdc->td', both_grads[:, sl], both_full, preferred_element...  13.3 us
    ppermute x4, starting transfers between devices, on_device(): lax.ppermute(part_low, ('pipe', 'tensor'), pairs).astype(jnp.float32)  9.85 us
    ppermute x4, starting transfers between devices, on_device(): lowers.append(lax.ppermute(held, ('pipe', 'tensor'), shift_pairs))  7.67 us
    dot_general x1, matrix products, sequence_grads(): jnp.einsum('kgij,ikgd->jkd', score_grad, query_g, preferred_element_type=...  7.48 us
    dot_general x1, matrix products, on_device(): jnp.einsum('td,wdc->wtc', normed, both_full, preferred_element_type=jnp.f...  7.02 us
  transfers between devices with their start and end apart: 10, of which 7 were waited for; matrix products, arithmetic and copies ran while one was open for 13% of the time, Pallas kernels for 0%

profile of v8, /device:TPU:1, one launch (start us, length us, event | category | flops | bytes accessed | tf_op | source)
XLA Modules:
  0.0 254.6 jit_solution(5297577957536231163)
XLA Ops:
  17.3 3.1 %fusion.6 = f32[256]{0:T(256)S(1)} fusion(bf16[1,256,8192]{2,1,0:T(8,128)(2,1)} %param.9), kind=kLoop, calls=%fused_computation.13 | loop fusion | flops 6291200 | bytes 4195328 | tf_op jit(solution)/shard_map/reduce_sum | solution.py:102
  20.5 71.1 %all-gather.2.cloned.1.call-done = bf16[2,8192,256]{1,2,0:T(8,128)(2,1)} async-done(((bf16[2,512,256]{1,2,0:T(8,128)(2,1)}), bf16[2,8192,256]{1,2,0:T(8,128)(2,1)}) %all-gather.2.cloned.1.call-update) | async-done | bytes 8388624 | tf_op jit(solution)/shard_map/all_gather | solution.py:89
  91.7 7.0 %fusion.20 = f32[2,256,256]{1,2,0:T(8,128)S(1)} fusion(bf16[2,8192,256]{1,2,0:T(8,128)(2,1)} %all-gather.2.cloned.1.call-done, f32[8192]{0:T(1024)S(1)} %bitcast.125, bf16[1,256,8192]{2,1,0:T(8,128)(2,1)} %param.9, f32[256]{0:T(256)S(1)} %add_rsqrt_fusion), kind=kOutput, calls=%fused_computation.44 | convolution fusion | flops 2155872256 | bytes 13140992 | tf_op jit(solution)/shard_map/td,wdc->wtc/dot_general | solution.py:105
  99.9 5.3 %fusion.60 = (f32[2,8,256]{2,1,0:T(8,128)S(1)}, f32[2,8,256,256]{2,3,1,0:T(8,128)}) fusion(pred[256,256]{0,1:T(8,128)(4,1)S(1)} %fusion.39, bf16[256,2,8,128]{0,3,2,1:T(8,128)(2,1)} %bitcast.137, f32[256,2,64]{2,0,1:T(8,128)S(1)} %bitcast.142, f32[256,2,64]{2,0,1:T(8,128)} %negate_bitcast_fusion, f32[256,2,128]{2,0,1:T(8,128)S(1)} %copy.15, ...), kind=kOutput, calls=%fused_computation.107 | convolution fusion | flops 274006272 | bytes 6111232 | tf_op jit(solution)/shard_map/while/body/eval_jaxpr/sub | solution.py:56
  105.1 3.0 %fusion.27 = bf16[2,128,256]{2,1,0:T(8,128)(2,1)S(1)} fusion(f32[256,2,8,128]{0,3,2,1:T(8,128)S(1)} %bitcast.123, f32[256]{0:T(256)S(1)} %broadcast_select_fusion, f32[2,8,256,256]{2,3,1,0:T(8,128)} %get-tuple-element.60, f32[2,8,256]{2,1,0:T(8,128)S(1)} %get-tuple-element.59), kind=kOutput, calls=%fused_computation.47 | convolution fusion | flops 271646720 | bytes 6439936 | tf_op jit(solution)/shard_map/while/body/eval_jaxpr/kgij,ikgd->jkd/dot_general | solution.py:59
  108.3 2.7 %fusion.30 = f32[2,256,256,8]{2,1,3,0:T(8,128)} fusion(bf16[256,2,128,1]{0,2,3,1:T(8,128)(2,1)S(1)} %bitcast.139, f32[256,2,8,128]{0,3,2,1:T(8,128)S(1)} %bitcast.124, f32[256]{0:T(256)S(1)} %broadcast_select_fusion), kind=kOutput, calls=%fused_computation.52 | convolution fusion | flops 269484032 | bytes 6423552 | tf_op jit(solution)/shard_map/while/body/eval_jaxpr/ikgd,jkd->kgij/dot_general | solution.py:62
  111.0 7.5 %fusion.23 = f32[2,256,128]{1,2,0:T(8,128)S(1)} fusion(bf16[256,2,8,128]{0,3,2,1:T(8,128)(2,1)} %bitcast.138, f32[2,256,256,8]{2,1,3,0:T(8,128)} %fusion.30, f32[2,8,256,256]{2,3,1,0:T(8,128)} %get-tuple-element.60, f32[2,8,256]{2,1,0:T(8,128)S(1)} %get-tuple-element.59), kind=kOutput, calls=%fused_computation.45 | convolution fusion | flops 275779840 | bytes 9715712 | tf_op jit(solution)/shard_map/while/body/eval_jaxpr/kgij,ikgd->jkd/dot_general | solution.py:65
  118.7 5.1 %fusion.4 = bf16[64,8192]{1,0:T(8,128)(2,1)S(1)} fusion(bf16[2,8192,256]{1,2,0:T(8,128)(2,1)} %all-gather.2.cloned.1.call-done, bf16[1,256,256]{2,1,0:T(8,128)(2,1)S(1)} %copy.26, bf16[1,256,256]{2,1,0:T(8,128)(2,1)S(1)} %copy.27), kind=kOutput, calls=%fused_computation.10 | convolution fusion | flops 537427968 | bytes 9699328 | tf_op jit(solution)/shard_map/wtc,wdc->td/dot_general | solution.py:169
  123.8 3.3 %collective-permute-start = (bf16[64,8192]{1,0:T(8,128)(2,1)S(1)}, bf16[64,8192]{1,0:T(8,128)(2,1)S(1)}, u32[]{:S(2)}, u32[]{:S(2)}) collective-permute-start(bf16[64,8192]{1,0:T(8,128)(2,1)S(1)} %fusion.4), channel_id=1, source_target_pairs={{32,33},{33,32},{64,65},{65,64},{96,97},{97,96},{34,35},{35,34},{6... | collective-permute-start | bytes 3145736 | tf_op jit(solution)/shard_map/ppermute | solution.py:183
  127.1 5.8 %convolution_convert_fusion = bf16[8192,512]{1,0:T(8,128)(2,1)} fusion(f32[8192]{0:T(1024)S(1)} %bitcast.126, bf16[256,256]{0,1:T(8,128)(2,1)S(1)} %bitcast.144, bf16[256,256]{0,1:T(8,128)(2,1)S(1)} %bitcast.141, bf16[1,256,8192]{2,1,0:T(8,128)(2,1)S(1)} %copy-done, f32[256]{0:T(256)S(1)} %add_rsqrt_fusion), kind=kOutput, calls=%fused_computation.2 | convolution fusion | flops 2160590848 | bytes 12878848 | tf_op jit(solution)/shard_map/dot_general | solution.py:139
  132.9 3.3 %convert_multiply_fusion = f32[256,8192]{1,0:T(8,128)S(1)} fusion(bf16[1,256,8192]{2,1,0:T(8,128)(2,1)} %param.9, f32[256]{0:T(256)S(1)} %add_rsqrt_fusion), kind=kLoop, calls=%fused_computation.3 | loop fusion | flops 4194304 | bytes 12583936 | tf_op jit(solution)/shard_map/mul | solution.py:103
  136.2 5.1 %fusion.3 = bf16[80,8192]{1,0:T(8,128)(2,1)S(1)} fusion(bf16[2,8192,256]{1,2,0:T(8,128)(2,1)} %all-gather.2.cloned.1.call-done, bf16[1,256,256]{2,1,0:T(8,128)(2,1)S(1)} %copy.26, bf16[1,256,256]{2,1,0:T(8,128)(2,1)S(1)} %copy.27), kind=kOutput, calls=%fused_computation.9 | convolution fusion | flops 671784960 | bytes 9961472 | tf_op jit(solution)/shard_map/wtc,wdc->td/dot_general | solution.py:169
  142.6 2.2 collective-permute-start.1
  146.4 1.9 collective-permute-start.2
  148.4 13.0 %collective-permute-done.1 = bf16[80,8192]{1,0:T(8,128)(2,1)S(1)} collective-permute-done((bf16[80,8192]{1,0:T(8,128)(2,1)S(1)}, bf16[80,8192]{1,0:T(8,128)(2,1)S(1)}, u32[]{:S(2)}, u32[]{:S(2)}) %collective-permute-start.1) | collective-permute-done | bytes 1310752 | tf_op jit(solution)/shard_map/ppermute | solution.py:183
  162.7 11.2 %collective-permute-done.2 = bf16[64,8192]{1,0:T(8,128)(2,1)S(1)} collective-permute-done((bf16[64,8192]{1,0:T(8,128)(2,1)S(1)}, bf16[64,8192]{1,0:T(8,128)(2,1)S(1)}, u32[]{:S(2)}, u32[]{:S(2)}) %collective-permute-start.2) | collective-permute-done | bytes 1048608 | tf_op jit(solution)/shard_map/ppermute | solution.py:180
  173.9 2.2 collective-permute-start.3
  177.7 1.9 collective-permute-start.4
  179.6 13.0 %collective-permute-done.3 = bf16[80,8192]{1,0:T(8,128)(2,1)S(1)} collective-permute-done((bf16[80,8192]{1,0:T(8,128)(2,1)S(1)}, bf16[80,8192]{1,0:T(8,128)(2,1)S(1)}, u32[]{:S(2)}, u32[]{:S(2)}) %collective-permute-start.3) | collective-permute-done | bytes 1310752 | tf_op jit(solution)/shard_map/ppermute | solution.py:183
  194.1 14.7 %collective-permute-done.4 = bf16[80,8192]{1,0:T(8,128)(2,1)S(1)} collective-permute-done((bf16[80,8192]{1,0:T(8,128)(2,1)S(1)}, bf16[80,8192]{1,0:T(8,128)(2,1)S(1)}, u32[]{:S(2)}, u32[]{:S(2)}) %collective-permute-start.4) | collective-permute-done | bytes 1310752 | tf_op jit(solution)/shard_map/ppermute | solution.py:180
  208.7 2.2 collective-permute-start.6
  212.9 5.7 %collective-permute-done.6 = bf16[32,8192]{1,0:T(8,128)(2,1)S(1)} collective-permute-done((bf16[32,8192]{1,0:T(8,128)(2,1)S(1)}, bf16[32,8192]{1,0:T(8,128)(2,1)S(1)}, u32[]{:S(2)}, u32[]{:S(2)}) %collective-permute-start.6) | collective-permute-done | bytes 524320 | tf_op jit(solution)/shard_map/ppermute | solution.py:183
  221.2 22.6 %collective-permute-done.7 = bf16[32,8192]{1,0:T(8,128)(2,1)S(1)} collective-permute-done((bf16[32,8192]{1,0:T(8,128)(2,1)S(1)}, bf16[32,8192]{1,0:T(8,128)(2,1)S(1)}, u32[]{:S(2)}, u32[]{:S(2)}) %collective-permute-start.7) | collective-permute-done | bytes 524320 | tf_op jit(solution)/shard_map/ppermute | solution.py:187
  243.8 2.1 maximum_bitcast_fusion
  (69 shorter events, 23.2 us)
Async XLA Ops:
  7.2 7.3 %copy-start.1 = (bf16[1,256,2048]{2,1,0:T(8,128)(2,1)S(1)}, bf16[1,256,2048]{2,1,0:T(8,128)(2,1)}, u32[]{:S(2)}) copy-start(bf16[1,256,2048]{2,1,0:T(8,128)(2,1)} %param.13) | copy-start | bytes 3145732
  7.2 84.5 %all-gather.2.cloned.1.call-start = ((), (), s32[]{:S(2)}) async-start(), calls=%async_computation.1 | async-start | bytes 8912896 | tf_op jit(solution)/shard_map/all_gather | solution.py:89
  10.4 235.6 %reduce-scatter.2.cloned.1.call-start = ((), (), s32[]{:S(2)}) async-start(), calls=%async_computation.2 | async-start | bytes 8912896 | tf_op jit(solution)/shard_map/reduce_scatter | solution.py:138
  20.4 115.8 %copy-start.2 = (f32[256]{0:T(256)}, f32[256]{0:T(256)S(1)}, u32[]{:S(2)}) copy-start(f32[256]{0:T(256)S(1)} %add_rsqrt_fusion) | copy-start | bytes 3076
  118.7 8.4 %copy-start = (bf16[1,256,8192]{2,1,0:T(8,128)(2,1)S(1)}, bf16[1,256,8192]{2,1,0:T(8,128)(2,1)}, u32[]{:S(2)}) copy-start(bf16[1,256,8192]{2,1,0:T(8,128)(2,1)} %param.9) | copy-start | bytes 12582916
  123.8 17.5 %collective-permute-start = (bf16[64,8192]{1,0:T(8,128)(2,1)S(1)}, bf16[64,8192]{1,0:T(8,128)(2,1)S(1)}, u32[]{:S(2)}, u32[]{:S(2)}) collective-permute-start(bf16[64,8192]{1,0:T(8,128)(2,1)S(1)} %fusion.4), channel_id=1, source_target_pairs={{32,33},{33,32},{64,65},{65,64},{96,97},{97,96},{34,35},{35,34},{6... | collective-permute-start | bytes 3145736 | tf_op jit(solution)/shard_map/ppermute | solution.py:183
  136.2 8.7 %slice-start = ((s8[8388608]{0:T(1024)(128)(4,1)}), s8[4194304]{0:T(1024)(128)(4,1)S(1)}, s32[]{:S(2)}) async-start(s8[8388608]{0:T(1024)(128)(4,1)} %bitcast.121), calls=%async_computation.3 | async-start | bytes 8388608
  136.2 8.7 %slice-start.1 = ((s8[8388608]{0:T(1024)(128)(4,1)}), s8[4194304]{0:T(1024)(128)(4,1)S(1)}, s32[]{:S(2)}) async-start(s8[8388608]{0:T(1024)(128)(4,1)} %bitcast.121), calls=%async_computation.4 | async-start | bytes 8388608
  141.3 0.7 slice-start.2
  141.3 3.5 %copy-start.3 = (f32[256]{0:T(256)S(1)}, f32[256]{0:T(256)}, u32[]{:S(2)}) copy-start(f32[256]{0:T(256)} %copy-done.2) | copy-start | bytes 3076
  142.6 18.8 %collective-permute-start.1 = (bf16[80,8192]{1,0:T(8,128)(2,1)S(1)}, bf16[80,8192]{1,0:T(8,128)(2,1)S(1)}, u32[]{:S(2)}, u32[]{:S(2)}) collective-permute-start(bf16[80,8192]{1,0:T(8,128)(2,1)S(1)} %fusion.3), channel_id=1, source_target_pairs={{32,33},{33,32},{64,65},{65,64},{96,97},{97,96},{34,35},{35,34},{6... | collective-permute-start | bytes 3932168 | tf_op jit(solution)/shard_map/ppermute | solution.py:183
  146.4 27.5 %collective-permute-start.2 = (bf16[64,8192]{1,0:T(8,128)(2,1)S(1)}, bf16[64,8192]{1,0:T(8,128)(2,1)S(1)}, u32[]{:S(2)}, u32[]{:S(2)}) collective-permute-start(bf16[64,8192]{1,0:T(8,128)(2,1)S(1)} %multiply_convert_fusion.3), channel_id=1, source_target_pairs={{32,0},{33,1},{65,32},{64,33},{96,64},{97,65},{34,2},{35,3},{67,34... | collective-permute-start | bytes 3145736 | tf_op jit(solution)/shard_map/ppermute | solution.py:180
  173.9 18.7 %collective-permute-start.3 = (bf16[80,8192]{1,0:T(8,128)(2,1)S(1)}, bf16[80,8192]{1,0:T(8,128)(2,1)S(1)}, u32[]{:S(2)}, u32[]{:S(2)}) collective-permute-start(bf16[80,8192]{1,0:T(8,128)(2,1)S(1)} %fusion.2), channel_id=1, source_target_pairs={{32,33},{33,32},{64,65},{65,64},{96,97},{97,96},{34,35},{35,34},{6... | collective-permute-start | bytes 3932168 | tf_op jit(solution)/shard_map/ppermute | solution.py:183
  177.7 31.1 %collective-permute-start.4 = (bf16[80,8192]{1,0:T(8,128)(2,1)S(1)}, bf16[80,8192]{1,0:T(8,128)(2,1)S(1)}, u32[]{:S(2)}, u32[]{:S(2)}) collective-permute-start(bf16[80,8192]{1,0:T(8,128)(2,1)S(1)} %multiply_convert_fusion.2), channel_id=1, source_target_pairs={{32,0},{33,1},{65,32},{64,33},{96,64},{97,65},{34,2},{35,3},{67,34... | collective-permute-start | bytes 3932168 | tf_op jit(solution)/shard_map/ppermute | solution.py:180
  208.7 9.9 %collective-permute-start.6 = (bf16[32,8192]{1,0:T(8,128)(2,1)S(1)}, bf16[32,8192]{1,0:T(8,128)(2,1)S(1)}, u32[]{:S(2)}, u32[]{:S(2)}) collective-permute-start(bf16[32,8192]{1,0:T(8,128)(2,1)S(1)} %fusion.5), channel_id=1, source_target_pairs={{32,33},{33,32},{64,65},{65,64},{96,97},{97,96},{34,35},{35,34},{6... | collective-permute-start | bytes 1572872 | tf_op jit(solution)/shard_map/ppermute | solution.py:183
  211.0 32.8 %collective-permute-start.5 = (bf16[80,8192]{1,0:T(8,128)(2,1)S(1)}, bf16[80,8192]{1,0:T(8,128)(2,1)S(1)}, u32[]{:S(2)}, u32[]{:S(2)}) collective-permute-start(bf16[80,8192]{1,0:T(8,128)(2,1)S(1)} %multiply_convert_fusion.1), channel_id=1, source_target_pairs={{32,0},{33,1},{65,32},{64,33},{96,64},{97,65},{34,2},{35,3},{67,34... | collective-permute-start | bytes 3932168 | tf_op jit(solution)/shard_map/ppermute | solution.py:180
  219.3 24.5 %collective-permute-start.7 = (bf16[32,8192]{1,0:T(8,128)(2,1)S(1)}, bf16[32,8192]{1,0:T(8,128)(2,1)S(1)}, u32[]{:S(2)}, u32[]{:S(2)}) collective-permute-start(bf16[32,8192]{1,0:T(8,128)(2,1)S(1)} %multiply_convert_fusion.7), channel_id=1, source_target_pairs={{32,0},{33,1},{65,32},{64,33},{96,64},{97,65},{34,2},{35,3},{67,34... | collective-permute-start | bytes 1572872 | tf_op jit(solution)/shard_map/ppermute | solution.py:187
Sparse Core Ops, SparseCore 0:
  10.7 80.9 all-gather.1
  133.0 84.3 reduce-scatter.1

commit v9 on v8

--- a/solution.py
+++ b/solution.py
@@ -1,8 +1,11 @@
+import functools
 import math
 
 import jax
 import jax.numpy as jnp
 from jax import lax
+from jax.experimental import pallas as pl
+from jax.experimental.pallas import tpu as pltpu
 from jax.sharding import PartitionSpec as P
 
 HD = 128
@@ -67,6 +70,55 @@
     )
     key_grad = rotated_grad * cosine[:, None, :] + rotate_back(rotated_grad * sine[:, None, :])
     return (key_grad.astype(jnp.bfloat16), value_grad)
+
+
+def attention_kernel(len_ref, q_ref, c_ref, k_ref, v_ref, rg_ref, vg_ref, *, group, head_dim):
+    seq_len = k_ref.shape[0]
+    scale = 1.0 / math.sqrt(head_dim)
+    length = len_ref[0]
+    keys = k_ref[...]
+    values = v_ref[...]
+    row = lax.broadcasted_iota(jnp.int32, (seq_len, seq_len), 0)
+    col = lax.broadcasted_iota(jnp.int32, (seq_len, seq_len), 1)
+    allowed = (col <= row) & (col < length)
+    rotated = jnp.zeros((seq_len, head_dim), jnp.float32)
+    value_grad = jnp.zeros((seq_len, head_dim), jnp.float32)
+    nt = (((1,), (1,)), ((), ()))
+    nn = (((1,), (0,)), ((), ()))
+    for g in range(group):
+        query = q_ref[:, g * head_dim:(g + 1) * head_dim]
+        cotan = c_ref[:, g * head_dim:(g + 1) * head_dim]
+        scores = lax.dot_general(query, keys, nt, preferred_element_type=jnp.float32) * scale
+        scores = jnp.where(allowed, scores, -1e30)
+        highest = jnp.max(scores, axis=-1, keepdims=True)
+        expd = jnp.where(allowed, jnp.exp(scores - highest), 0.0)
+        probs = expd / jnp.sum(expd, axis=-1, keepdims=True)
+        value_grad = value_grad + lax.dot_general(
+            probs.T.astype(jnp.bfloat16), cotan, nn, preferred_element_type=jnp.float32)
+        prob_grad = lax.dot_general(cotan, values, nt, preferred_element_type=jnp.float32)
+        centre = jnp.sum(probs * prob_grad, axis=-1, keepdims=True)
+        score_grad = probs * (prob_grad - centre) * scale
+        rotated = rotated + lax.dot_general(
+            score_grad.T.astype(jnp.bfloat16), query, nn, preferred_element_type=jnp.float32)
+    rg_ref[...] = rotated
+    vg_ref[...] = value_grad.astype(jnp.bfloat16)
+
+def attention_grads(length, queries, cotan, keys, values, head_dim):
+    seq_len, kv_cols = keys.shape
+    kv_heads = kv_cols // head_dim
+    group = queries.shape[1] // kv_cols
+    kernel = functools.partial(attention_kernel, group=group, head_dim=head_dim)
+    q_spec = pl.BlockSpec((seq_len, group * head_dim), lambda k, n: (0, k))
+    kv_spec = pl.BlockSpec((seq_len, head_dim), lambda k, n: (0, k))
+    return pl.pallas_call(
+        kernel,
+        grid_spec=pltpu.PrefetchScalarGridSpec(
+            num_scalar_prefetch=1, grid=(kv_heads,),
+            in_specs=[q_spec, q_spec, kv_spec, kv_spec],
+            out_specs=[kv_spec, kv_spec]),
+        out_shape=[jax.ShapeDtypeStruct((seq_len, kv_cols), jnp.float32),
+                   jax.ShapeDtypeStruct((seq_len, kv_cols), jnp.bfloat16)],
+    )(length, queries, cotan, keys, values)
 
 
 def norm_backward(normed_grad, gain_f, nhat, inv_rms):
@@ -119,19 +171,23 @@
         * factor[:, :, None, None]
     ).astype(jnp.bfloat16)
 
-    def one_sequence(items):
-        return sequence_grads(items[0], items[1], items[2], items[3], items[4], cosine, sine)
-
-    key_grad, value_grad = lax.map(
-        one_sequence,
-        (
-            queries[0].reshape(seq_count, seq_len, q_local, HD),
-            keys,
-            values.reshape(seq_count, seq_len, kv_local, HD),
-            scaled,
-            lengths[0],
-        ),
-    )
+    key_parts, value_parts = [], []
+    for n in range(seq_count):
+        rows_n = slice(n * seq_len, (n + 1) * seq_len)
+        rotated, value_part = attention_grads(
+            lengths[0][n:n + 1],
+            queries[0][rows_n],
+            scaled[n].reshape(seq_len, q_local * HD),
+            keys[n].reshape(seq_len, kv_cols),
+            values[rows_n],
+            HD,
+        )
+        rotated = rotated.reshape(seq_len, kv_local, HD)
+        key_part = rotated * cosine[:, None, :] + rotate_back(rotated * sine[:, None, :])
+        key_parts.append(key_part.astype(jnp.bfloat16))
+        value_parts.append(value_part)
+    key_grad = jnp.concatenate(key_parts, axis=0)
+    value_grad = jnp.concatenate(value_parts, axis=0)
     key_grad = key_grad.reshape(tok_rows, kv_cols)
     value_grad = value_grad.reshape(tok_rows, kv_cols)
     combined = jnp.concatenate([key_grad, value_grad], axis=1)

time: 255 us -> 255 us (level)
  matrix products: 44.6 us -> 28.3 us
  Pallas kernels: 0 us -> 8.14 us
  waiting for transfers between devices: 151 us -> 159 us
    dot_general x3 -> x0, matrix products: 13.2 us -> none  [the longest x1 7.48 us: sequence_grads(): jnp.einsum('kgij,ikgd->jkd', score_grad, query_g, preferred_element_type=...]
    pallas_call x0 -> x1, Pallas kernels: none -> 8.14 us  [attention_grads(): pl.pallas_call(kernel, grid_spec=pltpu.PrefetchScalarGridSpec(num_scalar_...]
    sub x1 -> x0, matrix products: 5.25 us -> none  [sequence_grads(): expd = jnp.where(allowed, jnp.exp(scores - highest), 0.0)]
    all_gather x1, waiting for transfers between devices: 71.1 us -> 73.8 us  [on_device(): lax.all_gather(jnp.stack([key_weight[0], value_weight[0]]), 'dp', axis=1,...]
  transfers between devices with their start and end apart: 10 -> 10, of which waited for: 7 -> 8; matrix products, arithmetic and copies ran while one was open for 13% -> 9% of each run, Pallas kernels for 0% -> 0%
where the time goes in v9:
time: 255 us
  waiting for transfers between devices  159 us (62%)
  matrix products  28.3 us (11%)
  starting transfers between devices  18.8 us (7%)
  other arithmetic  18.3 us (7%)
  between operations  16.5 us (6%)
  Pallas kernels  8.14 us (3%)
  local copies, waits for them, and re-layouts  6.37 us (2%)
    all_gather x1, waiting for transfers between devices, on_device(): lax.all_gather(jnp.stack([key_weight[0], value_weight[0]]), 'dp', axis=1,...  73.8 us
    ppermute x4, waiting for transfers between devices, on_device(): lowers.append(lax.ppermute(held, ('pipe', 'tensor'), shift_pairs))  50.6 us
    ppermute x4, waiting for transfers between devices, on_device(): lax.ppermute(part_low, ('pipe', 'tensor'), pairs).astype(jnp.float32)  34.2 us
    dot_general x4, matrix products, on_device(): jnp.einsum('wtc,wdc->td', both_grads[:, sl], both_full, preferred_element...  13.2 us
    ppermute x4, starting transfers between devices, on_device(): lax.ppermute(part_low, ('pipe', 'tensor'), pairs).astype(jnp.float32)  11 us
    dot_general x1, matrix products, on_device(): lax.dot_general(normed, combined, (((0,), (0,)), ((), ())), preferred_ele...  8.18 us
    pallas_call x1, Pallas kernels, attention_grads(): pl.pallas_call(kernel, grid_spec=pltpu.PrefetchScalarGridSpec(num_scalar_...  8.14 us
    ppermute x4, starting transfers between devices, on_device(): lowers.append(lax.ppermute(held, ('pipe', 'tensor'), shift_pairs))  7.67 us
  transfers between devices with their start and end apart: 10, of which 8 were waited for; matrix products, arithmetic and copies ran while one was open for 9% of the time, Pallas kernels for 0%

profile of v9, /device:TPU:1, one launch (start us, length us, event | category | flops | bytes accessed | tf_op | source)
XLA Modules:
  0.0 254.9 jit_solution(12105056147529902189)
XLA Ops:
  13.3 3.1 %fusion.4 = f32[256]{0:T(256)S(1)} fusion(bf16[1,256,8192]{2,1,0:T(8,128)(2,1)} %param.9), kind=kLoop, calls=%fused_computation.11 | loop fusion | flops 6291200 | bytes 4195328 | tf_op jit(solution)/shard_map/reduce_sum | solution.py:154
  17.6 73.8 %all-gather.2.cloned.1.call-done = bf16[2,8192,256]{1,2,0:T(8,128)(2,1)} async-done(((bf16[2,512,256]{1,2,0:T(8,128)(2,1)}), bf16[2,8192,256]{1,2,0:T(8,128)(2,1)}) %all-gather.2.cloned.1.call-update) | async-done | bytes 8388624 | tf_op jit(solution)/shard_map/all_gather | solution.py:141
  91.4 6.9 %fusion.8 = f32[2,256,256]{2,1,0:T(8,128)S(1)} fusion(bf16[2,8192,256]{1,2,0:T(8,128)(2,1)} %all-gather.2.cloned.1.call-done, f32[8192]{0:T(1024)S(1)} %bitcast.90, bf16[1,256,8192]{2,1,0:T(8,128)(2,1)} %param.9, f32[256]{0:T(256)S(1)} %add_rsqrt_fusion), kind=kOutput, calls=%fused_computation.27 | convolution fusion | flops 2155872256 | bytes 13140992 | tf_op jit(solution)/shard_map/td,wdc->wtc/dot_general | solution.py:157
  100.7 8.1 %shard_map.112 = (f32[256,256]{1,0:T(8,128)}, bf16[256,256]{1,0:T(8,128)(2,1)}) custom-call(s32[1]{0:T(128)} %bitcast.82.len_ref, bf16[256,2048]{1,0:T(8,128)(2,1)} %bitcast.107, bf16[256,2048]{1,0:T(8,128)(2,1)} %fusion.7.c_ref, bf16[256,256]{1,0:T(8,128)(2,1)} %fusion.13.k_ref, bf16[256,256]{1,0:T(8,128)(2,1)} %fusion.17.v_ref), custom_call_target="tpu_custom_call" | custom-call | tf_op jit(solution)/shard_map/pallas_call | solution.py:113
  111.0 8.2 %convolution_convert_fusion = bf16[8192,512]{1,0:T(8,128)(2,1)} fusion(f32[8192]{0:T(1024)S(1)} %bitcast.91, bf16[256,256]{1,0:T(8,128)(2,1)S(1)} %copy-done, bf16[256,256]{1,0:T(8,128)(2,1)S(1)} %fusion.11, bf16[1,256,8192]{2,1,0:T(8,128)(2,1)} %param.9, f32[256]{0:T(256)S(1)} %add_rsqrt_fusion), kind=kOutput, calls=%fused_computation | convolution fusion | flops 2160590848 | bytes 12878848 | tf_op jit(solution)/shard_map/dot_general | solution.py:195
  119.2 4.9 %fusion.2 = bf16[64,8192]{1,0:T(8,128)(2,1)S(1)} fusion(bf16[2,8192,256]{1,2,0:T(8,128)(2,1)} %all-gather.2.cloned.1.call-done, bf16[1,256,256]{2,1,0:T(8,128)(2,1)S(1)} %bitcast.86, bf16[1,256,256]{2,1,0:T(8,128)(2,1)S(1)} %bitcast.102), kind=kOutput, calls=%fused_computation.8 | convolution fusion | flops 537427968 | bytes 9699328 | tf_op jit(solution)/shard_map/wtc,wdc->td/dot_general | solution.py:225
  124.1 3.1 %collective-permute-start = (bf16[64,8192]{1,0:T(8,128)(2,1)S(1)}, bf16[64,8192]{1,0:T(8,128)(2,1)S(1)}, u32[]{:S(2)}, u32[]{:S(2)}) collective-permute-start(bf16[64,8192]{1,0:T(8,128)(2,1)S(1)} %fusion.2), channel_id=1, source_target_pairs={{32,33},{33,32},{64,65},{65,64},{96,97},{97,96},{34,35},{35,34},{6... | collective-permute-start | bytes 3145736 | tf_op jit(solution)/shard_map/ppermute | solution.py:239
  127.3 3.4 %convert_multiply_fusion = f32[256,8192]{1,0:T(8,128)S(1)} fusion(bf16[1,256,8192]{2,1,0:T(8,128)(2,1)} %param.9, f32[256]{0:T(256)S(1)} %add_rsqrt_fusion), kind=kLoop, calls=%fused_computation.1 | loop fusion | flops 4194304 | bytes 12583936 | tf_op jit(solution)/shard_map/mul | solution.py:155
  130.7 5.1 %fusion.1 = bf16[80,8192]{1,0:T(8,128)(2,1)S(1)} fusion(bf16[2,8192,256]{1,2,0:T(8,128)(2,1)} %all-gather.2.cloned.1.call-done, bf16[1,256,256]{2,1,0:T(8,128)(2,1)S(1)} %bitcast.87, bf16[1,256,256]{2,1,0:T(8,128)(2,1)S(1)} %bitcast.103), kind=kOutput, calls=%fused_computation.7 | convolution fusion | flops 671784960 | bytes 9961472 | tf_op jit(solution)/shard_map/wtc,wdc->td/dot_general | solution.py:225
  135.8 4.3 %collective-permute-done = bf16[64,8192]{1,0:T(8,128)(2,1)S(1)} collective-permute-done((bf16[64,8192]{1,0:T(8,128)(2,1)S(1)}, bf16[64,8192]{1,0:T(8,128)(2,1)S(1)}, u32[]{:S(2)}, u32[]{:S(2)}) %collective-permute-start) | collective-permute-done | bytes 1048608 | tf_op jit(solution)/shard_map/ppermute | solution.py:239
  141.2 3.3 %collective-permute-start.1 = (bf16[80,8192]{1,0:T(8,128)(2,1)S(1)}, bf16[80,8192]{1,0:T(8,128)(2,1)S(1)}, u32[]{:S(2)}, u32[]{:S(2)}) collective-permute-start(bf16[80,8192]{1,0:T(8,128)(2,1)S(1)} %fusion.1), channel_id=1, source_target_pairs={{32,33},{33,32},{64,65},{65,64},{96,97},{97,96},{34,35},{35,34},{6... | collective-permute-start | bytes 3932168 | tf_op jit(solution)/shard_map/ppermute | solution.py:239
  146.2 1.9 collective-permute-start.2
  148.1 11.8 %collective-permute-done.1 = bf16[80,8192]{1,0:T(8,128)(2,1)S(1)} collective-permute-done((bf16[80,8192]{1,0:T(8,128)(2,1)S(1)}, bf16[80,8192]{1,0:T(8,128)(2,1)S(1)}, u32[]{:S(2)}, u32[]{:S(2)}) %collective-permute-start.1) | collective-permute-done | bytes 1310752 | tf_op jit(solution)/shard_map/ppermute | solution.py:239
  161.4 13.1 %collective-permute-done.2 = bf16[64,8192]{1,0:T(8,128)(2,1)S(1)} collective-permute-done((bf16[64,8192]{1,0:T(8,128)(2,1)S(1)}, bf16[64,8192]{1,0:T(8,128)(2,1)S(1)}, u32[]{:S(2)}, u32[]{:S(2)}) %collective-permute-start.2) | collective-permute-done | bytes 1048608 | tf_op jit(solution)/shard_map/ppermute | solution.py:236
  174.5 2.2 collective-permute-start.3
  178.3 1.9 collective-permute-start.4
  180.2 12.6 %collective-permute-done.3 = bf16[80,8192]{1,0:T(8,128)(2,1)S(1)} collective-permute-done((bf16[80,8192]{1,0:T(8,128)(2,1)S(1)}, bf16[80,8192]{1,0:T(8,128)(2,1)S(1)}, u32[]{:S(2)}, u32[]{:S(2)}) %collective-permute-start.3) | collective-permute-done | bytes 1310752 | tf_op jit(solution)/shard_map/ppermute | solution.py:239
  194.2 14.7 %collective-permute-done.4 = bf16[80,8192]{1,0:T(8,128)(2,1)S(1)} collective-permute-done((bf16[80,8192]{1,0:T(8,128)(2,1)S(1)}, bf16[80,8192]{1,0:T(8,128)(2,1)S(1)}, u32[]{:S(2)}, u32[]{:S(2)}) %collective-permute-start.4) | collective-permute-done | bytes 1310752 | tf_op jit(solution)/shard_map/ppermute | solution.py:236
  208.9 2.4 collective-permute-start.6
  211.4 1.9 collective-permute-start.5
  213.3 5.5 %collective-permute-done.6 = bf16[32,8192]{1,0:T(8,128)(2,1)S(1)} collective-permute-done((bf16[32,8192]{1,0:T(8,128)(2,1)S(1)}, bf16[32,8192]{1,0:T(8,128)(2,1)S(1)}, u32[]{:S(2)}, u32[]{:S(2)}) %collective-permute-start.6) | collective-permute-done | bytes 524320 | tf_op jit(solution)/shard_map/ppermute | solution.py:239
  219.4 1.9 collective-permute-start.7
  221.4 22.7 %collective-permute-done.7 = bf16[32,8192]{1,0:T(8,128)(2,1)S(1)} collective-permute-done((bf16[32,8192]{1,0:T(8,128)(2,1)S(1)}, bf16[32,8192]{1,0:T(8,128)(2,1)S(1)}, u32[]{:S(2)}, u32[]{:S(2)}) %collective-permute-start.7) | collective-permute-done | bytes 524320 | tf_op jit(solution)/shard_map/ppermute | solution.py:243
  244.1 2.1 maximum_bitcast_fusion
  (66 shorter events, 19.2 us)
Async XLA Ops:
  7.2 5.3 %copy-start.3 = (bf16[1,8192]{1,0:T(2,128)(2,1)S(1)}, bf16[1,8192]{1,0:T(2,128)(2,1)}, u32[]{:S(2)}) copy-start(bf16[1,8192]{1,0:T(2,128)(2,1)} %param.10) | copy-start | bytes 49156
  7.2 84.2 %all-gather.2.cloned.1.call-start = ((), (), s32[]{:S(2)}) async-start(), calls=%async_computation.1 | async-start | bytes 8912896 | tf_op jit(solution)/shard_map/all_gather | solution.py:141
  10.3 6.1 %copy-start.2 = (bf16[1,256,2048]{2,1,0:T(8,128)(2,1)S(1)}, bf16[1,256,2048]{2,1,0:T(8,128)(2,1)}, u32[]{:S(2)}) copy-start(bf16[1,256,2048]{2,1,0:T(8,128)(2,1)} %param.14) | copy-start | bytes 3145732
  10.3 235.9 %reduce-scatter.2.cloned.1.call-start = ((), (), s32[]{:S(2)}) async-start(), calls=%async_computation.2 | async-start | bytes 8912896 | tf_op jit(solution)/shard_map/reduce_scatter | solution.py:194
  16.4 114.3 %copy-start.4 = (f32[256]{0:T(256)}, f32[256]{0:T(256)S(1)}, u32[]{:S(2)}) copy-start(f32[256]{0:T(256)S(1)} %add_rsqrt_fusion) | copy-start | bytes 3076
  108.9 2.0 copy-start.1
  108.9 2.1 copy-start
  124.1 15.9 %collective-permute-start = (bf16[64,8192]{1,0:T(8,128)(2,1)S(1)}, bf16[64,8192]{1,0:T(8,128)(2,1)S(1)}, u32[]{:S(2)}, u32[]{:S(2)}) collective-permute-start(bf16[64,8192]{1,0:T(8,128)(2,1)S(1)} %fusion.2), channel_id=1, source_target_pairs={{32,33},{33,32},{64,65},{65,64},{96,97},{97,96},{34,35},{35,34},{6... | collective-permute-start | bytes 3145736 | tf_op jit(solution)/shard_map/ppermute | solution.py:239
  127.3 17.4 %slice-start = ((s8[8388608]{0:T(1024)(128)(4,1)}), s8[4194304]{0:T(1024)(128)(4,1)S(1)}, s32[]{:S(2)}) async-start(s8[8388608]{0:T(1024)(128)(4,1)} %bitcast.84), calls=%async_computation.3 | async-start | bytes 8388608
  130.7 13.9 %slice-start.1 = ((s8[8388608]{0:T(1024)(128)(4,1)}), s8[4194304]{0:T(1024)(128)(4,1)S(1)}, s32[]{:S(2)}) async-start(s8[8388608]{0:T(1024)(128)(4,1)} %bitcast.84), calls=%async_computation.4 | async-start | bytes 8388608
  135.8 4.8 %slice-start.2 = ((f32[256]{0:T(256)}), f32[64]{0:T(128)S(1)}, s32[]{:S(2)}) async-start(f32[256]{0:T(256)} %copy-done.4), calls=%async_computation.5 | async-start | bytes 1024 | tf_op jit(solution)/shard_map/slice | solution.py:242
  140.7 3.9 %copy-start.5 = (f32[256]{0:T(256)S(1)}, f32[256]{0:T(256)}, u32[]{:S(2)}) copy-start(f32[256]{0:T(256)} %copy-done.4) | copy-start | bytes 3076
  141.2 18.8 %collective-permute-start.1 = (bf16[80,8192]{1,0:T(8,128)(2,1)S(1)}, bf16[80,8192]{1,0:T(8,128)(2,1)S(1)}, u32[]{:S(2)}, u32[]{:S(2)}) collective-permute-start(bf16[80,8192]{1,0:T(8,128)(2,1)S(1)} %fusion.1), channel_id=1, source_target_pairs={{32,33},{33,32},{64,65},{65,64},{96,97},{97,96},{34,35},{35,34},{6... | collective-permute-start | bytes 3932168 | tf_op jit(solution)/shard_map/ppermute | solution.py:239
  146.2 28.3 %collective-permute-start.2 = (bf16[64,8192]{1,0:T(8,128)(2,1)S(1)}, bf16[64,8192]{1,0:T(8,128)(2,1)S(1)}, u32[]{:S(2)}, u32[]{:S(2)}) collective-permute-start(bf16[64,8192]{1,0:T(8,128)(2,1)S(1)} %multiply_convert_fusion.3), channel_id=1, source_target_pairs={{32,0},{33,1},{65,32},{64,33},{96,64},{97,65},{34,2},{35,3},{67,34... | collective-permute-start | bytes 3145736 | tf_op jit(solution)/shard_map/ppermute | solution.py:236
  174.5 18.3 %collective-permute-start.3 = (bf16[80,8192]{1,0:T(8,128)(2,1)S(1)}, bf16[80,8192]{1,0:T(8,128)(2,1)S(1)}, u32[]{:S(2)}, u32[]{:S(2)}) collective-permute-start(bf16[80,8192]{1,0:T(8,128)(2,1)S(1)} %fusion), channel_id=1, source_target_pairs={{32,33},{33,32},{64,65},{65,64},{96,97},{97,96},{34,35},{35,34},{6... | collective-permute-start | bytes 3932168 | tf_op jit(solution)/shard_map/ppermute | solution.py:239
  178.3 30.6 %collective-permute-start.4 = (bf16[80,8192]{1,0:T(8,128)(2,1)S(1)}, bf16[80,8192]{1,0:T(8,128)(2,1)S(1)}, u32[]{:S(2)}, u32[]{:S(2)}) collective-permute-start(bf16[80,8192]{1,0:T(8,128)(2,1)S(1)} %multiply_convert_fusion.2), channel_id=1, source_target_pairs={{32,0},{33,1},{65,32},{64,33},{96,64},{97,65},{34,2},{35,3},{67,34... | collective-permute-start | bytes 3932168 | tf_op jit(solution)/shard_map/ppermute | solution.py:236
  208.9 9.9 %collective-permute-start.6 = (bf16[32,8192]{1,0:T(8,128)(2,1)S(1)}, bf16[32,8192]{1,0:T(8,128)(2,1)S(1)}, u32[]{:S(2)}, u32[]{:S(2)}) collective-permute-start(bf16[32,8192]{1,0:T(8,128)(2,1)S(1)} %fusion.3), channel_id=1, source_target_pairs={{32,33},{33,32},{64,65},{65,64},{96,97},{97,96},{34,35},{35,34},{6... | collective-permute-start | bytes 1572872 | tf_op jit(solution)/shard_map/ppermute | solution.py:239
  211.4 32.7 %collective-permute-start.5 = (bf16[80,8192]{1,0:T(8,128)(2,1)S(1)}, bf16[80,8192]{1,0:T(8,128)(2,1)S(1)}, u32[]{:S(2)}, u32[]{:S(2)}) collective-permute-start(bf16[80,8192]{1,0:T(8,128)(2,1)S(1)} %multiply_convert_fusion.1), channel_id=1, source_target_pairs={{32,0},{33,1},{65,32},{64,33},{96,64},{97,65},{34,2},{35,3},{67,34... | collective-permute-start | bytes 3932168 | tf_op jit(solution)/shard_map/ppermute | solution.py:236
  219.4 24.7 %collective-permute-start.7 = (bf16[32,8192]{1,0:T(8,128)(2,1)S(1)}, bf16[32,8192]{1,0:T(8,128)(2,1)S(1)}, u32[]{:S(2)}, u32[]{:S(2)}) collective-permute-start(bf16[32,8192]{1,0:T(8,128)(2,1)S(1)} %multiply_convert_fusion.6), channel_id=1, source_target_pairs={{32,0},{33,1},{65,32},{64,33},{96,64},{97,65},{34,2},{35,3},{67,34... | collective-permute-start | bytes 1572872 | tf_op jit(solution)/shard_map/ppermute | solution.py:243
Sparse Core Ops, SparseCore 0:
  10.4 80.8 all-gather.1
  127.4 83.7 reduce-scatter.1

commit v10 on v9

--- a/solution.py
+++ b/solution.py
@@ -191,14 +191,17 @@
     key_grad = key_grad.reshape(tok_rows, kv_cols)
     value_grad = value_grad.reshape(tok_rows, kv_cols)
     combined = jnp.concatenate([key_grad, value_grad], axis=1)
-    grad_total = lax.psum_scatter(
-        lax.dot_general(
-            normed, combined, (((0,), (0,)), ((), ())), preferred_element_type=jnp.float32
-        ).astype(jnp.bfloat16),
-        "dp",
-        scatter_dimension=0,
-        tiled=True,
-    )
+
+    def weight_grads(combined):
+        return lax.psum_scatter(
+            lax.dot_general(
+                normed, combined, (((0,), (0,)), ((), ())), preferred_element_type=jnp.float32
+            ).astype(jnp.bfloat16),
+            "dp",
+            scatter_dimension=0,
+            tiled=True,
+        )
+
     both_grads = jnp.stack([key_grad, value_grad])
     n_pipe = lax.axis_size("pipe")
     n_tensor = lax.axis_size("tensor")
@@ -226,6 +229,9 @@
             "wtc,wdc->td", both_grads[:, sl], both_full, preferred_element_type=jnp.float32
         )
         part_low = part.astype(jnp.bfloat16)
+        if c == 0:
+            part_low, combined = lax.optimization_barrier((part_low, combined))
+            grad_total = weight_grads(combined)
         if held is not None:
             if len(lowers) > 0:
                 part_low, held, lowers[-1] = lax.optimization_barrier(

time: 255 us -> 247 us (0.969)
  waiting for transfers between devices: 159 us -> 154 us
  transfers between devices with their start and end apart: 10 -> 10, of which waited for: 8 -> 7; matrix products, arithmetic and copies ran while one was open for 9% -> 12% of each run, Pallas kernels for 0% -> 0%
where the time goes in v10:
time: 247 us
  waiting for transfers between devices  154 us (62%)
  matrix products  26.4 us (11%)
  other arithmetic  18.3 us (7%)
  starting transfers between devices  17.6 us (7%)
  between operations  16.5 us (7%)
  Pallas kernels  8.15 us (3%)
  local copies, waits for them, and re-layouts  6.45 us (3%)
    all_gather x1, waiting for transfers between devices, on_device(): lax.all_gather(jnp.stack([key_weight[0], value_weight[0]]), 'dp', axis=1,...  73.8 us
    ppermute x4, waiting for transfers between devices, on_device(): lowers.append(lax.ppermute(held, ('pipe', 'tensor'), shift_pairs))  48.1 us
    ppermute x4, waiting for transfers between devices, on_device(): lax.ppermute(part_low, ('pipe', 'tensor'), pairs).astype(jnp.float32)  31.8 us
    dot_general x4, matrix products, on_device(): jnp.einsum('wtc,wdc->td', both_grads[:, sl], both_full, preferred_element...  13.3 us
    ppermute x4, starting transfers between devices, on_device(): lax.ppermute(part_low, ('pipe', 'tensor'), pairs).astype(jnp.float32)  9.81 us
    pallas_call x1, Pallas kernels, attention_grads(): pl.pallas_call(kernel, grid_spec=pltpu.PrefetchScalarGridSpec(num_scalar_...  8.15 us
    ppermute x4, starting transfers between devices, on_device(): lowers.append(lax.ppermute(held, ('pipe', 'tensor'), shift_pairs))  7.67 us
    dot_general x1, matrix products, on_device(): jnp.einsum('td,wdc->wtc', normed, both_full, preferred_element_type=jnp.f...  6.94 us
  transfers between devices with their start and end apart: 10, of which 7 were waited for; matrix products, arithmetic and copies ran while one was open for 12% of the time, Pallas kernels for 0%

profile of v10, /device:TPU:1, one launch (start us, length us, event | category | flops | bytes accessed | tf_op | source)
XLA Modules:
  0.0 247.0 jit_solution(10273348423631694706)
XLA Ops:
  13.3 3.1 %fusion.4 = f32[256]{0:T(256)S(1)} fusion(bf16[1,256,8192]{2,1,0:T(8,128)(2,1)} %param.9), kind=kLoop, calls=%fused_computation.11 | loop fusion | flops 6291200 | bytes 4195328 | tf_op jit(solution)/shard_map/reduce_sum | solution.py:154
  17.6 73.8 %all-gather.2.cloned.1.call-done = bf16[2,8192,256]{1,2,0:T(8,128)(2,1)} async-done(((bf16[2,512,256]{1,2,0:T(8,128)(2,1)}), bf16[2,8192,256]{1,2,0:T(8,128)(2,1)}) %all-gather.2.cloned.1.call-update) | async-done | bytes 8388624 | tf_op jit(solution)/shard_map/all_gather | solution.py:141
  91.4 6.9 %fusion.8 = f32[2,256,256]{2,1,0:T(8,128)S(1)} fusion(bf16[2,8192,256]{1,2,0:T(8,128)(2,1)} %all-gather.2.cloned.1.call-done, f32[8192]{0:T(1024)S(1)} %bitcast.95, bf16[1,256,8192]{2,1,0:T(8,128)(2,1)} %param.9, f32[256]{0:T(256)S(1)} %add_rsqrt_fusion), kind=kOutput, calls=%fused_computation.27 | convolution fusion | flops 2155872256 | bytes 13140992 | tf_op jit(solution)/shard_map/td,wdc->wtc/dot_general | solution.py:157
  100.7 8.1 %shard_map.112 = (f32[256,256]{1,0:T(8,128)}, bf16[256,256]{1,0:T(8,128)(2,1)}) custom-call(s32[1]{0:T(128)} %bitcast.83.len_ref, bf16[256,2048]{1,0:T(8,128)(2,1)} %bitcast.108, bf16[256,2048]{1,0:T(8,128)(2,1)} %fusion.7.c_ref, bf16[256,256]{1,0:T(8,128)(2,1)} %fusion.13.k_ref, bf16[256,256]{1,0:T(8,128)(2,1)} %fusion.14.v_ref), custom_call_target="tpu_custom_call" | custom-call | tf_op jit(solution)/shard_map/pallas_call | solution.py:113
  111.0 5.1 %fusion.2 = bf16[64,8192]{1,0:T(8,128)(2,1)S(1)} fusion(bf16[2,8192,256]{1,2,0:T(8,128)(2,1)} %all-gather.2.cloned.1.call-done, bf16[1,256,256]{2,1,0:T(8,128)(2,1)S(1)} %bitcast.87, bf16[1,256,256]{2,1,0:T(8,128)(2,1)S(1)} %bitcast.91), kind=kOutput, calls=%fused_computation.8 | convolution fusion | flops 537427968 | bytes 9699328 | tf_op jit(solution)/shard_map/wtc,wdc->td/dot_general | solution.py:228
  116.1 3.3 %collective-permute-start = (bf16[64,8192]{1,0:T(8,128)(2,1)S(1)}, bf16[64,8192]{1,0:T(8,128)(2,1)S(1)}, u32[]{:S(2)}, u32[]{:S(2)}) collective-permute-start(bf16[64,8192]{1,0:T(8,128)(2,1)S(1)} %fusion.2), channel_id=1, source_target_pairs={{32,33},{33,32},{64,65},{65,64},{96,97},{97,96},{34,35},{35,34},{6... | collective-permute-start | bytes 3145736 | tf_op jit(solution)/shard_map/ppermute | solution.py:245
  119.4 6.1 %convolution_convert_fusion = bf16[8192,512]{1,0:T(8,128)(2,1)} fusion(bf16[256,512]{1,0:T(8,128)(2,1)S(1)} %pad_maximum_fusion.3, f32[8192]{0:T(1024)S(1)} %bitcast.96, bf16[1,256,8192]{2,1,0:T(8,128)(2,1)S(1)} %copy-done, f32[256]{0:T(256)S(1)} %add_rsqrt_fusion), kind=kOutput, calls=%fused_computation | convolution fusion | flops 2160066560 | bytes 12878848 | tf_op jit(solution)/shard_map/dot_general | solution.py:197
  125.6 3.4 %convert_multiply_fusion = f32[256,8192]{1,0:T(8,128)S(1)} fusion(bf16[1,256,8192]{2,1,0:T(8,128)(2,1)} %param.9, f32[256]{0:T(256)S(1)} %add_rsqrt_fusion), kind=kLoop, calls=%fused_computation.1 | loop fusion | flops 4194304 | bytes 12583936 | tf_op jit(solution)/shard_map/mul | solution.py:155
  129.0 5.1 %fusion.1 = bf16[80,8192]{1,0:T(8,128)(2,1)S(1)} fusion(bf16[2,8192,256]{1,2,0:T(8,128)(2,1)} %all-gather.2.cloned.1.call-done, bf16[1,256,256]{2,1,0:T(8,128)(2,1)S(1)} %bitcast.88, bf16[1,256,256]{2,1,0:T(8,128)(2,1)S(1)} %bitcast.92), kind=kOutput, calls=%fused_computation.7 | convolution fusion | flops 671784960 | bytes 9961472 | tf_op jit(solution)/shard_map/wtc,wdc->td/dot_general | solution.py:228
  135.3 2.2 collective-permute-start.1
  139.2 1.9 collective-permute-start.2
  141.1 13.0 %collective-permute-done.1 = bf16[80,8192]{1,0:T(8,128)(2,1)S(1)} collective-permute-done((bf16[80,8192]{1,0:T(8,128)(2,1)S(1)}, bf16[80,8192]{1,0:T(8,128)(2,1)S(1)}, u32[]{:S(2)}, u32[]{:S(2)}) %collective-permute-start.1) | collective-permute-done | bytes 1310752 | tf_op jit(solution)/shard_map/ppermute | solution.py:245
  155.5 10.8 %collective-permute-done.2 = bf16[64,8192]{1,0:T(8,128)(2,1)S(1)} collective-permute-done((bf16[64,8192]{1,0:T(8,128)(2,1)S(1)}, bf16[64,8192]{1,0:T(8,128)(2,1)S(1)}, u32[]{:S(2)}, u32[]{:S(2)}) %collective-permute-start.2) | collective-permute-done | bytes 1048608 | tf_op jit(solution)/shard_map/ppermute | solution.py:242
  166.3 2.2 collective-permute-start.3
  170.0 1.9 collective-permute-start.4
  172.0 13.1 %collective-permute-done.3 = bf16[80,8192]{1,0:T(8,128)(2,1)S(1)} collective-permute-done((bf16[80,8192]{1,0:T(8,128)(2,1)S(1)}, bf16[80,8192]{1,0:T(8,128)(2,1)S(1)}, u32[]{:S(2)}, u32[]{:S(2)}) %collective-permute-start.3) | collective-permute-done | bytes 1310752 | tf_op jit(solution)/shard_map/ppermute | solution.py:245
  186.4 14.8 %collective-permute-done.4 = bf16[80,8192]{1,0:T(8,128)(2,1)S(1)} collective-permute-done((bf16[80,8192]{1,0:T(8,128)(2,1)S(1)}, bf16[80,8192]{1,0:T(8,128)(2,1)S(1)}, u32[]{:S(2)}, u32[]{:S(2)}) %collective-permute-start.4) | collective-permute-done | bytes 1310752 | tf_op jit(solution)/shard_map/ppermute | solution.py:242
  201.1 2.2 collective-permute-start.6
  203.4 1.9 collective-permute-start.5
  205.3 5.8 %collective-permute-done.6 = bf16[32,8192]{1,0:T(8,128)(2,1)S(1)} collective-permute-done((bf16[32,8192]{1,0:T(8,128)(2,1)S(1)}, bf16[32,8192]{1,0:T(8,128)(2,1)S(1)}, u32[]{:S(2)}, u32[]{:S(2)}) %collective-permute-start.6) | collective-permute-done | bytes 524320 | tf_op jit(solution)/shard_map/ppermute | solution.py:245
  211.7 1.9 collective-permute-start.7
  213.6 22.5 %collective-permute-done.7 = bf16[32,8192]{1,0:T(8,128)(2,1)S(1)} collective-permute-done((bf16[32,8192]{1,0:T(8,128)(2,1)S(1)}, bf16[32,8192]{1,0:T(8,128)(2,1)S(1)}, u32[]{:S(2)}, u32[]{:S(2)}) %collective-permute-start.7) | collective-permute-done | bytes 524320 | tf_op jit(solution)/shard_map/ppermute | solution.py:249
  236.1 2.1 maximum_bitcast_fusion
  238.3 1.9 slice_bitcast_fusion
  (69 shorter events, 17.5 us)
Async XLA Ops:
  7.2 5.3 %copy-start.4 = (bf16[1,8192]{1,0:T(2,128)(2,1)S(1)}, bf16[1,8192]{1,0:T(2,128)(2,1)}, u32[]{:S(2)}) copy-start(bf16[1,8192]{1,0:T(2,128)(2,1)} %param.10) | copy-start | bytes 49156
  7.2 84.2 %all-gather.2.cloned.1.call-start = ((), (), s32[]{:S(2)}) async-start(), calls=%async_computation.1 | async-start | bytes 8912896 | tf_op jit(solution)/shard_map/all_gather | solution.py:141
  10.3 6.1 %copy-start.3 = (bf16[1,256,2048]{2,1,0:T(8,128)(2,1)S(1)}, bf16[1,256,2048]{2,1,0:T(8,128)(2,1)}, u32[]{:S(2)}) copy-start(bf16[1,256,2048]{2,1,0:T(8,128)(2,1)} %param.14) | copy-start | bytes 3145732
  10.3 227.9 %reduce-scatter.2.cloned.1.call-start = ((), (), s32[]{:S(2)}) async-start(), calls=%async_computation.2 | async-start | bytes 8912896 | tf_op jit(solution)/shard_map/reduce_scatter | solution.py:196
  16.4 112.6 %copy-start.5 = (f32[256]{0:T(256)}, f32[256]{0:T(256)S(1)}, u32[]{:S(2)}) copy-start(f32[256]{0:T(256)S(1)} %add_rsqrt_fusion) | copy-start | bytes 3076
  108.9 2.0 copy-start.2
  108.9 2.1 copy-start.1
  111.0 8.4 %copy-start = (bf16[1,256,8192]{2,1,0:T(8,128)(2,1)S(1)}, bf16[1,256,8192]{2,1,0:T(8,128)(2,1)}, u32[]{:S(2)}) copy-start(bf16[1,256,8192]{2,1,0:T(8,128)(2,1)} %param.9) | copy-start | bytes 12582916
  116.1 18.0 %collective-permute-start = (bf16[64,8192]{1,0:T(8,128)(2,1)S(1)}, bf16[64,8192]{1,0:T(8,128)(2,1)S(1)}, u32[]{:S(2)}, u32[]{:S(2)}) collective-permute-start(bf16[64,8192]{1,0:T(8,128)(2,1)S(1)} %fusion.2), channel_id=1, source_target_pairs={{32,33},{33,32},{64,65},{65,64},{96,97},{97,96},{34,35},{35,34},{6... | collective-permute-start | bytes 3145736 | tf_op jit(solution)/shard_map/ppermute | solution.py:245
  125.6 12.1 %slice-start = ((s8[8388608]{0:T(1024)(128)(4,1)}), s8[4194304]{0:T(1024)(128)(4,1)S(1)}, s32[]{:S(2)}) async-start(s8[8388608]{0:T(1024)(128)(4,1)} %bitcast.85), calls=%async_computation.3 | async-start | bytes 8388608
  129.0 8.6 %slice-start.1 = ((s8[8388608]{0:T(1024)(128)(4,1)}), s8[4194304]{0:T(1024)(128)(4,1)S(1)}, s32[]{:S(2)}) async-start(s8[8388608]{0:T(1024)(128)(4,1)} %bitcast.85), calls=%async_computation.4 | async-start | bytes 8388608
  134.1 0.7 slice-start.2
  134.8 2.8 %copy-start.6 = (f32[256]{0:T(256)S(1)}, f32[256]{0:T(256)}, u32[]{:S(2)}) copy-start(f32[256]{0:T(256)} %copy-done.5) | copy-start | bytes 3076
  135.3 18.8 %collective-permute-start.1 = (bf16[80,8192]{1,0:T(8,128)(2,1)S(1)}, bf16[80,8192]{1,0:T(8,128)(2,1)S(1)}, u32[]{:S(2)}, u32[]{:S(2)}) collective-permute-start(bf16[80,8192]{1,0:T(8,128)(2,1)S(1)} %fusion.1), channel_id=1, source_target_pairs={{32,33},{33,32},{64,65},{65,64},{96,97},{97,96},{34,35},{35,34},{6... | collective-permute-start | bytes 3932168 | tf_op jit(solution)/shard_map/ppermute | solution.py:245
  139.2 27.1 %collective-permute-start.2 = (bf16[64,8192]{1,0:T(8,128)(2,1)S(1)}, bf16[64,8192]{1,0:T(8,128)(2,1)S(1)}, u32[]{:S(2)}, u32[]{:S(2)}) collective-permute-start(bf16[64,8192]{1,0:T(8,128)(2,1)S(1)} %multiply_convert_fusion.3), channel_id=1, source_target_pairs={{32,0},{33,1},{65,32},{64,33},{96,64},{97,65},{34,2},{35,3},{67,34... | collective-permute-start | bytes 3145736 | tf_op jit(solution)/shard_map/ppermute | solution.py:242
  166.3 18.7 %collective-permute-start.3 = (bf16[80,8192]{1,0:T(8,128)(2,1)S(1)}, bf16[80,8192]{1,0:T(8,128)(2,1)S(1)}, u32[]{:S(2)}, u32[]{:S(2)}) collective-permute-start(bf16[80,8192]{1,0:T(8,128)(2,1)S(1)} %fusion), channel_id=1, source_target_pairs={{32,33},{33,32},{64,65},{65,64},{96,97},{97,96},{34,35},{35,34},{6... | collective-permute-start | bytes 3932168 | tf_op jit(solution)/shard_map/ppermute | solution.py:245
  170.0 31.1 %collective-permute-start.4 = (bf16[80,8192]{1,0:T(8,128)(2,1)S(1)}, bf16[80,8192]{1,0:T(8,128)(2,1)S(1)}, u32[]{:S(2)}, u32[]{:S(2)}) collective-permute-start(bf16[80,8192]{1,0:T(8,128)(2,1)S(1)} %multiply_convert_fusion.2), channel_id=1, source_target_pairs={{32,0},{33,1},{65,32},{64,33},{96,64},{97,65},{34,2},{35,3},{67,34... | collective-permute-start | bytes 3932168 | tf_op jit(solution)/shard_map/ppermute | solution.py:242
  201.1 9.9 %collective-permute-start.6 = (bf16[32,8192]{1,0:T(8,128)(2,1)S(1)}, bf16[32,8192]{1,0:T(8,128)(2,1)S(1)}, u32[]{:S(2)}, u32[]{:S(2)}) collective-permute-start(bf16[32,8192]{1,0:T(8,128)(2,1)S(1)} %fusion.3), channel_id=1, source_target_pairs={{32,33},{33,32},{64,65},{65,64},{96,97},{97,96},{34,35},{35,34},{6... | collective-permute-start | bytes 1572872 | tf_op jit(solution)/shard_map/ppermute | solution.py:245
  203.4 32.8 %collective-permute-start.5 = (bf16[80,8192]{1,0:T(8,128)(2,1)S(1)}, bf16[80,8192]{1,0:T(8,128)(2,1)S(1)}, u32[]{:S(2)}, u32[]{:S(2)}) collective-permute-start(bf16[80,8192]{1,0:T(8,128)(2,1)S(1)} %multiply_convert_fusion.1), channel_id=1, source_target_pairs={{32,0},{33,1},{65,32},{64,33},{96,64},{97,65},{34,2},{35,3},{67,34... | collective-permute-start | bytes 3932168 | tf_op jit(solution)/shard_map/ppermute | solution.py:242
  211.7 24.4 %collective-permute-start.7 = (bf16[32,8192]{1,0:T(8,128)(2,1)S(1)}, bf16[32,8192]{1,0:T(8,128)(2,1)S(1)}, u32[]{:S(2)}, u32[]{:S(2)}) collective-permute-start(bf16[32,8192]{1,0:T(8,128)(2,1)S(1)} %multiply_convert_fusion.6), channel_id=1, source_target_pairs={{32,0},{33,1},{65,32},{64,33},{96,64},{97,65},{34,2},{35,3},{67,34... | collective-permute-start | bytes 1572872 | tf_op jit(solution)/shard_map/ppermute | solution.py:249
Sparse Core Ops, SparseCore 0:
  10.4 80.8 all-gather.1
  125.7 83.9 reduce-scatter.1

commit v11 on v10

--- a/solution.py
+++ b/solution.py
@@ -139,24 +139,23 @@
     reference_logp,
 ):
     both_full = lax.all_gather(
-        jnp.stack([key_weight[0], value_weight[0]]), "dp", axis=1, tiled=True
-    )
-    key_full, value_full = both_full[0], both_full[1]
+        jnp.concatenate([key_weight[0], value_weight[0]], axis=1), "dp", axis=0, tiled=True
+    )
+    kv_cols = key_weight.shape[2]
     hidden = hidden_states[0]
     gain_f = norm_gain[0].astype(jnp.float32)
     tok_rows = hidden.shape[0]
     seq_count = lengths.shape[1]
     seq_len = tok_rows // seq_count
-    kv_cols = key_full.shape[1]
     kv_local = kv_cols // HD
     q_local = queries.shape[2] // HD
     hidden_f = hidden.astype(jnp.float32)
     inv_rms = lax.rsqrt(jnp.mean(hidden_f * hidden_f, axis=-1, keepdims=True) + norm_eps)
     nhat = hidden_f * inv_rms
     normed = (nhat * gain_f).astype(jnp.bfloat16)
-    projected = jnp.einsum("td,wdc->wtc", normed, both_full, preferred_element_type=jnp.float32)
-    key_raw = projected[0]
-    values = projected[1].astype(jnp.bfloat16)
+    projected = jnp.dot(normed, both_full, preferred_element_type=jnp.float32)
+    key_raw = projected[:, :kv_cols]
+    values = projected[:, kv_cols:].astype(jnp.bfloat16)
     cosine, sine = rope_tables(seq_len, HD)
     key_four = key_raw.reshape(seq_count, seq_len, kv_local, HD)
     keys = (
@@ -202,7 +201,6 @@
             tiled=True,
         )
 
-    both_grads = jnp.stack([key_grad, value_grad])
     n_pipe = lax.axis_size("pipe")
     n_tensor = lax.axis_size("tensor")
     sizes = [tok_rows // 4, tok_rows * 5 // 16, tok_rows * 5 // 16, tok_rows // 8]
@@ -225,8 +223,8 @@
     held = None
     for c in range(chunks):
         sl = slice(bounds[c], bounds[c + 1])
-        part = jnp.einsum(
-            "wtc,wdc->td", both_grads[:, sl], both_full, preferred_element_type=jnp.float32
+        part = lax.dot_general(
+            combined[sl], both_full, (((1,), (1,)), ((), ())), preferred_element_type=jnp.float32
         )
         part_low = part.astype(jnp.bfloat16)
         if c == 0:

time: 247 us -> 243 us (0.984)
  waiting for transfers between devices: 154 us -> 145 us
  matrix products: 26.4 us -> 30.6 us
    all_gather x1, waiting for transfers between devices: 73.8 us -> 67.1 us  [on_device(): lax.all_gather(jnp.concatenate([key_weight[0], value_weight[0]], axis=1),...]
    dot_general x5, matrix products: 20.3 us -> 24.5 us  [the longest x4 17.5 us: on_device(): lax.dot_general(combined[sl], both_full, (((1,), (1,)), ((), ())), prefer...]
  transfers between devices with their start and end apart: 10 -> 10, of which waited for: 7 -> 7; matrix products, arithmetic and copies ran while one was open for 12% -> 14% of each run, Pallas kernels for 0% -> 0%
where the time goes in v11:
time: 243 us; the launch traced here: 242 us
  waiting for transfers between devices  145 us (60%)
  matrix products  30.6 us (13%)
  other arithmetic  19.8 us (8%)
  starting transfers between devices  18 us (7%)
  between operations  16.5 us (7%)
  Pallas kernels  8.15 us (3%)
  local copies, waits for them, and re-layouts  4.23 us (2%)
    all_gather x1, waiting for transfers between devices, on_device(): lax.all_gather(jnp.concatenate([key_weight[0], value_weight[0]], axis=1),...  67.1 us
    ppermute x4, waiting for transfers between devices, on_device(): lowers.append(lax.ppermute(held, ('pipe', 'tensor'), shift_pairs))  48.7 us
    ppermute x4, waiting for transfers between devices, on_device(): lax.ppermute(part_low, ('pipe', 'tensor'), pairs).astype(jnp.float32)  29.3 us
    dot_general x4, matrix products, on_device(): lax.dot_general(combined[sl], both_full, (((1,), (1,)), ((), ())), prefer...  17.5 us
    ppermute x4, starting transfers between devices, on_device(): lax.ppermute(part_low, ('pipe', 'tensor'), pairs).astype(jnp.float32)  10.2 us
    pallas_call x1, Pallas kernels, attention_grads(): pl.pallas_call(kernel, grid_spec=pltpu.PrefetchScalarGridSpec(num_scalar_...  8.15 us
    ppermute x4, starting transfers between devices, on_device(): lowers.append(lax.ppermute(held, ('pipe', 'tensor'), shift_pairs))  7.68 us
    dot_general x1, matrix products, on_device(): projected = jnp.dot(normed, both_full, preferred_element_type=jnp.float32)  7.03 us
  transfers between devices with their start and end apart: 10, of which 7 were waited for; matrix products, arithmetic and copies ran while one was open for 14% of the time, Pallas kernels for 0%

profile of v11, /device:TPU:1, one launch (start us, length us, event | category | flops | bytes accessed | tf_op | source)
XLA Modules:
  0.0 242.4 jit_solution(12340611968042187506)
XLA Ops:
  12.8 3.1 %fusion = f32[256]{0:T(256)S(1)} fusion(bf16[1,256,8192]{2,1,0:T(8,128)(2,1)} %param.9), kind=kLoop, calls=%fused_computation.7 | loop fusion | flops 6291200 | bytes 4195328 | tf_op jit(solution)/shard_map/reduce_sum | solution.py:153
  17.2 67.1 %all-gather.2.cloned.1.call-done = bf16[8192,512]{1,0:T(8,128)(2,1)} async-done(((bf16[512,512]{1,0:T(8,128)(2,1)}), bf16[8192,512]{1,0:T(8,128)(2,1)}) %all-gather.2.cloned.1.call-update) | async-done | bytes 8388624 | tf_op jit(solution)/shard_map/all_gather | solution.py:141
  84.3 7.0 %fusion.2 = f32[256,512]{1,0:T(8,128)S(1)} fusion(bf16[8192,512]{1,0:T(8,128)(2,1)} %all-gather.2.cloned.1.call-done, f32[8192]{0:T(1024)S(1)} %bitcast.60, bf16[1,256,8192]{2,1,0:T(8,128)(2,1)} %param.9, f32[256]{0:T(256)S(1)} %add_rsqrt_fusion), kind=kOutput, calls=%fused_computation.21 | convolution fusion | flops 2155872256 | bytes 13140992 | tf_op jit(solution)/shard_map/dot_general | solution.py:156
  93.8 8.1 %shard_map.112 = (f32[256,256]{1,0:T(8,128)}, bf16[256,256]{1,0:T(8,128)(2,1)}) custom-call(s32[1]{0:T(128)} %bitcast.56.len_ref, bf16[256,2048]{1,0:T(8,128)(2,1)} %bitcast.73, bf16[256,2048]{1,0:T(8,128)(2,1)} %fusion.1.c_ref, bf16[256,256]{1,0:T(8,128)(2,1)} %fusion.5.k_ref, bf16[256,256]{1,0:T(8,128)(2,1)} %slice.127.v_ref), custom_call_target="tpu_custom_call" | custom-call | tf_op jit(solution)/shard_map/pallas_call | solution.py:113
  104.1 6.2 %convolution_convert_fusion.3 = bf16[64,8192]{1,0:T(8,128)(2,1)S(1)} fusion(bf16[8192,512]{1,0:T(8,128)(2,1)} %all-gather.2.cloned.1.call-done, bf16[256,256]{1,0:T(8,128)(2,1)S(1)} %fusion.3, bf16[256,256]{1,0:T(8,128)(2,1)S(1)} %copy-done.3), kind=kOutput, calls=%fused_computation.5 | convolution fusion | flops 537526272 | bytes 9699328 | tf_op jit(solution)/shard_map/dot_general | solution.py:226
  110.2 3.3 %collective-permute-start = (bf16[64,8192]{1,0:T(8,128)(2,1)S(1)}, bf16[64,8192]{1,0:T(8,128)(2,1)S(1)}, u32[]{:S(2)}, u32[]{:S(2)}) collective-permute-start(bf16[64,8192]{1,0:T(8,128)(2,1)S(1)} %convolution_convert_fusion.3), channel_id=1, source_target_pairs={{32,33},{33,32},{64,65},{65,64},{96,97},{97,96},{34,35},{35,34},{6... | collective-permute-start | bytes 3145736 | tf_op jit(solution)/shard_map/ppermute | solution.py:243
  113.5 6.1 %convolution_convert_fusion = bf16[8192,512]{1,0:T(8,128)(2,1)} fusion(bf16[256,512]{1,0:T(8,128)(2,1)S(1)} %pad_maximum_fusion.1, f32[8192]{0:T(1024)S(1)} %bitcast.61, bf16[1,256,8192]{2,1,0:T(8,128)(2,1)S(1)} %copy-done, f32[256]{0:T(256)S(1)} %add_rsqrt_fusion), kind=kOutput, calls=%fused_computation | convolution fusion | flops 2160066560 | bytes 12878848 | tf_op jit(solution)/shard_map/dot_general | solution.py:196
  119.6 3.4 %convert_multiply_fusion = f32[256,8192]{1,0:T(8,128)S(1)} fusion(bf16[1,256,8192]{2,1,0:T(8,128)(2,1)} %param.9, f32[256]{0:T(256)S(1)} %add_rsqrt_fusion), kind=kLoop, calls=%fused_computation.1 | loop fusion | flops 4194304 | bytes 12583936 | tf_op jit(solution)/shard_map/mul | solution.py:154
  123.1 6.2 %convolution_convert_fusion.1 = bf16[80,8192]{1,0:T(8,128)(2,1)S(1)} fusion(bf16[8192,512]{1,0:T(8,128)(2,1)} %all-gather.2.cloned.1.call-done, bf16[256,512]{1,0:T(8,128)(2,1)S(1)} %pad_maximum_fusion.1), kind=kOutput, calls=%fused_computation.3 | convolution fusion | flops 671744000 | bytes 9781248 | tf_op jit(solution)/shard_map/dot_general | solution.py:226
  130.3 2.2 collective-permute-start.1
  132.6 2.6 %convolution_convert_fusion.2 = bf16[80,8192]{1,0:T(8,128)(2,1)S(1)} fusion(bf16[8192,512]{1,0:T(8,128)(2,1)S(1)} %bitcast.59, bf16[256,512]{1,0:T(8,128)(2,1)S(1)} %pad_maximum_fusion.1), kind=kOutput, calls=%fused_computation.4 | convolution fusion | flops 671744000 | bytes 9781248 | tf_op jit(solution)/shard_map/dot_general | solution.py:226
  135.3 1.9 collective-permute-start.2
  137.2 11.9 %collective-permute-done.1 = bf16[80,8192]{1,0:T(8,128)(2,1)S(1)} collective-permute-done((bf16[80,8192]{1,0:T(8,128)(2,1)S(1)}, bf16[80,8192]{1,0:T(8,128)(2,1)S(1)}, u32[]{:S(2)}, u32[]{:S(2)}) %collective-permute-start.1) | collective-permute-done | bytes 1310752 | tf_op jit(solution)/shard_map/ppermute | solution.py:243
  150.4 10.5 %collective-permute-done.2 = bf16[64,8192]{1,0:T(8,128)(2,1)S(1)} collective-permute-done((bf16[64,8192]{1,0:T(8,128)(2,1)S(1)}, bf16[64,8192]{1,0:T(8,128)(2,1)S(1)}, u32[]{:S(2)}, u32[]{:S(2)}) %collective-permute-start.2) | collective-permute-done | bytes 1048608 | tf_op jit(solution)/shard_map/ppermute | solution.py:240
  160.9 2.6 %collective-permute-start.3 = (bf16[80,8192]{1,0:T(8,128)(2,1)S(1)}, bf16[80,8192]{1,0:T(8,128)(2,1)S(1)}, u32[]{:S(2)}, u32[]{:S(2)}) collective-permute-start(bf16[80,8192]{1,0:T(8,128)(2,1)S(1)} %convolution_convert_fusion.2), channel_id=1, source_target_pairs={{32,33},{33,32},{64,65},{65,64},{96,97},{97,96},{34,35},{35,34},{6... | collective-permute-start | bytes 3932168 | tf_op jit(solution)/shard_map/ppermute | solution.py:243
  163.5 2.5 %convolution_convert_fusion.4 = bf16[32,8192]{1,0:T(8,128)(2,1)S(1)} fusion(bf16[8192,512]{1,0:T(8,128)(2,1)S(1)} %bitcast.59, bf16[256,512]{1,0:T(8,128)(2,1)S(1)} %pad_maximum_fusion.1), kind=kOutput, calls=%fused_computation.6 | convolution fusion | flops 268697600 | bytes 8945664 | tf_op jit(solution)/shard_map/dot_general | solution.py:226
  166.0 1.9 collective-permute-start.4
  168.0 11.7 %collective-permute-done.3 = bf16[80,8192]{1,0:T(8,128)(2,1)S(1)} collective-permute-done((bf16[80,8192]{1,0:T(8,128)(2,1)S(1)}, bf16[80,8192]{1,0:T(8,128)(2,1)S(1)}, u32[]{:S(2)}, u32[]{:S(2)}) %collective-permute-start.3) | collective-permute-done | bytes 1310752 | tf_op jit(solution)/shard_map/ppermute | solution.py:243
  180.9 15.4 %collective-permute-done.4 = bf16[80,8192]{1,0:T(8,128)(2,1)S(1)} collective-permute-done((bf16[80,8192]{1,0:T(8,128)(2,1)S(1)}, bf16[80,8192]{1,0:T(8,128)(2,1)S(1)}, u32[]{:S(2)}, u32[]{:S(2)}) %collective-permute-start.4) | collective-permute-done | bytes 1310752 | tf_op jit(solution)/shard_map/ppermute | solution.py:240
  196.4 2.2 collective-permute-start.6
  200.5 5.7 %collective-permute-done.6 = bf16[32,8192]{1,0:T(8,128)(2,1)S(1)} collective-permute-done((bf16[32,8192]{1,0:T(8,128)(2,1)S(1)}, bf16[32,8192]{1,0:T(8,128)(2,1)S(1)}, u32[]{:S(2)}, u32[]{:S(2)}) %collective-permute-start.6) | collective-permute-done | bytes 524320 | tf_op jit(solution)/shard_map/ppermute | solution.py:243
  206.9 1.9 collective-permute-start.7
  208.8 22.7 %collective-permute-done.7 = bf16[32,8192]{1,0:T(8,128)(2,1)S(1)} collective-permute-done((bf16[32,8192]{1,0:T(8,128)(2,1)S(1)}, bf16[32,8192]{1,0:T(8,128)(2,1)S(1)}, u32[]{:S(2)}, u32[]{:S(2)}) %collective-permute-start.7) | collective-permute-done | bytes 524320 | tf_op jit(solution)/shard_map/ppermute | solution.py:247
  231.5 2.2 maximum_bitcast_fusion
  (65 shorter events, 17.4 us)
Async XLA Ops:
  7.2 77.1 %all-gather.2.cloned.1.call-start = ((), (), s32[]{:S(2)}) async-start(), calls=%async_computation.1 | async-start | bytes 8912896 | tf_op jit(solution)/shard_map/all_gather | solution.py:141
  9.1 6.8 %copy-start.2 = (bf16[1,256,2048]{2,1,0:T(8,128)(2,1)S(1)}, bf16[1,256,2048]{2,1,0:T(8,128)(2,1)}, u32[]{:S(2)}) copy-start(bf16[1,256,2048]{2,1,0:T(8,128)(2,1)} %param.14) | copy-start | bytes 3145732
  9.1 224.6 %reduce-scatter.2.cloned.1.call-start = ((), (), s32[]{:S(2)}) async-start(), calls=%async_computation.2 | async-start | bytes 8912896 | tf_op jit(solution)/shard_map/reduce_scatter | solution.py:195
  15.9 107.1 %copy-start.4 = (f32[256]{0:T(256)}, f32[256]{0:T(256)S(1)}, u32[]{:S(2)}) copy-start(f32[256]{0:T(256)S(1)} %add_rsqrt_fusion) | copy-start | bytes 3076
  101.9 2.0 copy-start.1
  101.9 2.1 copy-start.3
  104.0 9.4 %copy-start = (bf16[1,256,8192]{2,1,0:T(8,128)(2,1)S(1)}, bf16[1,256,8192]{2,1,0:T(8,128)(2,1)}, u32[]{:S(2)}) copy-start(bf16[1,256,8192]{2,1,0:T(8,128)(2,1)} %param.9) | copy-start | bytes 12582916
  110.2 19.0 %collective-permute-start = (bf16[64,8192]{1,0:T(8,128)(2,1)S(1)}, bf16[64,8192]{1,0:T(8,128)(2,1)S(1)}, u32[]{:S(2)}, u32[]{:S(2)}) collective-permute-start(bf16[64,8192]{1,0:T(8,128)(2,1)S(1)} %convolution_convert_fusion.3), channel_id=1, source_target_pairs={{32,33},{33,32},{64,65},{65,64},{96,97},{97,96},{34,35},{35,34},{6... | collective-permute-start | bytes 3145736 | tf_op jit(solution)/shard_map/ppermute | solution.py:243
  119.6 13.0 %slice-start = ((s8[8388608]{0:T(1024)(128)(4,1)}), s8[4194304]{0:T(1024)(128)(4,1)S(1)}, s32[]{:S(2)}) async-start(s8[8388608]{0:T(1024)(128)(4,1)} %bitcast.58), calls=%async_computation.3 | async-start | bytes 8388608
  123.1 9.6 %slice-start.1 = ((s8[8388608]{0:T(1024)(128)(4,1)}), s8[4194304]{0:T(1024)(128)(4,1)S(1)}, s32[]{:S(2)}) async-start(s8[8388608]{0:T(1024)(128)(4,1)} %bitcast.58), calls=%async_computation.4 | async-start | bytes 8388608
  129.2 0.6 slice-start.2
  129.8 2.7 %copy-start.5 = (f32[256]{0:T(256)S(1)}, f32[256]{0:T(256)}, u32[]{:S(2)}) copy-start(f32[256]{0:T(256)} %copy-done.4) | copy-start | bytes 3076
  130.3 18.8 %collective-permute-start.1 = (bf16[80,8192]{1,0:T(8,128)(2,1)S(1)}, bf16[80,8192]{1,0:T(8,128)(2,1)S(1)}, u32[]{:S(2)}, u32[]{:S(2)}) collective-permute-start(bf16[80,8192]{1,0:T(8,128)(2,1)S(1)} %convolution_convert_fusion.1), channel_id=1, source_target_pairs={{32,33},{33,32},{64,65},{65,64},{96,97},{97,96},{34,35},{35,34},{6... | collective-permute-start | bytes 3932168 | tf_op jit(solution)/shard_map/ppermute | solution.py:243
  135.3 25.6 %collective-permute-start.2 = (bf16[64,8192]{1,0:T(8,128)(2,1)S(1)}, bf16[64,8192]{1,0:T(8,128)(2,1)S(1)}, u32[]{:S(2)}, u32[]{:S(2)}) collective-permute-start(bf16[64,8192]{1,0:T(8,128)(2,1)S(1)} %multiply_convert_fusion.3), channel_id=1, source_target_pairs={{32,0},{33,1},{65,32},{64,33},{96,64},{97,65},{34,2},{35,3},{67,34... | collective-permute-start | bytes 3145736 | tf_op jit(solution)/shard_map/ppermute | solution.py:240
  160.9 18.7 %collective-permute-start.3 = (bf16[80,8192]{1,0:T(8,128)(2,1)S(1)}, bf16[80,8192]{1,0:T(8,128)(2,1)S(1)}, u32[]{:S(2)}, u32[]{:S(2)}) collective-permute-start(bf16[80,8192]{1,0:T(8,128)(2,1)S(1)} %convolution_convert_fusion.2), channel_id=1, source_target_pairs={{32,33},{33,32},{64,65},{65,64},{96,97},{97,96},{34,35},{35,34},{6... | collective-permute-start | bytes 3932168 | tf_op jit(solution)/shard_map/ppermute | solution.py:243
  166.0 30.3 %collective-permute-start.4 = (bf16[80,8192]{1,0:T(8,128)(2,1)S(1)}, bf16[80,8192]{1,0:T(8,128)(2,1)S(1)}, u32[]{:S(2)}, u32[]{:S(2)}) collective-permute-start(bf16[80,8192]{1,0:T(8,128)(2,1)S(1)} %multiply_convert_fusion.2), channel_id=1, source_target_pairs={{32,0},{33,1},{65,32},{64,33},{96,64},{97,65},{34,2},{35,3},{67,34... | collective-permute-start | bytes 3932168 | tf_op jit(solution)/shard_map/ppermute | solution.py:240
  196.4 9.9 %collective-permute-start.6 = (bf16[32,8192]{1,0:T(8,128)(2,1)S(1)}, bf16[32,8192]{1,0:T(8,128)(2,1)S(1)}, u32[]{:S(2)}, u32[]{:S(2)}) collective-permute-start(bf16[32,8192]{1,0:T(8,128)(2,1)S(1)} %convolution_convert_fusion.4), channel_id=1, source_target_pairs={{32,33},{33,32},{64,65},{65,64},{96,97},{97,96},{34,35},{35,34},{6... | collective-permute-start | bytes 1572872 | tf_op jit(solution)/shard_map/ppermute | solution.py:243
  198.6 32.9 %collective-permute-start.5 = (bf16[80,8192]{1,0:T(8,128)(2,1)S(1)}, bf16[80,8192]{1,0:T(8,128)(2,1)S(1)}, u32[]{:S(2)}, u32[]{:S(2)}) collective-permute-start(bf16[80,8192]{1,0:T(8,128)(2,1)S(1)} %multiply_convert_fusion.1), channel_id=1, source_target_pairs={{32,0},{33,1},{65,32},{64,33},{96,64},{97,65},{34,2},{35,3},{67,34... | collective-permute-start | bytes 3932168 | tf_op jit(solution)/shard_map/ppermute | solution.py:240
  206.9 24.6 %collective-permute-start.7 = (bf16[32,8192]{1,0:T(8,128)(2,1)S(1)}, bf16[32,8192]{1,0:T(8,128)(2,1)S(1)}, u32[]{:S(2)}, u32[]{:S(2)}) collective-permute-start(bf16[32,8192]{1,0:T(8,128)(2,1)S(1)} %multiply_convert_fusion.6), channel_id=1, source_target_pairs={{32,0},{33,1},{65,32},{64,33},{96,64},{97,65},{34,2},{35,3},{67,34... | collective-permute-start | bytes 1572872 | tf_op jit(solution)/shard_map/ppermute | solution.py:247
Sparse Core Ops, SparseCore 0:
  10.1 74.0 all-gather.1
  119.7 83.2 reduce-scatter.1

commit v12 on v11

--- a/solution.py
+++ b/solution.py
@@ -203,7 +203,7 @@
 
     n_pipe = lax.axis_size("pipe")
     n_tensor = lax.axis_size("tensor")
-    sizes = [tok_rows // 4, tok_rows * 5 // 16, tok_rows * 5 // 16, tok_rows // 8]
+    sizes = [tok_rows // 8, tok_rows * 3 // 8, tok_rows * 3 // 8, tok_rows // 8]
     bounds = [sum(sizes[:c]) for c in range(len(sizes) + 1)]
     chunks = len(sizes)
     exchange_steps = [

time: 243 us -> 258 us (1.062)
  waiting for transfers between devices: 145 us -> 156 us
    ppermute x4, waiting for transfers between devices: 48.7 us -> 54.7 us  [on_device(): lowers.append(lax.ppermute(held, ('pipe', 'tensor'), shift_pairs))]
    ppermute x4, waiting for transfers between devices: 29.3 us -> 34.2 us  [on_device(): lax.ppermute(part_low, ('pipe', 'tensor'), pairs).astype(jnp.float32)]
  transfers between devices with their start and end apart: 10 -> 10, of which waited for: 7 -> 7; matrix products, arithmetic and copies ran while one was open for 14% -> 11% of each run, Pallas kernels for 0% -> 0%
where the time goes in v12:
time: 258 us; the launch traced here: 257 us
  waiting for transfers between devices  156 us (60%)
  matrix products  30.7 us (12%)
  other arithmetic  21.8 us (8%)
  starting transfers between devices  19.7 us (8%)
  between operations  16.4 us (6%)
  Pallas kernels  8.15 us (3%)
  local copies, waits for them, and re-layouts  4.16 us (2%)
    all_gather x1, waiting for transfers between devices, on_device(): lax.all_gather(jnp.concatenate([key_weight[0], value_weight[0]], axis=1),...  67.1 us
    ppermute x4, waiting for transfers between devices, on_device(): lowers.append(lax.ppermute(held, ('pipe', 'tensor'), shift_pairs))  54.7 us
    ppermute x4, waiting for transfers between devices, on_device(): lax.ppermute(part_low, ('pipe', 'tensor'), pairs).astype(jnp.float32)  34.2 us
    dot_general x4, matrix products, on_device(): lax.dot_general(combined[sl], both_full, (((1,), (1,)), ((), ())), prefer...  17.6 us
    ppermute x4, starting transfers between devices, on_device(): lax.ppermute(part_low, ('pipe', 'tensor'), pairs).astype(jnp.float32)  12 us
    pallas_call x1, Pallas kernels, attention_grads(): pl.pallas_call(kernel, grid_spec=pltpu.PrefetchScalarGridSpec(num_scalar_...  8.15 us
    ppermute x4, starting transfers between devices, on_device(): lowers.append(lax.ppermute(held, ('pipe', 'tensor'), shift_pairs))  7.69 us
    dot_general x1, matrix products, on_device(): projected = jnp.dot(normed, both_full, preferred_element_type=jnp.float32)  7.02 us
  transfers between devices with their start and end apart: 10, of which 7 were waited for; matrix products, arithmetic and copies ran while one was open for 11% of the time, Pallas kernels for 0%

profile of v12, /device:TPU:1, one launch (start us, length us, event | category | flops | bytes accessed | tf_op | source)
XLA Modules:
  0.0 257.0 jit_solution(4546114854001296962)
XLA Ops:
  7.2 2.0 pad_maximum_fusion
  12.8 3.1 %fusion = f32[256]{0:T(256)S(1)} fusion(bf16[1,256,8192]{2,1,0:T(8,128)(2,1)} %param.9), kind=kLoop, calls=%fused_computation.7 | loop fusion | flops 6291200 | bytes 4195328 | tf_op jit(solution)/shard_map/reduce_sum | solution.py:153
  17.2 67.1 %all-gather.2.cloned.1.call-done = bf16[8192,512]{1,0:T(8,128)(2,1)} async-done(((bf16[512,512]{1,0:T(8,128)(2,1)}), bf16[8192,512]{1,0:T(8,128)(2,1)}) %all-gather.2.cloned.1.call-update) | async-done | bytes 8388624 | tf_op jit(solution)/shard_map/all_gather | solution.py:141
  84.3 7.0 %fusion.2 = f32[256,512]{1,0:T(8,128)S(1)} fusion(bf16[8192,512]{1,0:T(8,128)(2,1)} %all-gather.2.cloned.1.call-done, f32[8192]{0:T(1024)S(1)} %bitcast.60, bf16[1,256,8192]{2,1,0:T(8,128)(2,1)} %param.9, f32[256]{0:T(256)S(1)} %add_rsqrt_fusion), kind=kOutput, calls=%fused_computation.18 | convolution fusion | flops 2155872256 | bytes 13140992 | tf_op jit(solution)/shard_map/dot_general | solution.py:156
  93.8 8.1 %shard_map.112 = (f32[256,256]{1,0:T(8,128)}, bf16[256,256]{1,0:T(8,128)(2,1)}) custom-call(s32[1]{0:T(128)} %bitcast.56.len_ref, bf16[256,2048]{1,0:T(8,128)(2,1)} %bitcast.73, bf16[256,2048]{1,0:T(8,128)(2,1)} %fusion.1.c_ref, bf16[256,256]{1,0:T(8,128)(2,1)} %fusion.5.k_ref, bf16[256,256]{1,0:T(8,128)(2,1)} %slice.127.v_ref), custom_call_target="tpu_custom_call" | custom-call | tf_op jit(solution)/shard_map/pallas_call | solution.py:113
  105.9 6.1 %convolution_convert_fusion.4 = bf16[32,8192]{1,0:T(8,128)(2,1)S(1)} fusion(bf16[8192,512]{1,0:T(8,128)(2,1)} %all-gather.2.cloned.1.call-done, bf16[256,256]{1,0:T(8,128)(2,1)S(1)} %fusion.3, bf16[256,256]{1,0:T(8,128)(2,1)S(1)} %copy-done.2), kind=kOutput, calls=%fused_computation.6 | convolution fusion | flops 268763136 | bytes 9175040 | tf_op jit(solution)/shard_map/dot_general | solution.py:226
  111.9 6.1 %convolution_convert_fusion = bf16[8192,512]{1,0:T(8,128)(2,1)} fusion(bf16[256,512]{1,0:T(8,128)(2,1)S(1)} %pad_maximum_fusion.1, f32[8192]{0:T(1024)S(1)} %bitcast.61, bf16[1,256,8192]{2,1,0:T(8,128)(2,1)S(1)} %copy-done, f32[256]{0:T(256)S(1)} %add_rsqrt_fusion), kind=kOutput, calls=%fused_computation | convolution fusion | flops 2160066560 | bytes 12878848 | tf_op jit(solution)/shard_map/dot_general | solution.py:196
  118.1 3.4 %convert_multiply_fusion = f32[256,8192]{1,0:T(8,128)S(1)} fusion(bf16[1,256,8192]{2,1,0:T(8,128)(2,1)} %param.9, f32[256]{0:T(256)S(1)} %add_rsqrt_fusion), kind=kLoop, calls=%fused_computation.1 | loop fusion | flops 4194304 | bytes 12583936 | tf_op jit(solution)/shard_map/mul | solution.py:154
  121.5 3.4 %collective-permute-start = (bf16[32,8192]{1,0:T(8,128)(2,1)S(1)}, bf16[32,8192]{1,0:T(8,128)(2,1)S(1)}, u32[]{:S(2)}, u32[]{:S(2)}) collective-permute-start(bf16[32,8192]{1,0:T(8,128)(2,1)S(1)} %convolution_convert_fusion.4), channel_id=1, source_target_pairs={{32,33},{33,32},{64,65},{65,64},{96,97},{97,96},{34,35},{35,34},{6... | collective-permute-start | bytes 1572872 | tf_op jit(solution)/shard_map/ppermute | solution.py:243
  124.9 6.4 %convolution_convert_fusion.1 = bf16[96,8192]{1,0:T(8,128)(2,1)S(1)} fusion(bf16[8192,512]{1,0:T(8,128)(2,1)} %all-gather.2.cloned.1.call-done, bf16[256,512]{1,0:T(8,128)(2,1)S(1)} %pad_maximum_fusion.1), kind=kOutput, calls=%fused_computation.3 | convolution fusion | flops 806092800 | bytes 10059776 | tf_op jit(solution)/shard_map/dot_general | solution.py:226
  132.7 3.3 %collective-permute-start.1 = (bf16[96,8192]{1,0:T(8,128)(2,1)S(1)}, bf16[96,8192]{1,0:T(8,128)(2,1)S(1)}, u32[]{:S(2)}, u32[]{:S(2)}) collective-permute-start(bf16[96,8192]{1,0:T(8,128)(2,1)S(1)} %convolution_convert_fusion.1), channel_id=1, source_target_pairs={{32,33},{33,32},{64,65},{65,64},{96,97},{97,96},{34,35},{35,34},{6... | collective-permute-start | bytes 4718600 | tf_op jit(solution)/shard_map/ppermute | solution.py:243
  136.1 2.6 %convolution_convert_fusion.2 = bf16[96,8192]{1,0:T(8,128)(2,1)S(1)} fusion(bf16[8192,512]{1,0:T(8,128)(2,1)S(1)} %bitcast.59, bf16[256,512]{1,0:T(8,128)(2,1)S(1)} %pad_maximum_fusion.1), kind=kOutput, calls=%fused_computation.4 | convolution fusion | flops 806092800 | bytes 10059776 | tf_op jit(solution)/shard_map/dot_general | solution.py:226
  138.8 1.9 collective-permute-start.2
  140.7 13.6 %collective-permute-done.1 = bf16[96,8192]{1,0:T(8,128)(2,1)S(1)} collective-permute-done((bf16[96,8192]{1,0:T(8,128)(2,1)S(1)}, bf16[96,8192]{1,0:T(8,128)(2,1)S(1)}, u32[]{:S(2)}, u32[]{:S(2)}) %collective-permute-start.1) | collective-permute-done | bytes 1572896 | tf_op jit(solution)/shard_map/ppermute | solution.py:243
  155.8 3.1 %collective-permute-start.3 = (bf16[96,8192]{1,0:T(8,128)(2,1)S(1)}, bf16[96,8192]{1,0:T(8,128)(2,1)S(1)}, u32[]{:S(2)}, u32[]{:S(2)}) collective-permute-start(bf16[96,8192]{1,0:T(8,128)(2,1)S(1)} %convolution_convert_fusion.2), channel_id=1, source_target_pairs={{32,33},{33,32},{64,65},{65,64},{96,97},{97,96},{34,35},{35,34},{6... | collective-permute-start | bytes 4718600 | tf_op jit(solution)/shard_map/ppermute | solution.py:243
  158.9 2.5 convolution_convert_fusion.3
  161.4 1.9 collective-permute-start.4
  163.4 14.0 %collective-permute-done.3 = bf16[96,8192]{1,0:T(8,128)(2,1)S(1)} collective-permute-done((bf16[96,8192]{1,0:T(8,128)(2,1)S(1)}, bf16[96,8192]{1,0:T(8,128)(2,1)S(1)}, u32[]{:S(2)}, u32[]{:S(2)}) %collective-permute-start.3) | collective-permute-done | bytes 1572896 | tf_op jit(solution)/shard_map/ppermute | solution.py:243
  178.9 26.1 %collective-permute-done.4 = bf16[96,8192]{1,0:T(8,128)(2,1)S(1)} collective-permute-done((bf16[96,8192]{1,0:T(8,128)(2,1)S(1)}, bf16[96,8192]{1,0:T(8,128)(2,1)S(1)}, u32[]{:S(2)}, u32[]{:S(2)}) %collective-permute-start.4) | collective-permute-done | bytes 1572896 | tf_op jit(solution)/shard_map/ppermute | solution.py:240
  205.0 2.2 collective-permute-start.6
  207.2 1.9 collective-permute-start.5
  209.1 5.8 %collective-permute-done.6 = bf16[32,8192]{1,0:T(8,128)(2,1)S(1)} collective-permute-done((bf16[32,8192]{1,0:T(8,128)(2,1)S(1)}, bf16[32,8192]{1,0:T(8,128)(2,1)S(1)}, u32[]{:S(2)}, u32[]{:S(2)}) %collective-permute-start.6) | collective-permute-done | bytes 524320 | tf_op jit(solution)/shard_map/ppermute | solution.py:243
  217.5 28.6 %collective-permute-done.7 = bf16[32,8192]{1,0:T(8,128)(2,1)S(1)} collective-permute-done((bf16[32,8192]{1,0:T(8,128)(2,1)S(1)}, bf16[32,8192]{1,0:T(8,128)(2,1)S(1)}, u32[]{:S(2)}, u32[]{:S(2)}) %collective-permute-start.7) | collective-permute-done | bytes 524320 | tf_op jit(solution)/shard_map/ppermute | solution.py:247
  246.0 2.2 maximum_bitcast_fusion
  (57 shorter events, 18.1 us)
Async XLA Ops:
  7.2 8.8 %copy-start.1 = (bf16[1,256,2048]{2,1,0:T(8,128)(2,1)S(1)}, bf16[1,256,2048]{2,1,0:T(8,128)(2,1)}, u32[]{:S(2)}) copy-start(bf16[1,256,2048]{2,1,0:T(8,128)(2,1)} %param.14) | copy-start | bytes 3145732
  7.2 77.1 %all-gather.2.cloned.1.call-start = ((), (), s32[]{:S(2)}) async-start(), calls=%async_computation.1 | async-start | bytes 8912896 | tf_op jit(solution)/shard_map/all_gather | solution.py:141
  9.2 239.1 %reduce-scatter.2.cloned.1.call-start = ((), (), s32[]{:S(2)}) async-start(), calls=%async_computation.2 | async-start | bytes 8912896 | tf_op jit(solution)/shard_map/reduce_scatter | solution.py:195
  101.9 3.9 %copy-start.2 = (bf16[256,256]{1,0:T(8,128)(2,1)S(1)}, bf16[256,256]{1,0:T(8,128)(2,1)}, u32[]{:S(2)}) copy-start(bf16[256,256]{1,0:T(8,128)(2,1)} %get-tuple-element.16) | copy-start | bytes 393220
  105.8 6.1 %copy-start = (bf16[1,256,8192]{2,1,0:T(8,128)(2,1)S(1)}, bf16[1,256,8192]{2,1,0:T(8,128)(2,1)}, u32[]{:S(2)}) copy-start(bf16[1,256,8192]{2,1,0:T(8,128)(2,1)} %param.9) | copy-start | bytes 12582916
  118.1 18.0 %slice-start = ((s8[8388608]{0:T(1024)(128)(4,1)}), s8[4194304]{0:T(1024)(128)(4,1)S(1)}, s32[]{:S(2)}) async-start(s8[8388608]{0:T(1024)(128)(4,1)} %bitcast.58), calls=%async_computation.3 | async-start | bytes 8388608
  121.5 14.6 %slice-start.1 = ((s8[8388608]{0:T(1024)(128)(4,1)}), s8[4194304]{0:T(1024)(128)(4,1)S(1)}, s32[]{:S(2)}) async-start(s8[8388608]{0:T(1024)(128)(4,1)} %bitcast.58), calls=%async_computation.4 | async-start | bytes 8388608
  121.5 10.6 %collective-permute-start = (bf16[32,8192]{1,0:T(8,128)(2,1)S(1)}, bf16[32,8192]{1,0:T(8,128)(2,1)S(1)}, u32[]{:S(2)}, u32[]{:S(2)}) collective-permute-start(bf16[32,8192]{1,0:T(8,128)(2,1)S(1)} %convolution_convert_fusion.4), channel_id=1, source_target_pairs={{32,33},{33,32},{64,65},{65,64},{96,97},{97,96},{34,35},{35,34},{6... | collective-permute-start | bytes 1572872 | tf_op jit(solution)/shard_map/ppermute | solution.py:243
  132.7 21.6 %collective-permute-start.1 = (bf16[96,8192]{1,0:T(8,128)(2,1)S(1)}, bf16[96,8192]{1,0:T(8,128)(2,1)S(1)}, u32[]{:S(2)}, u32[]{:S(2)}) collective-permute-start(bf16[96,8192]{1,0:T(8,128)(2,1)S(1)} %convolution_convert_fusion.1), channel_id=1, source_target_pairs={{32,33},{33,32},{64,65},{65,64},{96,97},{97,96},{34,35},{35,34},{6... | collective-permute-start | bytes 4718600 | tf_op jit(solution)/shard_map/ppermute | solution.py:243
  138.8 17.0 %collective-permute-start.2 = (bf16[32,8192]{1,0:T(8,128)(2,1)S(1)}, bf16[32,8192]{1,0:T(8,128)(2,1)S(1)}, u32[]{:S(2)}, u32[]{:S(2)}) collective-permute-start(bf16[32,8192]{1,0:T(8,128)(2,1)S(1)} %multiply_convert_fusion.6), channel_id=1, source_target_pairs={{32,0},{33,1},{65,32},{64,33},{96,64},{97,65},{34,2},{35,3},{67,34... | collective-permute-start | bytes 1572872 | tf_op jit(solution)/shard_map/ppermute | solution.py:240
  155.8 21.6 %collective-permute-start.3 = (bf16[96,8192]{1,0:T(8,128)(2,1)S(1)}, bf16[96,8192]{1,0:T(8,128)(2,1)S(1)}, u32[]{:S(2)}, u32[]{:S(2)}) collective-permute-start(bf16[96,8192]{1,0:T(8,128)(2,1)S(1)} %convolution_convert_fusion.2), channel_id=1, source_target_pairs={{32,33},{33,32},{64,65},{65,64},{96,97},{97,96},{34,35},{35,34},{6... | collective-permute-start | bytes 4718600 | tf_op jit(solution)/shard_map/ppermute | solution.py:243
  161.4 43.6 %collective-permute-start.4 = (bf16[96,8192]{1,0:T(8,128)(2,1)S(1)}, bf16[96,8192]{1,0:T(8,128)(2,1)S(1)}, u32[]{:S(2)}, u32[]{:S(2)}) collective-permute-start(bf16[96,8192]{1,0:T(8,128)(2,1)S(1)} %multiply_convert_fusion.2), channel_id=1, source_target_pairs={{32,0},{33,1},{65,32},{64,33},{96,64},{97,65},{34,2},{35,3},{67,34... | collective-permute-start | bytes 4718600 | tf_op jit(solution)/shard_map/ppermute | solution.py:240
  205.0 9.9 %collective-permute-start.6 = (bf16[32,8192]{1,0:T(8,128)(2,1)S(1)}, bf16[32,8192]{1,0:T(8,128)(2,1)S(1)}, u32[]{:S(2)}, u32[]{:S(2)}) collective-permute-start(bf16[32,8192]{1,0:T(8,128)(2,1)S(1)} %convolution_convert_fusion.3), channel_id=1, source_target_pairs={{32,33},{33,32},{64,65},{65,64},{96,97},{97,96},{34,35},{35,34},{6... | collective-permute-start | bytes 1572872 | tf_op jit(solution)/shard_map/ppermute | solution.py:243
  207.2 38.9 %collective-permute-start.5 = (bf16[96,8192]{1,0:T(8,128)(2,1)S(1)}, bf16[96,8192]{1,0:T(8,128)(2,1)S(1)}, u32[]{:S(2)}, u32[]{:S(2)}) collective-permute-start(bf16[96,8192]{1,0:T(8,128)(2,1)S(1)} %multiply_convert_fusion.1), channel_id=1, source_target_pairs={{32,0},{33,1},{65,32},{64,33},{96,64},{97,65},{34,2},{35,3},{67,34... | collective-permute-start | bytes 4718600 | tf_op jit(solution)/shard_map/ppermute | solution.py:240
  215.5 30.5 %collective-permute-start.7 = (bf16[32,8192]{1,0:T(8,128)(2,1)S(1)}, bf16[32,8192]{1,0:T(8,128)(2,1)S(1)}, u32[]{:S(2)}, u32[]{:S(2)}) collective-permute-start(bf16[32,8192]{1,0:T(8,128)(2,1)S(1)} %multiply_convert_fusion.5), channel_id=1, source_target_pairs={{32,0},{33,1},{65,32},{64,33},{96,64},{97,65},{34,2},{35,3},{67,34... | collective-permute-start | bytes 1572872 | tf_op jit(solution)/shard_map/ppermute | solution.py:247
Sparse Core Ops, SparseCore 0:
  10.2 74.0 all-gather.1
  118.2 83.3 reduce-scatter.1

commit v13 on v12

--- a/solution.py
+++ b/solution.py
@@ -203,49 +203,72 @@
 
     n_pipe = lax.axis_size("pipe")
     n_tensor = lax.axis_size("tensor")
-    sizes = [tok_rows // 8, tok_rows * 3 // 8, tok_rows * 3 // 8, tok_rows // 8]
-    bounds = [sum(sizes[:c]) for c in range(len(sizes) + 1)]
-    chunks = len(sizes)
-    exchange_steps = [
-        [
-            (p * n_tensor + t, p * n_tensor + (t + step) % n_tensor)
-            for p in range(1, n_pipe)
+    me_pipe = lax.axis_index("pipe")
+    axes = ("pipe", "tensor")
+
+    def at(p, t):
+        return p * n_tensor + t
+
+    same_chip = lambda p, q: p // 2 == q // 2
+    late = [q for q in range(2, n_pipe) if same_chip(q, q - 1)]
+    early = [q for q in range(1, n_pipe) if q not in late]
+
+    def swap(qs):
+        return [(at(q, t), at(q, (t + 1) % n_tensor)) for q in qs for t in range(n_tensor)]
+
+    def shift(qs):
+        return [
+            (at(q, t if same_chip(q, q - 1) else n_tensor - 1 - t), at(q - 1, t))
+            for q in qs
             for t in range(n_tensor)
         ]
-        for step in range(1, n_tensor)
-    ]
-    shift_pairs = [
-        ((p + 1) * n_tensor + (t if (p + 1) // 2 == p // 2 else n_tensor - 1 - t), p * n_tensor + t)
-        for p in range(n_pipe - 1)
-        for t in range(n_tensor)
-    ]
-    lowers = []
-    held = None
-    for c in range(chunks):
-        sl = slice(bounds[c], bounds[c + 1])
-        part = lax.dot_general(
-            combined[sl], both_full, (((1,), (1,)), ((), ())), preferred_element_type=jnp.float32
+
+    def reduce_and_send(sections, sizes, combined=None, gate=None):
+        bounds = [sum(sizes[:c]) for c in range(len(sizes) + 1)]
+        exchange_pairs, shift_pairs = swap(sections), shift(sections)
+        lowers, held, signal, grads = [], None, None, None
+        for c in range(len(sizes)):
+            sl = slice(bounds[c], bounds[c + 1])
+            part = lax.dot_general(
+                both_grads[sl], both_full, (((1,), (1,)), ((), ())),
+                preferred_element_type=jnp.float32,
+            )
+            if gate is not None:
+                part = part.at[0, 0].add(0.0 * gate[0, 0].astype(jnp.float32))
+                gate = None
+            part_low = part.astype(jnp.bfloat16)
+            if combined is not None:
+                part_low, combined = lax.optimization_barrier((part_low, combined))
+                grads = weight_grads(combined)
+                combined = None
+            if held is not None:
+                if len(lowers) > 0:
+                    part_low, held, lowers[-1] = lax.optimization_barrier(
+                        (part_low, held, lowers[-1])
+                    )
+                else:
+                    part_low, held = lax.optimization_barrier((part_low, held))
+                lowers.append(lax.ppermute(held, axes, shift_pairs))
+            received = lax.ppermute(part_low, axes, exchange_pairs)
+            signal = received[:8, :128]
+            normed_grad = part_low.astype(jnp.float32) + received.astype(jnp.float32)
+            held = norm_backward(normed_grad, gain_f, nhat[sl], inv_rms[sl])
+        lowers.append(lax.ppermute(held, axes, shift_pairs))
+        return jnp.concatenate(lowers, axis=0), signal, grads
+
+    both_grads = combined
+    first, signal, grad_total = reduce_and_send(
+        early, [tok_rows // 4, tok_rows * 5 // 16, tok_rows * 5 // 16, tok_rows // 8], combined
+    )
+    lower = first
+    if late:
+        release = [(at(q - 1, t), at(q, t)) for q in late for t in range(n_tensor)]
+        gate = lax.ppermute(signal, axes, release)
+        second, _, _ = reduce_and_send(late, [tok_rows // 2, tok_rows // 2], gate=gate)
+        from_late = functools.reduce(
+            jnp.logical_or, [me_pipe == q - 1 for q in late], me_pipe < 0
         )
-        part_low = part.astype(jnp.bfloat16)
-        if c == 0:
-            part_low, combined = lax.optimization_barrier((part_low, combined))
-            grad_total = weight_grads(combined)
-        if held is not None:
-            if len(lowers) > 0:
-                part_low, held, lowers[-1] = lax.optimization_barrier(
-                    (part_low, held, lowers[-1])
-                )
-            else:
-                part_low, held = lax.optimization_barrier((part_low, held))
-            lowers.append(lax.ppermute(held, ("pipe", "tensor"), shift_pairs))
-        normed_grad = part_low.astype(jnp.float32)
-        for pairs in exchange_steps:
-            normed_grad = normed_grad + lax.ppermute(
-                part_low, ("pipe", "tensor"), pairs
-            ).astype(jnp.float32)
-        held = norm_backward(normed_grad, gain_f, nhat[sl], inv_rms[sl])
-    lowers.append(lax.ppermute(held, ("pipe", "tensor"), shift_pairs))
-    lower = jnp.concatenate(lowers, axis=0)
+        lower = jnp.where(from_late, second, first)
     return (grad_total[:, :kv_cols][None], grad_total[:, kv_cols:][None], lower[None])
 
 

time: 258 us -> 283 us (1.097)
  the two profiles are of different devices: /device:TPU:1 before, /device:TPU:13 now
where the time goes in v13:
time: 283 us; the launch traced here: 282 us
  waiting for transfers between devices  146 us (52%)
  matrix products  43.1 us (15%)
  other arithmetic  37.6 us (13%)
  starting transfers between devices  20.5 us (7%)
  between operations  17.9 us (6%)
  local copies, waits for them, and re-layouts  9.07 us (3%)
  Pallas kernels  8.14 us (3%)
    all_gather x1, waiting for transfers between devices, on_device(): lax.all_gather(jnp.concatenate([key_weight[0], value_weight[0]], axis=1),...  66.2 us
    ppermute x1, waiting for transfers between devices, on_device(): gate = lax.ppermute(signal, axes, release)  40.9 us
    ppermute x6, waiting for transfers between devices, reduce_and_send(): received = lax.ppermute(part_low, axes, exchange_pairs)  36.7 us
    dot_general x6, matrix products, reduce_and_send(): lax.dot_general(both_grads[sl], both_full, (((1,), (1,)), ((), ())), pref...  30.1 us
    convert_element_type x6, other arithmetic, norm_backward(): return ((gain_grad_in - nhat * centre) * inv_rms).astype(jnp.bfloat16)  10.9 us
    ppermute x6, starting transfers between devices, reduce_and_send(): lowers.append(lax.ppermute(held, axes, shift_pairs))  10.1 us
    ppermute x6, starting transfers between devices, reduce_and_send(): received = lax.ppermute(part_low, axes, exchange_pairs)  8.76 us
    pallas_call x1, Pallas kernels, attention_grads(): pl.pallas_call(kernel, grid_spec=pltpu.PrefetchScalarGridSpec(num_scalar_...  8.14 us
  transfers between devices with their start and end apart: 15, of which 5 were waited for; matrix products, arithmetic and copies ran while one was open for 22% of the time, Pallas kernels for 0%

profile of v13, /device:TPU:13, one launch (start us, length us, event | category | flops | bytes accessed | tf_op | source)
XLA Modules:
  0.0 281.9 jit_solution(4680070666994160747)
XLA Ops:
  12.8 3.1 %fusion = f32[256]{0:T(256)S(1)} fusion(bf16[1,256,8192]{2,1,0:T(8,128)(2,1)} %param.11), kind=kLoop, calls=%fused_computation.8 | loop fusion | flops 6291200 | bytes 4195328 | tf_op jit(solution)/shard_map/reduce_sum | solution.py:153
  17.1 66.2 %all-gather.2.cloned.1.call-done = bf16[8192,512]{1,0:T(8,128)(2,1)} async-done(((bf16[512,512]{1,0:T(8,128)(2,1)}), bf16[8192,512]{1,0:T(8,128)(2,1)}) %all-gather.2.cloned.1.call-update) | async-done | bytes 8388624 | tf_op jit(solution)/shard_map/all_gather | solution.py:141
  83.3 7.0 %fusion.2 = f32[256,512]{1,0:T(8,128)S(1)} fusion(bf16[8192,512]{1,0:T(8,128)(2,1)} %all-gather.2.cloned.1.call-done, f32[8192]{0:T(1024)S(1)} %bitcast.68, bf16[1,256,8192]{2,1,0:T(8,128)(2,1)} %param.11, f32[256]{0:T(256)S(1)} %add_rsqrt_fusion), kind=kOutput, calls=%fused_computation.28 | convolution fusion | flops 2155872256 | bytes 13140992 | tf_op jit(solution)/shard_map/dot_general | solution.py:156
  92.8 8.1 %shard_map.112 = (f32[256,256]{1,0:T(8,128)}, bf16[256,256]{1,0:T(8,128)(2,1)}) custom-call(s32[1]{0:T(128)} %bitcast.62.len_ref, bf16[256,2048]{1,0:T(8,128)(2,1)} %bitcast.86, bf16[256,2048]{1,0:T(8,128)(2,1)} %fusion.1.c_ref, bf16[256,256]{1,0:T(8,128)(2,1)} %fusion.5.k_ref, bf16[256,256]{1,0:T(8,128)(2,1)} %slice.233.v_ref), custom_call_target="tpu_custom_call" | custom-call | tf_op jit(solution)/shard_map/pallas_call | solution.py:113
  105.2 6.2 %convolution_convert_fusion.4 = bf16[64,8192]{1,0:T(8,128)(2,1)S(1)} fusion(bf16[8192,512]{1,0:T(8,128)(2,1)} %all-gather.2.cloned.1.call-done, bf16[256,256]{1,0:T(8,128)(2,1)S(1)} %fusion.3, bf16[256,256]{1,0:T(8,128)(2,1)S(1)} %copy-done.4), kind=kOutput, calls=%fused_computation.6 | convolution fusion | flops 537526272 | bytes 9699328 | tf_op jit(solution)/shard_map/dot_general | solution.py:232
  113.4 2.6 convolution_convert_fusion.2
  118.1 2.6 convolution_convert_fusion.3
  125.4 6.0 %convolution_convert_fusion = bf16[8192,512]{1,0:T(8,128)(2,1)} fusion(bf16[256,512]{1,0:T(8,128)(2,1)S(1)} %pad_maximum_fusion.1, f32[8192]{0:T(1024)S(1)} %bitcast.73, bf16[1,256,8192]{2,1,0:T(8,128)(2,1)S(1)} %copy-done.3, f32[256]{0:T(256)S(1)} %copy-done.10), kind=kOutput, calls=%fused_computation | convolution fusion | flops 2160066560 | bytes 12878848 | tf_op jit(solution)/shard_map/dot_general | solution.py:196
  131.4 6.0 %convolution_convert_fusion.5 = bf16[32,8192]{1,0:T(8,128)(2,1)S(1)} fusion(bf16[8192,512]{1,0:T(8,128)(2,1)} %all-gather.2.cloned.1.call-done, bf16[256,256]{1,0:T(8,128)(2,1)S(1)} %fusion.3, bf16[256,256]{1,0:T(8,128)(2,1)S(1)} %copy-done.4), kind=kOutput, calls=%fused_computation.7 | convolution fusion | flops 268763136 | bytes 9175040 | tf_op jit(solution)/shard_map/dot_general | solution.py:232
  138.2 2.3 multiply_reduce_fusion.2
  140.6 3.5 %multiply_convert_fusion.3 = bf16[80,8192]{1,0:T(8,128)(2,1)} fusion(f32[256,8192]{1,0:T(8,128)} %copy-done, bf16[80,8192]{1,0:T(8,128)(2,1)S(1)} %collective-permute-done.3, bf16[80,8192]{1,0:T(8,128)(2,1)S(1)} %convolution_convert_fusion.3, f32[80]{0:T(128)S(1)} %get-tuple-element.53, f32[80]{0:T(128)S(1)} %broadcast_multiply_fusion.4, f32[8192]{0:T(1024)S(1)} %bitcast.75), kind=kLoop, calls=%fused_computation.17 | loop fusion | flops 5242880 | bytes 6587008 | tf_op jit(solution)/shard_map/convert_element_type | solution.py:127
  146.7 6.2 %fusion.9 = f32[128,8192]{1,0:T(8,128)S(1)} fusion(bf16[8192,512]{1,0:T(8,128)(2,1)} %all-gather.2.cloned.1.call-done, bf16[256,256]{1,0:T(8,128)(2,1)S(1)} %fusion.3, bf16[256,256]{1,0:T(8,128)(2,1)S(1)} %copy-done.4), kind=kOutput, calls=%fused_computation.64 | convolution fusion | flops 1074003968 | bytes 12845056 | tf_op jit(solution)/shard_map/dot_general | solution.py:232
  155.4 40.9 %collective-permute-done.6 = bf16[8,128]{1,0:T(8,128)(2,1)S(1)} collective-permute-done((bf16[8,128]{1,0:T(8,128)(2,1)S(1)}, bf16[8,128]{1,0:T(8,128)(2,1)S(1)}, u32[]{:S(2)}, u32[]{:S(2)}) %collective-permute-start.6) | collective-permute-done | bytes 2080 | tf_op jit(solution)/shard_map/ppermute | solution.py:266
  199.5 2.8 convert_element_type.168
  202.3 2.9 %collective-permute-start.7 = (bf16[128,8192]{1,0:T(8,128)(2,1)S(1)}, bf16[128,8192]{1,0:T(8,128)(2,1)S(1)}, u32[]{:S(2)}, u32[]{:S(2)}) collective-permute-start(bf16[128,8192]{1,0:T(8,128)(2,1)S(1)} %convert_element_type.168), channel_id=1, source_target_pairs={{96,97},{97,96},{98,99},{99,98},{100,101},{101,100},{102,103},{103... | collective-permute-start | bytes 6291464 | tf_op jit(solution)/shard_map/ppermute | solution.py:252
  205.2 6.5 %convolution_convert_fusion.1 = bf16[128,8192]{1,0:T(8,128)(2,1)S(1)} fusion(bf16[8192,512]{1,0:T(8,128)(2,1)} %all-gather.2.cloned.1.call-done, bf16[256,256]{1,0:T(8,128)(2,1)S(1)} %fusion.3, bf16[256,256]{1,0:T(8,128)(2,1)S(1)} %copy-done.4), kind=kOutput, calls=%fused_computation.3 | convolution fusion | flops 1075052544 | bytes 10747904 | tf_op jit(solution)/shard_map/dot_general | solution.py:232
  211.7 17.5 %collective-permute-done.7 = bf16[128,8192]{1,0:T(8,128)(2,1)S(1)} collective-permute-done((bf16[128,8192]{1,0:T(8,128)(2,1)S(1)}, bf16[128,8192]{1,0:T(8,128)(2,1)S(1)}, u32[]{:S(2)}, u32[]{:S(2)}) %collective-permute-start.7) | collective-permute-done | bytes 2097184 | tf_op jit(solution)/shard_map/ppermute | solution.py:252
  230.1 2.5 multiply_convert_fusion.2
  232.5 2.8 collective-permute-start.9
  237.5 2.7 collective-permute-start.8
  240.1 19.2 %collective-permute-done.9 = bf16[128,8192]{1,0:T(8,128)(2,1)S(1)} collective-permute-done((bf16[128,8192]{1,0:T(8,128)(2,1)S(1)}, bf16[128,8192]{1,0:T(8,128)(2,1)S(1)}, u32[]{:S(2)}, u32[]{:S(2)}) %collective-permute-start.9) | collective-permute-done | bytes 2097184 | tf_op jit(solution)/shard_map/ppermute | solution.py:252
  260.3 2.5 multiply_convert_fusion.1
  262.8 2.7 collective-permute-start.10
  268.2 5.0 %maximum_select_fusion = bf16[1,256,8192]{2,1,0:T(8,128)(2,1)} fusion(bf16[1,128,8192]{2,1,0:T(8,128)(2,1)} %bitcast.13, bf16[1,128,8192]{2,1,0:T(8,128)(2,1)} %bitcast.12, bf16[1,32,8192]{2,1,0:T(8,128)(2,1)S(1)} %bitcast.89, bf16[1,80,8192]{2,1,0:T(8,128)(2,1)} %bitcast.16, bf16[1,80,8192]{2,1,0:T(8,128)(2,1)S(1)} %bitcast.84, ...), kind=kLoop, calls=%fused_computation.10 | loop fusion | flops 27262976 | bytes 12582913 | tf_op jit(solution)/shard_map/jit(_where)/select_n | solution.py:271
  (104 shorter events, 36.3 us)
Async XLA Ops:
  7.2 8.7 %copy-start.8 = (bf16[1,256,2048]{2,1,0:T(8,128)(2,1)S(1)}, bf16[1,256,2048]{2,1,0:T(8,128)(2,1)}, u32[]{:S(2)}) copy-start(bf16[1,256,2048]{2,1,0:T(8,128)(2,1)} %param.16) | copy-start | bytes 3145732
  7.2 76.1 %all-gather.2.cloned.1.call-start = ((), (), s32[]{:S(2)}) async-start(), calls=%async_computation.1 | async-start | bytes 8912896 | tf_op jit(solution)/shard_map/all_gather | solution.py:141
  9.2 264.0 %reduce-scatter.2.cloned.1.call-start = ((), (), s32[]{:S(2)}) async-start(), calls=%async_computation.2 | async-start | bytes 8912896 | tf_op jit(solution)/shard_map/reduce_scatter | solution.py:195
  15.9 97.4 %copy-start.9 = (f32[256]{0:T(256)}, f32[256]{0:T(256)S(1)}, u32[]{:S(2)}) copy-start(f32[256]{0:T(256)S(1)} %add_rsqrt_fusion) | copy-start | bytes 3076
  102.9 10.5 %slice-start = ((s8[8388608]{0:T(1024)(128)(4,1)}), s8[4194304]{0:T(1024)(128)(4,1)S(1)}, s32[]{:S(2)}) async-start(s8[8388608]{0:T(1024)(128)(4,1)} %bitcast.64), calls=%async_computation.3 | async-start | bytes 8388608
  105.2 8.2 %slice-start.1 = ((s8[8388608]{0:T(1024)(128)(4,1)}), s8[4194304]{0:T(1024)(128)(4,1)S(1)}, s32[]{:S(2)}) async-start(s8[8388608]{0:T(1024)(128)(4,1)} %bitcast.64), calls=%async_computation.4 | async-start | bytes 8388608
  111.3 4.7 %collective-permute-start = (bf16[64,8192]{1,0:T(8,128)(2,1)S(1)}, bf16[64,8192]{1,0:T(8,128)(2,1)S(1)}, u32[]{:S(2)}, u32[]{:S(2)}) collective-permute-start(bf16[64,8192]{1,0:T(8,128)(2,1)S(1)} %convolution_convert_fusion.4), channel_id=1, source_target_pairs={{32,33},{33,32},{64,65},{65,64},{34,35},{35,34},{66,67},{67,66},{3... | collective-permute-start | bytes 3145736 | tf_op jit(solution)/shard_map/ppermute | solution.py:252
  113.4 9.6 %copy-start = (f32[256,8192]{1,0:T(8,128)}, f32[256,8192]{1,0:T(8,128)S(1)}, u32[]{:S(2)}) copy-start(f32[256,8192]{1,0:T(8,128)S(1)} %convert_multiply_fusion) | copy-start | bytes 25165828
  117.2 5.1 %collective-permute-start.1 = (bf16[80,8192]{1,0:T(8,128)(2,1)S(1)}, bf16[80,8192]{1,0:T(8,128)(2,1)S(1)}, u32[]{:S(2)}, u32[]{:S(2)}) collective-permute-start(bf16[80,8192]{1,0:T(8,128)(2,1)S(1)} %convolution_convert_fusion.2), channel_id=1, source_target_pairs={{32,33},{33,32},{64,65},{65,64},{34,35},{35,34},{66,67},{67,66},{3... | collective-permute-start | bytes 3932168 | tf_op jit(solution)/shard_map/ppermute | solution.py:252
  120.7 4.0 %collective-permute-start.2 = (bf16[64,8192]{1,0:T(8,128)(2,1)S(1)}, bf16[64,8192]{1,0:T(8,128)(2,1)}, u32[]{:S(2)}, u32[]{:S(2)}) collective-permute-start(bf16[64,8192]{1,0:T(8,128)(2,1)S(1)} %multiply_convert_fusion.5), channel_id=1, source_target_pairs={{32,0},{33,1},{65,32},{64,33},{34,2},{35,3},{67,34},{66,35},{36,4}... | collective-permute-start | bytes 3145736 | tf_op jit(solution)/shard_map/ppermute | solution.py:251
  124.7 13.6 %collective-permute-start.3 = (bf16[80,8192]{1,0:T(8,128)(2,1)S(1)}, bf16[80,8192]{1,0:T(8,128)(2,1)S(1)}, u32[]{:S(2)}, u32[]{:S(2)}) collective-permute-start(bf16[80,8192]{1,0:T(8,128)(2,1)S(1)} %convolution_convert_fusion.3), channel_id=1, source_target_pairs={{32,33},{33,32},{64,65},{65,64},{34,35},{35,34},{66,67},{67,66},{3... | collective-permute-start | bytes 3932168 | tf_op jit(solution)/shard_map/ppermute | solution.py:252
  137.5 6.6 %collective-permute-start.4 = (bf16[80,8192]{1,0:T(8,128)(2,1)S(1)}, bf16[80,8192]{1,0:T(8,128)(2,1)S(1)}, u32[]{:S(2)}, u32[]{:S(2)}) collective-permute-start(bf16[80,8192]{1,0:T(8,128)(2,1)S(1)} %copy-done.7), channel_id=1, source_target_pairs={{32,0},{33,1},{65,32},{64,33},{34,2},{35,3},{67,34},{66,35},{36,4}... | collective-permute-start | bytes 3932168 | tf_op jit(solution)/shard_map/ppermute | solution.py:251
  144.1 0.7 collective-permute-start.5
  145.2 51.2 %collective-permute-start.6 = (bf16[8,128]{1,0:T(8,128)(2,1)S(1)}, bf16[8,128]{1,0:T(8,128)(2,1)S(1)}, u32[]{:S(2)}, u32[]{:S(2)}) collective-permute-start(bf16[8,128]{1,0:T(8,128)(2,1)S(1)} %slice.163), channel_id=1, source_target_pairs={{64,96},{65,97},{66,98},{67,99},{68,100},{69,101},{70,102},{71,103... | collective-permute-start | bytes 6152 | tf_op jit(solution)/shard_map/ppermute | solution.py:266
  199.5 29.7 %slice-start.2 = ((s8[8388608]{0:T(1024)(128)(4,1)}), s8[4194304]{0:T(1024)(128)(4,1)S(1)}, s32[]{:S(2)}) async-start(s8[8388608]{0:T(1024)(128)(4,1)} %bitcast.66), calls=%async_computation.5 | async-start | bytes 8388608
  202.3 26.9 %collective-permute-start.7 = (bf16[128,8192]{1,0:T(8,128)(2,1)S(1)}, bf16[128,8192]{1,0:T(8,128)(2,1)S(1)}, u32[]{:S(2)}, u32[]{:S(2)}) collective-permute-start(bf16[128,8192]{1,0:T(8,128)(2,1)S(1)} %convert_element_type.168), channel_id=1, source_target_pairs={{96,97},{97,96},{98,99},{99,98},{100,101},{101,100},{102,103},{103... | collective-permute-start | bytes 6291464 | tf_op jit(solution)/shard_map/ppermute | solution.py:252
  205.2 24.0 %slice-start.3 = ((s8[8388608]{0:T(1024)(128)(4,1)}), s8[4194304]{0:T(1024)(128)(4,1)S(1)}, s32[]{:S(2)}) async-start(s8[8388608]{0:T(1024)(128)(4,1)} %bitcast.66), calls=%async_computation.6 | async-start | bytes 8388608
  205.2 24.0 %copy-start.2 = (f32[128,8192]{1,0:T(8,128)S(1)}, f32[128,8192]{1,0:T(8,128)}, u32[]{:S(2)}) copy-start(f32[128,8192]{1,0:T(8,128)} %scatter-add.4) | copy-start | bytes 12582916
  232.5 26.8 %collective-permute-start.9 = (bf16[128,8192]{1,0:T(8,128)(2,1)S(1)}, bf16[128,8192]{1,0:T(8,128)(2,1)S(1)}, u32[]{:S(2)}, u32[]{:S(2)}) collective-permute-start(bf16[128,8192]{1,0:T(8,128)(2,1)S(1)} %convolution_convert_fusion.1), channel_id=1, source_target_pairs={{96,97},{97,96},{98,99},{99,98},{100,101},{101,100},{102,103},{103... | collective-permute-start | bytes 6291464 | tf_op jit(solution)/shard_map/ppermute | solution.py:252
  235.4 31.1 %collective-permute-start.11 = (bf16[80,8192]{1,0:T(8,128)(2,1)}, bf16[80,8192]{1,0:T(8,128)(2,1)}, u32[]{:S(2)}, u32[]{:S(2)}) collective-permute-start(bf16[80,8192]{1,0:T(8,128)(2,1)} %multiply_convert_fusion.3), channel_id=1, source_target_pairs={{32,0},{33,1},{65,32},{64,33},{34,2},{35,3},{67,34},{66,35},{36,4}... | collective-permute-start | bytes 3932168 | tf_op jit(solution)/shard_map/ppermute | solution.py:251
  237.5 29.0 %collective-permute-start.8 = (bf16[128,8192]{1,0:T(8,128)(2,1)}, bf16[128,8192]{1,0:T(8,128)(2,1)}, u32[]{:S(2)}, u32[]{:S(2)}) collective-permute-start(bf16[128,8192]{1,0:T(8,128)(2,1)} %multiply_convert_fusion.2), channel_id=1, source_target_pairs={{96,64},{97,65},{98,66},{99,67},{100,68},{101,69},{102,70},{103,71... | collective-permute-start | bytes 6291464 | tf_op jit(solution)/shard_map/ppermute | solution.py:251
  260.3 7.9 %copy-start.6 = (bf16[80,8192]{1,0:T(8,128)(2,1)S(1)}, bf16[80,8192]{1,0:T(8,128)(2,1)}, u32[]{:S(2)}) copy-start(bf16[80,8192]{1,0:T(8,128)(2,1)} %copy-done.5) | copy-start | bytes 3932164
  262.8 5.4 %collective-permute-start.10 = (bf16[128,8192]{1,0:T(8,128)(2,1)}, bf16[128,8192]{1,0:T(8,128)(2,1)}, u32[]{:S(2)}, u32[]{:S(2)}) collective-permute-start(bf16[128,8192]{1,0:T(8,128)(2,1)} %multiply_convert_fusion.1), channel_id=1, source_target_pairs={{96,64},{97,65},{98,66},{99,67},{100,68},{101,69},{102,70},{103,71... | collective-permute-start | bytes 6291464 | tf_op jit(solution)/shard_map/ppermute | solution.py:256
  265.8 0.7 collective-permute-start.12
  (7 other events, 23.1 us)
Sparse Core Ops, SparseCore 0:
  10.2 73.1 all-gather.1
  131.6 111.4 reduce-scatter.1

commit v14 on v11

--- a/solution.py
+++ b/solution.py
@@ -72,7 +72,9 @@
     return (key_grad.astype(jnp.bfloat16), value_grad)
 
 
-def attention_kernel(len_ref, q_ref, c_ref, k_ref, v_ref, rg_ref, vg_ref, *, group, head_dim):
+def attention_kernel(
+    len_ref, q_ref, c_ref, k_ref, v_ref, cos_ref, sin_ref, kg_ref, vg_ref, *, group, head_dim
+):
     seq_len = k_ref.shape[0]
     scale = 1.0 / math.sqrt(head_dim)
     length = len_ref[0]
@@ -100,25 +102,29 @@
         score_grad = probs * (prob_grad - centre) * scale
         rotated = rotated + lax.dot_general(
             score_grad.T.astype(jnp.bfloat16), query, nn, preferred_element_type=jnp.float32)
-    rg_ref[...] = rotated
+    lane = lax.broadcasted_iota(jnp.int32, (seq_len, head_dim), 1)
+    turned = pltpu.roll(rotated * sin_ref[...], head_dim // 2, 1)
+    turned = jnp.where(lane < head_dim // 2, turned, -turned)
+    kg_ref[...] = (rotated * cos_ref[...] + turned).astype(jnp.bfloat16)
     vg_ref[...] = value_grad.astype(jnp.bfloat16)
 
-def attention_grads(length, queries, cotan, keys, values, head_dim):
+def attention_grads(length, queries, cotan, keys, values, cosine, sine, head_dim):
     seq_len, kv_cols = keys.shape
     kv_heads = kv_cols // head_dim
     group = queries.shape[1] // kv_cols
     kernel = functools.partial(attention_kernel, group=group, head_dim=head_dim)
     q_spec = pl.BlockSpec((seq_len, group * head_dim), lambda k, n: (0, k))
     kv_spec = pl.BlockSpec((seq_len, head_dim), lambda k, n: (0, k))
+    rope_spec = pl.BlockSpec((seq_len, head_dim), lambda k, n: (0, 0))
     return pl.pallas_call(
         kernel,
         grid_spec=pltpu.PrefetchScalarGridSpec(
             num_scalar_prefetch=1, grid=(kv_heads,),
-            in_specs=[q_spec, q_spec, kv_spec, kv_spec],
+            in_specs=[q_spec, q_spec, kv_spec, kv_spec, rope_spec, rope_spec],
             out_specs=[kv_spec, kv_spec]),
-        out_shape=[jax.ShapeDtypeStruct((seq_len, kv_cols), jnp.float32),
+        out_shape=[jax.ShapeDtypeStruct((seq_len, kv_cols), jnp.bfloat16),
                    jax.ShapeDtypeStruct((seq_len, kv_cols), jnp.bfloat16)],
-    )(length, queries, cotan, keys, values)
+    )(length, queries, cotan, keys, values, cosine, sine)
 
 
 def norm_backward(normed_grad, gain_f, nhat, inv_rms):
@@ -173,17 +179,17 @@
     key_parts, value_parts = [], []
     for n in range(seq_count):
         rows_n = slice(n * seq_len, (n + 1) * seq_len)
-        rotated, value_part = attention_grads(
+        key_part, value_part = attention_grads(
             lengths[0][n:n + 1],
             queries[0][rows_n],
             scaled[n].reshape(seq_len, q_local * HD),
             keys[n].reshape(seq_len, kv_cols),
             values[rows_n],
+            cosine,
+            sine,
             HD,
         )
-        rotated = rotated.reshape(seq_len, kv_local, HD)
-        key_part = rotated * cosine[:, None, :] + rotate_back(rotated * sine[:, None, :])
-        key_parts.append(key_part.astype(jnp.bfloat16))
+        key_parts.append(key_part)
         value_parts.append(value_part)
     key_grad = jnp.concatenate(key_parts, axis=0)
     value_grad = jnp.concatenate(value_parts, axis=0)

time: 243 us -> 243 us (level)
  no operation moved by 1% of the time
where the time goes in v14:
time: 243 us
  waiting for transfers between devices  145 us (60%)
  matrix products  30.6 us (13%)
  other arithmetic  19 us (8%)
  starting transfers between devices  17.9 us (7%)
  between operations  16.5 us (7%)
  Pallas kernels  8.62 us (4%)
  local copies, waits for them, and re-layouts  5.01 us (2%)
    all_gather x1, waiting for transfers between devices, on_device(): lax.all_gather(jnp.concatenate([key_weight[0], value_weight[0]], axis=1),...  67 us
    ppermute x4, waiting for transfers between devices, on_device(): lowers.append(lax.ppermute(held, ('pipe', 'tensor'), shift_pairs))  48.6 us
    ppermute x4, waiting for transfers between devices, on_device(): lax.ppermute(part_low, ('pipe', 'tensor'), pairs).astype(jnp.float32)  29.4 us
    dot_general x4, matrix products, on_device(): lax.dot_general(combined[sl], both_full, (((1,), (1,)), ((), ())), prefer...  17.5 us
    ppermute x4, starting transfers between devices, on_device(): lax.ppermute(part_low, ('pipe', 'tensor'), pairs).astype(jnp.float32)  10.2 us
    pallas_call x1, Pallas kernels, attention_grads(): pl.pallas_call(kernel, grid_spec=pltpu.PrefetchScalarGridSpec(num_scalar_...  8.62 us
    ppermute x4, starting transfers between devices, on_device(): lowers.append(lax.ppermute(held, ('pipe', 'tensor'), shift_pairs))  7.68 us
    dot_general x1, matrix products, on_device(): projected = jnp.dot(normed, both_full, preferred_element_type=jnp.float32)  7.03 us
  transfers between devices with their start and end apart: 10, of which 7 were waited for; matrix products, arithmetic and copies ran while one was open for 14% of the time, Pallas kernels for 0%

profile of v14, /device:TPU:1, one launch (start us, length us, event | category | flops | bytes accessed | tf_op | source)
XLA Modules:
  0.0 242.6 jit_solution(10432164014853796861)
XLA Ops:
  12.8 3.2 %fusion = f32[256]{0:T(256)S(1)} fusion(bf16[1,256,8192]{2,1,0:T(8,128)(2,1)} %param.9), kind=kLoop, calls=%fused_computation.7 | loop fusion | flops 6291200 | bytes 4195328 | tf_op jit(solution)/shard_map/reduce_sum | solution.py:159
  17.3 67.0 %all-gather.2.cloned.1.call-done = bf16[8192,512]{1,0:T(8,128)(2,1)} async-done(((bf16[512,512]{1,0:T(8,128)(2,1)}), bf16[8192,512]{1,0:T(8,128)(2,1)}) %all-gather.2.cloned.1.call-update) | async-done | bytes 8388624 | tf_op jit(solution)/shard_map/all_gather | solution.py:147
  84.3 7.0 %fusion.2 = f32[256,512]{1,0:T(8,128)S(1)} fusion(bf16[8192,512]{1,0:T(8,128)(2,1)} %all-gather.2.cloned.1.call-done, f32[8192]{0:T(1024)S(1)} %bitcast.52, bf16[1,256,8192]{2,1,0:T(8,128)(2,1)} %param.9, f32[256]{0:T(256)S(1)} %add_rsqrt_fusion), kind=kOutput, calls=%fused_computation.21 | convolution fusion | flops 2155872256 | bytes 13140992 | tf_op jit(solution)/shard_map/dot_general | solution.py:162
  93.8 8.6 %shard_map.112 = (bf16[256,256]{1,0:T(8,128)(2,1)}, bf16[256,256]{1,0:T(8,128)(2,1)}) custom-call(s32[1]{0:T(128)} %bitcast.48.len_ref, bf16[256,2048]{1,0:T(8,128)(2,1)} %bitcast.62, bf16[256,2048]{1,0:T(8,128)(2,1)} %fusion.1.c_ref, bf16[256,256]{1,0:T(8,128)(2,1)} %fusion.4.k_ref, bf16[256,256]{1,0:T(8,128)(2,1)} %slice.109.v_ref, f32[256,128]{1,0:T(8,128)} %copy-done.1, ...), custom_call_target="tpu_custom_call" | custom-call | tf_op jit(solution)/shard_map/pallas_call | solution.py:119
  104.2 6.2 %convolution_convert_fusion.3 = bf16[64,8192]{1,0:T(8,128)(2,1)S(1)} fusion(bf16[8192,512]{1,0:T(8,128)(2,1)} %all-gather.2.cloned.1.call-done, bf16[256,512]{1,0:T(8,128)(2,1)S(1)} %constant_dynamic-update-slice_fusion), kind=kOutput, calls=%fused_computation.5 | convolution fusion | flops 537395200 | bytes 9502720 | tf_op jit(solution)/shard_map/dot_general | solution.py:232
  110.4 3.3 %collective-permute-start = (bf16[64,8192]{1,0:T(8,128)(2,1)S(1)}, bf16[64,8192]{1,0:T(8,128)(2,1)S(1)}, u32[]{:S(2)}, u32[]{:S(2)}) collective-permute-start(bf16[64,8192]{1,0:T(8,128)(2,1)S(1)} %convolution_convert_fusion.3), channel_id=1, source_target_pairs={{32,33},{33,32},{64,65},{65,64},{96,97},{97,96},{34,35},{35,34},{6... | collective-permute-start | bytes 3145736 | tf_op jit(solution)/shard_map/ppermute | solution.py:249
  113.7 6.1 %convolution_convert_fusion = bf16[8192,512]{1,0:T(8,128)(2,1)} fusion(bf16[256,512]{1,0:T(8,128)(2,1)S(1)} %constant_dynamic-update-slice_fusion, f32[8192]{0:T(1024)S(1)} %bitcast.53, bf16[1,256,8192]{2,1,0:T(8,128)(2,1)S(1)} %copy-done, f32[256]{0:T(256)S(1)} %add_rsqrt_fusion), kind=kOutput, calls=%fused_computation | convolution fusion | flops 2160066560 | bytes 12878848 | tf_op jit(solution)/shard_map/dot_general | solution.py:202
  119.8 3.4 %convert_multiply_fusion = f32[256,8192]{1,0:T(8,128)S(1)} fusion(bf16[1,256,8192]{2,1,0:T(8,128)(2,1)} %param.9, f32[256]{0:T(256)S(1)} %add_rsqrt_fusion), kind=kLoop, calls=%fused_computation.1 | loop fusion | flops 4194304 | bytes 12583936 | tf_op jit(solution)/shard_map/mul | solution.py:160
  123.3 6.2 %convolution_convert_fusion.1 = bf16[80,8192]{1,0:T(8,128)(2,1)S(1)} fusion(bf16[8192,512]{1,0:T(8,128)(2,1)} %all-gather.2.cloned.1.call-done, bf16[256,512]{1,0:T(8,128)(2,1)S(1)} %constant_dynamic-update-slice_fusion), kind=kOutput, calls=%fused_computation.3 | convolution fusion | flops 671744000 | bytes 9781248 | tf_op jit(solution)/shard_map/dot_general | solution.py:232
  130.6 2.2 collective-permute-start.1
  132.9 2.6 %convolution_convert_fusion.2 = bf16[80,8192]{1,0:T(8,128)(2,1)S(1)} fusion(bf16[8192,512]{1,0:T(8,128)(2,1)S(1)} %bitcast.51, bf16[256,512]{1,0:T(8,128)(2,1)S(1)} %constant_dynamic-update-slice_fusion), kind=kOutput, calls=%fused_computation.4 | convolution fusion | flops 671744000 | bytes 9781248 | tf_op jit(solution)/shard_map/dot_general | solution.py:232
  135.6 1.9 collective-permute-start.2
  137.5 11.9 %collective-permute-done.1 = bf16[80,8192]{1,0:T(8,128)(2,1)S(1)} collective-permute-done((bf16[80,8192]{1,0:T(8,128)(2,1)S(1)}, bf16[80,8192]{1,0:T(8,128)(2,1)S(1)}, u32[]{:S(2)}, u32[]{:S(2)}) %collective-permute-start.1) | collective-permute-done | bytes 1310752 | tf_op jit(solution)/shard_map/ppermute | solution.py:249
  150.7 10.5 %collective-permute-done.2 = bf16[64,8192]{1,0:T(8,128)(2,1)S(1)} collective-permute-done((bf16[64,8192]{1,0:T(8,128)(2,1)S(1)}, bf16[64,8192]{1,0:T(8,128)(2,1)S(1)}, u32[]{:S(2)}, u32[]{:S(2)}) %collective-permute-start.2) | collective-permute-done | bytes 1048608 | tf_op jit(solution)/shard_map/ppermute | solution.py:246
  161.2 2.5 %collective-permute-start.3 = (bf16[80,8192]{1,0:T(8,128)(2,1)S(1)}, bf16[80,8192]{1,0:T(8,128)(2,1)S(1)}, u32[]{:S(2)}, u32[]{:S(2)}) collective-permute-start(bf16[80,8192]{1,0:T(8,128)(2,1)S(1)} %convolution_convert_fusion.2), channel_id=1, source_target_pairs={{32,33},{33,32},{64,65},{65,64},{96,97},{97,96},{34,35},{35,34},{6... | collective-permute-start | bytes 3932168 | tf_op jit(solution)/shard_map/ppermute | solution.py:249
  163.7 2.5 %convolution_convert_fusion.4 = bf16[32,8192]{1,0:T(8,128)(2,1)S(1)} fusion(bf16[8192,512]{1,0:T(8,128)(2,1)S(1)} %bitcast.51, bf16[256,512]{1,0:T(8,128)(2,1)S(1)} %constant_dynamic-update-slice_fusion), kind=kOutput, calls=%fused_computation.6 | convolution fusion | flops 268697600 | bytes 8945664 | tf_op jit(solution)/shard_map/dot_general | solution.py:232
  166.2 1.9 collective-permute-start.4
  168.2 11.8 %collective-permute-done.3 = bf16[80,8192]{1,0:T(8,128)(2,1)S(1)} collective-permute-done((bf16[80,8192]{1,0:T(8,128)(2,1)S(1)}, bf16[80,8192]{1,0:T(8,128)(2,1)S(1)}, u32[]{:S(2)}, u32[]{:S(2)}) %collective-permute-start.3) | collective-permute-done | bytes 1310752 | tf_op jit(solution)/shard_map/ppermute | solution.py:249
  181.2 15.4 %collective-permute-done.4 = bf16[80,8192]{1,0:T(8,128)(2,1)S(1)} collective-permute-done((bf16[80,8192]{1,0:T(8,128)(2,1)S(1)}, bf16[80,8192]{1,0:T(8,128)(2,1)S(1)}, u32[]{:S(2)}, u32[]{:S(2)}) %collective-permute-start.4) | collective-permute-done | bytes 1310752 | tf_op jit(solution)/shard_map/ppermute | solution.py:246
  196.6 2.2 collective-permute-start.6
  200.7 5.7 %collective-permute-done.6 = bf16[32,8192]{1,0:T(8,128)(2,1)S(1)} collective-permute-done((bf16[32,8192]{1,0:T(8,128)(2,1)S(1)}, bf16[32,8192]{1,0:T(8,128)(2,1)S(1)}, u32[]{:S(2)}, u32[]{:S(2)}) %collective-permute-start.6) | collective-permute-done | bytes 524320 | tf_op jit(solution)/shard_map/ppermute | solution.py:249
  207.1 1.9 collective-permute-start.7
  209.0 22.7 %collective-permute-done.7 = bf16[32,8192]{1,0:T(8,128)(2,1)S(1)} collective-permute-done((bf16[32,8192]{1,0:T(8,128)(2,1)S(1)}, bf16[32,8192]{1,0:T(8,128)(2,1)S(1)}, u32[]{:S(2)}, u32[]{:S(2)}) %collective-permute-start.7) | collective-permute-done | bytes 524320 | tf_op jit(solution)/shard_map/ppermute | solution.py:253
  231.7 2.2 maximum_bitcast_fusion
  (61 shorter events, 17.2 us)
Async XLA Ops:
  7.2 77.1 %all-gather.2.cloned.1.call-start = ((), (), s32[]{:S(2)}) async-start(), calls=%async_computation.1 | async-start | bytes 8912896 | tf_op jit(solution)/shard_map/all_gather | solution.py:147
  9.1 6.9 %copy-start.3 = (bf16[1,256,2048]{2,1,0:T(8,128)(2,1)S(1)}, bf16[1,256,2048]{2,1,0:T(8,128)(2,1)}, u32[]{:S(2)}) copy-start(bf16[1,256,2048]{2,1,0:T(8,128)(2,1)} %param.14) | copy-start | bytes 3145732
  9.1 224.8 %reduce-scatter.2.cloned.1.call-start = ((), (), s32[]{:S(2)}) async-start(), calls=%async_computation.2 | async-start | bytes 8912896 | tf_op jit(solution)/shard_map/reduce_scatter | solution.py:201
  12.8 80.0 %copy-start.1 = (f32[256,128]{1,0:T(8,128)}, f32[256,128]{1,0:T(8,128)S(1)}, u32[]{:S(2)}) copy-start(f32[256,128]{1,0:T(8,128)S(1)} %get-tuple-element.35.cos_ref) | copy-start | bytes 393220
  12.8 80.1 %copy-start.2 = (f32[256,128]{1,0:T(8,128)}, f32[256,128]{1,0:T(8,128)S(1)}, u32[]{:S(2)}) copy-start(f32[256,128]{1,0:T(8,128)S(1)} %get-tuple-element.36.sin_ref) | copy-start | bytes 393220
  16.0 107.2 %copy-start.4 = (f32[256]{0:T(256)}, f32[256]{0:T(256)S(1)}, u32[]{:S(2)}) copy-start(f32[256]{0:T(256)S(1)} %add_rsqrt_fusion) | copy-start | bytes 3076
  104.2 9.4 %copy-start = (bf16[1,256,8192]{2,1,0:T(8,128)(2,1)S(1)}, bf16[1,256,8192]{2,1,0:T(8,128)(2,1)}, u32[]{:S(2)}) copy-start(bf16[1,256,8192]{2,1,0:T(8,128)(2,1)} %param.9) | copy-start | bytes 12582916
  110.4 19.0 %collective-permute-start = (bf16[64,8192]{1,0:T(8,128)(2,1)S(1)}, bf16[64,8192]{1,0:T(8,128)(2,1)S(1)}, u32[]{:S(2)}, u32[]{:S(2)}) collective-permute-start(bf16[64,8192]{1,0:T(8,128)(2,1)S(1)} %convolution_convert_fusion.3), channel_id=1, source_target_pairs={{32,33},{33,32},{64,65},{65,64},{96,97},{97,96},{34,35},{35,34},{6... | collective-permute-start | bytes 3145736 | tf_op jit(solution)/shard_map/ppermute | solution.py:249
  119.8 13.1 %slice-start = ((s8[8388608]{0:T(1024)(128)(4,1)}), s8[4194304]{0:T(1024)(128)(4,1)S(1)}, s32[]{:S(2)}) async-start(s8[8388608]{0:T(1024)(128)(4,1)} %bitcast.50), calls=%async_computation.3 | async-start | bytes 8388608
  123.3 9.7 %slice-start.1 = ((s8[8388608]{0:T(1024)(128)(4,1)}), s8[4194304]{0:T(1024)(128)(4,1)S(1)}, s32[]{:S(2)}) async-start(s8[8388608]{0:T(1024)(128)(4,1)} %bitcast.50), calls=%async_computation.4 | async-start | bytes 8388608
  129.4 0.7 slice-start.2
  130.1 2.7 %copy-start.5 = (f32[256]{0:T(256)S(1)}, f32[256]{0:T(256)}, u32[]{:S(2)}) copy-start(f32[256]{0:T(256)} %copy-done.4) | copy-start | bytes 3076
  130.6 18.8 %collective-permute-start.1 = (bf16[80,8192]{1,0:T(8,128)(2,1)S(1)}, bf16[80,8192]{1,0:T(8,128)(2,1)S(1)}, u32[]{:S(2)}, u32[]{:S(2)}) collective-permute-start(bf16[80,8192]{1,0:T(8,128)(2,1)S(1)} %convolution_convert_fusion.1), channel_id=1, source_target_pairs={{32,33},{33,32},{64,65},{65,64},{96,97},{97,96},{34,35},{35,34},{6... | collective-permute-start | bytes 3932168 | tf_op jit(solution)/shard_map/ppermute | solution.py:249
  135.6 25.6 %collective-permute-start.2 = (bf16[64,8192]{1,0:T(8,128)(2,1)S(1)}, bf16[64,8192]{1,0:T(8,128)(2,1)S(1)}, u32[]{:S(2)}, u32[]{:S(2)}) collective-permute-start(bf16[64,8192]{1,0:T(8,128)(2,1)S(1)} %multiply_convert_fusion.3), channel_id=1, source_target_pairs={{32,0},{33,1},{65,32},{64,33},{96,64},{97,65},{34,2},{35,3},{67,34... | collective-permute-start | bytes 3145736 | tf_op jit(solution)/shard_map/ppermute | solution.py:246
  161.2 18.7 %collective-permute-start.3 = (bf16[80,8192]{1,0:T(8,128)(2,1)S(1)}, bf16[80,8192]{1,0:T(8,128)(2,1)S(1)}, u32[]{:S(2)}, u32[]{:S(2)}) collective-permute-start(bf16[80,8192]{1,0:T(8,128)(2,1)S(1)} %convolution_convert_fusion.2), channel_id=1, source_target_pairs={{32,33},{33,32},{64,65},{65,64},{96,97},{97,96},{34,35},{35,34},{6... | collective-permute-start | bytes 3932168 | tf_op jit(solution)/shard_map/ppermute | solution.py:249
  166.2 30.3 %collective-permute-start.4 = (bf16[80,8192]{1,0:T(8,128)(2,1)S(1)}, bf16[80,8192]{1,0:T(8,128)(2,1)S(1)}, u32[]{:S(2)}, u32[]{:S(2)}) collective-permute-start(bf16[80,8192]{1,0:T(8,128)(2,1)S(1)} %multiply_convert_fusion.2), channel_id=1, source_target_pairs={{32,0},{33,1},{65,32},{64,33},{96,64},{97,65},{34,2},{35,3},{67,34... | collective-permute-start | bytes 3932168 | tf_op jit(solution)/shard_map/ppermute | solution.py:246
  196.6 9.9 %collective-permute-start.6 = (bf16[32,8192]{1,0:T(8,128)(2,1)S(1)}, bf16[32,8192]{1,0:T(8,128)(2,1)S(1)}, u32[]{:S(2)}, u32[]{:S(2)}) collective-permute-start(bf16[32,8192]{1,0:T(8,128)(2,1)S(1)} %convolution_convert_fusion.4), channel_id=1, source_target_pairs={{32,33},{33,32},{64,65},{65,64},{96,97},{97,96},{34,35},{35,34},{6... | collective-permute-start | bytes 1572872 | tf_op jit(solution)/shard_map/ppermute | solution.py:249
  198.8 32.9 %collective-permute-start.5 = (bf16[80,8192]{1,0:T(8,128)(2,1)S(1)}, bf16[80,8192]{1,0:T(8,128)(2,1)S(1)}, u32[]{:S(2)}, u32[]{:S(2)}) collective-permute-start(bf16[80,8192]{1,0:T(8,128)(2,1)S(1)} %multiply_convert_fusion.1), channel_id=1, source_target_pairs={{32,0},{33,1},{65,32},{64,33},{96,64},{97,65},{34,2},{35,3},{67,34... | collective-permute-start | bytes 3932168 | tf_op jit(solution)/shard_map/ppermute | solution.py:246
  207.1 24.6 %collective-permute-start.7 = (bf16[32,8192]{1,0:T(8,128)(2,1)S(1)}, bf16[32,8192]{1,0:T(8,128)(2,1)S(1)}, u32[]{:S(2)}, u32[]{:S(2)}) collective-permute-start(bf16[32,8192]{1,0:T(8,128)(2,1)S(1)} %multiply_convert_fusion.6), channel_id=1, source_target_pairs={{32,0},{33,1},{65,32},{64,33},{96,64},{97,65},{34,2},{35,3},{67,34... | collective-permute-start | bytes 1572872 | tf_op jit(solution)/shard_map/ppermute | solution.py:253
Sparse Core Ops, SparseCore 0:
  10.1 74.0 all-gather.1
  119.9 83.3 reduce-scatter.1

commit v15 on v14

--- a/solution.py
+++ b/solution.py
@@ -73,7 +73,7 @@
 
 
 def attention_kernel(
-    len_ref, q_ref, c_ref, k_ref, v_ref, cos_ref, sin_ref, kg_ref, vg_ref, *, group, head_dim
+    len_ref, q_ref, c_ref, k_ref, v_ref, cos_ref, sin_ref, out_ref, *, group, head_dim
 ):
     seq_len = k_ref.shape[0]
     scale = 1.0 / math.sqrt(head_dim)
@@ -105,8 +105,12 @@
     lane = lax.broadcasted_iota(jnp.int32, (seq_len, head_dim), 1)
     turned = pltpu.roll(rotated * sin_ref[...], head_dim // 2, 1)
     turned = jnp.where(lane < head_dim // 2, turned, -turned)
-    kg_ref[...] = (rotated * cos_ref[...] + turned).astype(jnp.bfloat16)
-    vg_ref[...] = value_grad.astype(jnp.bfloat16)
+    head = pl.program_id(0)
+    kv_cols = out_ref.shape[1] // 2
+    key_at = pl.multiple_of(head * head_dim, head_dim)
+    value_at = pl.multiple_of(kv_cols + head * head_dim, head_dim)
+    out_ref[:, pl.ds(key_at, head_dim)] = (rotated * cos_ref[...] + turned).astype(jnp.bfloat16)
+    out_ref[:, pl.ds(value_at, head_dim)] = value_grad.astype(jnp.bfloat16)
 
 def attention_grads(length, queries, cotan, keys, values, cosine, sine, head_dim):
     seq_len, kv_cols = keys.shape
@@ -121,9 +125,8 @@
         grid_spec=pltpu.PrefetchScalarGridSpec(
             num_scalar_prefetch=1, grid=(kv_heads,),
             in_specs=[q_spec, q_spec, kv_spec, kv_spec, rope_spec, rope_spec],
-            out_specs=[kv_spec, kv_spec]),
-        out_shape=[jax.ShapeDtypeStruct((seq_len, kv_cols), jnp.bfloat16),
-                   jax.ShapeDtypeStruct((seq_len, kv_cols), jnp.bfloat16)],
+            out_specs=pl.BlockSpec((seq_len, 2 * kv_cols), lambda k, n: (0, 0))),
+        out_shape=jax.ShapeDtypeStruct((seq_len, 2 * kv_cols), jnp.bfloat16),
     )(length, queries, cotan, keys, values, cosine, sine)
 
 
@@ -176,10 +179,10 @@
         * factor[:, :, None, None]
     ).astype(jnp.bfloat16)
 
-    key_parts, value_parts = [], []
+    key_parts = []
     for n in range(seq_count):
         rows_n = slice(n * seq_len, (n + 1) * seq_len)
-        key_part, value_part = attention_grads(
+        both_part = attention_grads(
             lengths[0][n:n + 1],
             queries[0][rows_n],
             scaled[n].reshape(seq_len, q_local * HD),
@@ -189,13 +192,8 @@
             sine,
             HD,
         )
-        key_parts.append(key_part)
-        value_parts.append(value_part)
-    key_grad = jnp.concatenate(key_parts, axis=0)
-    value_grad = jnp.concatenate(value_parts, axis=0)
-    key_grad = key_grad.reshape(tok_rows, kv_cols)
-    value_grad = value_grad.reshape(tok_rows, kv_cols)
-    combined = jnp.concatenate([key_grad, value_grad], axis=1)
+        key_parts.append(both_part)
+    combined = jnp.concatenate(key_parts, axis=0)
 
     def weight_grads(combined):
         return lax.psum_scatter(

time: 243 us -> 241 us (level)
  no operation moved by 1% of the time
where the time goes in v15:
time: 241 us
  waiting for transfers between devices  145 us (60%)
  matrix products  30.7 us (13%)
  other arithmetic  19 us (8%)
  starting transfers between devices  18 us (7%)
  between operations  16.5 us (7%)
  Pallas kernels  8.53 us (4%)
  local copies, waits for them, and re-layouts  3.17 us (1%)
    all_gather x1, waiting for transfers between devices, on_device(): lax.all_gather(jnp.concatenate([key_weight[0], value_weight[0]], axis=1),...  67 us
    ppermute x4, waiting for transfers between devices, on_device(): lowers.append(lax.ppermute(held, ('pipe', 'tensor'), shift_pairs))  48.6 us
    ppermute x4, waiting for transfers between devices, on_device(): lax.ppermute(part_low, ('pipe', 'tensor'), pairs).astype(jnp.float32)  29.3 us
    dot_general x4, matrix products, on_device(): lax.dot_general(combined[sl], both_full, (((1,), (1,)), ((), ())), prefer...  17.5 us
    ppermute x4, starting transfers between devices, on_device(): lax.ppermute(part_low, ('pipe', 'tensor'), pairs).astype(jnp.float32)  10.2 us
    pallas_call x1, Pallas kernels, attention_grads(): pl.pallas_call(kernel, grid_spec=pltpu.PrefetchScalarGridSpec(num_scalar_...  8.53 us
    ppermute x4, starting transfers between devices, on_device(): lowers.append(lax.ppermute(held, ('pipe', 'tensor'), shift_pairs))  7.68 us
    dot_general x1, matrix products, on_device(): projected = jnp.dot(normed, both_full, preferred_element_type=jnp.float32)  7.03 us
  transfers between devices with their start and end apart: 10, of which 7 were waited for; matrix products, arithmetic and copies ran while one was open for 14% of the time, Pallas kernels for 0%

profile of v15, /device:TPU:1, one launch (start us, length us, event | category | flops | bytes accessed | tf_op | source)
XLA Modules:
  0.0 240.8 jit_solution(5573717743616881644)
XLA Ops:
  12.8 3.2 %fusion = f32[256]{0:T(256)S(1)} fusion(bf16[1,256,8192]{2,1,0:T(8,128)(2,1)} %param.9), kind=kLoop, calls=%fused_computation.7 | loop fusion | flops 6291200 | bytes 4195328 | tf_op jit(solution)/shard_map/reduce_sum | solution.py:162
  17.3 67.0 %all-gather.2.cloned.1.call-done = bf16[8192,512]{1,0:T(8,128)(2,1)} async-done(((bf16[512,512]{1,0:T(8,128)(2,1)}), bf16[8192,512]{1,0:T(8,128)(2,1)}) %all-gather.2.cloned.1.call-update) | async-done | bytes 8388624 | tf_op jit(solution)/shard_map/all_gather | solution.py:150
  84.3 7.0 %fusion.2 = f32[256,512]{1,0:T(8,128)S(1)} fusion(bf16[8192,512]{1,0:T(8,128)(2,1)} %all-gather.2.cloned.1.call-done, f32[8192]{0:T(1024)S(1)} %bitcast.52, bf16[1,256,8192]{2,1,0:T(8,128)(2,1)} %param.9, f32[256]{0:T(256)S(1)} %add_rsqrt_fusion), kind=kOutput, calls=%fused_computation.21 | convolution fusion | flops 2155872256 | bytes 13140992 | tf_op jit(solution)/shard_map/dot_general | solution.py:165
  93.8 8.5 %shard_map.112 = bf16[256,512]{1,0:T(8,128)(2,1)} custom-call(s32[1]{0:T(128)} %bitcast.48.len_ref, bf16[256,2048]{1,0:T(8,128)(2,1)} %bitcast.62, bf16[256,2048]{1,0:T(8,128)(2,1)} %fusion.1.c_ref, bf16[256,256]{1,0:T(8,128)(2,1)} %fusion.4.k_ref, bf16[256,256]{1,0:T(8,128)(2,1)} %slice.109.v_ref, f32[256,128]{1,0:T(8,128)} %copy-done.2, f32[256,128]{1,0:T(8,128)} %copy-done.3), custom_call_target="tpu_custom_call" | custom-call | tf_op jit(solution)/shard_map/pallas_call | solution.py:123
  102.3 6.2 %convolution_convert_fusion.3 = bf16[64,8192]{1,0:T(8,128)(2,1)S(1)} fusion(bf16[8192,512]{1,0:T(8,128)(2,1)} %all-gather.2.cloned.1.call-done, bf16[256,512]{1,0:T(8,128)(2,1)} %shard_map.112), kind=kOutput, calls=%fused_computation.5 | convolution fusion | flops 537395200 | bytes 9502720 | tf_op jit(solution)/shard_map/dot_general | solution.py:230
  108.5 3.3 %collective-permute-start = (bf16[64,8192]{1,0:T(8,128)(2,1)S(1)}, bf16[64,8192]{1,0:T(8,128)(2,1)S(1)}, u32[]{:S(2)}, u32[]{:S(2)}) collective-permute-start(bf16[64,8192]{1,0:T(8,128)(2,1)S(1)} %convolution_convert_fusion.3), channel_id=1, source_target_pairs={{32,33},{33,32},{64,65},{65,64},{96,97},{97,96},{34,35},{35,34},{6... | collective-permute-start | bytes 3145736 | tf_op jit(solution)/shard_map/ppermute | solution.py:247
  111.8 6.1 %convolution_convert_fusion = bf16[8192,512]{1,0:T(8,128)(2,1)} fusion(bf16[256,512]{1,0:T(8,128)(2,1)S(1)} %copy-done.1, f32[8192]{0:T(1024)S(1)} %bitcast.53, bf16[1,256,8192]{2,1,0:T(8,128)(2,1)S(1)} %copy-done, f32[256]{0:T(256)S(1)} %add_rsqrt_fusion), kind=kOutput, calls=%fused_computation | convolution fusion | flops 2160066560 | bytes 12878848 | tf_op jit(solution)/shard_map/dot_general | solution.py:200
  118.0 3.4 %convert_multiply_fusion = f32[256,8192]{1,0:T(8,128)S(1)} fusion(bf16[1,256,8192]{2,1,0:T(8,128)(2,1)} %param.9, f32[256]{0:T(256)S(1)} %add_rsqrt_fusion), kind=kLoop, calls=%fused_computation.1 | loop fusion | flops 4194304 | bytes 12583936 | tf_op jit(solution)/shard_map/mul | solution.py:163
  121.4 6.2 %convolution_convert_fusion.1 = bf16[80,8192]{1,0:T(8,128)(2,1)S(1)} fusion(bf16[8192,512]{1,0:T(8,128)(2,1)} %all-gather.2.cloned.1.call-done, bf16[256,512]{1,0:T(8,128)(2,1)S(1)} %copy-done.1), kind=kOutput, calls=%fused_computation.3 | convolution fusion | flops 671744000 | bytes 9781248 | tf_op jit(solution)/shard_map/dot_general | solution.py:230
  128.8 2.2 collective-permute-start.1
  131.0 2.6 %convolution_convert_fusion.2 = bf16[80,8192]{1,0:T(8,128)(2,1)S(1)} fusion(bf16[8192,512]{1,0:T(8,128)(2,1)S(1)} %bitcast.51, bf16[256,512]{1,0:T(8,128)(2,1)S(1)} %copy-done.1), kind=kOutput, calls=%fused_computation.4 | convolution fusion | flops 671744000 | bytes 9781248 | tf_op jit(solution)/shard_map/dot_general | solution.py:230
  133.7 1.9 collective-permute-start.2
  135.6 11.9 %collective-permute-done.1 = bf16[80,8192]{1,0:T(8,128)(2,1)S(1)} collective-permute-done((bf16[80,8192]{1,0:T(8,128)(2,1)S(1)}, bf16[80,8192]{1,0:T(8,128)(2,1)S(1)}, u32[]{:S(2)}, u32[]{:S(2)}) %collective-permute-start.1) | collective-permute-done | bytes 1310752 | tf_op jit(solution)/shard_map/ppermute | solution.py:247
  148.8 10.5 %collective-permute-done.2 = bf16[64,8192]{1,0:T(8,128)(2,1)S(1)} collective-permute-done((bf16[64,8192]{1,0:T(8,128)(2,1)S(1)}, bf16[64,8192]{1,0:T(8,128)(2,1)S(1)}, u32[]{:S(2)}, u32[]{:S(2)}) %collective-permute-start.2) | collective-permute-done | bytes 1048608 | tf_op jit(solution)/shard_map/ppermute | solution.py:244
  159.2 2.6 %collective-permute-start.3 = (bf16[80,8192]{1,0:T(8,128)(2,1)S(1)}, bf16[80,8192]{1,0:T(8,128)(2,1)S(1)}, u32[]{:S(2)}, u32[]{:S(2)}) collective-permute-start(bf16[80,8192]{1,0:T(8,128)(2,1)S(1)} %convolution_convert_fusion.2), channel_id=1, source_target_pairs={{32,33},{33,32},{64,65},{65,64},{96,97},{97,96},{34,35},{35,34},{6... | collective-permute-start | bytes 3932168 | tf_op jit(solution)/shard_map/ppermute | solution.py:247
  161.8 2.5 %convolution_convert_fusion.4 = bf16[32,8192]{1,0:T(8,128)(2,1)S(1)} fusion(bf16[8192,512]{1,0:T(8,128)(2,1)S(1)} %bitcast.51, bf16[256,512]{1,0:T(8,128)(2,1)S(1)} %copy-done.1), kind=kOutput, calls=%fused_computation.6 | convolution fusion | flops 268697600 | bytes 8945664 | tf_op jit(solution)/shard_map/dot_general | solution.py:230
  164.3 1.9 collective-permute-start.4
  166.3 11.7 %collective-permute-done.3 = bf16[80,8192]{1,0:T(8,128)(2,1)S(1)} collective-permute-done((bf16[80,8192]{1,0:T(8,128)(2,1)S(1)}, bf16[80,8192]{1,0:T(8,128)(2,1)S(1)}, u32[]{:S(2)}, u32[]{:S(2)}) %collective-permute-start.3) | collective-permute-done | bytes 1310752 | tf_op jit(solution)/shard_map/ppermute | solution.py:247
  179.3 15.4 %collective-permute-done.4 = bf16[80,8192]{1,0:T(8,128)(2,1)S(1)} collective-permute-done((bf16[80,8192]{1,0:T(8,128)(2,1)S(1)}, bf16[80,8192]{1,0:T(8,128)(2,1)S(1)}, u32[]{:S(2)}, u32[]{:S(2)}) %collective-permute-start.4) | collective-permute-done | bytes 1310752 | tf_op jit(solution)/shard_map/ppermute | solution.py:244
  194.7 2.2 collective-permute-start.6
  198.9 5.7 %collective-permute-done.6 = bf16[32,8192]{1,0:T(8,128)(2,1)S(1)} collective-permute-done((bf16[32,8192]{1,0:T(8,128)(2,1)S(1)}, bf16[32,8192]{1,0:T(8,128)(2,1)S(1)}, u32[]{:S(2)}, u32[]{:S(2)}) %collective-permute-start.6) | collective-permute-done | bytes 524320 | tf_op jit(solution)/shard_map/ppermute | solution.py:247
  205.2 1.9 collective-permute-start.7
  207.1 22.7 %collective-permute-done.7 = bf16[32,8192]{1,0:T(8,128)(2,1)S(1)} collective-permute-done((bf16[32,8192]{1,0:T(8,128)(2,1)S(1)}, bf16[32,8192]{1,0:T(8,128)(2,1)S(1)}, u32[]{:S(2)}, u32[]{:S(2)}) %collective-permute-start.7) | collective-permute-done | bytes 524320 | tf_op jit(solution)/shard_map/ppermute | solution.py:251
  229.8 2.2 maximum_bitcast_fusion
  (61 shorter events, 15.4 us)
Async XLA Ops:
  7.2 77.1 %all-gather.2.cloned.1.call-start = ((), (), s32[]{:S(2)}) async-start(), calls=%async_computation.1 | async-start | bytes 8912896 | tf_op jit(solution)/shard_map/all_gather | solution.py:150
  9.1 6.9 %copy-start.4 = (bf16[1,256,2048]{2,1,0:T(8,128)(2,1)S(1)}, bf16[1,256,2048]{2,1,0:T(8,128)(2,1)}, u32[]{:S(2)}) copy-start(bf16[1,256,2048]{2,1,0:T(8,128)(2,1)} %param.14) | copy-start | bytes 3145732
  9.1 222.9 %reduce-scatter.2.cloned.1.call-start = ((), (), s32[]{:S(2)}) async-start(), calls=%async_computation.2 | async-start | bytes 8912896 | tf_op jit(solution)/shard_map/reduce_scatter | solution.py:199
  12.8 80.0 %copy-start.2 = (f32[256,128]{1,0:T(8,128)}, f32[256,128]{1,0:T(8,128)S(1)}, u32[]{:S(2)}) copy-start(f32[256,128]{1,0:T(8,128)S(1)} %get-tuple-element.31.cos_ref) | copy-start | bytes 393220
  12.8 80.1 %copy-start.3 = (f32[256,128]{1,0:T(8,128)}, f32[256,128]{1,0:T(8,128)S(1)}, u32[]{:S(2)}) copy-start(f32[256,128]{1,0:T(8,128)S(1)} %get-tuple-element.32.sin_ref) | copy-start | bytes 393220
  16.0 105.3 %copy-start.5 = (f32[256]{0:T(256)}, f32[256]{0:T(256)S(1)}, u32[]{:S(2)}) copy-start(f32[256]{0:T(256)S(1)} %add_rsqrt_fusion) | copy-start | bytes 3076
  102.3 9.5 %copy-start = (bf16[1,256,8192]{2,1,0:T(8,128)(2,1)S(1)}, bf16[1,256,8192]{2,1,0:T(8,128)(2,1)}, u32[]{:S(2)}) copy-start(bf16[1,256,8192]{2,1,0:T(8,128)(2,1)} %param.9) | copy-start | bytes 12582916
  102.3 9.5 %copy-start.1 = (bf16[256,512]{1,0:T(8,128)(2,1)S(1)}, bf16[256,512]{1,0:T(8,128)(2,1)}, u32[]{:S(2)}) copy-start(bf16[256,512]{1,0:T(8,128)(2,1)} %shard_map.112) | copy-start | bytes 786436
  108.5 19.1 %collective-permute-start = (bf16[64,8192]{1,0:T(8,128)(2,1)S(1)}, bf16[64,8192]{1,0:T(8,128)(2,1)S(1)}, u32[]{:S(2)}, u32[]{:S(2)}) collective-permute-start(bf16[64,8192]{1,0:T(8,128)(2,1)S(1)} %convolution_convert_fusion.3), channel_id=1, source_target_pairs={{32,33},{33,32},{64,65},{65,64},{96,97},{97,96},{34,35},{35,34},{6... | collective-permute-start | bytes 3145736 | tf_op jit(solution)/shard_map/ppermute | solution.py:247
  117.9 13.1 %slice-start = ((s8[8388608]{0:T(1024)(128)(4,1)}), s8[4194304]{0:T(1024)(128)(4,1)S(1)}, s32[]{:S(2)}) async-start(s8[8388608]{0:T(1024)(128)(4,1)} %bitcast.50), calls=%async_computation.3 | async-start | bytes 8388608
  121.4 9.7 %slice-start.1 = ((s8[8388608]{0:T(1024)(128)(4,1)}), s8[4194304]{0:T(1024)(128)(4,1)S(1)}, s32[]{:S(2)}) async-start(s8[8388608]{0:T(1024)(128)(4,1)} %bitcast.50), calls=%async_computation.4 | async-start | bytes 8388608
  127.6 0.7 slice-start.2
  128.2 2.7 %copy-start.6 = (f32[256]{0:T(256)S(1)}, f32[256]{0:T(256)}, u32[]{:S(2)}) copy-start(f32[256]{0:T(256)} %copy-done.5) | copy-start | bytes 3076
  128.8 18.8 %collective-permute-start.1 = (bf16[80,8192]{1,0:T(8,128)(2,1)S(1)}, bf16[80,8192]{1,0:T(8,128)(2,1)S(1)}, u32[]{:S(2)}, u32[]{:S(2)}) collective-permute-start(bf16[80,8192]{1,0:T(8,128)(2,1)S(1)} %convolution_convert_fusion.1), channel_id=1, source_target_pairs={{32,33},{33,32},{64,65},{65,64},{96,97},{97,96},{34,35},{35,34},{6... | collective-permute-start | bytes 3932168 | tf_op jit(solution)/shard_map/ppermute | solution.py:247
  133.7 25.6 %collective-permute-start.2 = (bf16[64,8192]{1,0:T(8,128)(2,1)S(1)}, bf16[64,8192]{1,0:T(8,128)(2,1)S(1)}, u32[]{:S(2)}, u32[]{:S(2)}) collective-permute-start(bf16[64,8192]{1,0:T(8,128)(2,1)S(1)} %multiply_convert_fusion.3), channel_id=1, source_target_pairs={{32,0},{33,1},{65,32},{64,33},{96,64},{97,65},{34,2},{35,3},{67,34... | collective-permute-start | bytes 3145736 | tf_op jit(solution)/shard_map/ppermute | solution.py:244
  159.2 18.7 %collective-permute-start.3 = (bf16[80,8192]{1,0:T(8,128)(2,1)S(1)}, bf16[80,8192]{1,0:T(8,128)(2,1)S(1)}, u32[]{:S(2)}, u32[]{:S(2)}) collective-permute-start(bf16[80,8192]{1,0:T(8,128)(2,1)S(1)} %convolution_convert_fusion.2), channel_id=1, source_target_pairs={{32,33},{33,32},{64,65},{65,64},{96,97},{97,96},{34,35},{35,34},{6... | collective-permute-start | bytes 3932168 | tf_op jit(solution)/shard_map/ppermute | solution.py:247
  164.3 30.3 %collective-permute-start.4 = (bf16[80,8192]{1,0:T(8,128)(2,1)S(1)}, bf16[80,8192]{1,0:T(8,128)(2,1)S(1)}, u32[]{:S(2)}, u32[]{:S(2)}) collective-permute-start(bf16[80,8192]{1,0:T(8,128)(2,1)S(1)} %multiply_convert_fusion.2), channel_id=1, source_target_pairs={{32,0},{33,1},{65,32},{64,33},{96,64},{97,65},{34,2},{35,3},{67,34... | collective-permute-start | bytes 3932168 | tf_op jit(solution)/shard_map/ppermute | solution.py:244
  194.7 9.9 %collective-permute-start.6 = (bf16[32,8192]{1,0:T(8,128)(2,1)S(1)}, bf16[32,8192]{1,0:T(8,128)(2,1)S(1)}, u32[]{:S(2)}, u32[]{:S(2)}) collective-permute-start(bf16[32,8192]{1,0:T(8,128)(2,1)S(1)} %convolution_convert_fusion.4), channel_id=1, source_target_pairs={{32,33},{33,32},{64,65},{65,64},{96,97},{97,96},{34,35},{35,34},{6... | collective-permute-start | bytes 1572872 | tf_op jit(solution)/shard_map/ppermute | solution.py:247
  196.9 32.9 %collective-permute-start.5 = (bf16[80,8192]{1,0:T(8,128)(2,1)S(1)}, bf16[80,8192]{1,0:T(8,128)(2,1)S(1)}, u32[]{:S(2)}, u32[]{:S(2)}) collective-permute-start(bf16[80,8192]{1,0:T(8,128)(2,1)S(1)} %multiply_convert_fusion.1), channel_id=1, source_target_pairs={{32,0},{33,1},{65,32},{64,33},{96,64},{97,65},{34,2},{35,3},{67,34... | collective-permute-start | bytes 3932168 | tf_op jit(solution)/shard_map/ppermute | solution.py:244
  205.2 24.6 %collective-permute-start.7 = (bf16[32,8192]{1,0:T(8,128)(2,1)S(1)}, bf16[32,8192]{1,0:T(8,128)(2,1)S(1)}, u32[]{:S(2)}, u32[]{:S(2)}) collective-permute-start(bf16[32,8192]{1,0:T(8,128)(2,1)S(1)} %multiply_convert_fusion.6), channel_id=1, source_target_pairs={{32,0},{33,1},{65,32},{64,33},{96,64},{97,65},{34,2},{35,3},{67,34... | collective-permute-start | bytes 1572872 | tf_op jit(solution)/shard_map/ppermute | solution.py:251
Sparse Core Ops, SparseCore 0:
  10.1 74.0 all-gather.1
  118.1 83.2 reduce-scatter.1

commit v16 on v15

--- a/solution.py
+++ b/solution.py
@@ -78,8 +78,12 @@
     seq_len = k_ref.shape[0]
     scale = 1.0 / math.sqrt(head_dim)
     length = len_ref[0]
-    keys = k_ref[...]
-    values = v_ref[...]
+    lane = lax.broadcasted_iota(jnp.int32, (seq_len, head_dim), 1)
+    key_raw = k_ref[...]
+    half_turn = pltpu.roll(key_raw, head_dim // 2, 1)
+    half_turn = jnp.where(lane < head_dim // 2, -half_turn, half_turn)
+    keys = (key_raw * cos_ref[...] + half_turn * sin_ref[...]).astype(jnp.bfloat16)
+    values = v_ref[...].astype(jnp.bfloat16)
     row = lax.broadcasted_iota(jnp.int32, (seq_len, seq_len), 0)
     col = lax.broadcasted_iota(jnp.int32, (seq_len, seq_len), 1)
     allowed = (col <= row) & (col < length)
@@ -112,22 +116,23 @@
     out_ref[:, pl.ds(key_at, head_dim)] = (rotated * cos_ref[...] + turned).astype(jnp.bfloat16)
     out_ref[:, pl.ds(value_at, head_dim)] = value_grad.astype(jnp.bfloat16)
 
-def attention_grads(length, queries, cotan, keys, values, cosine, sine, head_dim):
-    seq_len, kv_cols = keys.shape
+def attention_grads(length, queries, cotan, projected, cosine, sine, head_dim):
+    seq_len, kv_cols = projected.shape[0], projected.shape[1] // 2
     kv_heads = kv_cols // head_dim
     group = queries.shape[1] // kv_cols
     kernel = functools.partial(attention_kernel, group=group, head_dim=head_dim)
     q_spec = pl.BlockSpec((seq_len, group * head_dim), lambda k, n: (0, k))
-    kv_spec = pl.BlockSpec((seq_len, head_dim), lambda k, n: (0, k))
+    key_spec = pl.BlockSpec((seq_len, head_dim), lambda k, n: (0, k))
+    value_spec = pl.BlockSpec((seq_len, head_dim), lambda k, n: (0, k + kv_heads))
     rope_spec = pl.BlockSpec((seq_len, head_dim), lambda k, n: (0, 0))
     return pl.pallas_call(
         kernel,
         grid_spec=pltpu.PrefetchScalarGridSpec(
             num_scalar_prefetch=1, grid=(kv_heads,),
-            in_specs=[q_spec, q_spec, kv_spec, kv_spec, rope_spec, rope_spec],
+            in_specs=[q_spec, q_spec, key_spec, value_spec, rope_spec, rope_spec],
             out_specs=pl.BlockSpec((seq_len, 2 * kv_cols), lambda k, n: (0, 0))),
         out_shape=jax.ShapeDtypeStruct((seq_len, 2 * kv_cols), jnp.bfloat16),
-    )(length, queries, cotan, keys, values, cosine, sine)
+    )(length, queries, cotan, projected, projected, cosine, sine)
 
 
 def norm_backward(normed_grad, gain_f, nhat, inv_rms):
@@ -186,8 +191,7 @@
             lengths[0][n:n + 1],
             queries[0][rows_n],
             scaled[n].reshape(seq_len, q_local * HD),
-            keys[n].reshape(seq_len, kv_cols),
-            values[rows_n],
+            projected[rows_n],
             cosine,
             sine,
             HD,

time: 241 us -> 240 us (level)
  no operation moved by 1% of the time
where the time goes in v16:
time: 240 us; the launch traced here: 239 us
  waiting for transfers between devices  145 us (60%)
  matrix products  31.5 us (13%)
  other arithmetic  18.2 us (8%)
  starting transfers between devices  17.9 us (7%)
  between operations  16.4 us (7%)
  Pallas kernels  8.83 us (4%)
    all_gather x1, waiting for transfers between devices, on_device(): lax.all_gather(jnp.concatenate([key_weight[0], value_weight[0]], axis=1),...  66.4 us
    ppermute x4, waiting for transfers between devices, on_device(): lowers.append(lax.ppermute(held, ('pipe', 'tensor'), shift_pairs))  48.6 us
    ppermute x4, waiting for transfers between devices, on_device(): lax.ppermute(part_low, ('pipe', 'tensor'), pairs).astype(jnp.float32)  29.4 us
    dot_general x4, matrix products, on_device(): lax.dot_general(combined[sl], both_full, (((1,), (1,)), ((), ())), prefer...  17.5 us
    ppermute x4, starting transfers between devices, on_device(): lax.ppermute(part_low, ('pipe', 'tensor'), pairs).astype(jnp.float32)  10.1 us
    pallas_call x1, Pallas kernels, attention_grads(): pl.pallas_call(kernel, grid_spec=pltpu.PrefetchScalarGridSpec(num_scalar_...  8.83 us
    dot_general x1, matrix products, on_device(): projected = jnp.dot(normed, both_full, preferred_element_type=jnp.float32)  7.86 us
    ppermute x4, starting transfers between devices, on_device(): lowers.append(lax.ppermute(held, ('pipe', 'tensor'), shift_pairs))  7.68 us
  transfers between devices with their start and end apart: 10, of which 7 were waited for; matrix products, arithmetic and copies ran while one was open for 14% of the time, Pallas kernels for 0%

profile of v16, /device:TPU:1, one launch (start us, length us, event | category | flops | bytes accessed | tf_op | source)
XLA Modules:
  0.0 239.4 jit_solution(3555400885291861064)
XLA Ops:
  13.5 3.1 %fusion = f32[256]{0:T(256)S(1)} fusion(bf16[1,256,8192]{2,1,0:T(8,128)(2,1)} %param.9), kind=kLoop, calls=%fused_computation.7 | loop fusion | flops 6291200 | bytes 4195328 | tf_op jit(solution)/shard_map/reduce_sum | solution.py:167
  17.8 66.4 %all-gather.2.cloned.1.call-done = bf16[8192,512]{1,0:T(8,128)(2,1)} async-done(((bf16[512,512]{1,0:T(8,128)(2,1)}), bf16[8192,512]{1,0:T(8,128)(2,1)}) %all-gather.2.cloned.1.call-update) | async-done | bytes 8388624 | tf_op jit(solution)/shard_map/all_gather | solution.py:155
  84.3 7.9 %fusion.2.k_ref.v_ref = f32[256,512]{1,0:T(8,128)} fusion(bf16[8192,512]{1,0:T(8,128)(2,1)} %all-gather.2.cloned.1.call-done, f32[8192]{0:T(1024)S(1)} %bitcast.36, bf16[1,256,8192]{2,1,0:T(8,128)(2,1)} %param.9, f32[256]{0:T(256)S(1)} %add_rsqrt_fusion), kind=kOutput, calls=%fused_computation.21 | convolution fusion | flops 2155872256 | bytes 13140992 | tf_op jit(solution)/shard_map/dot_general | solution.py:170
  92.1 8.8 %shard_map.112 = bf16[256,512]{1,0:T(8,128)(2,1)} custom-call(s32[1]{0:T(128)} %bitcast.32.len_ref, bf16[256,2048]{1,0:T(8,128)(2,1)} %bitcast.46, bf16[256,2048]{1,0:T(8,128)(2,1)} %fusion.1.c_ref, f32[256,512]{1,0:T(8,128)} %fusion.2.k_ref.v_ref, f32[256,512]{1,0:T(8,128)} %fusion.2.k_ref.v_ref, f32[256,128]{1,0:T(8,128)} %get-tuple-element.29.cos_ref, ...), custom_call_target="tpu_custom_call" | custom-call | tf_op jit(solution)/shard_map/pallas_call | solution.py:128
  101.0 6.2 %convolution_convert_fusion.3 = bf16[64,8192]{1,0:T(8,128)(2,1)S(1)} fusion(bf16[8192,512]{1,0:T(8,128)(2,1)} %all-gather.2.cloned.1.call-done, bf16[256,512]{1,0:T(8,128)(2,1)} %shard_map.112), kind=kOutput, calls=%fused_computation.5 | convolution fusion | flops 537395200 | bytes 9502720 | tf_op jit(solution)/shard_map/dot_general | solution.py:234
  107.1 3.3 %collective-permute-start = (bf16[64,8192]{1,0:T(8,128)(2,1)S(1)}, bf16[64,8192]{1,0:T(8,128)(2,1)S(1)}, u32[]{:S(2)}, u32[]{:S(2)}) collective-permute-start(bf16[64,8192]{1,0:T(8,128)(2,1)S(1)} %convolution_convert_fusion.3), channel_id=1, source_target_pairs={{32,33},{33,32},{64,65},{65,64},{96,97},{97,96},{34,35},{35,34},{6... | collective-permute-start | bytes 3145736 | tf_op jit(solution)/shard_map/ppermute | solution.py:251
  110.5 6.1 %convolution_convert_fusion = bf16[8192,512]{1,0:T(8,128)(2,1)} fusion(bf16[256,512]{1,0:T(8,128)(2,1)S(1)} %copy-done.1, f32[8192]{0:T(1024)S(1)} %bitcast.37, bf16[1,256,8192]{2,1,0:T(8,128)(2,1)S(1)} %copy-done, f32[256]{0:T(256)S(1)} %add_rsqrt_fusion), kind=kOutput, calls=%fused_computation | convolution fusion | flops 2160066560 | bytes 12878848 | tf_op jit(solution)/shard_map/dot_general | solution.py:204
  116.6 3.4 %convert_multiply_fusion = f32[256,8192]{1,0:T(8,128)S(1)} fusion(bf16[1,256,8192]{2,1,0:T(8,128)(2,1)} %param.9, f32[256]{0:T(256)S(1)} %add_rsqrt_fusion), kind=kLoop, calls=%fused_computation.1 | loop fusion | flops 4194304 | bytes 12583936 | tf_op jit(solution)/shard_map/mul | solution.py:168
  120.0 6.2 %convolution_convert_fusion.1 = bf16[80,8192]{1,0:T(8,128)(2,1)S(1)} fusion(bf16[8192,512]{1,0:T(8,128)(2,1)} %all-gather.2.cloned.1.call-done, bf16[256,512]{1,0:T(8,128)(2,1)S(1)} %copy-done.1), kind=kOutput, calls=%fused_computation.3 | convolution fusion | flops 671744000 | bytes 9781248 | tf_op jit(solution)/shard_map/dot_general | solution.py:234
  127.3 2.2 collective-permute-start.1
  129.6 2.6 %convolution_convert_fusion.2 = bf16[80,8192]{1,0:T(8,128)(2,1)S(1)} fusion(bf16[8192,512]{1,0:T(8,128)(2,1)S(1)} %bitcast.35, bf16[256,512]{1,0:T(8,128)(2,1)S(1)} %copy-done.1), kind=kOutput, calls=%fused_computation.4 | convolution fusion | flops 671744000 | bytes 9781248 | tf_op jit(solution)/shard_map/dot_general | solution.py:234
  132.3 1.9 collective-permute-start.2
  134.2 11.9 %collective-permute-done.1 = bf16[80,8192]{1,0:T(8,128)(2,1)S(1)} collective-permute-done((bf16[80,8192]{1,0:T(8,128)(2,1)S(1)}, bf16[80,8192]{1,0:T(8,128)(2,1)S(1)}, u32[]{:S(2)}, u32[]{:S(2)}) %collective-permute-start.1) | collective-permute-done | bytes 1310752 | tf_op jit(solution)/shard_map/ppermute | solution.py:251
  147.4 10.6 %collective-permute-done.2 = bf16[64,8192]{1,0:T(8,128)(2,1)S(1)} collective-permute-done((bf16[64,8192]{1,0:T(8,128)(2,1)S(1)}, bf16[64,8192]{1,0:T(8,128)(2,1)S(1)}, u32[]{:S(2)}, u32[]{:S(2)}) %collective-permute-start.2) | collective-permute-done | bytes 1048608 | tf_op jit(solution)/shard_map/ppermute | solution.py:248
  158.0 2.5 %collective-permute-start.3 = (bf16[80,8192]{1,0:T(8,128)(2,1)S(1)}, bf16[80,8192]{1,0:T(8,128)(2,1)S(1)}, u32[]{:S(2)}, u32[]{:S(2)}) collective-permute-start(bf16[80,8192]{1,0:T(8,128)(2,1)S(1)} %convolution_convert_fusion.2), channel_id=1, source_target_pairs={{32,33},{33,32},{64,65},{65,64},{96,97},{97,96},{34,35},{35,34},{6... | collective-permute-start | bytes 3932168 | tf_op jit(solution)/shard_map/ppermute | solution.py:251
  160.4 2.5 %convolution_convert_fusion.4 = bf16[32,8192]{1,0:T(8,128)(2,1)S(1)} fusion(bf16[8192,512]{1,0:T(8,128)(2,1)S(1)} %bitcast.35, bf16[256,512]{1,0:T(8,128)(2,1)S(1)} %copy-done.1), kind=kOutput, calls=%fused_computation.6 | convolution fusion | flops 268697600 | bytes 8945664 | tf_op jit(solution)/shard_map/dot_general | solution.py:234
  163.0 1.9 collective-permute-start.4
  164.9 11.8 %collective-permute-done.3 = bf16[80,8192]{1,0:T(8,128)(2,1)S(1)} collective-permute-done((bf16[80,8192]{1,0:T(8,128)(2,1)S(1)}, bf16[80,8192]{1,0:T(8,128)(2,1)S(1)}, u32[]{:S(2)}, u32[]{:S(2)}) %collective-permute-start.3) | collective-permute-done | bytes 1310752 | tf_op jit(solution)/shard_map/ppermute | solution.py:251
  178.0 15.3 %collective-permute-done.4 = bf16[80,8192]{1,0:T(8,128)(2,1)S(1)} collective-permute-done((bf16[80,8192]{1,0:T(8,128)(2,1)S(1)}, bf16[80,8192]{1,0:T(8,128)(2,1)S(1)}, u32[]{:S(2)}, u32[]{:S(2)}) %collective-permute-start.4) | collective-permute-done | bytes 1310752 | tf_op jit(solution)/shard_map/ppermute | solution.py:248
  193.3 2.2 collective-permute-start.6
  197.5 5.7 %collective-permute-done.6 = bf16[32,8192]{1,0:T(8,128)(2,1)S(1)} collective-permute-done((bf16[32,8192]{1,0:T(8,128)(2,1)S(1)}, bf16[32,8192]{1,0:T(8,128)(2,1)S(1)}, u32[]{:S(2)}, u32[]{:S(2)}) %collective-permute-start.6) | collective-permute-done | bytes 524320 | tf_op jit(solution)/shard_map/ppermute | solution.py:251
  203.8 1.9 collective-permute-start.7
  205.8 22.7 %collective-permute-done.7 = bf16[32,8192]{1,0:T(8,128)(2,1)S(1)} collective-permute-done((bf16[32,8192]{1,0:T(8,128)(2,1)S(1)}, bf16[32,8192]{1,0:T(8,128)(2,1)S(1)}, u32[]{:S(2)}, u32[]{:S(2)}) %collective-permute-start.7) | collective-permute-done | bytes 524320 | tf_op jit(solution)/shard_map/ppermute | solution.py:255
  228.5 2.2 maximum_bitcast_fusion
  (49 shorter events, 13.6 us)
Async XLA Ops:
  7.2 77.1 %all-gather.2.cloned.1.call-start = ((), (), s32[]{:S(2)}) async-start(), calls=%async_computation.1 | async-start | bytes 8912896 | tf_op jit(solution)/shard_map/all_gather | solution.py:155
  9.1 7.5 %copy-start.2 = (bf16[1,256,2048]{2,1,0:T(8,128)(2,1)S(1)}, bf16[1,256,2048]{2,1,0:T(8,128)(2,1)}, u32[]{:S(2)}) copy-start(bf16[1,256,2048]{2,1,0:T(8,128)(2,1)} %param.14) | copy-start | bytes 3145732
  9.1 221.6 %reduce-scatter.2.cloned.1.call-start = ((), (), s32[]{:S(2)}) async-start(), calls=%async_computation.2 | async-start | bytes 8912896 | tf_op jit(solution)/shard_map/reduce_scatter | solution.py:203
  16.6 103.4 %copy-start.3 = (f32[256]{0:T(256)}, f32[256]{0:T(256)S(1)}, u32[]{:S(2)}) copy-start(f32[256]{0:T(256)S(1)} %add_rsqrt_fusion) | copy-start | bytes 3076
  100.9 9.5 %copy-start = (bf16[1,256,8192]{2,1,0:T(8,128)(2,1)S(1)}, bf16[1,256,8192]{2,1,0:T(8,128)(2,1)}, u32[]{:S(2)}) copy-start(bf16[1,256,8192]{2,1,0:T(8,128)(2,1)} %param.9) | copy-start | bytes 12582916
  100.9 9.5 %copy-start.1 = (bf16[256,512]{1,0:T(8,128)(2,1)S(1)}, bf16[256,512]{1,0:T(8,128)(2,1)}, u32[]{:S(2)}) copy-start(bf16[256,512]{1,0:T(8,128)(2,1)} %shard_map.112) | copy-start | bytes 786436
  107.1 19.1 %collective-permute-start = (bf16[64,8192]{1,0:T(8,128)(2,1)S(1)}, bf16[64,8192]{1,0:T(8,128)(2,1)S(1)}, u32[]{:S(2)}, u32[]{:S(2)}) collective-permute-start(bf16[64,8192]{1,0:T(8,128)(2,1)S(1)} %convolution_convert_fusion.3), channel_id=1, source_target_pairs={{32,33},{33,32},{64,65},{65,64},{96,97},{97,96},{34,35},{35,34},{6... | collective-permute-start | bytes 3145736 | tf_op jit(solution)/shard_map/ppermute | solution.py:251
  116.6 13.0 %slice-start = ((s8[8388608]{0:T(1024)(128)(4,1)}), s8[4194304]{0:T(1024)(128)(4,1)S(1)}, s32[]{:S(2)}) async-start(s8[8388608]{0:T(1024)(128)(4,1)} %bitcast.34), calls=%async_computation.3 | async-start | bytes 8388608
  120.0 9.6 %slice-start.1 = ((s8[8388608]{0:T(1024)(128)(4,1)}), s8[4194304]{0:T(1024)(128)(4,1)S(1)}, s32[]{:S(2)}) async-start(s8[8388608]{0:T(1024)(128)(4,1)} %bitcast.34), calls=%async_computation.4 | async-start | bytes 8388608
  126.2 0.6 slice-start.2
  126.8 2.7 %copy-start.4 = (f32[256]{0:T(256)S(1)}, f32[256]{0:T(256)}, u32[]{:S(2)}) copy-start(f32[256]{0:T(256)} %copy-done.3) | copy-start | bytes 3076
  127.3 18.8 %collective-permute-start.1 = (bf16[80,8192]{1,0:T(8,128)(2,1)S(1)}, bf16[80,8192]{1,0:T(8,128)(2,1)S(1)}, u32[]{:S(2)}, u32[]{:S(2)}) collective-permute-start(bf16[80,8192]{1,0:T(8,128)(2,1)S(1)} %convolution_convert_fusion.1), channel_id=1, source_target_pairs={{32,33},{33,32},{64,65},{65,64},{96,97},{97,96},{34,35},{35,34},{6... | collective-permute-start | bytes 3932168 | tf_op jit(solution)/shard_map/ppermute | solution.py:251
  132.3 25.7 %collective-permute-start.2 = (bf16[64,8192]{1,0:T(8,128)(2,1)S(1)}, bf16[64,8192]{1,0:T(8,128)(2,1)S(1)}, u32[]{:S(2)}, u32[]{:S(2)}) collective-permute-start(bf16[64,8192]{1,0:T(8,128)(2,1)S(1)} %multiply_convert_fusion.3), channel_id=1, source_target_pairs={{32,0},{33,1},{65,32},{64,33},{96,64},{97,65},{34,2},{35,3},{67,34... | collective-permute-start | bytes 3145736 | tf_op jit(solution)/shard_map/ppermute | solution.py:248
  158.0 18.7 %collective-permute-start.3 = (bf16[80,8192]{1,0:T(8,128)(2,1)S(1)}, bf16[80,8192]{1,0:T(8,128)(2,1)S(1)}, u32[]{:S(2)}, u32[]{:S(2)}) collective-permute-start(bf16[80,8192]{1,0:T(8,128)(2,1)S(1)} %convolution_convert_fusion.2), channel_id=1, source_target_pairs={{32,33},{33,32},{64,65},{65,64},{96,97},{97,96},{34,35},{35,34},{6... | collective-permute-start | bytes 3932168 | tf_op jit(solution)/shard_map/ppermute | solution.py:251
  163.0 30.3 %collective-permute-start.4 = (bf16[80,8192]{1,0:T(8,128)(2,1)S(1)}, bf16[80,8192]{1,0:T(8,128)(2,1)S(1)}, u32[]{:S(2)}, u32[]{:S(2)}) collective-permute-start(bf16[80,8192]{1,0:T(8,128)(2,1)S(1)} %multiply_convert_fusion.2), channel_id=1, source_target_pairs={{32,0},{33,1},{65,32},{64,33},{96,64},{97,65},{34,2},{35,3},{67,34... | collective-permute-start | bytes 3932168 | tf_op jit(solution)/shard_map/ppermute | solution.py:248
  193.3 9.9 %collective-permute-start.6 = (bf16[32,8192]{1,0:T(8,128)(2,1)S(1)}, bf16[32,8192]{1,0:T(8,128)(2,1)S(1)}, u32[]{:S(2)}, u32[]{:S(2)}) collective-permute-start(bf16[32,8192]{1,0:T(8,128)(2,1)S(1)} %convolution_convert_fusion.4), channel_id=1, source_target_pairs={{32,33},{33,32},{64,65},{65,64},{96,97},{97,96},{34,35},{35,34},{6... | collective-permute-start | bytes 1572872 | tf_op jit(solution)/shard_map/ppermute | solution.py:251
  195.6 32.9 %collective-permute-start.5 = (bf16[80,8192]{1,0:T(8,128)(2,1)S(1)}, bf16[80,8192]{1,0:T(8,128)(2,1)S(1)}, u32[]{:S(2)}, u32[]{:S(2)}) collective-permute-start(bf16[80,8192]{1,0:T(8,128)(2,1)S(1)} %multiply_convert_fusion.1), channel_id=1, source_target_pairs={{32,0},{33,1},{65,32},{64,33},{96,64},{97,65},{34,2},{35,3},{67,34... | collective-permute-start | bytes 3932168 | tf_op jit(solution)/shard_map/ppermute | solution.py:248
  203.8 24.6 %collective-permute-start.7 = (bf16[32,8192]{1,0:T(8,128)(2,1)S(1)}, bf16[32,8192]{1,0:T(8,128)(2,1)S(1)}, u32[]{:S(2)}, u32[]{:S(2)}) collective-permute-start(bf16[32,8192]{1,0:T(8,128)(2,1)S(1)} %multiply_convert_fusion.6), channel_id=1, source_target_pairs={{32,0},{33,1},{65,32},{64,33},{96,64},{97,65},{34,2},{35,3},{67,34... | collective-permute-start | bytes 1572872 | tf_op jit(solution)/shard_map/ppermute | solution.py:255
Sparse Core Ops, SparseCore 0:
  10.1 74.0 all-gather.1
  116.7 83.3 reduce-scatter.1

commit v17 on v16

--- a/solution.py
+++ b/solution.py
@@ -211,7 +211,7 @@
 
     n_pipe = lax.axis_size("pipe")
     n_tensor = lax.axis_size("tensor")
-    sizes = [tok_rows // 4, tok_rows * 5 // 16, tok_rows * 5 // 16, tok_rows // 8]
+    sizes = [tok_rows * 3 // 16, tok_rows * 3 // 8, tok_rows * 5 // 16, tok_rows // 8]
     bounds = [sum(sizes[:c]) for c in range(len(sizes) + 1)]
     chunks = len(sizes)
     exchange_steps = [

time: 240 us -> 240 us (level)
    ppermute x4, waiting for transfers between devices: 29.4 us -> 32.5 us  [on_device(): lax.ppermute(part_low, ('pipe', 'tensor'), pairs).astype(jnp.float32)]
    ppermute x4, waiting for transfers between devices: 48.6 us -> 45.8 us  [on_device(): lowers.append(lax.ppermute(held, ('pipe', 'tensor'), shift_pairs))]
  transfers between devices with their start and end apart: 10 -> 10, of which waited for: 7 -> 6; matrix products, arithmetic and copies ran while one was open for 14% -> 14% of each run, Pallas kernels for 0% -> 0%
where the time goes in v17:
time: 240 us; the launch traced here: 239 us
  waiting for transfers between devices  145 us (60%)
  matrix products  31.4 us (13%)
  other arithmetic  18.2 us (8%)
  starting transfers between devices  17.6 us (7%)
  between operations  16.3 us (7%)
  Pallas kernels  8.82 us (4%)
    all_gather x1, waiting for transfers between devices, on_device(): lax.all_gather(jnp.concatenate([key_weight[0], value_weight[0]], axis=1),...  66.4 us
    ppermute x4, waiting for transfers between devices, on_device(): lowers.append(lax.ppermute(held, ('pipe', 'tensor'), shift_pairs))  45.8 us
    ppermute x4, waiting for transfers between devices, on_device(): lax.ppermute(part_low, ('pipe', 'tensor'), pairs).astype(jnp.float32)  32.5 us
    dot_general x4, matrix products, on_device(): lax.dot_general(combined[sl], both_full, (((1,), (1,)), ((), ())), prefer...  17.4 us
    ppermute x4, starting transfers between devices, on_device(): lax.ppermute(part_low, ('pipe', 'tensor'), pairs).astype(jnp.float32)  9.85 us
    pallas_call x1, Pallas kernels, attention_grads(): pl.pallas_call(kernel, grid_spec=pltpu.PrefetchScalarGridSpec(num_scalar_...  8.82 us
    dot_general x1, matrix products, on_device(): projected = jnp.dot(normed, both_full, preferred_element_type=jnp.float32)  7.88 us
    ppermute x4, starting transfers between devices, on_device(): lowers.append(lax.ppermute(held, ('pipe', 'tensor'), shift_pairs))  7.68 us
  transfers between devices with their start and end apart: 10, of which 6 were waited for; matrix products, arithmetic and copies ran while one was open for 14% of the time, Pallas kernels for 0%

profile of v17, /device:TPU:1, one launch (start us, length us, event | category | flops | bytes accessed | tf_op | source)
XLA Modules:
  0.0 239.3 jit_solution(697583935425678909)
XLA Ops:
  7.2 2.0 pad_maximum_fusion
  13.5 3.1 %fusion = f32[256]{0:T(256)S(1)} fusion(bf16[1,256,8192]{2,1,0:T(8,128)(2,1)} %param.9), kind=kLoop, calls=%fused_computation.7 | loop fusion | flops 6291200 | bytes 4195328 | tf_op jit(solution)/shard_map/reduce_sum | solution.py:167
  17.9 66.4 %all-gather.2.cloned.1.call-done = bf16[8192,512]{1,0:T(8,128)(2,1)} async-done(((bf16[512,512]{1,0:T(8,128)(2,1)}), bf16[8192,512]{1,0:T(8,128)(2,1)}) %all-gather.2.cloned.1.call-update) | async-done | bytes 8388624 | tf_op jit(solution)/shard_map/all_gather | solution.py:155
  84.3 7.9 %fusion.2.k_ref.v_ref = f32[256,512]{1,0:T(8,128)} fusion(bf16[8192,512]{1,0:T(8,128)(2,1)} %all-gather.2.cloned.1.call-done, f32[8192]{0:T(1024)S(1)} %bitcast.36, bf16[1,256,8192]{2,1,0:T(8,128)(2,1)} %param.9, f32[256]{0:T(256)S(1)} %add_rsqrt_fusion), kind=kOutput, calls=%fused_computation.18 | convolution fusion | flops 2155872256 | bytes 13140992 | tf_op jit(solution)/shard_map/dot_general | solution.py:170
  92.1 8.8 %shard_map.112 = bf16[256,512]{1,0:T(8,128)(2,1)} custom-call(s32[1]{0:T(128)} %bitcast.32.len_ref, bf16[256,2048]{1,0:T(8,128)(2,1)} %bitcast.46, bf16[256,2048]{1,0:T(8,128)(2,1)} %fusion.1.c_ref, f32[256,512]{1,0:T(8,128)} %fusion.2.k_ref.v_ref, f32[256,512]{1,0:T(8,128)} %fusion.2.k_ref.v_ref, f32[256,128]{1,0:T(8,128)} %get-tuple-element.27.cos_ref, ...), custom_call_target="tpu_custom_call" | custom-call | tf_op jit(solution)/shard_map/pallas_call | solution.py:128
  101.0 6.1 %convolution_convert_fusion.3 = bf16[48,8192]{1,0:T(8,128)(2,1)S(1)} fusion(bf16[8192,512]{1,0:T(8,128)(2,1)} %all-gather.2.cloned.1.call-done, bf16[256,512]{1,0:T(8,128)(2,1)} %shard_map.112), kind=kOutput, calls=%fused_computation.5 | convolution fusion | flops 403046400 | bytes 9224192 | tf_op jit(solution)/shard_map/dot_general | solution.py:234
  107.1 3.3 %collective-permute-start = (bf16[48,8192]{1,0:T(8,128)(2,1)S(1)}, bf16[48,8192]{1,0:T(8,128)(2,1)S(1)}, u32[]{:S(2)}, u32[]{:S(2)}) collective-permute-start(bf16[48,8192]{1,0:T(8,128)(2,1)S(1)} %convolution_convert_fusion.3), channel_id=1, source_target_pairs={{32,33},{33,32},{64,65},{65,64},{96,97},{97,96},{34,35},{35,34},{6... | collective-permute-start | bytes 2359304 | tf_op jit(solution)/shard_map/ppermute | solution.py:251
  110.4 6.1 %convolution_convert_fusion = bf16[8192,512]{1,0:T(8,128)(2,1)} fusion(bf16[256,512]{1,0:T(8,128)(2,1)S(1)} %copy-done.1, f32[8192]{0:T(1024)S(1)} %bitcast.37, bf16[1,256,8192]{2,1,0:T(8,128)(2,1)S(1)} %copy-done, f32[256]{0:T(256)S(1)} %add_rsqrt_fusion), kind=kOutput, calls=%fused_computation | convolution fusion | flops 2160066560 | bytes 12878848 | tf_op jit(solution)/shard_map/dot_general | solution.py:204
  116.5 3.3 %convert_multiply_fusion = f32[256,8192]{1,0:T(8,128)S(1)} fusion(bf16[1,256,8192]{2,1,0:T(8,128)(2,1)} %param.9, f32[256]{0:T(256)S(1)} %add_rsqrt_fusion), kind=kLoop, calls=%fused_computation.1 | loop fusion | flops 4194304 | bytes 12583936 | tf_op jit(solution)/shard_map/mul | solution.py:168
  119.8 6.2 %convolution_convert_fusion.1 = bf16[96,8192]{1,0:T(8,128)(2,1)S(1)} fusion(bf16[8192,512]{1,0:T(8,128)(2,1)} %all-gather.2.cloned.1.call-done, bf16[256,512]{1,0:T(8,128)(2,1)S(1)} %copy-done.1), kind=kOutput, calls=%fused_computation.3 | convolution fusion | flops 806092800 | bytes 10059776 | tf_op jit(solution)/shard_map/dot_general | solution.py:234
  127.0 2.2 collective-permute-start.1
  129.3 2.6 %convolution_convert_fusion.2 = bf16[80,8192]{1,0:T(8,128)(2,1)S(1)} fusion(bf16[8192,512]{1,0:T(8,128)(2,1)S(1)} %bitcast.35, bf16[256,512]{1,0:T(8,128)(2,1)S(1)} %copy-done.1), kind=kOutput, calls=%fused_computation.4 | convolution fusion | flops 671744000 | bytes 9781248 | tf_op jit(solution)/shard_map/dot_general | solution.py:234
  131.9 1.9 collective-permute-start.2
  133.9 14.7 %collective-permute-done.1 = bf16[96,8192]{1,0:T(8,128)(2,1)S(1)} collective-permute-done((bf16[96,8192]{1,0:T(8,128)(2,1)S(1)}, bf16[96,8192]{1,0:T(8,128)(2,1)S(1)}, u32[]{:S(2)}, u32[]{:S(2)}) %collective-permute-start.1) | collective-permute-done | bytes 1572896 | tf_op jit(solution)/shard_map/ppermute | solution.py:251
  150.1 2.2 collective-permute-start.3
  152.4 2.5 %convolution_convert_fusion.4 = bf16[32,8192]{1,0:T(8,128)(2,1)S(1)} fusion(bf16[8192,512]{1,0:T(8,128)(2,1)S(1)} %bitcast.35, bf16[256,512]{1,0:T(8,128)(2,1)S(1)} %copy-done.1), kind=kOutput, calls=%fused_computation.6 | convolution fusion | flops 268697600 | bytes 8945664 | tf_op jit(solution)/shard_map/dot_general | solution.py:234
  154.9 1.9 collective-permute-start.4
  156.8 12.0 %collective-permute-done.3 = bf16[80,8192]{1,0:T(8,128)(2,1)S(1)} collective-permute-done((bf16[80,8192]{1,0:T(8,128)(2,1)S(1)}, bf16[80,8192]{1,0:T(8,128)(2,1)S(1)}, u32[]{:S(2)}, u32[]{:S(2)}) %collective-permute-start.3) | collective-permute-done | bytes 1310752 | tf_op jit(solution)/shard_map/ppermute | solution.py:251
  170.2 26.3 %collective-permute-done.4 = bf16[96,8192]{1,0:T(8,128)(2,1)S(1)} collective-permute-done((bf16[96,8192]{1,0:T(8,128)(2,1)S(1)}, bf16[96,8192]{1,0:T(8,128)(2,1)S(1)}, u32[]{:S(2)}, u32[]{:S(2)}) %collective-permute-start.4) | collective-permute-done | bytes 1572896 | tf_op jit(solution)/shard_map/ppermute | solution.py:248
  196.5 2.2 collective-permute-start.6
  200.7 5.7 %collective-permute-done.6 = bf16[32,8192]{1,0:T(8,128)(2,1)S(1)} collective-permute-done((bf16[32,8192]{1,0:T(8,128)(2,1)S(1)}, bf16[32,8192]{1,0:T(8,128)(2,1)S(1)}, u32[]{:S(2)}, u32[]{:S(2)}) %collective-permute-start.6) | collective-permute-done | bytes 524320 | tf_op jit(solution)/shard_map/ppermute | solution.py:251
  207.0 1.9 collective-permute-start.7
  209.0 19.4 %collective-permute-done.7 = bf16[32,8192]{1,0:T(8,128)(2,1)S(1)} collective-permute-done((bf16[32,8192]{1,0:T(8,128)(2,1)S(1)}, bf16[32,8192]{1,0:T(8,128)(2,1)S(1)}, u32[]{:S(2)}, u32[]{:S(2)}) %collective-permute-start.7) | collective-permute-done | bytes 524320 | tf_op jit(solution)/shard_map/ppermute | solution.py:255
  228.4 2.2 maximum_bitcast_fusion
  (50 shorter events, 11.9 us)
Async XLA Ops:
  7.2 77.1 %all-gather.2.cloned.1.call-start = ((), (), s32[]{:S(2)}) async-start(), calls=%async_computation.1 | async-start | bytes 8912896 | tf_op jit(solution)/shard_map/all_gather | solution.py:155
  7.2 9.4 %copy-start.2 = (bf16[1,256,2048]{2,1,0:T(8,128)(2,1)S(1)}, bf16[1,256,2048]{2,1,0:T(8,128)(2,1)}, u32[]{:S(2)}) copy-start(bf16[1,256,2048]{2,1,0:T(8,128)(2,1)} %param.14) | copy-start | bytes 3145732
  9.2 221.4 %reduce-scatter.2.cloned.1.call-start = ((), (), s32[]{:S(2)}) async-start(), calls=%async_computation.2 | async-start | bytes 8912896 | tf_op jit(solution)/shard_map/reduce_scatter | solution.py:203
  16.6 103.2 %copy-start.3 = (f32[256]{0:T(256)}, f32[256]{0:T(256)S(1)}, u32[]{:S(2)}) copy-start(f32[256]{0:T(256)S(1)} %add_rsqrt_fusion) | copy-start | bytes 3076
  101.0 9.4 %copy-start = (bf16[1,256,8192]{2,1,0:T(8,128)(2,1)S(1)}, bf16[1,256,8192]{2,1,0:T(8,128)(2,1)}, u32[]{:S(2)}) copy-start(bf16[1,256,8192]{2,1,0:T(8,128)(2,1)} %param.9) | copy-start | bytes 12582916
  101.0 9.4 %copy-start.1 = (bf16[256,512]{1,0:T(8,128)(2,1)S(1)}, bf16[256,512]{1,0:T(8,128)(2,1)}, u32[]{:S(2)}) copy-start(bf16[256,512]{1,0:T(8,128)(2,1)} %shard_map.112) | copy-start | bytes 786436
  107.1 18.9 %collective-permute-start = (bf16[48,8192]{1,0:T(8,128)(2,1)S(1)}, bf16[48,8192]{1,0:T(8,128)(2,1)S(1)}, u32[]{:S(2)}, u32[]{:S(2)}) collective-permute-start(bf16[48,8192]{1,0:T(8,128)(2,1)S(1)} %convolution_convert_fusion.3), channel_id=1, source_target_pairs={{32,33},{33,32},{64,65},{65,64},{96,97},{97,96},{34,35},{35,34},{6... | collective-permute-start | bytes 2359304 | tf_op jit(solution)/shard_map/ppermute | solution.py:251
  119.8 9.5 %slice-start = ((s8[8388608]{0:T(1024)(128)(4,1)}), s8[4194304]{0:T(1024)(128)(4,1)S(1)}, s32[]{:S(2)}) async-start(s8[8388608]{0:T(1024)(128)(4,1)} %bitcast.34), calls=%async_computation.3 | async-start | bytes 8388608
  119.8 9.5 %slice-start.1 = ((s8[8388608]{0:T(1024)(128)(4,1)}), s8[4194304]{0:T(1024)(128)(4,1)S(1)}, s32[]{:S(2)}) async-start(s8[8388608]{0:T(1024)(128)(4,1)} %bitcast.34), calls=%async_computation.4 | async-start | bytes 8388608
  126.0 0.6 slice-start.2
  126.0 3.2 %copy-start.4 = (f32[256]{0:T(256)S(1)}, f32[256]{0:T(256)}, u32[]{:S(2)}) copy-start(f32[256]{0:T(256)} %copy-done.3) | copy-start | bytes 3076
  127.0 21.6 %collective-permute-start.1 = (bf16[96,8192]{1,0:T(8,128)(2,1)S(1)}, bf16[96,8192]{1,0:T(8,128)(2,1)S(1)}, u32[]{:S(2)}, u32[]{:S(2)}) collective-permute-start(bf16[96,8192]{1,0:T(8,128)(2,1)S(1)} %convolution_convert_fusion.1), channel_id=1, source_target_pairs={{32,33},{33,32},{64,65},{65,64},{96,97},{97,96},{34,35},{35,34},{6... | collective-permute-start | bytes 4718600 | tf_op jit(solution)/shard_map/ppermute | solution.py:251
  131.9 18.2 %collective-permute-start.2 = (bf16[48,8192]{1,0:T(8,128)(2,1)S(1)}, bf16[48,8192]{1,0:T(8,128)(2,1)S(1)}, u32[]{:S(2)}, u32[]{:S(2)}) collective-permute-start(bf16[48,8192]{1,0:T(8,128)(2,1)S(1)} %multiply_convert_fusion.5), channel_id=1, source_target_pairs={{32,0},{33,1},{65,32},{64,33},{96,64},{97,65},{34,2},{35,3},{67,34... | collective-permute-start | bytes 2359304 | tf_op jit(solution)/shard_map/ppermute | solution.py:248
  150.1 18.8 %collective-permute-start.3 = (bf16[80,8192]{1,0:T(8,128)(2,1)S(1)}, bf16[80,8192]{1,0:T(8,128)(2,1)S(1)}, u32[]{:S(2)}, u32[]{:S(2)}) collective-permute-start(bf16[80,8192]{1,0:T(8,128)(2,1)S(1)} %convolution_convert_fusion.2), channel_id=1, source_target_pairs={{32,33},{33,32},{64,65},{65,64},{96,97},{97,96},{34,35},{35,34},{6... | collective-permute-start | bytes 3932168 | tf_op jit(solution)/shard_map/ppermute | solution.py:251
  154.9 41.6 %collective-permute-start.4 = (bf16[96,8192]{1,0:T(8,128)(2,1)S(1)}, bf16[96,8192]{1,0:T(8,128)(2,1)S(1)}, u32[]{:S(2)}, u32[]{:S(2)}) collective-permute-start(bf16[96,8192]{1,0:T(8,128)(2,1)S(1)} %multiply_convert_fusion.1), channel_id=1, source_target_pairs={{32,0},{33,1},{65,32},{64,33},{96,64},{97,65},{34,2},{35,3},{67,34... | collective-permute-start | bytes 4718600 | tf_op jit(solution)/shard_map/ppermute | solution.py:248
  196.5 9.9 %collective-permute-start.6 = (bf16[32,8192]{1,0:T(8,128)(2,1)S(1)}, bf16[32,8192]{1,0:T(8,128)(2,1)S(1)}, u32[]{:S(2)}, u32[]{:S(2)}) collective-permute-start(bf16[32,8192]{1,0:T(8,128)(2,1)S(1)} %convolution_convert_fusion.4), channel_id=1, source_target_pairs={{32,33},{33,32},{64,65},{65,64},{96,97},{97,96},{34,35},{35,34},{6... | collective-permute-start | bytes 1572872 | tf_op jit(solution)/shard_map/ppermute | solution.py:251
  198.8 29.6 %collective-permute-start.5 = (bf16[80,8192]{1,0:T(8,128)(2,1)S(1)}, bf16[80,8192]{1,0:T(8,128)(2,1)S(1)}, u32[]{:S(2)}, u32[]{:S(2)}) collective-permute-start(bf16[80,8192]{1,0:T(8,128)(2,1)S(1)} %multiply_convert_fusion.2), channel_id=1, source_target_pairs={{32,0},{33,1},{65,32},{64,33},{96,64},{97,65},{34,2},{35,3},{67,34... | collective-permute-start | bytes 3932168 | tf_op jit(solution)/shard_map/ppermute | solution.py:248
  207.0 21.4 %collective-permute-start.7 = (bf16[32,8192]{1,0:T(8,128)(2,1)S(1)}, bf16[32,8192]{1,0:T(8,128)(2,1)S(1)}, u32[]{:S(2)}, u32[]{:S(2)}) collective-permute-start(bf16[32,8192]{1,0:T(8,128)(2,1)S(1)} %multiply_convert_fusion.6), channel_id=1, source_target_pairs={{32,0},{33,1},{65,32},{64,33},{96,64},{97,65},{34,2},{35,3},{67,34... | collective-permute-start | bytes 1572872 | tf_op jit(solution)/shard_map/ppermute | solution.py:255
Sparse Core Ops, SparseCore 0:
  10.1 74.0 all-gather.1
  116.6 83.3 reduce-scatter.1

commit v18 on v16

--- a/solution.py
+++ b/solution.py
@@ -228,7 +228,7 @@
         for t in range(n_tensor)
     ]
     lowers = []
-    held = None
+    pending = None
     for c in range(chunks):
         sl = slice(bounds[c], bounds[c + 1])
         part = lax.dot_general(
@@ -238,20 +238,27 @@
         if c == 0:
             part_low, combined = lax.optimization_barrier((part_low, combined))
             grad_total = weight_grads(combined)
-        if held is not None:
+        if pending is not None:
+            prev_low, prev_recv, prev_sl = pending
             if len(lowers) > 0:
-                part_low, held, lowers[-1] = lax.optimization_barrier(
-                    (part_low, held, lowers[-1])
+                part_low, prev_recv, lowers[-1] = lax.optimization_barrier(
+                    (part_low, prev_recv, lowers[-1])
                 )
             else:
-                part_low, held = lax.optimization_barrier((part_low, held))
+                part_low, prev_recv = lax.optimization_barrier((part_low, prev_recv))
+        received = [lax.ppermute(part_low, ("pipe", "tensor"), pairs) for pairs in exchange_steps]
+        if pending is not None:
+            held = norm_backward(
+                sum([prev_low.astype(jnp.float32)] + [r.astype(jnp.float32) for r in prev_recv]),
+                gain_f, nhat[prev_sl], inv_rms[prev_sl],
+            )
             lowers.append(lax.ppermute(held, ("pipe", "tensor"), shift_pairs))
-        normed_grad = part_low.astype(jnp.float32)
-        for pairs in exchange_steps:
-            normed_grad = normed_grad + lax.ppermute(
-                part_low, ("pipe", "tensor"), pairs
-            ).astype(jnp.float32)
-        held = norm_backward(normed_grad, gain_f, nhat[sl], inv_rms[sl])
+        pending = (part_low, received, sl)
+    prev_low, prev_recv, prev_sl = pending
+    held = norm_backward(
+        sum([prev_low.astype(jnp.float32)] + [r.astype(jnp.float32) for r in prev_recv]),
+        gain_f, nhat[prev_sl], inv_rms[prev_sl],
+    )
     lowers.append(lax.ppermute(held, ("pipe", "tensor"), shift_pairs))
     lower = jnp.concatenate(lowers, axis=0)
     return (grad_total[:, :kv_cols][None], grad_total[:, kv_cols:][None], lower[None])

time: 240 us -> 249 us (1.038)
  waiting for transfers between devices: 145 us -> 153 us
    ppermute x4, waiting for transfers between devices: 48.6 us -> 79.8 us  [on_device(): lowers.append(lax.ppermute(held, ('pipe', 'tensor'), shift_pairs))]
    ppermute x4, waiting for transfers between devices: 29.4 us -> 6.87 us  [on_device(): lax.ppermute(part_low, ('pipe', 'tensor'), pairs)]
  transfers between devices with their start and end apart: 10 -> 10, of which waited for: 7 -> 6; matrix products, arithmetic and copies ran while one was open for 14% -> 11% of each run, Pallas kernels for 0% -> 0%
where the time goes in v18:
time: 249 us
  waiting for transfers between devices  153 us (61%)
  matrix products  31.9 us (13%)
  starting transfers between devices  18.4 us (7%)
  other arithmetic  18.3 us (7%)
  between operations  16.4 us (7%)
  Pallas kernels  8.83 us (4%)
    ppermute x4, waiting for transfers between devices, on_device(): lowers.append(lax.ppermute(held, ('pipe', 'tensor'), shift_pairs))  79.8 us
    all_gather x1, waiting for transfers between devices, on_device(): lax.all_gather(jnp.concatenate([key_weight[0], value_weight[0]], axis=1),...  66.4 us
    dot_general x4, matrix products, on_device(): lax.dot_general(combined[sl], both_full, (((1,), (1,)), ((), ())), prefer...  17.9 us
    ppermute x4, starting transfers between devices, on_device(): lax.ppermute(part_low, ('pipe', 'tensor'), pairs)  10.6 us
    pallas_call x1, Pallas kernels, attention_grads(): pl.pallas_call(kernel, grid_spec=pltpu.PrefetchScalarGridSpec(num_scalar_...  8.83 us
    dot_general x1, matrix products, on_device(): projected = jnp.dot(normed, both_full, preferred_element_type=jnp.float32)  7.86 us
    ppermute x4, starting transfers between devices, on_device(): lowers.append(lax.ppermute(held, ('pipe', 'tensor'), shift_pairs))  7.68 us
    ppermute x4, waiting for transfers between devices, on_device(): lax.ppermute(part_low, ('pipe', 'tensor'), pairs)  6.87 us
  transfers between devices with their start and end apart: 10, of which 6 were waited for; matrix products, arithmetic and copies ran while one was open for 11% of the time, Pallas kernels for 0%

profile of v18, /device:TPU:1, one launch (start us, length us, event | category | flops | bytes accessed | tf_op | source)
XLA Modules:
  0.0 248.9 jit_solution(15207286005054949556)
XLA Ops:
  13.5 3.1 %fusion = f32[256]{0:T(256)S(1)} fusion(bf16[1,256,8192]{2,1,0:T(8,128)(2,1)} %param.9), kind=kLoop, calls=%fused_computation.7 | loop fusion | flops 6291200 | bytes 4195328 | tf_op jit(solution)/shard_map/reduce_sum | solution.py:167
  17.8 66.4 %all-gather.2.cloned.1.call-done = bf16[8192,512]{1,0:T(8,128)(2,1)} async-done(((bf16[512,512]{1,0:T(8,128)(2,1)}), bf16[8192,512]{1,0:T(8,128)(2,1)}) %all-gather.2.cloned.1.call-update) | async-done | bytes 8388624 | tf_op jit(solution)/shard_map/all_gather | solution.py:155
  84.3 7.9 %fusion.2.k_ref.v_ref = f32[256,512]{1,0:T(8,128)} fusion(bf16[8192,512]{1,0:T(8,128)(2,1)} %all-gather.2.cloned.1.call-done, f32[8192]{0:T(1024)S(1)} %bitcast.36, bf16[1,256,8192]{2,1,0:T(8,128)(2,1)} %param.9, f32[256]{0:T(256)S(1)} %add_rsqrt_fusion), kind=kOutput, calls=%fused_computation.21 | convolution fusion | flops 2155872256 | bytes 13140992 | tf_op jit(solution)/shard_map/dot_general | solution.py:170
  92.1 8.8 %shard_map.112 = bf16[256,512]{1,0:T(8,128)(2,1)} custom-call(s32[1]{0:T(128)} %bitcast.32.len_ref, bf16[256,2048]{1,0:T(8,128)(2,1)} %bitcast.46, bf16[256,2048]{1,0:T(8,128)(2,1)} %fusion.1.c_ref, f32[256,512]{1,0:T(8,128)} %fusion.2.k_ref.v_ref, f32[256,512]{1,0:T(8,128)} %fusion.2.k_ref.v_ref, f32[256,128]{1,0:T(8,128)} %get-tuple-element.29.cos_ref, ...), custom_call_target="tpu_custom_call" | custom-call | tf_op jit(solution)/shard_map/pallas_call | solution.py:128
  101.0 6.2 %convolution_convert_fusion.3 = bf16[64,8192]{1,0:T(8,128)(2,1)S(1)} fusion(bf16[8192,512]{1,0:T(8,128)(2,1)} %all-gather.2.cloned.1.call-done, bf16[256,512]{1,0:T(8,128)(2,1)} %shard_map.112), kind=kOutput, calls=%fused_computation.5 | convolution fusion | flops 537395200 | bytes 9502720 | tf_op jit(solution)/shard_map/dot_general | solution.py:234
  107.2 6.1 %convolution_convert_fusion = bf16[8192,512]{1,0:T(8,128)(2,1)} fusion(bf16[256,512]{1,0:T(8,128)(2,1)S(1)} %copy-done.1, f32[8192]{0:T(1024)S(1)} %bitcast.37, bf16[1,256,8192]{2,1,0:T(8,128)(2,1)S(1)} %copy-done, f32[256]{0:T(256)S(1)} %add_rsqrt_fusion), kind=kOutput, calls=%fused_computation | convolution fusion | flops 2160066560 | bytes 12878848 | tf_op jit(solution)/shard_map/dot_general | solution.py:204
  113.3 3.3 %collective-permute-start = (bf16[64,8192]{1,0:T(8,128)(2,1)S(1)}, bf16[64,8192]{1,0:T(8,128)(2,1)S(1)}, u32[]{:S(2)}, u32[]{:S(2)}) collective-permute-start(bf16[64,8192]{1,0:T(8,128)(2,1)S(1)} %convolution_convert_fusion.3), channel_id=1, source_target_pairs={{32,33},{33,32},{64,65},{65,64},{96,97},{97,96},{34,35},{35,34},{6... | collective-permute-start | bytes 3145736 | tf_op jit(solution)/shard_map/ppermute | solution.py:249
  116.6 3.4 %convert_multiply_fusion = f32[256,8192]{1,0:T(8,128)S(1)} fusion(bf16[1,256,8192]{2,1,0:T(8,128)(2,1)} %param.9, f32[256]{0:T(256)S(1)} %add_rsqrt_fusion), kind=kLoop, calls=%fused_computation.1 | loop fusion | flops 4194304 | bytes 12583936 | tf_op jit(solution)/shard_map/mul | solution.py:168
  120.0 6.5 %convolution_convert_fusion.1 = bf16[80,8192]{1,0:T(8,128)(2,1)S(1)} fusion(bf16[8192,512]{1,0:T(8,128)(2,1)} %all-gather.2.cloned.1.call-done, bf16[256,512]{1,0:T(8,128)(2,1)S(1)} %copy-done.1), kind=kOutput, calls=%fused_computation.3 | convolution fusion | flops 671744000 | bytes 9781248 | tf_op jit(solution)/shard_map/dot_general | solution.py:234
  126.6 2.3 collective-permute-done
  128.9 3.1 %collective-permute-start.1 = (bf16[80,8192]{1,0:T(8,128)(2,1)S(1)}, bf16[80,8192]{1,0:T(8,128)(2,1)S(1)}, u32[]{:S(2)}, u32[]{:S(2)}) collective-permute-start(bf16[80,8192]{1,0:T(8,128)(2,1)S(1)} %convolution_convert_fusion.1), channel_id=1, source_target_pairs={{32,33},{33,32},{64,65},{65,64},{96,97},{97,96},{34,35},{35,34},{6... | collective-permute-start | bytes 3932168 | tf_op jit(solution)/shard_map/ppermute | solution.py:249
  133.0 1.9 collective-permute-start.2
  135.0 2.6 %convolution_convert_fusion.2 = bf16[80,8192]{1,0:T(8,128)(2,1)S(1)} fusion(bf16[8192,512]{1,0:T(8,128)(2,1)S(1)} %bitcast.35, bf16[256,512]{1,0:T(8,128)(2,1)S(1)} %copy-done.1), kind=kOutput, calls=%fused_computation.4 | convolution fusion | flops 671744000 | bytes 9781248 | tf_op jit(solution)/shard_map/dot_general | solution.py:234
  137.7 24.0 %collective-permute-done.2 = bf16[64,8192]{1,0:T(8,128)(2,1)S(1)} collective-permute-done((bf16[64,8192]{1,0:T(8,128)(2,1)S(1)}, bf16[64,8192]{1,0:T(8,128)(2,1)S(1)}, u32[]{:S(2)}, u32[]{:S(2)}) %collective-permute-start.2) | collective-permute-done | bytes 1048608 | tf_op jit(solution)/shard_map/ppermute | solution.py:255
  163.0 1.9 collective-permute-start.4
  164.9 2.2 collective-permute-start.3
  167.2 2.5 %convolution_convert_fusion.4 = bf16[32,8192]{1,0:T(8,128)(2,1)S(1)} fusion(bf16[8192,512]{1,0:T(8,128)(2,1)S(1)} %bitcast.35, bf16[256,512]{1,0:T(8,128)(2,1)S(1)} %copy-done.1), kind=kOutput, calls=%fused_computation.6 | convolution fusion | flops 268697600 | bytes 8945664 | tf_op jit(solution)/shard_map/dot_general | solution.py:234
  169.7 23.7 %collective-permute-done.4 = bf16[80,8192]{1,0:T(8,128)(2,1)S(1)} collective-permute-done((bf16[80,8192]{1,0:T(8,128)(2,1)S(1)}, bf16[80,8192]{1,0:T(8,128)(2,1)S(1)}, u32[]{:S(2)}, u32[]{:S(2)}) %collective-permute-start.4) | collective-permute-done | bytes 1310752 | tf_op jit(solution)/shard_map/ppermute | solution.py:255
  193.4 2.0 collective-permute-start.6
  196.8 1.9 collective-permute-start.5
  198.7 4.6 %collective-permute-done.6 = bf16[32,8192]{1,0:T(8,128)(2,1)S(1)} collective-permute-done((bf16[32,8192]{1,0:T(8,128)(2,1)S(1)}, bf16[32,8192]{1,0:T(8,128)(2,1)S(1)}, u32[]{:S(2)}, u32[]{:S(2)}) %collective-permute-start.6) | collective-permute-done | bytes 524320 | tf_op jit(solution)/shard_map/ppermute | solution.py:249
  204.0 1.9 collective-permute-start.7
  205.9 32.1 %collective-permute-done.7 = bf16[32,8192]{1,0:T(8,128)(2,1)S(1)} collective-permute-done((bf16[32,8192]{1,0:T(8,128)(2,1)S(1)}, bf16[32,8192]{1,0:T(8,128)(2,1)S(1)}, u32[]{:S(2)}, u32[]{:S(2)}) %collective-permute-start.7) | collective-permute-done | bytes 524320 | tf_op jit(solution)/shard_map/ppermute | solution.py:262
  238.0 2.2 maximum_bitcast_fusion
  (49 shorter events, 11.7 us)
Async XLA Ops:
  7.2 77.1 %all-gather.2.cloned.1.call-start = ((), (), s32[]{:S(2)}) async-start(), calls=%async_computation.1 | async-start | bytes 8912896 | tf_op jit(solution)/shard_map/all_gather | solution.py:155
  9.1 7.5 %copy-start.2 = (bf16[1,256,2048]{2,1,0:T(8,128)(2,1)S(1)}, bf16[1,256,2048]{2,1,0:T(8,128)(2,1)}, u32[]{:S(2)}) copy-start(bf16[1,256,2048]{2,1,0:T(8,128)(2,1)} %param.14) | copy-start | bytes 3145732
  9.1 231.1 %reduce-scatter.2.cloned.1.call-start = ((), (), s32[]{:S(2)}) async-start(), calls=%async_computation.2 | async-start | bytes 8912896 | tf_op jit(solution)/shard_map/reduce_scatter | solution.py:203
  16.6 103.4 %copy-start.3 = (f32[256]{0:T(256)}, f32[256]{0:T(256)S(1)}, u32[]{:S(2)}) copy-start(f32[256]{0:T(256)S(1)} %add_rsqrt_fusion) | copy-start | bytes 3076
  100.9 6.2 %copy-start = (bf16[1,256,8192]{2,1,0:T(8,128)(2,1)S(1)}, bf16[1,256,8192]{2,1,0:T(8,128)(2,1)}, u32[]{:S(2)}) copy-start(bf16[1,256,8192]{2,1,0:T(8,128)(2,1)} %param.9) | copy-start | bytes 12582916
  100.9 6.2 %copy-start.1 = (bf16[256,512]{1,0:T(8,128)(2,1)S(1)}, bf16[256,512]{1,0:T(8,128)(2,1)}, u32[]{:S(2)}) copy-start(bf16[256,512]{1,0:T(8,128)(2,1)} %shard_map.112) | copy-start | bytes 786436
  113.3 15.6 %collective-permute-start = (bf16[64,8192]{1,0:T(8,128)(2,1)S(1)}, bf16[64,8192]{1,0:T(8,128)(2,1)S(1)}, u32[]{:S(2)}, u32[]{:S(2)}) collective-permute-start(bf16[64,8192]{1,0:T(8,128)(2,1)S(1)} %convolution_convert_fusion.3), channel_id=1, source_target_pairs={{32,33},{33,32},{64,65},{65,64},{96,97},{97,96},{34,35},{35,34},{6... | collective-permute-start | bytes 3145736 | tf_op jit(solution)/shard_map/ppermute | solution.py:249
  116.6 18.5 %slice-start = ((s8[8388608]{0:T(1024)(128)(4,1)}), s8[4194304]{0:T(1024)(128)(4,1)S(1)}, s32[]{:S(2)}) async-start(s8[8388608]{0:T(1024)(128)(4,1)} %bitcast.34), calls=%async_computation.3 | async-start | bytes 8388608
  120.0 15.0 %slice-start.1 = ((s8[8388608]{0:T(1024)(128)(4,1)}), s8[4194304]{0:T(1024)(128)(4,1)S(1)}, s32[]{:S(2)}) async-start(s8[8388608]{0:T(1024)(128)(4,1)} %bitcast.34), calls=%async_computation.4 | async-start | bytes 8388608
  126.6 5.9 %slice-start.2 = ((f32[256]{0:T(256)}), f32[64]{0:T(128)S(1)}, s32[]{:S(2)}) async-start(f32[256]{0:T(256)} %copy-done.3), calls=%async_computation.5 | async-start | bytes 1024 | tf_op jit(solution)/shard_map/slice | solution.py:253
  128.9 32.8 %collective-permute-start.1 = (bf16[80,8192]{1,0:T(8,128)(2,1)S(1)}, bf16[80,8192]{1,0:T(8,128)(2,1)S(1)}, u32[]{:S(2)}, u32[]{:S(2)}) collective-permute-start(bf16[80,8192]{1,0:T(8,128)(2,1)S(1)} %convolution_convert_fusion.1), channel_id=1, source_target_pairs={{32,33},{33,32},{64,65},{65,64},{96,97},{97,96},{34,35},{35,34},{6... | collective-permute-start | bytes 3932168 | tf_op jit(solution)/shard_map/ppermute | solution.py:249
  132.5 2.5 copy-start.4
  133.0 28.6 %collective-permute-start.2 = (bf16[64,8192]{1,0:T(8,128)(2,1)S(1)}, bf16[64,8192]{1,0:T(8,128)(2,1)S(1)}, u32[]{:S(2)}, u32[]{:S(2)}) collective-permute-start(bf16[64,8192]{1,0:T(8,128)(2,1)S(1)} %multiply_convert_fusion.3), channel_id=1, source_target_pairs={{32,0},{33,1},{65,32},{64,33},{96,64},{97,65},{34,2},{35,3},{67,34... | collective-permute-start | bytes 3145736 | tf_op jit(solution)/shard_map/ppermute | solution.py:255
  163.0 30.5 %collective-permute-start.4 = (bf16[80,8192]{1,0:T(8,128)(2,1)S(1)}, bf16[80,8192]{1,0:T(8,128)(2,1)S(1)}, u32[]{:S(2)}, u32[]{:S(2)}) collective-permute-start(bf16[80,8192]{1,0:T(8,128)(2,1)S(1)} %multiply_convert_fusion.2), channel_id=1, source_target_pairs={{32,0},{33,1},{65,32},{64,33},{96,64},{97,65},{34,2},{35,3},{67,34... | collective-permute-start | bytes 3932168 | tf_op jit(solution)/shard_map/ppermute | solution.py:255
  164.9 28.5 %collective-permute-start.3 = (bf16[80,8192]{1,0:T(8,128)(2,1)S(1)}, bf16[80,8192]{1,0:T(8,128)(2,1)S(1)}, u32[]{:S(2)}, u32[]{:S(2)}) collective-permute-start(bf16[80,8192]{1,0:T(8,128)(2,1)S(1)} %convolution_convert_fusion.2), channel_id=1, source_target_pairs={{32,33},{33,32},{64,65},{65,64},{96,97},{97,96},{34,35},{35,34},{6... | collective-permute-start | bytes 3932168 | tf_op jit(solution)/shard_map/ppermute | solution.py:249
  193.4 9.9 %collective-permute-start.6 = (bf16[32,8192]{1,0:T(8,128)(2,1)S(1)}, bf16[32,8192]{1,0:T(8,128)(2,1)S(1)}, u32[]{:S(2)}, u32[]{:S(2)}) collective-permute-start(bf16[32,8192]{1,0:T(8,128)(2,1)S(1)} %convolution_convert_fusion.4), channel_id=1, source_target_pairs={{32,33},{33,32},{64,65},{65,64},{96,97},{97,96},{34,35},{35,34},{6... | collective-permute-start | bytes 1572872 | tf_op jit(solution)/shard_map/ppermute | solution.py:249
  196.8 41.2 %collective-permute-start.5 = (bf16[80,8192]{1,0:T(8,128)(2,1)S(1)}, bf16[80,8192]{1,0:T(8,128)(2,1)S(1)}, u32[]{:S(2)}, u32[]{:S(2)}) collective-permute-start(bf16[80,8192]{1,0:T(8,128)(2,1)S(1)} %multiply_convert_fusion.1), channel_id=1, source_target_pairs={{32,0},{33,1},{65,32},{64,33},{96,64},{97,65},{34,2},{35,3},{67,34... | collective-permute-start | bytes 3932168 | tf_op jit(solution)/shard_map/ppermute | solution.py:255
  204.0 34.0 %collective-permute-start.7 = (bf16[32,8192]{1,0:T(8,128)(2,1)S(1)}, bf16[32,8192]{1,0:T(8,128)(2,1)S(1)}, u32[]{:S(2)}, u32[]{:S(2)}) collective-permute-start(bf16[32,8192]{1,0:T(8,128)(2,1)S(1)} %multiply_convert_fusion.6), channel_id=1, source_target_pairs={{32,0},{33,1},{65,32},{64,33},{96,64},{97,65},{34,2},{35,3},{67,34... | collective-permute-start | bytes 1572872 | tf_op jit(solution)/shard_map/ppermute | solution.py:262
Sparse Core Ops, SparseCore 0:
  10.1 74.0 all-gather.1
  113.4 83.8 reduce-scatter.1

commit v19 on v17

--- a/solution.py
+++ b/solution.py
@@ -211,7 +211,7 @@
 
     n_pipe = lax.axis_size("pipe")
     n_tensor = lax.axis_size("tensor")
-    sizes = [tok_rows * 3 // 16, tok_rows * 3 // 8, tok_rows * 5 // 16, tok_rows // 8]
+    sizes = [tok_rows // 4, tok_rows * 3 // 8, tok_rows // 4, tok_rows // 8]
     bounds = [sum(sizes[:c]) for c in range(len(sizes) + 1)]
     chunks = len(sizes)
     exchange_steps = [

time: 240 us -> 239 us (level)
    ppermute x4, waiting for transfers between devices: 32.5 us -> 29.4 us  [on_device(): lax.ppermute(part_low, ('pipe', 'tensor'), pairs).astype(jnp.float32)]
  transfers between devices with their start and end apart: 10 -> 10, of which waited for: 6 -> 7; matrix products, arithmetic and copies ran while one was open for 14% -> 14% of each run, Pallas kernels for 0% -> 0%
where the time goes in v19:
time: 239 us; the launch traced here: 238 us
  waiting for transfers between devices  143 us (60%)
  matrix products  31.5 us (13%)
  other arithmetic  18.3 us (8%)
  starting transfers between devices  17.9 us (7%)
  between operations  16.3 us (7%)
  Pallas kernels  8.83 us (4%)
    all_gather x1, waiting for transfers between devices, on_device(): lax.all_gather(jnp.concatenate([key_weight[0], value_weight[0]], axis=1),...  66.4 us
    ppermute x4, waiting for transfers between devices, on_device(): lowers.append(lax.ppermute(held, ('pipe', 'tensor'), shift_pairs))  47.3 us
    ppermute x4, waiting for transfers between devices, on_device(): lax.ppermute(part_low, ('pipe', 'tensor'), pairs).astype(jnp.float32)  29.4 us
    dot_general x4, matrix products, on_device(): lax.dot_general(combined[sl], both_full, (((1,), (1,)), ((), ())), prefer...  17.5 us
    ppermute x4, starting transfers between devices, on_device(): lax.ppermute(part_low, ('pipe', 'tensor'), pairs).astype(jnp.float32)  10.2 us
    pallas_call x1, Pallas kernels, attention_grads(): pl.pallas_call(kernel, grid_spec=pltpu.PrefetchScalarGridSpec(num_scalar_...  8.83 us
    dot_general x1, matrix products, on_device(): projected = jnp.dot(normed, both_full, preferred_element_type=jnp.float32)  7.88 us
    ppermute x4, starting transfers between devices, on_device(): lowers.append(lax.ppermute(held, ('pipe', 'tensor'), shift_pairs))  7.68 us
  transfers between devices with their start and end apart: 10, of which 7 were waited for; matrix products, arithmetic and copies ran while one was open for 14% of the time, Pallas kernels for 0%

profile of v19, /device:TPU:1, one launch (start us, length us, event | category | flops | bytes accessed | tf_op | source)
XLA Modules:
  0.0 238.1 jit_solution(17411067167691804180)
XLA Ops:
  7.2 2.0 pad_maximum_fusion
  13.5 3.1 %fusion = f32[256]{0:T(256)S(1)} fusion(bf16[1,256,8192]{2,1,0:T(8,128)(2,1)} %param.9), kind=kLoop, calls=%fused_computation.7 | loop fusion | flops 6291200 | bytes 4195328 | tf_op jit(solution)/shard_map/reduce_sum | solution.py:167
  17.9 66.4 %all-gather.2.cloned.1.call-done = bf16[8192,512]{1,0:T(8,128)(2,1)} async-done(((bf16[512,512]{1,0:T(8,128)(2,1)}), bf16[8192,512]{1,0:T(8,128)(2,1)}) %all-gather.2.cloned.1.call-update) | async-done | bytes 8388624 | tf_op jit(solution)/shard_map/all_gather | solution.py:155
  84.3 7.9 %fusion.2.k_ref.v_ref = f32[256,512]{1,0:T(8,128)} fusion(bf16[8192,512]{1,0:T(8,128)(2,1)} %all-gather.2.cloned.1.call-done, f32[8192]{0:T(1024)S(1)} %bitcast.36, bf16[1,256,8192]{2,1,0:T(8,128)(2,1)} %param.9, f32[256]{0:T(256)S(1)} %add_rsqrt_fusion), kind=kOutput, calls=%fused_computation.21 | convolution fusion | flops 2155872256 | bytes 13140992 | tf_op jit(solution)/shard_map/dot_general | solution.py:170
  92.1 8.8 %shard_map.112 = bf16[256,512]{1,0:T(8,128)(2,1)} custom-call(s32[1]{0:T(128)} %bitcast.32.len_ref, bf16[256,2048]{1,0:T(8,128)(2,1)} %bitcast.46, bf16[256,2048]{1,0:T(8,128)(2,1)} %fusion.1.c_ref, f32[256,512]{1,0:T(8,128)} %fusion.2.k_ref.v_ref, f32[256,512]{1,0:T(8,128)} %fusion.2.k_ref.v_ref, f32[256,128]{1,0:T(8,128)} %get-tuple-element.29.cos_ref, ...), custom_call_target="tpu_custom_call" | custom-call | tf_op jit(solution)/shard_map/pallas_call | solution.py:128
  101.0 6.2 %convolution_convert_fusion.3 = bf16[64,8192]{1,0:T(8,128)(2,1)S(1)} fusion(bf16[8192,512]{1,0:T(8,128)(2,1)} %all-gather.2.cloned.1.call-done, bf16[256,512]{1,0:T(8,128)(2,1)} %shard_map.112), kind=kOutput, calls=%fused_computation.5 | convolution fusion | flops 537395200 | bytes 9502720 | tf_op jit(solution)/shard_map/dot_general | solution.py:234
  107.2 3.3 %collective-permute-start = (bf16[64,8192]{1,0:T(8,128)(2,1)S(1)}, bf16[64,8192]{1,0:T(8,128)(2,1)S(1)}, u32[]{:S(2)}, u32[]{:S(2)}) collective-permute-start(bf16[64,8192]{1,0:T(8,128)(2,1)S(1)} %convolution_convert_fusion.3), channel_id=1, source_target_pairs={{32,33},{33,32},{64,65},{65,64},{96,97},{97,96},{34,35},{35,34},{6... | collective-permute-start | bytes 3145736 | tf_op jit(solution)/shard_map/ppermute | solution.py:251
  110.5 6.1 %convolution_convert_fusion = bf16[8192,512]{1,0:T(8,128)(2,1)} fusion(bf16[256,512]{1,0:T(8,128)(2,1)S(1)} %copy-done.1, f32[8192]{0:T(1024)S(1)} %bitcast.37, bf16[1,256,8192]{2,1,0:T(8,128)(2,1)S(1)} %copy-done, f32[256]{0:T(256)S(1)} %add_rsqrt_fusion), kind=kOutput, calls=%fused_computation | convolution fusion | flops 2160066560 | bytes 12878848 | tf_op jit(solution)/shard_map/dot_general | solution.py:204
  116.6 3.4 %convert_multiply_fusion = f32[256,8192]{1,0:T(8,128)S(1)} fusion(bf16[1,256,8192]{2,1,0:T(8,128)(2,1)} %param.9, f32[256]{0:T(256)S(1)} %add_rsqrt_fusion), kind=kLoop, calls=%fused_computation.1 | loop fusion | flops 4194304 | bytes 12583936 | tf_op jit(solution)/shard_map/mul | solution.py:168
  120.1 6.2 %convolution_convert_fusion.1 = bf16[96,8192]{1,0:T(8,128)(2,1)S(1)} fusion(bf16[8192,512]{1,0:T(8,128)(2,1)} %all-gather.2.cloned.1.call-done, bf16[256,512]{1,0:T(8,128)(2,1)S(1)} %copy-done.1), kind=kOutput, calls=%fused_computation.3 | convolution fusion | flops 806092800 | bytes 10059776 | tf_op jit(solution)/shard_map/dot_general | solution.py:234
  127.3 2.2 collective-permute-start.1
  129.6 2.6 %convolution_convert_fusion.2 = bf16[64,8192]{1,0:T(8,128)(2,1)S(1)} fusion(bf16[8192,512]{1,0:T(8,128)(2,1)S(1)} %bitcast.35, bf16[256,512]{1,0:T(8,128)(2,1)S(1)} %copy-done.1), kind=kOutput, calls=%fused_computation.4 | convolution fusion | flops 537395200 | bytes 9502720 | tf_op jit(solution)/shard_map/dot_general | solution.py:234
  132.2 1.9 collective-permute-start.2
  134.2 14.7 %collective-permute-done.1 = bf16[96,8192]{1,0:T(8,128)(2,1)S(1)} collective-permute-done((bf16[96,8192]{1,0:T(8,128)(2,1)S(1)}, bf16[96,8192]{1,0:T(8,128)(2,1)S(1)}, u32[]{:S(2)}, u32[]{:S(2)}) %collective-permute-start.1) | collective-permute-done | bytes 1572896 | tf_op jit(solution)/shard_map/ppermute | solution.py:251
  150.4 7.5 %collective-permute-done.2 = bf16[64,8192]{1,0:T(8,128)(2,1)S(1)} collective-permute-done((bf16[64,8192]{1,0:T(8,128)(2,1)S(1)}, bf16[64,8192]{1,0:T(8,128)(2,1)S(1)}, u32[]{:S(2)}, u32[]{:S(2)}) %collective-permute-start.2) | collective-permute-done | bytes 1048608 | tf_op jit(solution)/shard_map/ppermute | solution.py:248
  157.9 2.5 %collective-permute-start.3 = (bf16[64,8192]{1,0:T(8,128)(2,1)S(1)}, bf16[64,8192]{1,0:T(8,128)(2,1)S(1)}, u32[]{:S(2)}, u32[]{:S(2)}) collective-permute-start(bf16[64,8192]{1,0:T(8,128)(2,1)S(1)} %convolution_convert_fusion.2), channel_id=1, source_target_pairs={{32,33},{33,32},{64,65},{65,64},{96,97},{97,96},{34,35},{35,34},{6... | collective-permute-start | bytes 3145736 | tf_op jit(solution)/shard_map/ppermute | solution.py:251
  160.4 2.5 %convolution_convert_fusion.4 = bf16[32,8192]{1,0:T(8,128)(2,1)S(1)} fusion(bf16[8192,512]{1,0:T(8,128)(2,1)S(1)} %bitcast.35, bf16[256,512]{1,0:T(8,128)(2,1)S(1)} %copy-done.1), kind=kOutput, calls=%fused_computation.6 | convolution fusion | flops 268697600 | bytes 8945664 | tf_op jit(solution)/shard_map/dot_general | solution.py:234
  162.9 1.9 collective-permute-start.4
  164.9 8.9 %collective-permute-done.3 = bf16[64,8192]{1,0:T(8,128)(2,1)S(1)} collective-permute-done((bf16[64,8192]{1,0:T(8,128)(2,1)S(1)}, bf16[64,8192]{1,0:T(8,128)(2,1)S(1)}, u32[]{:S(2)}, u32[]{:S(2)}) %collective-permute-start.3) | collective-permute-done | bytes 1048608 | tf_op jit(solution)/shard_map/ppermute | solution.py:251
  174.9 27.1 %collective-permute-done.4 = bf16[96,8192]{1,0:T(8,128)(2,1)S(1)} collective-permute-done((bf16[96,8192]{1,0:T(8,128)(2,1)S(1)}, bf16[96,8192]{1,0:T(8,128)(2,1)S(1)}, u32[]{:S(2)}, u32[]{:S(2)}) %collective-permute-start.4) | collective-permute-done | bytes 1572896 | tf_op jit(solution)/shard_map/ppermute | solution.py:248
  202.0 2.2 collective-permute-start.6
  206.1 5.7 %collective-permute-done.6 = bf16[32,8192]{1,0:T(8,128)(2,1)S(1)} collective-permute-done((bf16[32,8192]{1,0:T(8,128)(2,1)S(1)}, bf16[32,8192]{1,0:T(8,128)(2,1)S(1)}, u32[]{:S(2)}, u32[]{:S(2)}) %collective-permute-start.6) | collective-permute-done | bytes 524320 | tf_op jit(solution)/shard_map/ppermute | solution.py:251
  214.4 12.7 %collective-permute-done.7 = bf16[32,8192]{1,0:T(8,128)(2,1)S(1)} collective-permute-done((bf16[32,8192]{1,0:T(8,128)(2,1)S(1)}, bf16[32,8192]{1,0:T(8,128)(2,1)S(1)}, u32[]{:S(2)}, u32[]{:S(2)}) %collective-permute-start.7) | collective-permute-done | bytes 524320 | tf_op jit(solution)/shard_map/ppermute | solution.py:255
  227.2 2.2 maximum_bitcast_fusion
  (44 shorter events, 13.6 us)
Async XLA Ops:
  7.2 77.1 %all-gather.2.cloned.1.call-start = ((), (), s32[]{:S(2)}) async-start(), calls=%async_computation.1 | async-start | bytes 8912896 | tf_op jit(solution)/shard_map/all_gather | solution.py:155
  7.2 9.4 %copy-start.2 = (bf16[1,256,2048]{2,1,0:T(8,128)(2,1)S(1)}, bf16[1,256,2048]{2,1,0:T(8,128)(2,1)}, u32[]{:S(2)}) copy-start(bf16[1,256,2048]{2,1,0:T(8,128)(2,1)} %param.14) | copy-start | bytes 3145732
  9.2 220.2 %reduce-scatter.2.cloned.1.call-start = ((), (), s32[]{:S(2)}) async-start(), calls=%async_computation.2 | async-start | bytes 8912896 | tf_op jit(solution)/shard_map/reduce_scatter | solution.py:203
  101.0 9.5 %copy-start = (bf16[1,256,8192]{2,1,0:T(8,128)(2,1)S(1)}, bf16[1,256,8192]{2,1,0:T(8,128)(2,1)}, u32[]{:S(2)}) copy-start(bf16[1,256,8192]{2,1,0:T(8,128)(2,1)} %param.9) | copy-start | bytes 12582916
  101.0 9.5 %copy-start.1 = (bf16[256,512]{1,0:T(8,128)(2,1)S(1)}, bf16[256,512]{1,0:T(8,128)(2,1)}, u32[]{:S(2)}) copy-start(bf16[256,512]{1,0:T(8,128)(2,1)} %shard_map.112) | copy-start | bytes 786436
  107.2 19.1 %collective-permute-start = (bf16[64,8192]{1,0:T(8,128)(2,1)S(1)}, bf16[64,8192]{1,0:T(8,128)(2,1)S(1)}, u32[]{:S(2)}, u32[]{:S(2)}) collective-permute-start(bf16[64,8192]{1,0:T(8,128)(2,1)S(1)} %convolution_convert_fusion.3), channel_id=1, source_target_pairs={{32,33},{33,32},{64,65},{65,64},{96,97},{97,96},{34,35},{35,34},{6... | collective-permute-start | bytes 3145736 | tf_op jit(solution)/shard_map/ppermute | solution.py:251
  116.6 13.0 %slice-start = ((s8[8388608]{0:T(1024)(128)(4,1)}), s8[4194304]{0:T(1024)(128)(4,1)S(1)}, s32[]{:S(2)}) async-start(s8[8388608]{0:T(1024)(128)(4,1)} %bitcast.34), calls=%async_computation.3 | async-start | bytes 8388608
  120.1 9.5 %slice-start.1 = ((s8[8388608]{0:T(1024)(128)(4,1)}), s8[4194304]{0:T(1024)(128)(4,1)S(1)}, s32[]{:S(2)}) async-start(s8[8388608]{0:T(1024)(128)(4,1)} %bitcast.34), calls=%async_computation.4 | async-start | bytes 8388608
  127.3 21.6 %collective-permute-start.1 = (bf16[96,8192]{1,0:T(8,128)(2,1)S(1)}, bf16[96,8192]{1,0:T(8,128)(2,1)S(1)}, u32[]{:S(2)}, u32[]{:S(2)}) collective-permute-start(bf16[96,8192]{1,0:T(8,128)(2,1)S(1)} %convolution_convert_fusion.1), channel_id=1, source_target_pairs={{32,33},{33,32},{64,65},{65,64},{96,97},{97,96},{34,35},{35,34},{6... | collective-permute-start | bytes 4718600 | tf_op jit(solution)/shard_map/ppermute | solution.py:251
  132.2 25.6 %collective-permute-start.2 = (bf16[64,8192]{1,0:T(8,128)(2,1)S(1)}, bf16[64,8192]{1,0:T(8,128)(2,1)S(1)}, u32[]{:S(2)}, u32[]{:S(2)}) collective-permute-start(bf16[64,8192]{1,0:T(8,128)(2,1)S(1)} %multiply_convert_fusion.3), channel_id=1, source_target_pairs={{32,0},{33,1},{65,32},{64,33},{96,64},{97,65},{34,2},{35,3},{67,34... | collective-permute-start | bytes 3145736 | tf_op jit(solution)/shard_map/ppermute | solution.py:248
  157.9 15.9 %collective-permute-start.3 = (bf16[64,8192]{1,0:T(8,128)(2,1)S(1)}, bf16[64,8192]{1,0:T(8,128)(2,1)S(1)}, u32[]{:S(2)}, u32[]{:S(2)}) collective-permute-start(bf16[64,8192]{1,0:T(8,128)(2,1)S(1)} %convolution_convert_fusion.2), channel_id=1, source_target_pairs={{32,33},{33,32},{64,65},{65,64},{96,97},{97,96},{34,35},{35,34},{6... | collective-permute-start | bytes 3145736 | tf_op jit(solution)/shard_map/ppermute | solution.py:251
  162.9 39.0 %collective-permute-start.4 = (bf16[96,8192]{1,0:T(8,128)(2,1)S(1)}, bf16[96,8192]{1,0:T(8,128)(2,1)S(1)}, u32[]{:S(2)}, u32[]{:S(2)}) collective-permute-start(bf16[96,8192]{1,0:T(8,128)(2,1)S(1)} %multiply_convert_fusion.1), channel_id=1, source_target_pairs={{32,0},{33,1},{65,32},{64,33},{96,64},{97,65},{34,2},{35,3},{67,34... | collective-permute-start | bytes 4718600 | tf_op jit(solution)/shard_map/ppermute | solution.py:248
  202.0 9.9 %collective-permute-start.6 = (bf16[32,8192]{1,0:T(8,128)(2,1)S(1)}, bf16[32,8192]{1,0:T(8,128)(2,1)S(1)}, u32[]{:S(2)}, u32[]{:S(2)}) collective-permute-start(bf16[32,8192]{1,0:T(8,128)(2,1)S(1)} %convolution_convert_fusion.4), channel_id=1, source_target_pairs={{32,33},{33,32},{64,65},{65,64},{96,97},{97,96},{34,35},{35,34},{6... | collective-permute-start | bytes 1572872 | tf_op jit(solution)/shard_map/ppermute | solution.py:251
  204.2 22.9 %collective-permute-start.5 = (bf16[64,8192]{1,0:T(8,128)(2,1)S(1)}, bf16[64,8192]{1,0:T(8,128)(2,1)S(1)}, u32[]{:S(2)}, u32[]{:S(2)}) collective-permute-start(bf16[64,8192]{1,0:T(8,128)(2,1)S(1)} %multiply_convert_fusion.2), channel_id=1, source_target_pairs={{32,0},{33,1},{65,32},{64,33},{96,64},{97,65},{34,2},{35,3},{67,34... | collective-permute-start | bytes 3145736 | tf_op jit(solution)/shard_map/ppermute | solution.py:248
  212.5 14.7 %collective-permute-start.7 = (bf16[32,8192]{1,0:T(8,128)(2,1)S(1)}, bf16[32,8192]{1,0:T(8,128)(2,1)S(1)}, u32[]{:S(2)}, u32[]{:S(2)}) collective-permute-start(bf16[32,8192]{1,0:T(8,128)(2,1)S(1)} %multiply_convert_fusion.6), channel_id=1, source_target_pairs={{32,0},{33,1},{65,32},{64,33},{96,64},{97,65},{34,2},{35,3},{67,34... | collective-permute-start | bytes 1572872 | tf_op jit(solution)/shard_map/ppermute | solution.py:255
Sparse Core Ops, SparseCore 0:
  10.1 74.0 all-gather.1
  116.7 83.5 reduce-scatter.1
